TPU v7x, 32 devices: a whole 2x2x4 slice. The times are simulated.
32 devices in a mesh: grp: 2 (over x), ep: 16 (over z, y, core).
Axes of the slice: x: 2, y: 2, z: 4, core: 2. Of those that a mesh axis runs over, the one named last changes fastest.
Arguments:
- tokens: bfloat16 [2048, 7168], P(('grp', 'ep')), parts along dimension 0, may hold values from -6 to 6
- parents: int32 [2048], P(('grp', 'ep')), parts along dimension 0, may hold values from -1 to 62, as said below
- expert_ids: int32 [2048, 1], P(('grp', 'ep')), parts along dimension 0, may hold values from 0 to 1; in each aligned block of 64 rows (0 to 63, 64 to 127, ...) at most 40 rows name the same one
- route_weights: float32 [2048, 1], P(('grp', 'ep')), parts along dimension 0, may hold values from 0.2 to 2
- w_gate: bfloat16 [16, 7168, 256], P('ep'), may hold values from -0.0625 to 0.0625
- w_up: bfloat16 [16, 7168, 256], P('ep'), may hold values from -0.0625 to 0.0625
- w_down: bfloat16 [16, 256, 7168], P('ep'), may hold values from -0.125 to 0.125
Outputs:
- expert_out: bfloat16 [2048, 7168], P(('grp', 'ep')), parts along dimension 0
There are 2 independent parts, one for each index of `grp`. A program takes and returns all parts, laid end to end along the dimension named above; an argument that names none is the same for every part. Nothing has to cross between parts.
Inputs may be any that keep to these rules, and one draw needn't show every extreme that they name: `parents`: rows 64 * r to 64 * r + 63 form request r. Its first node is the root with parent -1; node n of a request has a parent below n, given as its index within the request. The last node of the last request has parent 64 - 2. `expert_ids`: each row names 1 different experts; among the rows of one device no expert is named more than 40 times, and in every draw some device names some expert exactly 40 times.
All inputs are finite; a program needn't handle non-finite values.
Results may differ from a plain program's by a relative error of at most 0.0072.
Values may be sent and summed in bfloat16 or wider, within the bound.
No kernel may reach another device: no remote copies, remote signals or barrier semaphores. Data moves between devices by JAX's collectives and lax.ppermute only.
A program may use at most 128 MiB of HBM per device.

v0:
```python
import jax
import jax.numpy as jnp
from jax import lax
from jax.sharding import PartitionSpec as P

SLICES = 8


def slice_ffn(rows, gate_w, up_w, down_w):
    gate = jnp.dot(rows, gate_w, preferred_element_type=jnp.float32)
    upper = jnp.dot(rows, up_w, preferred_element_type=jnp.float32)
    hidden = (jax.nn.silu(gate) * upper).astype(jnp.bfloat16)
    return jnp.dot(hidden, down_w, preferred_element_type=jnp.float32).astype(jnp.bfloat16)


def shards(tokens, parents, expert_ids, route_weights, w_gate, w_up, w_down):
    count, width = tokens.shape
    picks_row = expert_ids.shape[1]
    devices = lax.axis_size("ep")
    experts = devices // SLICES
    slots = 5 * count * picks_row // (4 * experts)
    nodes = jnp.arange(count, dtype=jnp.int32)
    parent_hot = (parents[:, None] == nodes[None, :]).astype(jnp.bfloat16)
    lifted = tokens.astype(jnp.float32) + jnp.dot(
        parent_hot, tokens, preferred_element_type=jnp.float32
    )
    normed = (lifted * lax.rsqrt(jnp.mean(lifted * lifted, axis=1, keepdims=True) + 1e-06)).astype(
        jnp.bfloat16
    )
    picks = expert_ids[:, :, None] == jnp.arange(experts, dtype=jnp.int32)[None, None, :]
    chosen = jnp.any(picks, axis=1).astype(jnp.int32)
    before = jnp.cumsum(chosen, axis=0) - chosen
    slot_iota = jnp.arange(slots, dtype=jnp.int32)
    place = (chosen[:, :, None] * (before[:, :, None] == slot_iota[None, None, :])).astype(
        jnp.float32
    )
    weight_te = jnp.sum(jnp.where(picks, route_weights[:, :, None], 0.0), axis=1)
    packed = jnp.einsum(
        "tec,td->ecd", place.astype(jnp.bfloat16), normed, preferred_element_type=jnp.float32
    ).astype(jnp.bfloat16)
    spread = jnp.broadcast_to(packed[:, None], (experts, SLICES, slots, width)).reshape(
        devices, slots, width
    )
    received = lax.all_to_all(spread, "ep", split_axis=0, concat_axis=0, tiled=True)
    sources, items, columns = received.shape
    outputs = slice_ffn(received.reshape(sources * items, columns), w_gate[0], w_up[0], w_down[0])
    returned = lax.all_to_all(
        outputs.reshape(sources, items, columns), "ep", split_axis=0, concat_axis=0, tiled=True
    )
    summed = jnp.sum(returned.astype(jnp.float32).reshape(experts, SLICES, slots, width), axis=1)
    weighted = place * weight_te[:, :, None]
    result = jnp.einsum(
        "tec,ecd->td",
        weighted,
        summed,
        preferred_element_type=jnp.float32,
        precision=lax.Precision.HIGHEST,
    )
    return result.astype(jnp.bfloat16)


def solution(mesh):
    placed = (
        P(("grp", "ep"), None),
        P(("grp", "ep")),
        P(("grp", "ep"), None),
        P(("grp", "ep"), None),
        P("ep", None, None),
        P("ep", None, None),
        P("ep", None, None),
    )
    return jax.shard_map(
        shards, mesh=mesh, in_specs=placed, out_specs=P(("grp", "ep"), None), check_vma=False
    )
```

profile of v0, /device:TPU:15, one launch (start us, length us, event | category | flops | bytes accessed | tf_op | source)
XLA Modules:
  0.0 449.3 jit_solution(6266789740144781522)
XLA Ops:
  0.0 0.7 fusion.27
  0.7 0.1 copy.9
  0.8 0.1 reduce_window_sum.11
  0.9 0.7 fusion.36
  1.6 0.1 copy.8
  1.7 2.1 multiply_reduce_fusion
  3.8 0.5 convolution_convert_fusion.1
  4.3 1.1 broadcast_in_dim.12
  5.5 0.0 copy-start.3
  5.5 205.6 %all_to_all.10 = bf16[16,40,7168]{2,1,0:T(8,128)(2,1)S(1)} all-to-all(bf16[16,40,7168]{2,1,0:T(8,128)(2,1)S(1)} %bitcast.37), channel_id=1, replica_groups=mesh['grp'=2,'ep'=16] {'ep'}, dimensions={0} | all-to-all | bytes 18350080 | tf_op jit(solution)/shard_map/all_to_all | solution.py:44
  211.1 0.0 copy-start
  211.1 3.5 copy-done
  214.6 0.0 copy-done.3
  214.6 2.5 fusion.4
  217.2 18.9 %convolution_convert_fusion = bf16[640,7168]{1,0:T(8,128)(2,1)} fusion(bf16[1,256,7168]{2,1,0:T(8,128)(2,1)} %param.13, bf16[640,7168]{1,0:T(8,128)(2,1)} %bitcast.36, bf16[1,7168,256]{2,1,0:T(8,128)(2,1)} %param.12, f32[640,256]{1,0:T(8,128)S(1)} %fusion.4), kind=kOutput, calls=%fused_computation.1 | convolution fusion | flops 4703191040 | bytes 26345472 | tf_op jit(solution)/shard_map/dot_general | solution.py:13
  236.0 0.0 copy-start.1
  236.0 0.0 copy-start.2
  236.0 5.9 %all-to-all-start.1 = ((bf16[16,40,7168]{2,1,0:T(8,128)(2,1)}), bf16[16,40,7168]{2,1,0:T(8,128)(2,1)}, u32[]{:S(2)}, u32[]{:S(2)}) async-start(bf16[16,40,7168]{2,1,0:T(8,128)(2,1)} %bitcast.34), calls=%async_computation.1 | async-start | bytes 18350080 | tf_op jit(solution)/shard_map/all_to_all | solution.py:47
  241.9 0.0 copy-done.1
  242.0 0.0 copy-done.2
  242.0 0.1 fusion.26
  242.0 0.1 copy.10
  242.1 199.0 %all-to-all-done.1 = bf16[16,40,7168]{2,1,0:T(8,128)(2,1)} async-done(((bf16[16,40,7168]{2,1,0:T(8,128)(2,1)}), bf16[16,40,7168]{2,1,0:T(8,128)(2,1)}, u32[]{:S(2)}, u32[]{:S(2)}) %all-to-all-start.1) | async-done | bytes 9175072 | tf_op jit(solution)/shard_map/all_to_all | solution.py:47
  441.2 5.3 %convert_reduce_fusion = f32[2,40,7168]{2,1,0:T(8,128)S(1)} fusion(bf16[16,40,7168]{2,1,0:T(8,128)(2,1)} %all-to-all-done.1), kind=kLoop, calls=%fused_computation | loop fusion | flops 8601600 | bytes 11468800 | tf_op jit(solution)/shard_map/reduce_sum | solution.py:50
  446.5 2.8 fusion
  (1 shorter events, 0.0 us)
Async XLA Ops:
  5.5 209.2 %copy-start.3 = (bf16[1,7168,256]{2,1,0:T(8,128)(2,1)S(1)}, bf16[1,7168,256]{2,1,0:T(8,128)(2,1)}, u32[]{:S(2)}) copy-start(bf16[1,7168,256]{2,1,0:T(8,128)(2,1)} %param.11) | copy-start | bytes 11010052
  211.1 3.6 copy-start
  236.0 5.9 %copy-start.1 = (s32[64,1]{0,1:T(1,128)S(1)}, s32[64,1]{0,1:T(1,128)}, u32[]{:S(2)}) copy-start(s32[64,1]{0,1:T(1,128)} %param.9) | copy-start | bytes 772
  236.0 5.9 %copy-start.2 = (f32[64,1]{0,1:T(1,128)S(1)}, f32[64,1]{0,1:T(1,128)}, u32[]{:S(2)}) copy-start(f32[64,1]{0,1:T(1,128)} %param.10) | copy-start | bytes 772
  236.0 205.1 %all-to-all-start.1 = ((bf16[16,40,7168]{2,1,0:T(8,128)(2,1)}), bf16[16,40,7168]{2,1,0:T(8,128)(2,1)}, u32[]{:S(2)}, u32[]{:S(2)}) async-start(bf16[16,40,7168]{2,1,0:T(8,128)(2,1)} %bitcast.34), calls=%async_computation.1 | async-start | bytes 18350080 | tf_op jit(solution)/shard_map/all_to_all | solution.py:47
where the time goes:
time: 450 us; the launch traced here: 449 us
  blocking collectives  206 us (46%)
  waiting for transfers between devices  199 us (44%)
  matrix products  26.8 us (6%)
  other arithmetic  6.96 us (2%)
  starting transfers between devices  5.91 us (1%)
  local copies, waits for them, and re-layouts  4.89 us (1%)
    all_to_all x1, blocking collectives, shards(): lax.all_to_all(spread, 'ep', split_axis=0, concat_axis=0, tiled=True)  206 us
    all_to_all x1, waiting for transfers between devices, shards(): lax.all_to_all(outputs.reshape(sources, items, columns), 'ep', split_axis...  199 us
    dot_general x1, matrix products, slice_ffn(): jnp.dot(hidden, down_w, preferred_element_type=jnp.float32)  18.9 us
  transfers between devices with their start and end apart: 1, of which 1 were waited for; matrix products, arithmetic and copies ran while one was open for 0% of the time, Pallas kernels for 0%

commit v1 on v0

v1 whole, which is shorter than its diff:
```python
import jax
import jax.numpy as jnp
from jax import lax
from jax.sharding import Mesh
from jax.sharding import PartitionSpec as P

SLICES = 8


def slice_ffn(rows, gate_w, up_w, down_w):
    gate = jnp.dot(rows, gate_w, preferred_element_type=jnp.float32)
    upper = jnp.dot(rows, up_w, preferred_element_type=jnp.float32)
    hidden = (jax.nn.silu(gate) * upper).astype(jnp.bfloat16)
    return jnp.dot(hidden, down_w, preferred_element_type=jnp.float32).astype(jnp.bfloat16)


def shards(tokens, parents, expert_ids, route_weights, w_gate, w_up, w_down):
    count, width = tokens.shape
    picks_row = expert_ids.shape[1]
    experts = lax.axis_size("eg")
    slices = lax.axis_size("sl")
    slots = 5 * count * picks_row // (4 * experts)
    nodes = jnp.arange(count, dtype=jnp.int32)
    parent_hot = (parents[:, None] == nodes[None, :]).astype(jnp.bfloat16)
    lifted = tokens.astype(jnp.float32) + jnp.dot(
        parent_hot, tokens, preferred_element_type=jnp.float32
    )
    normed = (lifted * lax.rsqrt(jnp.mean(lifted * lifted, axis=1, keepdims=True) + 1e-06)).astype(
        jnp.bfloat16
    )
    picks = expert_ids[:, :, None] == jnp.arange(experts, dtype=jnp.int32)[None, None, :]
    chosen = jnp.any(picks, axis=1).astype(jnp.int32)
    before = jnp.cumsum(chosen, axis=0) - chosen
    slot_iota = jnp.arange(slots, dtype=jnp.int32)
    place = (chosen[:, :, None] * (before[:, :, None] == slot_iota[None, None, :])) > 0
    weight_te = jnp.sum(jnp.where(picks, route_weights[:, :, None], 0.0), axis=1)
    packed = jnp.einsum(
        "tec,td->ecd", place.astype(jnp.bfloat16), normed, preferred_element_type=jnp.float32
    ).astype(jnp.bfloat16)
    packed_w = jnp.sum(jnp.where(place, weight_te[:, :, None], 0.0), axis=0)
    mine = lax.all_to_all(packed, "eg", split_axis=0, concat_axis=0, tiled=True)
    mine_w = lax.all_to_all(packed_w, "eg", split_axis=0, concat_axis=0, tiled=True)
    held = mine.reshape(experts * slots, width)
    gathered = lax.all_gather(held, "sl", axis=0, tiled=True)
    parts = slice_ffn(gathered, w_gate[0], w_up[0], w_down[0])
    back = lax.all_to_all(
        parts.reshape(slices, experts * slots, width), "sl", split_axis=0, concat_axis=0, tiled=True
    )
    summed = jnp.sum(back.astype(jnp.float32), axis=0)
    weighted = (summed * mine_w.reshape(experts * slots, 1)).astype(jnp.bfloat16)
    home = lax.all_to_all(
        weighted.reshape(experts, slots, width), "eg", split_axis=0, concat_axis=0, tiled=True
    )
    result = jnp.einsum(
        "tec,ecd->td", place.astype(jnp.bfloat16), home, preferred_element_type=jnp.float32
    )
    return result.astype(jnp.bfloat16)


def solution(mesh):
    groups, ranks = mesh.devices.shape
    experts = ranks // SLICES
    split = Mesh(mesh.devices.reshape(groups, experts, SLICES), ("grp", "eg", "sl"))
    rows = ("grp", "eg", "sl")
    placed = (
        P(rows, None),
        P(rows),
        P(rows, None),
        P(rows, None),
        P(("eg", "sl"), None, None),
        P(("eg", "sl"), None, None),
        P(("eg", "sl"), None, None),
    )
    return jax.shard_map(
        shards, mesh=split, in_specs=placed, out_specs=P(rows, None), check_vma=False
    )
```

time: 450 us -> 275 us (0.61)
  the two profiles are of different devices: /device:TPU:15 before, /device:TPU:0 now
where the time goes in v1:
time: 275 us
  waiting for transfers between devices  150 us (55%)
  blocking collectives  64.1 us (23%)
  matrix products  30.1 us (11%)
  between operations  13.5 us (5%)
  starting transfers between devices  8.83 us (3%)
  other arithmetic  7.89 us (3%)
    all_to_all x1, waiting for transfers between devices, shards(): lax.all_to_all(parts.reshape(slices, experts * slots, width), 'sl', split...  101 us
    all_gather x1, waiting for transfers between devices, shards(): gathered = lax.all_gather(held, 'sl', axis=0, tiled=True)  49.3 us
    all_to_all x1, blocking collectives, shards(): mine = lax.all_to_all(packed, 'eg', split_axis=0, concat_axis=0, tiled=True)  33 us
    all_to_all x1, blocking collectives, shards(): lax.all_to_all(weighted.reshape(experts, slots, width), 'eg', split_axis=...  31.1 us
    dot_general x1, matrix products, slice_ffn(): jnp.dot(hidden, down_w, preferred_element_type=jnp.float32)  18.9 us
    dot_general x1, matrix products, slice_ffn(): gate = jnp.dot(rows, gate_w, preferred_element_type=jnp.float32)  7.17 us
  transfers between devices with their start and end apart: 3, of which 2 were waited for; matrix products, arithmetic and copies ran while one was open for 2% of the time, Pallas kernels for 0%

profile of v1, /device:TPU:0, one launch (start us, length us, event | category | flops | bytes accessed | tf_op | source)
XLA Modules:
  0.0 274.7 jit_solution(15553781186721040926)
XLA Ops:
  6.5 0.0 all-gather.2.cloned.1.call-start
  6.5 0.7 fusion.24
  7.3 0.1 copy.12
  7.3 0.1 reduce_window_sum.11
  7.4 0.7 fusion.32
  8.2 0.1 copy.11
  8.2 2.1 multiply_reduce_fusion
  10.4 0.5 convolution_convert_fusion.1
  10.9 33.0 %all_to_all.24 = bf16[2,40,7168]{2,1,0:T(8,128)(2,1)} all-to-all(bf16[2,40,7168]{2,1,0:T(8,128)(2,1)S(1)} %convolution_convert_fusion.1), channel_id=1, replica_groups=mesh['grp'=2,'eg'=2,'sl'=8] {'eg'}, dimensions={0} | all-to-all | bytes 2293760 | tf_op jit(solution)/shard_map/all_to_all | solution.py:41
  44.0 0.0 all-gather.2.cloned.1.call-update
  44.0 49.3 %all-gather.2.cloned.1.call-done = bf16[640,7168]{1,0:T(8,128)(2,1)} async-done(((bf16[80,7168]{1,0:T(8,128)(2,1)}), bf16[640,7168]{1,0:T(8,128)(2,1)}) %all-gather.2.cloned.1.call-update) | async-done | bytes 9175056 | tf_op jit(solution)/shard_map/all_gather | solution.py:44
  93.3 7.2 %fusion.4 = f32[640,256]{1,0:T(8,128)S(1)} fusion(bf16[640,7168]{1,0:T(8,128)(2,1)} %all-gather.2.cloned.1.call-done, bf16[1,7168,256]{2,1,0:T(8,128)(2,1)} %param.11), kind=kOutput, calls=%fused_computation.9 | convolution fusion | flops 2348810240 | bytes 13500416 | tf_op jit(solution)/shard_map/dot_general | solution.py:11
  100.5 18.9 %convolution_convert_fusion = bf16[640,7168]{1,0:T(8,128)(2,1)} fusion(bf16[1,256,7168]{2,1,0:T(8,128)(2,1)} %param.13, bf16[640,7168]{1,0:T(8,128)(2,1)} %all-gather.2.cloned.1.call-done, bf16[1,7168,256]{2,1,0:T(8,128)(2,1)} %param.12, f32[640,256]{1,0:T(8,128)S(1)} %fusion.4), kind=kOutput, calls=%fused_computation.1 | convolution fusion | flops 4703191040 | bytes 26345472 | tf_op jit(solution)/shard_map/dot_general | solution.py:14
  119.4 0.0 copy-start
  119.4 0.0 copy-start.1
  119.4 5.1 %all-to-all-start.1 = ((bf16[8,80,7168]{2,1,0:T(8,128)(2,1)}), bf16[8,80,7168]{2,1,0:T(8,128)(2,1)}, u32[]{:S(2)}, u32[]{:S(2)}) async-start(bf16[8,80,7168]{2,1,0:T(8,128)(2,1)} %bitcast.35), calls=%async_computation.1 | async-start | bytes 18350080 | tf_op jit(solution)/shard_map/all_to_all | solution.py:46
  124.6 0.0 copy-done
  124.6 0.0 copy-done.1
  124.6 0.1 fusion.23
  124.7 0.1 copy.13
  124.7 0.7 select_reduce_fusion
  125.4 100.7 %all-to-all-done.1 = bf16[8,80,7168]{2,1,0:T(8,128)(2,1)} async-done(((bf16[8,80,7168]{2,1,0:T(8,128)(2,1)}), bf16[8,80,7168]{2,1,0:T(8,128)(2,1)}, u32[]{:S(2)}, u32[]{:S(2)}) %all-to-all-start.1) | async-done | bytes 9175072 | tf_op jit(solution)/shard_map/all_to_all | solution.py:46
  226.1 3.7 %all-to-all-start.2 = ((f32[2,1,40]{2,1,0:T(1,128)}), f32[2,1,40]{2,1,0:T(1,128)S(1)}, u32[]{:S(2)}, u32[]{:S(2)}) async-start(f32[2,1,40]{2,1,0:T(1,128)} %bitcast.10), calls=%async_computation.2 | async-start | bytes 2048 | tf_op jit(solution)/shard_map/all_to_all | solution.py:42
  229.8 5.4 %convert_reduce_fusion = f32[80,7168]{1,0:T(8,128)S(1)} fusion(bf16[8,80,7168]{2,1,0:T(8,128)(2,1)} %all-to-all-done.1), kind=kLoop, calls=%fused_computation | loop fusion | flops 8601600 | bytes 11468800 | tf_op jit(solution)/shard_map/reduce_sum | solution.py:49
  235.1 0.0 all-to-all-done.2
  235.2 0.2 multiply_convert_fusion
  235.4 31.1 %all_to_all.25 = bf16[2,40,7168]{2,1,0:T(8,128)(2,1)S(1)} all-to-all(bf16[2,40,7168]{2,1,0:T(8,128)(2,1)S(1)} %multiply_convert_fusion), channel_id=1, replica_groups=mesh['grp'=2,'eg'=2,'sl'=8] {'eg'}, dimensions={0} | all-to-all | bytes 2293760 | tf_op jit(solution)/shard_map/all_to_all | solution.py:51
  266.4 1.4 fusion
  (1 shorter events, 0.0 us)
Async XLA Ops:
  6.5 86.8 %all-gather.2.cloned.1.call-start = ((), (), s32[]{:S(2)}) async-start(), calls=%async_computation.4 | async-start | bytes 10321920 | tf_op jit(solution)/shard_map/all_gather | solution.py:44
  119.4 5.2 %copy-start = (s32[64,1]{0,1:T(1,128)S(1)}, s32[64,1]{0,1:T(1,128)}, u32[]{:S(2)}) copy-start(s32[64,1]{0,1:T(1,128)} %param.9) | copy-start | bytes 772
  119.4 5.2 %copy-start.1 = (f32[64,1]{0,1:T(1,128)S(1)}, f32[64,1]{0,1:T(1,128)}, u32[]{:S(2)}) copy-start(f32[64,1]{0,1:T(1,128)} %param.10) | copy-start | bytes 772
  119.4 106.7 %all-to-all-start.1 = ((bf16[8,80,7168]{2,1,0:T(8,128)(2,1)}), bf16[8,80,7168]{2,1,0:T(8,128)(2,1)}, u32[]{:S(2)}, u32[]{:S(2)}) async-start(bf16[8,80,7168]{2,1,0:T(8,128)(2,1)} %bitcast.35), calls=%async_computation.1 | async-start | bytes 18350080 | tf_op jit(solution)/shard_map/all_to_all | solution.py:46
  226.1 9.1 %all-to-all-start.2 = ((f32[2,1,40]{2,1,0:T(1,128)}), f32[2,1,40]{2,1,0:T(1,128)S(1)}, u32[]{:S(2)}, u32[]{:S(2)}) async-start(f32[2,1,40]{2,1,0:T(1,128)} %bitcast.10), calls=%async_computation.2 | async-start | bytes 2048 | tf_op jit(solution)/shard_map/all_to_all | solution.py:42
Sparse Core Ops, SparseCore 0:
  44.1 49.1 all-gather.1

commit v2 on v1

--- a/solution.py
+++ b/solution.py
@@ -18,7 +18,8 @@
     count, width = tokens.shape
     picks_row = expert_ids.shape[1]
     experts = lax.axis_size("eg")
-    slices = lax.axis_size("sl")
+    chips = lax.axis_size("sc")
+    cores = lax.axis_size("core")
     slots = 5 * count * picks_row // (4 * experts)
     nodes = jnp.arange(count, dtype=jnp.int32)
     parent_hot = (parents[:, None] == nodes[None, :]).astype(jnp.bfloat16)
@@ -41,10 +42,13 @@
     mine = lax.all_to_all(packed, "eg", split_axis=0, concat_axis=0, tiled=True)
     mine_w = lax.all_to_all(packed_w, "eg", split_axis=0, concat_axis=0, tiled=True)
     held = mine.reshape(experts * slots, width)
-    gathered = lax.all_gather(held, "sl", axis=0, tiled=True)
+    gathered = lax.all_gather(held, ("core", "sc"), axis=0, tiled=True)
     parts = slice_ffn(gathered, w_gate[0], w_up[0], w_down[0])
+    paired = lax.psum_scatter(
+        parts.reshape(cores, chips * experts * slots, width), "core", scatter_dimension=0, tiled=True
+    )
     back = lax.all_to_all(
-        parts.reshape(slices, experts * slots, width), "sl", split_axis=0, concat_axis=0, tiled=True
+        paired.reshape(chips, experts * slots, width), "sc", split_axis=0, concat_axis=0, tiled=True
     )
     summed = jnp.sum(back.astype(jnp.float32), axis=0)
     weighted = (summed * mine_w.reshape(experts * slots, 1)).astype(jnp.bfloat16)
@@ -60,16 +64,19 @@
 def solution(mesh):
     groups, ranks = mesh.devices.shape
     experts = ranks // SLICES
-    split = Mesh(mesh.devices.reshape(groups, experts, SLICES), ("grp", "eg", "sl"))
-    rows = ("grp", "eg", "sl")
+    cores = 2
+    split = Mesh(
+        mesh.devices.reshape(groups, experts, SLICES // cores, cores), ("grp", "eg", "sc", "core")
+    )
+    rows = ("grp", "eg", "sc", "core")
     placed = (
         P(rows, None),
         P(rows),
         P(rows, None),
         P(rows, None),
-        P(("eg", "sl"), None, None),
-        P(("eg", "sl"), None, None),
-        P(("eg", "sl"), None, None),
+        P(("eg", "sc", "core"), None, None),
+        P(("eg", "sc", "core"), None, None),
+        P(("eg", "sc", "core"), None, None),
     )
     return jax.shard_map(
         shards, mesh=split, in_specs=placed, out_specs=P(rows, None), check_vma=False

time: 275 us -> 241 us (0.88)
  waiting for transfers between devices: 150 us -> 120 us
    all_to_all x1, waiting for transfers between devices: 101 us -> 51.6 us  [shards(): lax.all_to_all(paired.reshape(chips, experts * slots, width), 'sc', split...]
    reduce_scatter x0 -> x1, waiting for transfers between devices: none -> 17.6 us  [shards(): lax.psum_scatter(parts.reshape(cores, chips * experts * slots, width), 'c...]
  transfers between devices with their start and end apart: 3 -> 4, of which waited for: 2 -> 4; matrix products, arithmetic and copies ran while one was open for 2% -> 2% of each run, Pallas kernels for 0% -> 0%
where the time goes in v2:
time: 241 us
  waiting for transfers between devices  120 us (50%)
  blocking collectives  62.4 us (26%)
  matrix products  30.1 us (12%)
  between operations  13.5 us (6%)
  starting transfers between devices  8.96 us (4%)
  other arithmetic  5.74 us (2%)
    all_to_all x1, waiting for transfers between devices, shards(): lax.all_to_all(paired.reshape(chips, experts * slots, width), 'sc', split...  51.6 us
    all_gather x1, waiting for transfers between devices, shards(): gathered = lax.all_gather(held, ('core', 'sc'), axis=0, tiled=True)  49.3 us
    all_to_all x1, blocking collectives, shards(): mine = lax.all_to_all(packed, 'eg', split_axis=0, concat_axis=0, tiled=True)  33 us
    all_to_all x1, blocking collectives, shards(): lax.all_to_all(weighted.reshape(experts, slots, width), 'eg', split_axis=...  29.4 us
    dot_general x1, matrix products, slice_ffn(): jnp.dot(hidden, down_w, preferred_element_type=jnp.float32)  18.9 us
    reduce_scatter x1, waiting for transfers between devices, shards(): lax.psum_scatter(parts.reshape(cores, chips * experts * slots, width), 'c...  17.6 us
    dot_general x1, matrix products, slice_ffn(): gate = jnp.dot(rows, gate_w, preferred_element_type=jnp.float32)  7.17 us
    all_to_all x1, starting transfers between devices, shards(): lax.all_to_all(paired.reshape(chips, experts * slots, width), 'sc', split...  5.08 us
  transfers between devices with their start and end apart: 4, of which 4 were waited for; matrix products, arithmetic and copies ran while one was open for 2% of the time, Pallas kernels for 0%

profile of v2, /device:TPU:0, one launch (start us, length us, event | category | flops | bytes accessed | tf_op | source)
XLA Modules:
  0.0 240.8 jit_solution(5281493341241450761)
XLA Ops:
  6.5 0.0 all-gather.2.cloned.1.call-start
  6.5 0.7 fusion.24
  7.3 0.1 copy.12
  7.3 0.1 reduce_window_sum.11
  7.4 0.7 fusion.32
  8.2 0.1 copy.11
  8.2 2.1 multiply_reduce_fusion
  10.4 0.5 convolution_convert_fusion.1
  10.9 33.0 %all_to_all.24 = bf16[2,40,7168]{2,1,0:T(8,128)(2,1)} all-to-all(bf16[2,40,7168]{2,1,0:T(8,128)(2,1)S(1)} %convolution_convert_fusion.1), channel_id=1, replica_groups=mesh['grp'=2,'eg'=2,'sc'=4,'core'=2] {'eg'}, dimensions={0} | all-to-all | bytes 2293760 | tf_op jit(solution)/shard_map/all_to_all | solution.py:42
  44.0 0.0 all-gather.2.cloned.1.call-update
  44.0 0.0 reduce-scatter.2.cloned.1.call-start
  44.0 49.3 %all-gather.2.cloned.1.call-done = bf16[640,7168]{1,0:T(8,128)(2,1)} async-done(((bf16[80,7168]{1,0:T(8,128)(2,1)}), bf16[640,7168]{1,0:T(8,128)(2,1)}) %all-gather.2.cloned.1.call-update) | async-done | bytes 9175056 | tf_op jit(solution)/shard_map/all_gather | solution.py:45
  93.3 7.2 %fusion.4 = f32[640,256]{1,0:T(8,128)S(1)} fusion(bf16[640,7168]{1,0:T(8,128)(2,1)} %all-gather.2.cloned.1.call-done, bf16[1,7168,256]{2,1,0:T(8,128)(2,1)} %param.11), kind=kOutput, calls=%fused_computation.9 | convolution fusion | flops 2348810240 | bytes 13500416 | tf_op jit(solution)/shard_map/dot_general | solution.py:11
  100.5 18.9 %convolution_convert_fusion = bf16[640,7168]{1,0:T(8,128)(2,1)} fusion(bf16[1,256,7168]{2,1,0:T(8,128)(2,1)} %param.13, bf16[640,7168]{1,0:T(8,128)(2,1)} %all-gather.2.cloned.1.call-done, bf16[1,7168,256]{2,1,0:T(8,128)(2,1)} %param.12, f32[640,256]{1,0:T(8,128)S(1)} %fusion.4), kind=kOutput, calls=%fused_computation | convolution fusion | flops 4703191040 | bytes 26345472 | tf_op jit(solution)/shard_map/dot_general | solution.py:14
  119.4 0.0 reduce-scatter.2.cloned.1.call-update
  119.4 17.6 %reduce-scatter.2.cloned.1.call-done = bf16[1,320,7168]{2,1,0:T(8,128)(2,1)} async-done(((bf16[2,320,7168]{2,1,0:T(8,128)(2,1)}), bf16[1,320,7168]{2,1,0:T(8,128)(2,1)}) %reduce-scatter.2.cloned.1.call-update) | async-done | bytes 4587536 | tf_op jit(solution)/shard_map/reduce_scatter | solution.py:47
  137.1 0.0 copy-start
  137.1 0.0 copy-start.1
  137.1 5.1 %all-to-all-start.1 = ((bf16[4,80,7168]{2,1,0:T(8,128)(2,1)}), bf16[4,80,7168]{2,1,0:T(8,128)(2,1)}, u32[]{:S(2)}, u32[]{:S(2)}) async-start(bf16[4,80,7168]{2,1,0:T(8,128)(2,1)} %bitcast.38), calls=%async_computation.2 | async-start | bytes 9175040 | tf_op jit(solution)/shard_map/all_to_all | solution.py:50
  142.1 0.0 copy-done
  142.2 0.0 copy-done.1
  142.2 0.1 fusion.23
  142.2 0.1 copy.13
  142.3 0.7 select_reduce_fusion
  143.0 51.6 %all-to-all-done.1 = bf16[4,80,7168]{2,1,0:T(8,128)(2,1)} async-done(((bf16[4,80,7168]{2,1,0:T(8,128)(2,1)}), bf16[4,80,7168]{2,1,0:T(8,128)(2,1)}, u32[]{:S(2)}, u32[]{:S(2)}) %all-to-all-start.1) | async-done | bytes 4587552 | tf_op jit(solution)/shard_map/all_to_all | solution.py:50
  194.6 3.8 %all-to-all-start.2 = ((f32[2,1,40]{2,1,0:T(1,128)}), f32[2,1,40]{2,1,0:T(1,128)S(1)}, u32[]{:S(2)}, u32[]{:S(2)}) async-start(f32[2,1,40]{2,1,0:T(1,128)} %bitcast.11), calls=%async_computation.3 | async-start | bytes 2048 | tf_op jit(solution)/shard_map/all_to_all | solution.py:43
  198.4 3.2 %convert_reduce_fusion = f32[80,7168]{1,0:T(8,128)S(1)} fusion(bf16[4,80,7168]{2,1,0:T(8,128)(2,1)} %all-to-all-done.1), kind=kLoop, calls=%fused_computation.1 | loop fusion | flops 4014080 | bytes 6881280 | tf_op jit(solution)/shard_map/reduce_sum | solution.py:53
  201.7 1.4 all-to-all-done.2
  203.0 0.2 multiply_convert_fusion
  203.2 29.4 %all_to_all.25 = bf16[2,40,7168]{2,1,0:T(8,128)(2,1)S(1)} all-to-all(bf16[2,40,7168]{2,1,0:T(8,128)(2,1)S(1)} %multiply_convert_fusion), channel_id=1, replica_groups=mesh['grp'=2,'eg'=2,'sc'=4,'core'=2] {'eg'}, dimensions={0} | all-to-all | bytes 2293760 | tf_op jit(solution)/shard_map/all_to_all | solution.py:55
  232.6 1.4 fusion
  (1 shorter events, 0.0 us)
Async XLA Ops:
  6.5 86.8 %all-gather.2.cloned.1.call-start = ((), (), s32[]{:S(2)}) async-start(), calls=%async_computation.5 | async-start | bytes 10321920 | tf_op jit(solution)/shard_map/all_gather | solution.py:45
  44.0 93.1 %reduce-scatter.2.cloned.1.call-start = ((), (), s32[]{:S(2)}) async-start(), calls=%async_computation.6 | async-start | bytes 13762560 | tf_op jit(solution)/shard_map/reduce_scatter | solution.py:47
  137.1 5.1 %copy-start = (s32[64,1]{0,1:T(1,128)S(1)}, s32[64,1]{0,1:T(1,128)}, u32[]{:S(2)}) copy-start(s32[64,1]{0,1:T(1,128)} %param.9) | copy-start | bytes 772
  137.1 5.1 %copy-start.1 = (f32[64,1]{0,1:T(1,128)S(1)}, f32[64,1]{0,1:T(1,128)}, u32[]{:S(2)}) copy-start(f32[64,1]{0,1:T(1,128)} %param.10) | copy-start | bytes 772
  137.1 57.5 %all-to-all-start.1 = ((bf16[4,80,7168]{2,1,0:T(8,128)(2,1)}), bf16[4,80,7168]{2,1,0:T(8,128)(2,1)}, u32[]{:S(2)}, u32[]{:S(2)}) async-start(bf16[4,80,7168]{2,1,0:T(8,128)(2,1)} %bitcast.38), calls=%async_computation.2 | async-start | bytes 9175040 | tf_op jit(solution)/shard_map/all_to_all | solution.py:50
  194.6 8.4 %all-to-all-start.2 = ((f32[2,1,40]{2,1,0:T(1,128)}), f32[2,1,40]{2,1,0:T(1,128)S(1)}, u32[]{:S(2)}, u32[]{:S(2)}) async-start(f32[2,1,40]{2,1,0:T(1,128)} %bitcast.11), calls=%async_computation.3 | async-start | bytes 2048 | tf_op jit(solution)/shard_map/all_to_all | solution.py:43
Sparse Core Ops, SparseCore 0:
  44.1 49.1 all-gather.1
  119.5 17.4 reduce-scatter.1

commit v3 on v2

v3 whole, which is shorter than its diff:
```python
import jax
import jax.numpy as jnp
from jax import lax
from jax.sharding import Mesh
from jax.sharding import PartitionSpec as P

SLICES = 8


def slice_ffn(rows, gate_w, up_w, down_w):
    gate = jnp.dot(rows, gate_w, preferred_element_type=jnp.float32)
    upper = jnp.dot(rows, up_w, preferred_element_type=jnp.float32)
    hidden = (jax.nn.silu(gate) * upper).astype(jnp.bfloat16)
    return jnp.dot(hidden, down_w, preferred_element_type=jnp.float32).astype(jnp.bfloat16)


def expert_rows(held, weights, gate_w, up_w, down_w):
    chips = lax.axis_size("sc")
    cores = lax.axis_size("core")
    count, width = held.shape
    gathered = lax.all_gather(held, ("core", "sc"), axis=0, tiled=True)
    parts = slice_ffn(gathered, gate_w, up_w, down_w)
    paired = lax.psum_scatter(
        parts.reshape(cores, chips * count, width), "core", scatter_dimension=0, tiled=True
    )
    back = lax.all_to_all(
        paired.reshape(chips, count, width), "sc", split_axis=0, concat_axis=0, tiled=True
    )
    summed = jnp.sum(back.astype(jnp.float32), axis=0)
    return (summed * weights[:, None]).astype(jnp.bfloat16)


def shards(tokens, parents, expert_ids, route_weights, w_gate, w_up, w_down):
    count, width = tokens.shape
    picks_row = expert_ids.shape[1]
    experts = lax.axis_size("eg")
    group = lax.axis_index("eg")
    slots = 5 * count * picks_row // (4 * experts)
    nodes = jnp.arange(count, dtype=jnp.int32)
    parent_hot = (parents[:, None] == nodes[None, :]).astype(jnp.bfloat16)
    lifted = tokens.astype(jnp.float32) + jnp.dot(
        parent_hot, tokens, preferred_element_type=jnp.float32
    )
    normed = (lifted * lax.rsqrt(jnp.mean(lifted * lifted, axis=1, keepdims=True) + 1e-06)).astype(
        jnp.bfloat16
    )
    relative = (expert_ids - group) % experts
    picks = relative[:, :, None] == jnp.arange(experts, dtype=jnp.int32)[None, None, :]
    chosen = jnp.any(picks, axis=1).astype(jnp.int32)
    before = jnp.cumsum(chosen, axis=0) - chosen
    slot_iota = jnp.arange(slots, dtype=jnp.int32)
    place = (chosen[:, :, None] * (before[:, :, None] == slot_iota[None, None, :])) > 0
    weight_te = jnp.sum(jnp.where(picks, route_weights[:, :, None], 0.0), axis=1)
    packed = jnp.einsum(
        "tkc,td->kcd", place.astype(jnp.bfloat16), normed, preferred_element_type=jnp.float32
    ).astype(jnp.bfloat16)
    packed_w = jnp.sum(jnp.where(place, weight_te[:, :, None], 0.0), axis=0)
    weights = (w_gate[0], w_up[0], w_down[0])

    def shift(k):
        return [(g, (g + k) % experts) for g in range(experts)]

    away = [lax.ppermute(packed[k], "eg", shift(k)) for k in range(1, experts)]
    away_w = [lax.ppermute(packed_w[k], "eg", shift(k)) for k in range(1, experts)]
    own = expert_rows(packed[0], packed_w[0], *weights)
    done = expert_rows(
        jnp.concatenate(away, axis=0), jnp.concatenate(away_w, axis=0), *weights
    )
    home = [own] + [
        lax.ppermute(done[(k - 1) * slots:k * slots], "eg", shift(experts - k))
        for k in range(1, experts)
    ]
    result = jnp.einsum(
        "tkc,kcd->td",
        place.astype(jnp.bfloat16),
        jnp.stack(home),
        preferred_element_type=jnp.float32,
    )
    return result.astype(jnp.bfloat16)


def solution(mesh):
    groups, ranks = mesh.devices.shape
    experts = ranks // SLICES
    cores = 2
    split = Mesh(
        mesh.devices.reshape(groups, experts, SLICES // cores, cores), ("grp", "eg", "sc", "core")
    )
    rows = ("grp", "eg", "sc", "core")
    placed = (
        P(rows, None),
        P(rows),
        P(rows, None),
        P(rows, None),
        P(("eg", "sc", "core"), None, None),
        P(("eg", "sc", "core"), None, None),
        P(("eg", "sc", "core"), None, None),
    )
    return jax.shard_map(
        shards, mesh=split, in_specs=placed, out_specs=P(rows, None), check_vma=False
    )
```

time: 241 us -> 205 us (0.85)
  blocking collectives: 62.4 us -> 0 us
  waiting for transfers between devices: 120 us -> 140 us
  starting transfers between devices: 8.96 us -> 18.2 us
  matrix products: 30.1 us -> 23.9 us
  local copies, waits for them, and re-layouts: 0.22 us -> 5.1 us
    all_to_all x2 -> x0, blocking collectives: 62.4 us -> none  [the longest x1 33 us: shards(): mine = lax.all_to_all(packed, 'eg', split_axis=0, concat_axis=0, tiled=True)]
    ppermute x0 -> x3, waiting for transfers between devices: none -> 49.5 us  [the longest x1 25.3 us: shards(): away = [lax.ppermute(packed[k], 'eg', shift(k)) for k in range(1, experts)]]
    all_to_all x2, waiting for transfers between devices: 53 us -> 39.4 us  [expert_rows(): lax.all_to_all(paired.reshape(chips, count, width), 'sc', split_axis=0, c...]
    all_gather x1 -> x2, waiting for transfers between devices: 49.3 us -> 36.3 us  [expert_rows(): gathered = lax.all_gather(held, ('core', 'sc'), axis=0, tiled=True)]
    dot_general x1 -> x2, matrix products: 18.9 us -> 7.34 us  [slice_ffn(): jnp.dot(hidden, down_w, preferred_element_type=jnp.float32)]
    ppermute x0 -> x3, starting transfers between devices: none -> 9.49 us  [the longest x1 4.11 us: shards(): away = [lax.ppermute(packed[k], 'eg', shift(k)) for k in range(1, experts)]]
    dot_general x2 -> x4, matrix products: 1.9 us -> 8.23 us  [the longest x2 6.33 us: slice_ffn(): upper = jnp.dot(rows, up_w, preferred_element_type=jnp.float32)]
    unnamed x4 -> x16, local copies, waits for them, and re-layouts: 0.01 us -> 3.99 us
  transfers between devices with their start and end apart: 4 -> 9, of which waited for: 4 -> 8; matrix products, arithmetic and copies ran while one was open for 2% -> 11% of each run, Pallas kernels for 0% -> 0%
where the time goes in v3:
time: 205 us; the launch traced here: 204 us
  waiting for transfers between devices  140 us (68%)
  matrix products  23.9 us (12%)
  starting transfers between devices  18.2 us (9%)
  between operations  13.2 us (6%)
  local copies, waits for them, and re-layouts  5.1 us (2%)
  other arithmetic  3.89 us (2%)
    all_to_all x2, waiting for transfers between devices, expert_rows(): lax.all_to_all(paired.reshape(chips, count, width), 'sc', split_axis=0, c...  39.4 us
    all_gather x2, waiting for transfers between devices, expert_rows(): gathered = lax.all_gather(held, ('core', 'sc'), axis=0, tiled=True)  36.3 us
    ppermute x1, waiting for transfers between devices, shards(): away = [lax.ppermute(packed[k], 'eg', shift(k)) for k in range(1, experts)]  25.3 us
    ppermute x1, waiting for transfers between devices, shards(): lax.ppermute(done[(k - 1) * slots:k * slots], 'eg', shift(experts - k))  24.2 us
    reduce_scatter x2, waiting for transfers between devices, expert_rows(): lax.psum_scatter(parts.reshape(cores, chips * count, width), 'core', scat...  14.9 us
    all_to_all x2, starting transfers between devices, expert_rows(): lax.all_to_all(paired.reshape(chips, count, width), 'sc', split_axis=0, c...  8.57 us
    dot_general x2, matrix products, slice_ffn(): jnp.dot(hidden, down_w, preferred_element_type=jnp.float32)  7.34 us
    dot_general x2, matrix products, slice_ffn(): upper = jnp.dot(rows, up_w, preferred_element_type=jnp.float32)  6.33 us
  transfers between devices with their start and end apart: 9, of which 8 were waited for; matrix products, arithmetic and copies ran while one was open for 11% of the time, Pallas kernels for 0%

profile of v3, /device:TPU:0, one launch (start us, length us, event | category | flops | bytes accessed | tf_op | source)
XLA Modules:
  0.0 204.5 jit_solution(12947237742108732540)
XLA Ops:
  6.5 0.7 fusion.41
  7.2 0.1 fusion.32
  7.3 0.1 copy.9
  7.4 0.1 reduce_window_sum.11
  7.5 0.1 fusion.40
  7.5 0.1 copy.8
  7.6 2.1 %multiply_reduce_fusion = (f32[64]{0:T(128)S(1)}, f32[64,7168]{1,0:T(8,128)S(1)}) fusion(bf16[64,7168]{1,0:T(8,128)(2,1)} %param.7, s32[64]{0:T(128)} %param.8), kind=kOutput, calls=%fused_computation.21 | convolution fusion | flops 60559296 | bytes 2753024 | tf_op jit(solution)/shard_map/dot_general | solution.py:41
  9.7 0.5 convolution_convert_fusion.2
  10.2 0.9 fusion.47
  11.1 0.0 all-gather.6.cloned.1.call-update
  11.1 0.0 all-gather.4.cloned.1.call-start
  11.2 4.1 %collective-permute-start = (bf16[40,7168]{1,0:T(8,128)(2,1)S(1)}, bf16[40,7168]{1,0:T(8,128)(2,1)S(1)}, u32[]{:S(2)}, u32[]{:S(2)}) collective-permute-start(bf16[40,7168]{1,0:T(8,128)(2,1)S(1)} %get-tuple-element.6), channel_id=1, source_target_pairs={{0,8},{8,0},{1,9},{9,1},{2,10},{10,2},{3,11},{11,3},{4,12},{12,4},... | collective-permute-start | bytes 1720328 | tf_op jit(solution)/shard_map/ppermute | solution.py:63
  15.3 25.3 %collective-permute-done = bf16[40,7168]{1,0:T(8,128)(2,1)S(1)} collective-permute-done((bf16[40,7168]{1,0:T(8,128)(2,1)S(1)}, bf16[40,7168]{1,0:T(8,128)(2,1)S(1)}, u32[]{:S(2)}, u32[]{:S(2)}) %collective-permute-start) | collective-permute-done | bytes 573472 | tf_op jit(solution)/shard_map/ppermute | solution.py:63
  40.6 0.8 copy-done.2
  41.4 0.0 all-gather.4.cloned.1.call-update
  41.5 0.0 reduce-scatter.3.cloned.1.call-start
  41.5 14.2 %all-gather.6.cloned.1.call-done = bf16[1,320,7168]{2,1,0:T(8,128)(2,1)} async-done(((bf16[1,40,7168]{2,1,0:T(8,128)(2,1)}), bf16[1,320,7168]{2,1,0:T(8,128)(2,1)}) %all-gather.6.cloned.1.call-update) | async-done | bytes 4587536 | tf_op jit(solution)/shard_map/all_gather | solution.py:21
  55.7 4.9 %fusion.3 = f32[320,256]{1,0:T(8,128)S(1)} fusion(bf16[1,320,7168]{2,1,0:T(8,128)(2,1)} %all-gather.6.cloned.1.call-done, bf16[1,7168,256]{2,1,0:T(8,128)(2,1)} %param.11), kind=kOutput, calls=%fused_computation.8 | convolution fusion | flops 1174405120 | bytes 8585216 | tf_op jit(solution)/shard_map/dot_general | solution.py:11
  60.6 0.9 copy-done.6
  61.6 1.4 fusion.18
  63.0 0.6 copy-done
  63.6 3.4 %convolution_convert_fusion.1 = bf16[320,7168]{1,0:T(8,128)(2,1)} fusion(bf16[320,256]{1,0:T(8,128)(2,1)S(1)} %fusion.18, bf16[1,256,7168]{2,1,0:T(8,128)(2,1)S(1)} %copy-done), kind=kOutput, calls=%fused_computation.1 | convolution fusion | flops 1176698880 | bytes 8421376 | tf_op jit(solution)/shard_map/dot_general | solution.py:14
  67.1 0.0 reduce-scatter.3.cloned.1.call-update
  67.1 0.0 reduce-scatter.5.cloned.1.call-start
  67.1 22.1 %all-gather.4.cloned.1.call-done = bf16[320,7168]{1,0:T(8,128)(2,1)} async-done(((bf16[40,7168]{1,0:T(8,128)(2,1)}), bf16[320,7168]{1,0:T(8,128)(2,1)}) %all-gather.4.cloned.1.call-update) | async-done | bytes 4587536 | tf_op jit(solution)/shard_map/all_gather | solution.py:21
  89.2 4.9 %fusion.7 = f32[320,256]{1,0:T(8,128)S(1)} fusion(bf16[320,7168]{1,0:T(8,128)(2,1)} %all-gather.4.cloned.1.call-done, bf16[1,7168,256]{2,1,0:T(8,128)(2,1)} %param.12), kind=kOutput, calls=%fused_computation.14 | convolution fusion | flops 1174405120 | bytes 8585216 | tf_op jit(solution)/shard_map/dot_general | solution.py:12
  94.1 0.9 copy-done.7
  95.1 1.3 fusion.10
  96.4 0.7 copy-done.1
  97.1 3.9 %convolution_convert_fusion = bf16[320,7168]{1,0:T(8,128)(2,1)} fusion(bf16[1,256,7168]{2,1,0:T(8,128)(2,1)S(1)} %copy-done.1, f32[320,256]{1,0:T(8,128)S(1)} %fusion.7, f32[320,256]{1,0:T(8,128)S(1)} %fusion.10), kind=kOutput, calls=%fused_computation | convolution fusion | flops 1177190400 | bytes 8912896 | tf_op jit(solution)/shard_map/dot_general | solution.py:14
  101.0 0.0 reduce-scatter.5.cloned.1.call-update
  101.0 3.0 %reduce-scatter.3.cloned.1.call-done = bf16[1,160,7168]{2,1,0:T(8,128)(2,1)} async-done(((bf16[2,160,7168]{2,1,0:T(8,128)(2,1)}), bf16[1,160,7168]{2,1,0:T(8,128)(2,1)}) %reduce-scatter.3.cloned.1.call-update) | async-done | bytes 2293776 | tf_op jit(solution)/shard_map/reduce_scatter | solution.py:23
  104.0 4.1 %all-to-all-start = ((bf16[4,40,7168]{2,1,0:T(8,128)(2,1)}), bf16[4,40,7168]{2,1,0:T(8,128)(2,1)S(1)}, u32[]{:S(2)}, u32[]{:S(2)}) async-start(bf16[4,40,7168]{2,1,0:T(8,128)(2,1)} %bitcast.60), calls=%async_computation.1 | async-start | bytes 4587520 | tf_op jit(solution)/shard_map/all_to_all | solution.py:26
  108.1 11.9 %reduce-scatter.5.cloned.1.call-done = bf16[1,160,7168]{2,1,0:T(8,128)(2,1)} async-done(((bf16[2,160,7168]{2,1,0:T(8,128)(2,1)}), bf16[1,160,7168]{2,1,0:T(8,128)(2,1)}) %reduce-scatter.5.cloned.1.call-update) | async-done | bytes 2293776 | tf_op jit(solution)/shard_map/reduce_scatter | solution.py:23
  120.0 15.5 %all-to-all-done = bf16[4,40,7168]{2,1,0:T(8,128)(2,1)S(1)} async-done(((bf16[4,40,7168]{2,1,0:T(8,128)(2,1)}), bf16[4,40,7168]{2,1,0:T(8,128)(2,1)S(1)}, u32[]{:S(2)}, u32[]{:S(2)}) %all-to-all-start) | async-done | bytes 2293792 | tf_op jit(solution)/shard_map/all_to_all | solution.py:26
  135.5 4.5 %all-to-all-start.1 = ((bf16[4,40,7168]{2,1,0:T(8,128)(2,1)}), bf16[4,40,7168]{2,1,0:T(8,128)(2,1)}, u32[]{:S(2)}, u32[]{:S(2)}) async-start(bf16[4,40,7168]{2,1,0:T(8,128)(2,1)} %bitcast.59), calls=%async_computation.3 | async-start | bytes 4587520 | tf_op jit(solution)/shard_map/all_to_all | solution.py:26
  140.0 0.1 fusion.31
  140.1 0.1 copy.10
  140.2 0.1 select_reduce_fusion
  140.3 2.7 %collective-permute-start.1 = (f32[40]{0:T(128)S(1)}, f32[40]{0:T(128)S(1)}, u32[]{:S(2)}, u32[]{:S(2)}) collective-permute-start(f32[40]{0:T(128)S(1)} %get-tuple-element.8), channel_id=1, source_target_pairs={{0,8},{8,0},{1,9},{9,1},{2,10},{10,2},{3,11},{11,3},{4,12},{12,4},... | collective-permute-start | bytes 488 | tf_op jit(solution)/shard_map/ppermute | solution.py:64
  143.0 0.4 convert_reduce_fusion.1
  143.3 23.9 %all-to-all-done.1 = bf16[4,40,7168]{2,1,0:T(8,128)(2,1)} async-done(((bf16[4,40,7168]{2,1,0:T(8,128)(2,1)}), bf16[4,40,7168]{2,1,0:T(8,128)(2,1)}, u32[]{:S(2)}, u32[]{:S(2)}) %all-to-all-start.1) | async-done | bytes 2293792 | tf_op jit(solution)/shard_map/all_to_all | solution.py:26
  167.2 2.2 %convert_reduce_fusion = f32[40,7168]{1,0:T(8,128)S(1)} fusion(bf16[4,40,7168]{2,1,0:T(8,128)(2,1)} %all-to-all-done.1), kind=kLoop, calls=%fused_computation.10 | loop fusion | flops 2007040 | bytes 3440640 | tf_op jit(solution)/shard_map/reduce_sum | solution.py:29
  169.4 0.1 multiply_convert_fusion.1
  169.5 2.7 %collective-permute-start.2 = (bf16[40,7168]{1,0:T(8,128)(2,1)S(1)}, bf16[40,7168]{1,0:T(8,128)(2,1)S(1)}, u32[]{:S(2)}, u32[]{:S(2)}) collective-permute-start(bf16[40,7168]{1,0:T(8,128)(2,1)S(1)} %multiply_convert_fusion.1), channel_id=1, source_target_pairs={{0,8},{8,0},{1,9},{9,1},{2,10},{10,2},{3,11},{11,3},{4,12},{12,4},... | collective-permute-start | bytes 1720328 | tf_op jit(solution)/shard_map/ppermute | solution.py:70
  172.2 0.1 fusion.26
  172.4 24.2 %collective-permute-done.2 = bf16[40,7168]{1,0:T(8,128)(2,1)S(1)} collective-permute-done((bf16[40,7168]{1,0:T(8,128)(2,1)S(1)}, bf16[40,7168]{1,0:T(8,128)(2,1)S(1)}, u32[]{:S(2)}, u32[]{:S(2)}) %collective-permute-start.2) | collective-permute-done | bytes 573472 | tf_op jit(solution)/shard_map/ppermute | solution.py:70
  196.6 1.4 fusion
  (15 shorter events, 0.0 us)
Async XLA Ops:
  6.5 49.2 %all-gather.6.cloned.1.call-start = ((), (), s32[]{:S(2)}) async-start(), calls=%async_computation.7 | async-start | bytes 5160960 | tf_op jit(solution)/shard_map/all_gather | solution.py:21
  11.1 78.0 %all-gather.4.cloned.1.call-start = ((), (), s32[]{:S(2)}) async-start(), calls=%async_computation.5 | async-start | bytes 5160960 | tf_op jit(solution)/shard_map/all_gather | solution.py:21
  11.2 29.4 %collective-permute-start = (bf16[40,7168]{1,0:T(8,128)(2,1)S(1)}, bf16[40,7168]{1,0:T(8,128)(2,1)S(1)}, u32[]{:S(2)}, u32[]{:S(2)}) collective-permute-start(bf16[40,7168]{1,0:T(8,128)(2,1)S(1)} %get-tuple-element.6), channel_id=1, source_target_pairs={{0,8},{8,0},{1,9},{9,1},{2,10},{10,2},{3,11},{11,3},{4,12},{12,4},... | collective-permute-start | bytes 1720328 | tf_op jit(solution)/shard_map/ppermute | solution.py:63
  40.6 0.8 copy-start.2
  41.5 62.5 %reduce-scatter.3.cloned.1.call-start = ((), (), s32[]{:S(2)}) async-start(), calls=%async_computation.4 | async-start | bytes 6881280 | tf_op jit(solution)/shard_map/reduce_scatter | solution.py:23
  55.7 4.9 %copy-start.5 = (bf16[1,320,7168]{2,1,0:T(8,128)(2,1)S(1)}, bf16[1,320,7168]{2,1,0:T(8,128)(2,1)}, u32[]{:S(2)}) copy-start(bf16[1,320,7168]{2,1,0:T(8,128)(2,1)} %all-gather.6.cloned.1.call-done) | copy-start | bytes 13762564
  55.7 5.9 %copy-start.6 = (bf16[1,7168,256]{2,1,0:T(8,128)(2,1)S(1)}, bf16[1,7168,256]{2,1,0:T(8,128)(2,1)}, u32[]{:S(2)}) copy-start(bf16[1,7168,256]{2,1,0:T(8,128)(2,1)} %param.12) | copy-start | bytes 11010052
  61.6 2.0 copy-start
  67.1 52.9 %reduce-scatter.5.cloned.1.call-start = ((), (), s32[]{:S(2)}) async-start(), calls=%async_computation.6 | async-start | bytes 6881280 | tf_op jit(solution)/shard_map/reduce_scatter | solution.py:23
  89.2 4.9 %copy-start.4 = (bf16[320,7168]{1,0:T(8,128)(2,1)S(1)}, bf16[320,7168]{1,0:T(8,128)(2,1)}, u32[]{:S(2)}) copy-start(bf16[320,7168]{1,0:T(8,128)(2,1)} %all-gather.4.cloned.1.call-done) | copy-start | bytes 13762564
  89.2 5.9 %copy-start.7 = (bf16[1,7168,256]{2,1,0:T(8,128)(2,1)S(1)}, bf16[1,7168,256]{2,1,0:T(8,128)(2,1)}, u32[]{:S(2)}) copy-start(bf16[1,7168,256]{2,1,0:T(8,128)(2,1)} %param.11) | copy-start | bytes 11010052
  95.1 2.0 copy-start.1
  104.0 36.0 %copy-start.3 = (f32[64,1]{0,1:T(1,128)S(1)}, f32[64,1]{0,1:T(1,128)}, u32[]{:S(2)}) copy-start(f32[64,1]{0,1:T(1,128)} %param.10) | copy-start | bytes 772
  104.0 31.5 %all-to-all-start = ((bf16[4,40,7168]{2,1,0:T(8,128)(2,1)}), bf16[4,40,7168]{2,1,0:T(8,128)(2,1)S(1)}, u32[]{:S(2)}, u32[]{:S(2)}) async-start(bf16[4,40,7168]{2,1,0:T(8,128)(2,1)} %bitcast.60), calls=%async_computation.1 | async-start | bytes 4587520 | tf_op jit(solution)/shard_map/all_to_all | solution.py:26
  135.5 31.7 %all-to-all-start.1 = ((bf16[4,40,7168]{2,1,0:T(8,128)(2,1)}), bf16[4,40,7168]{2,1,0:T(8,128)(2,1)}, u32[]{:S(2)}, u32[]{:S(2)}) async-start(bf16[4,40,7168]{2,1,0:T(8,128)(2,1)} %bitcast.59), calls=%async_computation.3 | async-start | bytes 4587520 | tf_op jit(solution)/shard_map/all_to_all | solution.py:26
  140.3 29.1 %collective-permute-start.1 = (f32[40]{0:T(128)S(1)}, f32[40]{0:T(128)S(1)}, u32[]{:S(2)}, u32[]{:S(2)}) collective-permute-start(f32[40]{0:T(128)S(1)} %get-tuple-element.8), channel_id=1, source_target_pairs={{0,8},{8,0},{1,9},{9,1},{2,10},{10,2},{3,11},{11,3},{4,12},{12,4},... | collective-permute-start | bytes 488 | tf_op jit(solution)/shard_map/ppermute | solution.py:64
  169.5 27.0 %collective-permute-start.2 = (bf16[40,7168]{1,0:T(8,128)(2,1)S(1)}, bf16[40,7168]{1,0:T(8,128)(2,1)S(1)}, u32[]{:S(2)}, u32[]{:S(2)}) collective-permute-start(bf16[40,7168]{1,0:T(8,128)(2,1)S(1)} %multiply_convert_fusion.1), channel_id=1, source_target_pairs={{0,8},{8,0},{1,9},{9,1},{2,10},{10,2},{3,11},{11,3},{4,12},{12,4},... | collective-permute-start | bytes 1720328 | tf_op jit(solution)/shard_map/ppermute | solution.py:70
Sparse Core Ops, SparseCore 0:
  11.3 44.4 all-gather.5
  57.3 31.8 all-gather.3
  91.5 12.4 reduce-scatter.2
  106.3 13.6 reduce-scatter.4

commit v4 on v3

--- a/solution.py
+++ b/solution.py
@@ -20,9 +20,11 @@
     count, width = held.shape
     gathered = lax.all_gather(held, ("core", "sc"), axis=0, tiled=True)
     parts = slice_ffn(gathered, gate_w, up_w, down_w)
-    paired = lax.psum_scatter(
-        parts.reshape(cores, chips * count, width), "core", scatter_dimension=0, tiled=True
-    )
+    halves = parts.reshape(cores, chips * count, width)
+    core = lax.axis_index("core")
+    swap = [(c, (c + 1) % cores) for c in range(cores)]
+    sibling = lax.ppermute(halves[(core + 1) % cores], "core", swap)
+    paired = (halves[core].astype(jnp.float32) + sibling.astype(jnp.float32)).astype(jnp.bfloat16)
     back = lax.all_to_all(
         paired.reshape(chips, count, width), "sc", split_axis=0, concat_axis=0, tiled=True
     )

time: 205 us -> 205 us (level)
  other arithmetic: 3.89 us -> 12.3 us
  waiting for transfers between devices: 140 us -> 133 us
  matrix products: 23.9 us -> 19.3 us
  local copies, waits for them, and re-layouts: 5.1 us -> 9.27 us
    reduce_scatter x2 -> x0, waiting for transfers between devices: 14.9 us -> none  [expert_rows(): lax.psum_scatter(parts.reshape(cores, chips * count, width), 'core', scat...]
    convert_element_type x0 -> x2, other arithmetic: none -> 8.4 us  [expert_rows(): (halves[core].astype(jnp.float32) + sibling.astype(jnp.float32)).astype(j...]
    all_to_all x2, waiting for transfers between devices: 39.4 us -> 47.2 us  [expert_rows(): lax.all_to_all(paired.reshape(chips, count, width), 'sc', split_axis=0, c...]
    dot_general x2, matrix products: 7.34 us -> 2.75 us  [slice_ffn(): jnp.dot(hidden, down_w, preferred_element_type=jnp.float32)]
    unnamed x16 -> x24, local copies, waits for them, and re-layouts: 3.99 us -> 6.34 us
  transfers between devices with their start and end apart: 9 -> 9, of which waited for: 8 -> 6; matrix products, arithmetic and copies ran while one was open for 11% -> 14% of each run, Pallas kernels for 0% -> 0%
where the time goes in v4:
time: 205 us
  waiting for transfers between devices  133 us (65%)
  matrix products  19.3 us (9%)
  starting transfers between devices  17.8 us (9%)
  between operations  13.6 us (7%)
  other arithmetic  12.3 us (6%)
  local copies, waits for them, and re-layouts  9.27 us (5%)
    all_to_all x2, waiting for transfers between devices, expert_rows(): lax.all_to_all(paired.reshape(chips, count, width), 'sc', split_axis=0, c...  47.2 us
    all_gather x2, waiting for transfers between devices, expert_rows(): gathered = lax.all_gather(held, ('core', 'sc'), axis=0, tiled=True)  35.8 us
    ppermute x1, waiting for transfers between devices, shards(): away = [lax.ppermute(packed[k], 'eg', shift(k)) for k in range(1, experts)]  25.3 us
    ppermute x1, waiting for transfers between devices, shards(): lax.ppermute(done[(k - 1) * slots:k * slots], 'eg', shift(experts - k))  24.4 us
    convert_element_type x2, other arithmetic, expert_rows(): (halves[core].astype(jnp.float32) + sibling.astype(jnp.float32)).astype(j...  8.4 us
    all_to_all x2, starting transfers between devices, expert_rows(): lax.all_to_all(paired.reshape(chips, count, width), 'sc', split_axis=0, c...  8.1 us
    unnamed x24, local copies, waits for them, and re-layouts  6.34 us
    dot_general x2, matrix products, slice_ffn(): gate = jnp.dot(rows, gate_w, preferred_element_type=jnp.float32)  6.28 us
  transfers between devices with their start and end apart: 9, of which 6 were waited for; matrix products, arithmetic and copies ran while one was open for 14% of the time, Pallas kernels for 0%

profile of v4, /device:TPU:0, one launch (start us, length us, event | category | flops | bytes accessed | tf_op | source)
XLA Modules:
  0.0 205.1 jit_solution(5822819006727093533)
XLA Ops:
  6.5 0.7 fusion.45
  7.2 0.1 fusion.34
  7.3 0.1 copy.9
  7.4 0.1 reduce_window_sum.11
  7.5 0.1 fusion.42
  7.5 0.1 copy.8
  7.6 2.1 %multiply_reduce_fusion = (f32[64]{0:T(128)S(1)}, f32[64,7168]{1,0:T(8,128)S(1)}) fusion(bf16[64,7168]{1,0:T(8,128)(2,1)} %param.7, s32[64]{0:T(128)} %param.8), kind=kOutput, calls=%fused_computation.27 | convolution fusion | flops 60559296 | bytes 2753024 | tf_op jit(solution)/shard_map/dot_general | solution.py:43
  9.7 0.5 convolution_convert_fusion.2
  10.2 0.9 fusion.49
  11.1 0.0 all-gather.6.cloned.1.call-update
  11.1 0.0 all-gather.4.cloned.1.call-start
  11.2 4.1 %collective-permute-start.1 = (bf16[40,7168]{1,0:T(8,128)(2,1)S(1)}, bf16[40,7168]{1,0:T(8,128)(2,1)S(1)}, u32[]{:S(2)}, u32[]{:S(2)}) collective-permute-start(bf16[40,7168]{1,0:T(8,128)(2,1)S(1)} %get-tuple-element.6), channel_id=1, source_target_pairs={{0,8},{8,0},{1,9},{9,1},{2,10},{10,2},{3,11},{11,3},{4,12},{12,4},... | collective-permute-start | bytes 1720328 | tf_op jit(solution)/shard_map/ppermute | solution.py:65
  15.3 25.3 %collective-permute-done.1 = bf16[40,7168]{1,0:T(8,128)(2,1)S(1)} collective-permute-done((bf16[40,7168]{1,0:T(8,128)(2,1)S(1)}, bf16[40,7168]{1,0:T(8,128)(2,1)S(1)}, u32[]{:S(2)}, u32[]{:S(2)}) %collective-permute-start.1) | collective-permute-done | bytes 573472 | tf_op jit(solution)/shard_map/ppermute | solution.py:65
  40.6 0.8 copy-done.4
  41.5 14.2 %all-gather.6.cloned.1.call-done = bf16[1,320,7168]{2,1,0:T(8,128)(2,1)} async-done(((bf16[1,40,7168]{2,1,0:T(8,128)(2,1)}), bf16[1,320,7168]{2,1,0:T(8,128)(2,1)}) %all-gather.6.cloned.1.call-update) | async-done | bytes 4587536 | tf_op jit(solution)/shard_map/all_gather | solution.py:21
  55.7 4.9 %fusion.5 = f32[320,256]{1,0:T(8,128)S(1)} fusion(bf16[1,320,7168]{2,1,0:T(8,128)(2,1)} %all-gather.6.cloned.1.call-done, bf16[1,7168,256]{2,1,0:T(8,128)(2,1)} %param.11), kind=kOutput, calls=%fused_computation.12 | convolution fusion | flops 1174405120 | bytes 8585216 | tf_op jit(solution)/shard_map/dot_general | solution.py:11
  60.6 0.9 copy-done.8
  61.6 1.3 fusion.20
  62.9 0.7 copy-done.2
  63.6 1.4 convolution_convert_fusion.1
  65.0 2.1 %copy-done = bf16[320,7168]{1,0:T(8,128)(2,1)} copy-done((bf16[320,7168]{1,0:T(8,128)(2,1)}, bf16[320,7168]{1,0:T(8,128)(2,1)S(1)}, u32[]{:S(2)}) %copy-start) | copy-done | bytes 4587544
  67.1 0.1 dynamic-slice_bitcast_fusion.1
  67.3 0.3 collective-permute-start
  67.6 21.6 %all-gather.4.cloned.1.call-done = bf16[320,7168]{1,0:T(8,128)(2,1)} async-done(((bf16[40,7168]{1,0:T(8,128)(2,1)}), bf16[320,7168]{1,0:T(8,128)(2,1)}) %all-gather.4.cloned.1.call-update) | async-done | bytes 4587536 | tf_op jit(solution)/shard_map/all_gather | solution.py:21
  89.2 4.9 %fusion.9 = f32[320,256]{1,0:T(8,128)S(1)} fusion(bf16[320,7168]{1,0:T(8,128)(2,1)} %all-gather.4.cloned.1.call-done, bf16[1,7168,256]{2,1,0:T(8,128)(2,1)} %param.12), kind=kOutput, calls=%fused_computation.18 | convolution fusion | flops 1174405120 | bytes 8585216 | tf_op jit(solution)/shard_map/dot_general | solution.py:12
  94.1 0.9 copy-done.9
  95.1 1.4 fusion.12
  96.4 0.8 copy-done.3
  97.3 1.4 convolution_convert_fusion
  98.7 1.7 dynamic-slice_bitcast_fusion
  100.3 0.2 collective-permute-start.2
  100.6 3.9 %fusion.2 = bf16[160,7168]{1,0:T(8,128)(2,1)} fusion(bf16[160,7168]{1,0:T(8,128)(2,1)} %collective-permute-done, bf16[2,160,7168]{2,1,0:T(8,128)(2,1)S(1)} %bitcast.70, s32[]{:T(128)S(6)} %select_n.41), kind=kLoop, calls=%fused_computation.9 | loop fusion | flops 4587520 | bytes 6881284 | tf_op jit(solution)/shard_map/convert_element_type | solution.py:27
  104.5 3.6 %all-to-all-start = ((bf16[4,40,7168]{2,1,0:T(8,128)(2,1)}), bf16[4,40,7168]{2,1,0:T(8,128)(2,1)S(1)}, u32[]{:S(2)}, u32[]{:S(2)}) async-start(bf16[4,40,7168]{2,1,0:T(8,128)(2,1)} %bitcast.74), calls=%async_computation | async-start | bytes 4587520 | tf_op jit(solution)/shard_map/all_to_all | solution.py:28
  108.1 4.5 %fusion.1 = bf16[160,7168]{1,0:T(8,128)(2,1)} fusion(bf16[160,7168]{1,0:T(8,128)(2,1)} %collective-permute-done.2, bf16[2,160,7168]{2,1,0:T(8,128)(2,1)} %bitcast.72, s32[]{:T(128)S(6)} %select_n.41), kind=kLoop, calls=%fused_computation.7 | loop fusion | flops 4587520 | bytes 6881284 | tf_op jit(solution)/shard_map/convert_element_type | solution.py:27
  112.6 23.1 %all-to-all-done = bf16[4,40,7168]{2,1,0:T(8,128)(2,1)S(1)} async-done(((bf16[4,40,7168]{2,1,0:T(8,128)(2,1)}), bf16[4,40,7168]{2,1,0:T(8,128)(2,1)S(1)}, u32[]{:S(2)}, u32[]{:S(2)}) %all-to-all-start) | async-done | bytes 2293792 | tf_op jit(solution)/shard_map/all_to_all | solution.py:28
  135.7 4.5 %all-to-all-start.1 = ((bf16[4,40,7168]{2,1,0:T(8,128)(2,1)}), bf16[4,40,7168]{2,1,0:T(8,128)(2,1)}, u32[]{:S(2)}, u32[]{:S(2)}) async-start(bf16[4,40,7168]{2,1,0:T(8,128)(2,1)} %bitcast.73), calls=%async_computation.1 | async-start | bytes 4587520 | tf_op jit(solution)/shard_map/all_to_all | solution.py:28
  140.2 0.1 fusion.33
  140.3 0.1 copy.10
  140.4 0.1 select_reduce_fusion
  140.5 2.5 %collective-permute-start.3 = (f32[40]{0:T(128)S(1)}, f32[40]{0:T(128)S(1)}, u32[]{:S(2)}, u32[]{:S(2)}) collective-permute-start(f32[40]{0:T(128)S(1)} %get-tuple-element.8), channel_id=1, source_target_pairs={{0,8},{8,0},{1,9},{9,1},{2,10},{10,2},{3,11},{11,3},{4,12},{12,4},... | collective-permute-start | bytes 488 | tf_op jit(solution)/shard_map/ppermute | solution.py:66
  143.0 0.4 convert_reduce_fusion.1
  143.4 24.1 %all-to-all-done.1 = bf16[4,40,7168]{2,1,0:T(8,128)(2,1)} async-done(((bf16[4,40,7168]{2,1,0:T(8,128)(2,1)}), bf16[4,40,7168]{2,1,0:T(8,128)(2,1)}, u32[]{:S(2)}, u32[]{:S(2)}) %all-to-all-start.1) | async-done | bytes 2293792 | tf_op jit(solution)/shard_map/all_to_all | solution.py:28
  167.5 2.2 %convert_reduce_fusion = f32[40,7168]{1,0:T(8,128)S(1)} fusion(bf16[4,40,7168]{2,1,0:T(8,128)(2,1)} %all-to-all-done.1), kind=kLoop, calls=%fused_computation.14 | loop fusion | flops 2007040 | bytes 3440640 | tf_op jit(solution)/shard_map/reduce_sum | solution.py:31
  169.6 0.1 multiply_convert_fusion.1
  169.8 2.5 %collective-permute-start.4 = (bf16[40,7168]{1,0:T(8,128)(2,1)S(1)}, bf16[40,7168]{1,0:T(8,128)(2,1)S(1)}, u32[]{:S(2)}, u32[]{:S(2)}) collective-permute-start(bf16[40,7168]{1,0:T(8,128)(2,1)S(1)} %multiply_convert_fusion.1), channel_id=1, source_target_pairs={{0,8},{8,0},{1,9},{9,1},{2,10},{10,2},{3,11},{11,3},{4,12},{12,4},... | collective-permute-start | bytes 1720328 | tf_op jit(solution)/shard_map/ppermute | solution.py:72
  172.3 0.1 fusion.28
  172.4 24.4 %collective-permute-done.4 = bf16[40,7168]{1,0:T(8,128)(2,1)S(1)} collective-permute-done((bf16[40,7168]{1,0:T(8,128)(2,1)S(1)}, bf16[40,7168]{1,0:T(8,128)(2,1)S(1)}, u32[]{:S(2)}, u32[]{:S(2)}) %collective-permute-start.4) | collective-permute-done | bytes 573472 | tf_op jit(solution)/shard_map/ppermute | solution.py:72
  196.8 1.4 fusion
  (26 shorter events, 0.1 us)
Async XLA Ops:
  6.5 49.2 %all-gather.6.cloned.1.call-start = ((), (), s32[]{:S(2)}) async-start(), calls=%async_computation.3 | async-start | bytes 5160960 | tf_op jit(solution)/shard_map/all_gather | solution.py:21
  11.1 78.0 %all-gather.4.cloned.1.call-start = ((), (), s32[]{:S(2)}) async-start(), calls=%async_computation.2 | async-start | bytes 5160960 | tf_op jit(solution)/shard_map/all_gather | solution.py:21
  11.2 29.4 %collective-permute-start.1 = (bf16[40,7168]{1,0:T(8,128)(2,1)S(1)}, bf16[40,7168]{1,0:T(8,128)(2,1)S(1)}, u32[]{:S(2)}, u32[]{:S(2)}) collective-permute-start(bf16[40,7168]{1,0:T(8,128)(2,1)S(1)} %get-tuple-element.6), channel_id=1, source_target_pairs={{0,8},{8,0},{1,9},{9,1},{2,10},{10,2},{3,11},{11,3},{4,12},{12,4},... | collective-permute-start | bytes 1720328 | tf_op jit(solution)/shard_map/ppermute | solution.py:65
  40.6 0.8 copy-start.4
  55.7 4.9 %copy-start.6 = (bf16[1,320,7168]{2,1,0:T(8,128)(2,1)S(1)}, bf16[1,320,7168]{2,1,0:T(8,128)(2,1)}, u32[]{:S(2)}) copy-start(bf16[1,320,7168]{2,1,0:T(8,128)(2,1)} %all-gather.6.cloned.1.call-done) | copy-start | bytes 13762564
  55.7 5.9 %copy-start.8 = (bf16[1,7168,256]{2,1,0:T(8,128)(2,1)S(1)}, bf16[1,7168,256]{2,1,0:T(8,128)(2,1)}, u32[]{:S(2)}) copy-start(bf16[1,7168,256]{2,1,0:T(8,128)(2,1)} %param.12) | copy-start | bytes 11010052
  61.6 2.0 copy-start.2
  65.0 2.1 %copy-start = (bf16[320,7168]{1,0:T(8,128)(2,1)}, bf16[320,7168]{1,0:T(8,128)(2,1)S(1)}, u32[]{:S(2)}) copy-start(bf16[320,7168]{1,0:T(8,128)(2,1)S(1)} %convolution_convert_fusion.1) | copy-start | bytes 13762564
  67.3 33.3 %collective-permute-start = (bf16[160,7168]{1,0:T(8,128)(2,1)S(1)}, bf16[160,7168]{1,0:T(8,128)(2,1)}, u32[]{:S(2)}, u32[]{:S(2)}) collective-permute-start(bf16[160,7168]{1,0:T(8,128)(2,1)S(1)} %dynamic-slice_bitcast_fusion.1), channel_id=1, source_target_pairs={{0,1},{1,0},{2,3},{3,2},{4,5},{5,4},{6,7},{7,6},{8,9},{9,8},{10,11... | collective-permute-start | bytes 6881288 | tf_op jit(solution)/shard_map/ppermute | solution.py:26
  89.2 4.9 %copy-start.7 = (bf16[320,7168]{1,0:T(8,128)(2,1)S(1)}, bf16[320,7168]{1,0:T(8,128)(2,1)}, u32[]{:S(2)}) copy-start(bf16[320,7168]{1,0:T(8,128)(2,1)} %all-gather.4.cloned.1.call-done) | copy-start | bytes 13762564
  89.2 5.9 %copy-start.9 = (bf16[1,7168,256]{2,1,0:T(8,128)(2,1)S(1)}, bf16[1,7168,256]{2,1,0:T(8,128)(2,1)}, u32[]{:S(2)}) copy-start(bf16[1,7168,256]{2,1,0:T(8,128)(2,1)} %param.11) | copy-start | bytes 11010052
  89.2 11.4 %slice-start = ((s8[4587520]{0:T(1024)(128)(4,1)}), s8[4194304]{0:T(1024)(128)(4,1)S(1)}, s32[]{:S(2)}) async-start(s8[4587520]{0:T(1024)(128)(4,1)} %bitcast.68), calls=%async_computation.4 | async-start | bytes 8388608
  95.1 2.2 %copy-start.3 = (bf16[1,256,7168]{2,1,0:T(8,128)(2,1)S(1)}, bf16[1,256,7168]{2,1,0:T(8,128)(2,1)}, u32[]{:S(2)}) copy-start(bf16[1,256,7168]{2,1,0:T(8,128)(2,1)} %param.13) | copy-start | bytes 11010052
  95.1 5.5 %slice-start.1 = ((s8[4587520]{0:T(1024)(128)(4,1)}), s8[393216]{0:T(1024)(128)(4,1)S(1)}, s32[]{:S(2)}) async-start(s8[4587520]{0:T(1024)(128)(4,1)} %bitcast.68), calls=%async_computation.5 | async-start | bytes 786432
  98.7 5.8 %copy-start.1 = (bf16[320,7168]{1,0:T(8,128)(2,1)}, bf16[320,7168]{1,0:T(8,128)(2,1)S(1)}, u32[]{:S(2)}) copy-start(bf16[320,7168]{1,0:T(8,128)(2,1)S(1)} %convolution_convert_fusion) | copy-start | bytes 13762564
  100.3 7.8 %collective-permute-start.2 = (bf16[160,7168]{1,0:T(8,128)(2,1)}, bf16[160,7168]{1,0:T(8,128)(2,1)}, u32[]{:S(2)}, u32[]{:S(2)}) collective-permute-start(bf16[160,7168]{1,0:T(8,128)(2,1)} %dynamic-slice_bitcast_fusion), channel_id=1, source_target_pairs={{0,1},{1,0},{2,3},{3,2},{4,5},{5,4},{6,7},{7,6},{8,9},{9,8},{10,11... | collective-permute-start | bytes 6881288 | tf_op jit(solution)/shard_map/ppermute | solution.py:26
  104.5 31.2 %all-to-all-start = ((bf16[4,40,7168]{2,1,0:T(8,128)(2,1)}), bf16[4,40,7168]{2,1,0:T(8,128)(2,1)S(1)}, u32[]{:S(2)}, u32[]{:S(2)}) async-start(bf16[4,40,7168]{2,1,0:T(8,128)(2,1)} %bitcast.74), calls=%async_computation | async-start | bytes 4587520 | tf_op jit(solution)/shard_map/all_to_all | solution.py:28
  112.6 27.6 %copy-start.5 = (f32[64,1]{0,1:T(1,128)S(1)}, f32[64,1]{0,1:T(1,128)}, u32[]{:S(2)}) copy-start(f32[64,1]{0,1:T(1,128)} %param.10) | copy-start | bytes 772
  135.7 31.7 %all-to-all-start.1 = ((bf16[4,40,7168]{2,1,0:T(8,128)(2,1)}), bf16[4,40,7168]{2,1,0:T(8,128)(2,1)}, u32[]{:S(2)}, u32[]{:S(2)}) async-start(bf16[4,40,7168]{2,1,0:T(8,128)(2,1)} %bitcast.73), calls=%async_computation.1 | async-start | bytes 4587520 | tf_op jit(solution)/shard_map/all_to_all | solution.py:28
  140.5 29.1 %collective-permute-start.3 = (f32[40]{0:T(128)S(1)}, f32[40]{0:T(128)S(1)}, u32[]{:S(2)}, u32[]{:S(2)}) collective-permute-start(f32[40]{0:T(128)S(1)} %get-tuple-element.8), channel_id=1, source_target_pairs={{0,8},{8,0},{1,9},{9,1},{2,10},{10,2},{3,11},{11,3},{4,12},{12,4},... | collective-permute-start | bytes 488 | tf_op jit(solution)/shard_map/ppermute | solution.py:66
  169.8 27.1 %collective-permute-start.4 = (bf16[40,7168]{1,0:T(8,128)(2,1)S(1)}, bf16[40,7168]{1,0:T(8,128)(2,1)S(1)}, u32[]{:S(2)}, u32[]{:S(2)}) collective-permute-start(bf16[40,7168]{1,0:T(8,128)(2,1)S(1)} %multiply_convert_fusion.1), channel_id=1, source_target_pairs={{0,8},{8,0},{1,9},{9,1},{2,10},{10,2},{3,11},{11,3},{4,12},{12,4},... | collective-permute-start | bytes 1720328 | tf_op jit(solution)/shard_map/ppermute | solution.py:72
Sparse Core Ops, SparseCore 0:
  11.3 44.4 all-gather.5
  57.3 31.8 all-gather.3

commit v5 on v4

--- a/solution.py
+++ b/solution.py
@@ -14,20 +14,29 @@
     return jnp.dot(hidden, down_w, preferred_element_type=jnp.float32).astype(jnp.bfloat16)
 
 
-def expert_rows(held, weights, gate_w, up_w, down_w):
+def gather(held):
+    return lax.all_gather(held, ("core", "sc"), axis=0, tiled=True)
+
+
+def expert_parts(gathered, gate_w, up_w, down_w):
     chips = lax.axis_size("sc")
     cores = lax.axis_size("core")
-    count, width = held.shape
-    gathered = lax.all_gather(held, ("core", "sc"), axis=0, tiled=True)
+    count = gathered.shape[0] // (chips * cores)
+    width = gathered.shape[1]
     parts = slice_ffn(gathered, gate_w, up_w, down_w)
     halves = parts.reshape(cores, chips * count, width)
     core = lax.axis_index("core")
     swap = [(c, (c + 1) % cores) for c in range(cores)]
     sibling = lax.ppermute(halves[(core + 1) % cores], "core", swap)
     paired = (halves[core].astype(jnp.float32) + sibling.astype(jnp.float32)).astype(jnp.bfloat16)
-    back = lax.all_to_all(
-        paired.reshape(chips, count, width), "sc", split_axis=0, concat_axis=0, tiled=True
-    )
+    return paired.reshape(chips, count, width)
+
+
+def chip_sums(paired):
+    return lax.all_to_all(paired, "sc", split_axis=0, concat_axis=0, tiled=True)
+
+
+def finish(back, weights):
     summed = jnp.sum(back.astype(jnp.float32), axis=0)
     return (summed * weights[:, None]).astype(jnp.bfloat16)
 
@@ -64,10 +73,14 @@
 
     away = [lax.ppermute(packed[k], "eg", shift(k)) for k in range(1, experts)]
     away_w = [lax.ppermute(packed_w[k], "eg", shift(k)) for k in range(1, experts)]
-    own = expert_rows(packed[0], packed_w[0], *weights)
-    done = expert_rows(
-        jnp.concatenate(away, axis=0), jnp.concatenate(away_w, axis=0), *weights
-    )
+    own_rows = gather(packed[0])
+    own_rows, away = lax.optimization_barrier((own_rows, away))
+    own_parts = expert_parts(own_rows, *weights)
+    away_parts = expert_parts(gather(jnp.concatenate(away, axis=0)), *weights)
+    away_back = chip_sums(away_parts)
+    own_parts, away_back = lax.optimization_barrier((own_parts, away_back))
+    done = finish(away_back, jnp.concatenate(away_w, axis=0))
+    own = finish(chip_sums(own_parts), packed_w[0])
     home = [own] + [
         lax.ppermute(done[(k - 1) * slots:k * slots], "eg", shift(experts - k))
         for k in range(1, experts)

time: 205 us -> 204 us (level)
  waiting for transfers between devices: 133 us -> 140 us
  local copies, waits for them, and re-layouts: 9.27 us -> 4.9 us
  matrix products: 19.3 us -> 15.7 us
    all_to_all x2, waiting for transfers between devices: 47.2 us -> 23.2 us  [chip_sums(): return lax.all_to_all(paired, 'sc', split_axis=0, concat_axis=0, tiled=True)]
    ppermute x1, waiting for transfers between devices: 0.01 us -> 21.6 us  [shards(): lax.ppermute(packed_w[k], 'eg', shift(k))]
    all_gather x2, waiting for transfers between devices: 35.8 us -> 48.5 us  [gather(): return lax.all_gather(held, ('core', 'sc'), axis=0, tiled=True)]
    unnamed x24 -> x18, local copies, waits for them, and re-layouts: 6.34 us -> 1.96 us
    dot_general x2, matrix products: 6.26 us -> 2.73 us  [slice_ffn(): upper = jnp.dot(rows, up_w, preferred_element_type=jnp.float32)]
    ppermute x1, waiting for transfers between devices: 24.4 us -> 21.7 us  [shards(): lax.ppermute(done[(k - 1) * slots:k * slots], 'eg', shift(experts - k))]
  transfers between devices with their start and end apart: 9 -> 9, of which waited for: 6 -> 6; matrix products, arithmetic and copies ran while one was open for 14% -> 8% of each run, Pallas kernels for 0% -> 0%
where the time goes in v5:
time: 204 us
  waiting for transfers between devices  140 us (69%)
  starting transfers between devices  18.6 us (9%)
  matrix products  15.7 us (8%)
  between operations  13.6 us (7%)
  other arithmetic  10.5 us (5%)
  local copies, waits for them, and re-layouts  4.9 us (2%)
    all_gather x2, waiting for transfers between devices, gather(): return lax.all_gather(held, ('core', 'sc'), axis=0, tiled=True)  48.5 us
    ppermute x1, waiting for transfers between devices, shards(): away = [lax.ppermute(packed[k], 'eg', shift(k)) for k in range(1, experts)]  25.3 us
    all_to_all x2, waiting for transfers between devices, chip_sums(): return lax.all_to_all(paired, 'sc', split_axis=0, concat_axis=0, tiled=True)  23.2 us
    ppermute x1, waiting for transfers between devices, shards(): lax.ppermute(done[(k - 1) * slots:k * slots], 'eg', shift(experts - k))  21.7 us
    ppermute x1, waiting for transfers between devices, shards(): lax.ppermute(packed_w[k], 'eg', shift(k))  21.6 us
    all_to_all x2, starting transfers between devices, chip_sums(): return lax.all_to_all(paired, 'sc', split_axis=0, concat_axis=0, tiled=True)  8.1 us
    convert_element_type x2, other arithmetic, expert_parts(): (halves[core].astype(jnp.float32) + sibling.astype(jnp.float32)).astype(j...  6.56 us
    dot_general x2, matrix products, slice_ffn(): gate = jnp.dot(rows, gate_w, preferred_element_type=jnp.float32)  6.28 us
  transfers between devices with their start and end apart: 9, of which 6 were waited for; matrix products, arithmetic and copies ran while one was open for 8% of the time, Pallas kernels for 0%

profile of v5, /device:TPU:0, one launch (start us, length us, event | category | flops | bytes accessed | tf_op | source)
XLA Modules:
  0.0 203.7 jit_solution(3730095952675687586)
XLA Ops:
  6.5 2.0 %multiply_reduce_fusion = (f32[64]{0:T(128)S(1)}, f32[64,7168]{1,0:T(8,128)S(1)}) fusion(bf16[64,7168]{1,0:T(8,128)(2,1)} %param.7, s32[64]{0:T(128)} %param.8), kind=kOutput, calls=%fused_computation.25 | convolution fusion | flops 60559296 | bytes 2753024 | tf_op jit(solution)/shard_map/dot_general | solution.py:52
  8.6 0.7 fusion.39
  9.3 0.1 fusion.28
  9.3 0.1 copy.9
  9.4 0.1 reduce_window_sum.11
  9.5 0.1 fusion.36
  9.6 0.1 copy.8
  9.7 0.5 convolution_convert_fusion.2
  10.2 0.9 slice_bitcast_fusion
  11.1 0.0 all-gather.6.cloned.1.call-update
  11.1 0.0 all-gather.4.cloned.1.call-start
  11.2 4.1 %collective-permute-start = (bf16[40,7168]{1,0:T(8,128)(2,1)S(1)}, bf16[40,7168]{1,0:T(8,128)(2,1)S(1)}, u32[]{:S(2)}, u32[]{:S(2)}) collective-permute-start(bf16[40,7168]{1,0:T(8,128)(2,1)S(1)} %get-tuple-element.13), channel_id=1, source_target_pairs={{0,8},{8,0},{1,9},{9,1},{2,10},{10,2},{3,11},{11,3},{4,12},{12,4},... | collective-permute-start | bytes 1720328 | tf_op jit(solution)/shard_map/ppermute | solution.py:74
  15.3 25.3 %collective-permute-done = bf16[40,7168]{1,0:T(8,128)(2,1)S(1)} collective-permute-done((bf16[40,7168]{1,0:T(8,128)(2,1)S(1)}, bf16[40,7168]{1,0:T(8,128)(2,1)S(1)}, u32[]{:S(2)}, u32[]{:S(2)}) %collective-permute-start) | collective-permute-done | bytes 573472 | tf_op jit(solution)/shard_map/ppermute | solution.py:74
  40.6 15.1 %all-gather.6.cloned.1.call-done = bf16[1,320,7168]{2,1,0:T(8,128)(2,1)} async-done(((bf16[1,40,7168]{2,1,0:T(8,128)(2,1)}), bf16[1,320,7168]{2,1,0:T(8,128)(2,1)}) %all-gather.6.cloned.1.call-update) | async-done | bytes 4587536 | tf_op jit(solution)/shard_map/all_gather | solution.py:18
  55.7 0.0 all-gather.4.cloned.1.call-update
  55.7 33.4 %all-gather.4.cloned.1.call-done = bf16[320,7168]{1,0:T(8,128)(2,1)} async-done(((bf16[40,7168]{1,0:T(8,128)(2,1)}), bf16[320,7168]{1,0:T(8,128)(2,1)}) %all-gather.4.cloned.1.call-update) | async-done | bytes 4587536 | tf_op jit(solution)/shard_map/all_gather | solution.py:18
  89.2 4.9 %fusion.9 = f32[320,256]{1,0:T(8,128)S(1)} fusion(bf16[320,7168]{1,0:T(8,128)(2,1)} %all-gather.4.cloned.1.call-done, bf16[1,7168,256]{2,1,0:T(8,128)(2,1)} %param.11), kind=kOutput, calls=%fused_computation.18 | convolution fusion | flops 1174405120 | bytes 8585216 | tf_op jit(solution)/shard_map/dot_general | solution.py:11
  94.1 0.9 copy-done.5
  95.0 1.4 fusion.16
  96.4 0.6 copy-done.1
  97.1 1.4 convolution_convert_fusion
  98.4 0.2 dynamic-slice_bitcast_fusion
  98.6 0.0 copy-start.6
  98.6 0.3 collective-permute-start.2
  98.9 1.3 fusion.7
  100.3 0.4 copy-done.6
  100.7 1.4 fusion.11
  102.0 1.4 convolution_convert_fusion.1
  103.4 1.7 dynamic-slice_bitcast_fusion.1
  105.1 0.3 collective-permute-start.1
  105.3 0.0 collective-permute-done.2
  105.3 2.1 %fusion.1 = bf16[160,7168]{1,0:T(8,128)(2,1)} fusion(bf16[160,7168]{1,0:T(8,128)(2,1)S(1)} %collective-permute-done.2, bf16[2,160,7168]{2,1,0:T(8,128)(2,1)S(1)} %bitcast.64, s32[]{:T(128)S(6)} %select_n.41), kind=kLoop, calls=%fused_computation.7 | loop fusion | flops 4587520 | bytes 6881284 | tf_op jit(solution)/shard_map/convert_element_type | solution.py:31
  107.5 3.6 %all-to-all-start = ((bf16[4,40,7168]{2,1,0:T(8,128)(2,1)}), bf16[4,40,7168]{2,1,0:T(8,128)(2,1)S(1)}, u32[]{:S(2)}, u32[]{:S(2)}) async-start(bf16[4,40,7168]{2,1,0:T(8,128)(2,1)} %bitcast.65), calls=%async_computation | async-start | bytes 4587520 | tf_op jit(solution)/shard_map/all_to_all | solution.py:36
  111.1 4.4 %fusion.2 = bf16[160,7168]{1,0:T(8,128)(2,1)} fusion(bf16[160,7168]{1,0:T(8,128)(2,1)} %collective-permute-done.1, bf16[2,160,7168]{2,1,0:T(8,128)(2,1)} %bitcast.62, s32[]{:T(128)S(6)} %select_n.41), kind=kLoop, calls=%fused_computation.9 | loop fusion | flops 4587520 | bytes 6881284 | tf_op jit(solution)/shard_map/convert_element_type | solution.py:31
  115.5 23.2 %all-to-all-done = bf16[4,40,7168]{2,1,0:T(8,128)(2,1)S(1)} async-done(((bf16[4,40,7168]{2,1,0:T(8,128)(2,1)}), bf16[4,40,7168]{2,1,0:T(8,128)(2,1)S(1)}, u32[]{:S(2)}, u32[]{:S(2)}) %all-to-all-start) | async-done | bytes 2293792 | tf_op jit(solution)/shard_map/all_to_all | solution.py:36
  138.8 4.5 %all-to-all-start.1 = ((bf16[4,40,7168]{2,1,0:T(8,128)(2,1)}), bf16[4,40,7168]{2,1,0:T(8,128)(2,1)}, u32[]{:S(2)}, u32[]{:S(2)}) async-start(bf16[4,40,7168]{2,1,0:T(8,128)(2,1)} %bitcast.10), calls=%async_computation.1 | async-start | bytes 4587520 | tf_op jit(solution)/shard_map/all_to_all | solution.py:36
  143.3 0.1 fusion.27
  143.3 0.1 copy.10
  143.4 0.1 select_reduce_fusion
  143.5 2.5 %collective-permute-start.3 = (f32[40]{0:T(128)S(1)}, f32[40]{0:T(128)S(1)}, u32[]{:S(2)}, u32[]{:S(2)}) collective-permute-start(f32[40]{0:T(128)S(1)} %get-tuple-element.16), channel_id=1, source_target_pairs={{0,8},{8,0},{1,9},{9,1},{2,10},{10,2},{3,11},{11,3},{4,12},{12,4},... | collective-permute-start | bytes 488 | tf_op jit(solution)/shard_map/ppermute | solution.py:75
  146.0 0.4 convert_reduce_fusion
  146.4 21.6 %collective-permute-done.3 = f32[40]{0:T(128)S(1)} collective-permute-done((f32[40]{0:T(128)S(1)}, f32[40]{0:T(128)S(1)}, u32[]{:S(2)}, u32[]{:S(2)}) %collective-permute-start.3) | collective-permute-done | bytes 192 | tf_op jit(solution)/shard_map/ppermute | solution.py:75
  168.0 0.1 multiply_convert_fusion.1
  168.1 3.3 %collective-permute-start.4 = (bf16[40,7168]{1,0:T(8,128)(2,1)S(1)}, bf16[40,7168]{1,0:T(8,128)(2,1)S(1)}, u32[]{:S(2)}, u32[]{:S(2)}) collective-permute-start(bf16[40,7168]{1,0:T(8,128)(2,1)S(1)} %multiply_convert_fusion.1), channel_id=1, source_target_pairs={{0,8},{8,0},{1,9},{9,1},{2,10},{10,2},{3,11},{11,3},{4,12},{12,4},... | collective-permute-start | bytes 1720328 | tf_op jit(solution)/shard_map/ppermute | solution.py:85
  171.5 2.2 %convert_reduce_fusion.1 = f32[40,7168]{1,0:T(8,128)S(1)} fusion(bf16[4,40,7168]{2,1,0:T(8,128)(2,1)} %all-to-all-done.1), kind=kLoop, calls=%fused_computation.11 | loop fusion | flops 2007040 | bytes 3440640 | tf_op jit(solution)/shard_map/reduce_sum | solution.py:40
  173.6 0.1 fusion.22
  173.8 21.7 %collective-permute-done.4 = bf16[40,7168]{1,0:T(8,128)(2,1)S(1)} collective-permute-done((bf16[40,7168]{1,0:T(8,128)(2,1)S(1)}, bf16[40,7168]{1,0:T(8,128)(2,1)S(1)}, u32[]{:S(2)}, u32[]{:S(2)}) %collective-permute-start.4) | collective-permute-done | bytes 573472 | tf_op jit(solution)/shard_map/ppermute | solution.py:85
  195.4 1.4 fusion
  (20 shorter events, 0.0 us)
Async XLA Ops:
  6.5 49.2 %all-gather.6.cloned.1.call-start = ((), (), s32[]{:S(2)}) async-start(), calls=%async_computation.3 | async-start | bytes 5160960 | tf_op jit(solution)/shard_map/all_gather | solution.py:18
  11.1 78.0 %all-gather.4.cloned.1.call-start = ((), (), s32[]{:S(2)}) async-start(), calls=%async_computation.2 | async-start | bytes 5160960 | tf_op jit(solution)/shard_map/all_gather | solution.py:18
  11.2 29.4 %collective-permute-start = (bf16[40,7168]{1,0:T(8,128)(2,1)S(1)}, bf16[40,7168]{1,0:T(8,128)(2,1)S(1)}, u32[]{:S(2)}, u32[]{:S(2)}) collective-permute-start(bf16[40,7168]{1,0:T(8,128)(2,1)S(1)} %get-tuple-element.13), channel_id=1, source_target_pairs={{0,8},{8,0},{1,9},{9,1},{2,10},{10,2},{3,11},{11,3},{4,12},{12,4},... | collective-permute-start | bytes 1720328 | tf_op jit(solution)/shard_map/ppermute | solution.py:74
  40.6 15.1 %copy-start.2 = (bf16[40,7168]{1,0:T(8,128)(2,1)}, bf16[40,7168]{1,0:T(8,128)(2,1)S(1)}, u32[]{:S(2)}) copy-start(bf16[40,7168]{1,0:T(8,128)(2,1)S(1)} %collective-permute-done) | copy-start | bytes 1720324
  89.2 4.9 %copy-start.4 = (bf16[320,7168]{1,0:T(8,128)(2,1)S(1)}, bf16[320,7168]{1,0:T(8,128)(2,1)}, u32[]{:S(2)}) copy-start(bf16[320,7168]{1,0:T(8,128)(2,1)} %all-gather.4.cloned.1.call-done) | copy-start | bytes 13762564
  89.2 5.9 %copy-start.5 = (bf16[1,7168,256]{2,1,0:T(8,128)(2,1)S(1)}, bf16[1,7168,256]{2,1,0:T(8,128)(2,1)}, u32[]{:S(2)}) copy-start(bf16[1,7168,256]{2,1,0:T(8,128)(2,1)} %param.12) | copy-start | bytes 11010052
  95.0 2.0 %copy-start.1 = (bf16[1,256,7168]{2,1,0:T(8,128)(2,1)S(1)}, bf16[1,256,7168]{2,1,0:T(8,128)(2,1)}, u32[]{:S(2)}) copy-start(bf16[1,256,7168]{2,1,0:T(8,128)(2,1)} %param.13) | copy-start | bytes 11010052
  95.0 3.9 %slice-start = ((s8[4587520]{0:T(1024)(128)(4,1)}), s8[4194304]{0:T(1024)(128)(4,1)S(1)}, s32[]{:S(2)}) async-start(s8[4587520]{0:T(1024)(128)(4,1)} %bitcast.68), calls=%async_computation.4 | async-start | bytes 8388608
  97.1 1.9 slice-start.1
  98.6 2.0 %copy-start.6 = (bf16[1,7168,256]{2,1,0:T(8,128)(2,1)S(1)}, bf16[1,7168,256]{2,1,0:T(8,128)(2,1)}, u32[]{:S(2)}) copy-start(bf16[1,7168,256]{2,1,0:T(8,128)(2,1)} %param.11) | copy-start | bytes 11010052
  98.6 6.7 %collective-permute-start.2 = (bf16[160,7168]{1,0:T(8,128)(2,1)S(1)}, bf16[160,7168]{1,0:T(8,128)(2,1)S(1)}, u32[]{:S(2)}, u32[]{:S(2)}) collective-permute-start(bf16[160,7168]{1,0:T(8,128)(2,1)S(1)} %dynamic-slice_bitcast_fusion), channel_id=1, source_target_pairs={{0,1},{1,0},{2,3},{3,2},{4,5},{5,4},{6,7},{7,6},{8,9},{9,8},{10,11... | collective-permute-start | bytes 6881288 | tf_op jit(solution)/shard_map/ppermute | solution.py:30
  103.4 4.1 %copy-start = (bf16[320,7168]{1,0:T(8,128)(2,1)}, bf16[320,7168]{1,0:T(8,128)(2,1)S(1)}, u32[]{:S(2)}) copy-start(bf16[320,7168]{1,0:T(8,128)(2,1)S(1)} %convolution_convert_fusion.1) | copy-start | bytes 13762564
  105.1 6.0 %collective-permute-start.1 = (bf16[160,7168]{1,0:T(8,128)(2,1)}, bf16[160,7168]{1,0:T(8,128)(2,1)}, u32[]{:S(2)}, u32[]{:S(2)}) collective-permute-start(bf16[160,7168]{1,0:T(8,128)(2,1)} %dynamic-slice_bitcast_fusion.1), channel_id=1, source_target_pairs={{0,1},{1,0},{2,3},{3,2},{4,5},{5,4},{6,7},{7,6},{8,9},{9,8},{10,11... | collective-permute-start | bytes 6881288 | tf_op jit(solution)/shard_map/ppermute | solution.py:30
  107.5 31.3 %all-to-all-start = ((bf16[4,40,7168]{2,1,0:T(8,128)(2,1)}), bf16[4,40,7168]{2,1,0:T(8,128)(2,1)S(1)}, u32[]{:S(2)}, u32[]{:S(2)}) async-start(bf16[4,40,7168]{2,1,0:T(8,128)(2,1)} %bitcast.65), calls=%async_computation | async-start | bytes 4587520 | tf_op jit(solution)/shard_map/all_to_all | solution.py:36
  115.5 27.7 %copy-start.3 = (f32[64,1]{0,1:T(1,128)S(1)}, f32[64,1]{0,1:T(1,128)}, u32[]{:S(2)}) copy-start(f32[64,1]{0,1:T(1,128)} %param.10) | copy-start | bytes 772
  138.8 32.7 %all-to-all-start.1 = ((bf16[4,40,7168]{2,1,0:T(8,128)(2,1)}), bf16[4,40,7168]{2,1,0:T(8,128)(2,1)}, u32[]{:S(2)}, u32[]{:S(2)}) async-start(bf16[4,40,7168]{2,1,0:T(8,128)(2,1)} %bitcast.10), calls=%async_computation.1 | async-start | bytes 4587520 | tf_op jit(solution)/shard_map/all_to_all | solution.py:36
  143.5 24.5 %collective-permute-start.3 = (f32[40]{0:T(128)S(1)}, f32[40]{0:T(128)S(1)}, u32[]{:S(2)}, u32[]{:S(2)}) collective-permute-start(f32[40]{0:T(128)S(1)} %get-tuple-element.16), channel_id=1, source_target_pairs={{0,8},{8,0},{1,9},{9,1},{2,10},{10,2},{3,11},{11,3},{4,12},{12,4},... | collective-permute-start | bytes 488 | tf_op jit(solution)/shard_map/ppermute | solution.py:75
  168.1 27.3 %collective-permute-start.4 = (bf16[40,7168]{1,0:T(8,128)(2,1)S(1)}, bf16[40,7168]{1,0:T(8,128)(2,1)S(1)}, u32[]{:S(2)}, u32[]{:S(2)}) collective-permute-start(bf16[40,7168]{1,0:T(8,128)(2,1)S(1)} %multiply_convert_fusion.1), channel_id=1, source_target_pairs={{0,8},{8,0},{1,9},{9,1},{2,10},{10,2},{3,11},{11,3},{4,12},{12,4},... | collective-permute-start | bytes 1720328 | tf_op jit(solution)/shard_map/ppermute | solution.py:85
Sparse Core Ops, SparseCore 0:
  11.2 44.3 all-gather.5
  57.3 31.8 all-gather.3

commit v6 on v5

--- a/solution.py
+++ b/solution.py
@@ -74,7 +74,7 @@
     away = [lax.ppermute(packed[k], "eg", shift(k)) for k in range(1, experts)]
     away_w = [lax.ppermute(packed_w[k], "eg", shift(k)) for k in range(1, experts)]
     own_rows = gather(packed[0])
-    own_rows, away = lax.optimization_barrier((own_rows, away))
+    own_rows, away, away_w = lax.optimization_barrier((own_rows, away, away_w))
     own_parts = expert_parts(own_rows, *weights)
     away_parts = expert_parts(gather(jnp.concatenate(away, axis=0)), *weights)
     away_back = chip_sums(away_parts)

time: 204 us -> 194 us (0.951)
  waiting for transfers between devices: 140 us -> 133 us
  starting transfers between devices: 18.6 us -> 15.3 us
    all_to_all x2, waiting for transfers between devices: 23.2 us -> 59.8 us  [chip_sums(): return lax.all_to_all(paired, 'sc', split_axis=0, concat_axis=0, tiled=True)]
    ppermute x1, waiting for transfers between devices: 25.3 us -> 0.01 us  [shards(): away = [lax.ppermute(packed[k], 'eg', shift(k)) for k in range(1, experts)]]
    ppermute x1, waiting for transfers between devices: 21.7 us -> 0.01 us  [shards(): lax.ppermute(done[(k - 1) * slots:k * slots], 'eg', shift(experts - k))]
    ppermute x1, waiting for transfers between devices: 21.6 us -> 25 us  [shards(): lax.ppermute(packed_w[k], 'eg', shift(k))]
    ppermute x1, starting transfers between devices: 2.49 us -> 0.09 us  [shards(): lax.ppermute(packed_w[k], 'eg', shift(k))]
  transfers between devices with their start and end apart: 9 -> 9, of which waited for: 6 -> 5; matrix products, arithmetic and copies ran while one was open for 8% -> 8% of each run, Pallas kernels for 0% -> 0%
where the time goes in v6:
time: 194 us; the launch traced here: 193 us
  waiting for transfers between devices  133 us (69%)
  matrix products  15.7 us (8%)
  starting transfers between devices  15.3 us (8%)
  between operations  13.6 us (7%)
  other arithmetic  10.4 us (5%)
  local copies, waits for them, and re-layouts  4.91 us (3%)
    all_to_all x2, waiting for transfers between devices, chip_sums(): return lax.all_to_all(paired, 'sc', split_axis=0, concat_axis=0, tiled=True)  59.8 us
    all_gather x2, waiting for transfers between devices, gather(): return lax.all_gather(held, ('core', 'sc'), axis=0, tiled=True)  48.5 us
    ppermute x1, waiting for transfers between devices, shards(): lax.ppermute(packed_w[k], 'eg', shift(k))  25 us
    all_to_all x2, starting transfers between devices, chip_sums(): return lax.all_to_all(paired, 'sc', split_axis=0, concat_axis=0, tiled=True)  8.1 us
    convert_element_type x2, other arithmetic, expert_parts(): (halves[core].astype(jnp.float32) + sibling.astype(jnp.float32)).astype(j...  6.56 us
    dot_general x2, matrix products, slice_ffn(): gate = jnp.dot(rows, gate_w, preferred_element_type=jnp.float32)  6.28 us
    ppermute x1, starting transfers between devices, shards(): away = [lax.ppermute(packed[k], 'eg', shift(k)) for k in range(1, experts)]  4.1 us
  transfers between devices with their start and end apart: 9, of which 5 were waited for; matrix products, arithmetic and copies ran while one was open for 8% of the time, Pallas kernels for 0%

profile of v6, /device:TPU:0, one launch (start us, length us, event | category | flops | bytes accessed | tf_op | source)
XLA Modules:
  0.0 193.3 jit_solution(9296408139941177842)
XLA Ops:
  6.5 0.7 fusion.39
  7.2 0.1 fusion.28
  7.3 0.1 copy.9
  7.4 0.1 reduce_window_sum.11
  7.5 0.1 fusion.36
  7.5 0.1 copy.8
  7.6 2.1 %multiply_reduce_fusion = (f32[64]{0:T(128)S(1)}, f32[64,7168]{1,0:T(8,128)S(1)}) fusion(bf16[64,7168]{1,0:T(8,128)(2,1)} %param.7, s32[64]{0:T(128)} %param.8), kind=kOutput, calls=%fused_computation.25 | convolution fusion | flops 60559296 | bytes 2753024 | tf_op jit(solution)/shard_map/dot_general | solution.py:52
  9.7 0.5 convolution_convert_fusion.2
  10.2 0.9 slice_bitcast_fusion
  11.1 0.0 all-gather.6.cloned.1.call-update
  11.1 0.0 all-gather.4.cloned.1.call-start
  11.2 4.1 %collective-permute-start = (bf16[40,7168]{1,0:T(8,128)(2,1)S(1)}, bf16[40,7168]{1,0:T(8,128)(2,1)S(1)}, u32[]{:S(2)}, u32[]{:S(2)}) collective-permute-start(bf16[40,7168]{1,0:T(8,128)(2,1)S(1)} %get-tuple-element.15), channel_id=1, source_target_pairs={{0,8},{8,0},{1,9},{9,1},{2,10},{10,2},{3,11},{11,3},{4,12},{12,4},... | collective-permute-start | bytes 1720328 | tf_op jit(solution)/shard_map/ppermute | solution.py:74
  15.3 0.1 fusion.27
  15.4 0.1 copy.10
  15.5 0.1 select_reduce_fusion
  15.6 0.1 collective-permute-start.1
  15.6 25.0 %collective-permute-done.1 = f32[40]{0:T(128)S(1)} collective-permute-done((f32[40]{0:T(128)S(1)}, f32[40]{0:T(128)S(1)}, u32[]{:S(2)}, u32[]{:S(2)}) %collective-permute-start.1) | collective-permute-done | bytes 192 | tf_op jit(solution)/shard_map/ppermute | solution.py:75
  40.7 15.0 %all-gather.6.cloned.1.call-done = bf16[1,320,7168]{2,1,0:T(8,128)(2,1)} async-done(((bf16[1,40,7168]{2,1,0:T(8,128)(2,1)}), bf16[1,320,7168]{2,1,0:T(8,128)(2,1)}) %all-gather.6.cloned.1.call-update) | async-done | bytes 4587536 | tf_op jit(solution)/shard_map/all_gather | solution.py:18
  55.7 0.0 all-gather.4.cloned.1.call-update
  55.8 33.4 %all-gather.4.cloned.1.call-done = bf16[320,7168]{1,0:T(8,128)(2,1)} async-done(((bf16[40,7168]{1,0:T(8,128)(2,1)}), bf16[320,7168]{1,0:T(8,128)(2,1)}) %all-gather.4.cloned.1.call-update) | async-done | bytes 4587536 | tf_op jit(solution)/shard_map/all_gather | solution.py:18
  89.2 4.9 %fusion.9 = f32[320,256]{1,0:T(8,128)S(1)} fusion(bf16[320,7168]{1,0:T(8,128)(2,1)} %all-gather.4.cloned.1.call-done, bf16[1,7168,256]{2,1,0:T(8,128)(2,1)} %param.11), kind=kOutput, calls=%fused_computation.18 | convolution fusion | flops 1174405120 | bytes 8585216 | tf_op jit(solution)/shard_map/dot_general | solution.py:11
  94.1 0.9 copy-done.5
  95.1 1.4 fusion.16
  96.4 0.6 copy-done.1
  97.1 1.4 convolution_convert_fusion
  98.5 0.2 dynamic-slice_bitcast_fusion
  98.6 0.0 copy-start.6
  98.7 0.3 collective-permute-start.3
  99.0 1.3 fusion.7
  100.3 0.4 copy-done.6
  100.7 1.4 fusion.11
  102.1 1.4 convolution_convert_fusion.1
  103.5 1.7 dynamic-slice_bitcast_fusion.1
  105.1 0.2 collective-permute-start.2
  105.3 0.0 collective-permute-done.3
  105.4 2.1 %fusion.1 = bf16[160,7168]{1,0:T(8,128)(2,1)} fusion(bf16[160,7168]{1,0:T(8,128)(2,1)S(1)} %collective-permute-done.3, bf16[2,160,7168]{2,1,0:T(8,128)(2,1)S(1)} %bitcast.64, s32[]{:T(128)S(6)} %select_n.43), kind=kLoop, calls=%fused_computation.7 | loop fusion | flops 4587520 | bytes 6881284 | tf_op jit(solution)/shard_map/convert_element_type | solution.py:31
  107.5 3.6 %all-to-all-start = ((bf16[4,40,7168]{2,1,0:T(8,128)(2,1)}), bf16[4,40,7168]{2,1,0:T(8,128)(2,1)S(1)}, u32[]{:S(2)}, u32[]{:S(2)}) async-start(bf16[4,40,7168]{2,1,0:T(8,128)(2,1)} %bitcast.66), calls=%async_computation | async-start | bytes 4587520 | tf_op jit(solution)/shard_map/all_to_all | solution.py:36
  111.1 0.0 collective-permute-done.2
  111.1 4.4 %fusion.2 = bf16[160,7168]{1,0:T(8,128)(2,1)} fusion(bf16[160,7168]{1,0:T(8,128)(2,1)} %collective-permute-done.2, bf16[2,160,7168]{2,1,0:T(8,128)(2,1)} %bitcast.62, s32[]{:T(128)S(6)} %select_n.43), kind=kLoop, calls=%fused_computation.9 | loop fusion | flops 4587520 | bytes 6881284 | tf_op jit(solution)/shard_map/convert_element_type | solution.py:31
  115.6 23.3 %all-to-all-done = bf16[4,40,7168]{2,1,0:T(8,128)(2,1)S(1)} async-done(((bf16[4,40,7168]{2,1,0:T(8,128)(2,1)}), bf16[4,40,7168]{2,1,0:T(8,128)(2,1)S(1)}, u32[]{:S(2)}, u32[]{:S(2)}) %all-to-all-start) | async-done | bytes 2293792 | tf_op jit(solution)/shard_map/all_to_all | solution.py:36
  138.8 4.5 %all-to-all-start.1 = ((bf16[4,40,7168]{2,1,0:T(8,128)(2,1)}), bf16[4,40,7168]{2,1,0:T(8,128)(2,1)}, u32[]{:S(2)}, u32[]{:S(2)}) async-start(bf16[4,40,7168]{2,1,0:T(8,128)(2,1)} %bitcast.65), calls=%async_computation.1 | async-start | bytes 4587520 | tf_op jit(solution)/shard_map/all_to_all | solution.py:36
  143.3 0.3 convert_reduce_fusion
  143.6 0.1 multiply_convert_fusion.1
  143.8 2.5 %collective-permute-start.4 = (bf16[40,7168]{1,0:T(8,128)(2,1)S(1)}, bf16[40,7168]{1,0:T(8,128)(2,1)S(1)}, u32[]{:S(2)}, u32[]{:S(2)}) collective-permute-start(bf16[40,7168]{1,0:T(8,128)(2,1)S(1)} %multiply_convert_fusion.1), channel_id=1, source_target_pairs={{0,8},{8,0},{1,9},{9,1},{2,10},{10,2},{3,11},{11,3},{4,12},{12,4},... | collective-permute-start | bytes 1720328 | tf_op jit(solution)/shard_map/ppermute | solution.py:85
  146.2 36.6 %all-to-all-done.1 = bf16[4,40,7168]{2,1,0:T(8,128)(2,1)} async-done(((bf16[4,40,7168]{2,1,0:T(8,128)(2,1)}), bf16[4,40,7168]{2,1,0:T(8,128)(2,1)}, u32[]{:S(2)}, u32[]{:S(2)}) %all-to-all-start.1) | async-done | bytes 2293792 | tf_op jit(solution)/shard_map/all_to_all | solution.py:36
  182.8 2.1 %convert_reduce_fusion.1 = f32[40,7168]{1,0:T(8,128)S(1)} fusion(bf16[4,40,7168]{2,1,0:T(8,128)(2,1)} %all-to-all-done.1), kind=kLoop, calls=%fused_computation.11 | loop fusion | flops 2007040 | bytes 3440640 | tf_op jit(solution)/shard_map/reduce_sum | solution.py:40
  185.0 0.1 fusion.22
  185.1 1.4 fusion
  (20 shorter events, 0.0 us)
Async XLA Ops:
  6.5 49.2 %all-gather.6.cloned.1.call-start = ((), (), s32[]{:S(2)}) async-start(), calls=%async_computation.3 | async-start | bytes 5160960 | tf_op jit(solution)/shard_map/all_gather | solution.py:18
  7.6 7.7 %copy-start.3 = (f32[64,1]{0,1:T(1,128)S(1)}, f32[64,1]{0,1:T(1,128)}, u32[]{:S(2)}) copy-start(f32[64,1]{0,1:T(1,128)} %param.10) | copy-start | bytes 772
  11.1 78.0 %all-gather.4.cloned.1.call-start = ((), (), s32[]{:S(2)}) async-start(), calls=%async_computation.2 | async-start | bytes 5160960 | tf_op jit(solution)/shard_map/all_gather | solution.py:18
  11.2 29.5 %collective-permute-start = (bf16[40,7168]{1,0:T(8,128)(2,1)S(1)}, bf16[40,7168]{1,0:T(8,128)(2,1)S(1)}, u32[]{:S(2)}, u32[]{:S(2)}) collective-permute-start(bf16[40,7168]{1,0:T(8,128)(2,1)S(1)} %get-tuple-element.15), channel_id=1, source_target_pairs={{0,8},{8,0},{1,9},{9,1},{2,10},{10,2},{3,11},{11,3},{4,12},{12,4},... | collective-permute-start | bytes 1720328 | tf_op jit(solution)/shard_map/ppermute | solution.py:74
  15.6 25.1 %collective-permute-start.1 = (f32[40]{0:T(128)S(1)}, f32[40]{0:T(128)S(1)}, u32[]{:S(2)}, u32[]{:S(2)}) collective-permute-start(f32[40]{0:T(128)S(1)} %get-tuple-element.18), channel_id=1, source_target_pairs={{0,8},{8,0},{1,9},{9,1},{2,10},{10,2},{3,11},{11,3},{4,12},{12,4},... | collective-permute-start | bytes 488 | tf_op jit(solution)/shard_map/ppermute | solution.py:75
  40.7 15.0 %copy-start.2 = (bf16[40,7168]{1,0:T(8,128)(2,1)}, bf16[40,7168]{1,0:T(8,128)(2,1)S(1)}, u32[]{:S(2)}) copy-start(bf16[40,7168]{1,0:T(8,128)(2,1)S(1)} %collective-permute-done) | copy-start | bytes 1720324
  89.2 4.9 %copy-start.4 = (bf16[320,7168]{1,0:T(8,128)(2,1)S(1)}, bf16[320,7168]{1,0:T(8,128)(2,1)}, u32[]{:S(2)}) copy-start(bf16[320,7168]{1,0:T(8,128)(2,1)} %all-gather.4.cloned.1.call-done) | copy-start | bytes 13762564
  89.2 5.9 %copy-start.5 = (bf16[1,7168,256]{2,1,0:T(8,128)(2,1)S(1)}, bf16[1,7168,256]{2,1,0:T(8,128)(2,1)}, u32[]{:S(2)}) copy-start(bf16[1,7168,256]{2,1,0:T(8,128)(2,1)} %param.12) | copy-start | bytes 11010052
  95.1 2.0 %copy-start.1 = (bf16[1,256,7168]{2,1,0:T(8,128)(2,1)S(1)}, bf16[1,256,7168]{2,1,0:T(8,128)(2,1)}, u32[]{:S(2)}) copy-start(bf16[1,256,7168]{2,1,0:T(8,128)(2,1)} %param.13) | copy-start | bytes 11010052
  95.1 3.9 %slice-start = ((s8[4587520]{0:T(1024)(128)(4,1)}), s8[4194304]{0:T(1024)(128)(4,1)S(1)}, s32[]{:S(2)}) async-start(s8[4587520]{0:T(1024)(128)(4,1)} %bitcast.69), calls=%async_computation.4 | async-start | bytes 8388608
  97.1 1.9 slice-start.1
  98.6 2.0 %copy-start.6 = (bf16[1,7168,256]{2,1,0:T(8,128)(2,1)S(1)}, bf16[1,7168,256]{2,1,0:T(8,128)(2,1)}, u32[]{:S(2)}) copy-start(bf16[1,7168,256]{2,1,0:T(8,128)(2,1)} %param.11) | copy-start | bytes 11010052
  98.7 6.7 %collective-permute-start.3 = (bf16[160,7168]{1,0:T(8,128)(2,1)S(1)}, bf16[160,7168]{1,0:T(8,128)(2,1)S(1)}, u32[]{:S(2)}, u32[]{:S(2)}) collective-permute-start(bf16[160,7168]{1,0:T(8,128)(2,1)S(1)} %dynamic-slice_bitcast_fusion), channel_id=1, source_target_pairs={{0,1},{1,0},{2,3},{3,2},{4,5},{5,4},{6,7},{7,6},{8,9},{9,8},{10,11... | collective-permute-start | bytes 6881288 | tf_op jit(solution)/shard_map/ppermute | solution.py:30
  103.5 4.0 %copy-start = (bf16[320,7168]{1,0:T(8,128)(2,1)}, bf16[320,7168]{1,0:T(8,128)(2,1)S(1)}, u32[]{:S(2)}) copy-start(bf16[320,7168]{1,0:T(8,128)(2,1)S(1)} %convolution_convert_fusion.1) | copy-start | bytes 13762564
  105.1 6.0 %collective-permute-start.2 = (bf16[160,7168]{1,0:T(8,128)(2,1)}, bf16[160,7168]{1,0:T(8,128)(2,1)}, u32[]{:S(2)}, u32[]{:S(2)}) collective-permute-start(bf16[160,7168]{1,0:T(8,128)(2,1)} %dynamic-slice_bitcast_fusion.1), channel_id=1, source_target_pairs={{0,1},{1,0},{2,3},{3,2},{4,5},{5,4},{6,7},{7,6},{8,9},{9,8},{10,11... | collective-permute-start | bytes 6881288 | tf_op jit(solution)/shard_map/ppermute | solution.py:30
  107.5 31.3 %all-to-all-start = ((bf16[4,40,7168]{2,1,0:T(8,128)(2,1)}), bf16[4,40,7168]{2,1,0:T(8,128)(2,1)S(1)}, u32[]{:S(2)}, u32[]{:S(2)}) async-start(bf16[4,40,7168]{2,1,0:T(8,128)(2,1)} %bitcast.66), calls=%async_computation | async-start | bytes 4587520 | tf_op jit(solution)/shard_map/all_to_all | solution.py:36
  138.8 44.0 %all-to-all-start.1 = ((bf16[4,40,7168]{2,1,0:T(8,128)(2,1)}), bf16[4,40,7168]{2,1,0:T(8,128)(2,1)}, u32[]{:S(2)}, u32[]{:S(2)}) async-start(bf16[4,40,7168]{2,1,0:T(8,128)(2,1)} %bitcast.65), calls=%async_computation.1 | async-start | bytes 4587520 | tf_op jit(solution)/shard_map/all_to_all | solution.py:36
  143.8 41.3 %collective-permute-start.4 = (bf16[40,7168]{1,0:T(8,128)(2,1)S(1)}, bf16[40,7168]{1,0:T(8,128)(2,1)S(1)}, u32[]{:S(2)}, u32[]{:S(2)}) collective-permute-start(bf16[40,7168]{1,0:T(8,128)(2,1)S(1)} %multiply_convert_fusion.1), channel_id=1, source_target_pairs={{0,8},{8,0},{1,9},{9,1},{2,10},{10,2},{3,11},{11,3},{4,12},{12,4},... | collective-permute-start | bytes 1720328 | tf_op jit(solution)/shard_map/ppermute | solution.py:85
Sparse Core Ops, SparseCore 0:
  11.3 44.4 all-gather.5
  57.3 31.8 all-gather.3

commit v7 on v6

--- a/solution.py
+++ b/solution.py
@@ -76,7 +76,9 @@
     own_rows = gather(packed[0])
     own_rows, away, away_w = lax.optimization_barrier((own_rows, away, away_w))
     own_parts = expert_parts(own_rows, *weights)
-    away_parts = expert_parts(gather(jnp.concatenate(away, axis=0)), *weights)
+    away_rows = gather(jnp.concatenate(away, axis=0))
+    own_parts, away_rows = lax.optimization_barrier((own_parts, away_rows))
+    away_parts = expert_parts(away_rows, *weights)
     away_back = chip_sums(away_parts)
     own_parts, away_back = lax.optimization_barrier((own_parts, away_back))
     done = finish(away_back, jnp.concatenate(away_w, axis=0))

time: 194 us -> 187 us (0.964)
  waiting for transfers between devices: 133 us -> 95.5 us
  blocking collectives: 0 us -> 31.6 us
  starting transfers between devices: 15.3 us -> 11 us
  matrix products: 15.7 us -> 19.3 us
    all_to_all x0 -> x1, blocking collectives: none -> 31.6 us  [chip_sums(): return lax.all_to_all(paired, 'sc', split_axis=0, concat_axis=0, tiled=True)]
    all_to_all x2 -> x1, waiting for transfers between devices: 59.8 us -> 34.2 us  [chip_sums(): return lax.all_to_all(paired, 'sc', split_axis=0, concat_axis=0, tiled=True)]
    all_gather x2, waiting for transfers between devices: 48.5 us -> 27.8 us  [gather(): return lax.all_gather(held, ('core', 'sc'), axis=0, tiled=True)]
    ppermute x2, waiting for transfers between devices: 0.01 us -> 8.52 us  [expert_parts(): sibling = lax.ppermute(halves[(core + 1) % cores], 'core', swap)]
    all_to_all x2 -> x1, starting transfers between devices: 8.1 us -> 3.63 us  [chip_sums(): return lax.all_to_all(paired, 'sc', split_axis=0, concat_axis=0, tiled=True)]
    dot_general x2, matrix products: 2.72 us -> 6.26 us  [slice_ffn(): upper = jnp.dot(rows, up_w, preferred_element_type=jnp.float32)]
    unnamed x18 -> x20, local copies, waits for them, and re-layouts: 1.97 us -> 5.25 us
  transfers between devices with their start and end apart: 9 -> 8, of which waited for: 5 -> 6; matrix products, arithmetic and copies ran while one was open for 8% -> 8% of each run, Pallas kernels for 0% -> 0%
where the time goes in v7:
time: 187 us
  waiting for transfers between devices  95.5 us (51%)
  blocking collectives  31.6 us (17%)
  matrix products  19.3 us (10%)
  between operations  13.6 us (7%)
  starting transfers between devices  11 us (6%)
  other arithmetic  9.07 us (5%)
  local copies, waits for them, and re-layouts  6.68 us (4%)
    all_to_all x1, waiting for transfers between devices, chip_sums(): return lax.all_to_all(paired, 'sc', split_axis=0, concat_axis=0, tiled=True)  34.2 us
    all_to_all x1, blocking collectives, chip_sums(): return lax.all_to_all(paired, 'sc', split_axis=0, concat_axis=0, tiled=True)  31.6 us
    all_gather x2, waiting for transfers between devices, gather(): return lax.all_gather(held, ('core', 'sc'), axis=0, tiled=True)  27.8 us
    ppermute x1, waiting for transfers between devices, shards(): lax.ppermute(packed_w[k], 'eg', shift(k))  25 us
    ppermute x2, waiting for transfers between devices, expert_parts(): sibling = lax.ppermute(halves[(core + 1) % cores], 'core', swap)  8.52 us
    dot_general x2, matrix products, slice_ffn(): gate = jnp.dot(rows, gate_w, preferred_element_type=jnp.float32)  6.31 us
    dot_general x2, matrix products, slice_ffn(): upper = jnp.dot(rows, up_w, preferred_element_type=jnp.float32)  6.26 us
    unnamed x20, local copies, waits for them, and re-layouts  5.25 us
  transfers between devices with their start and end apart: 8, of which 6 were waited for; matrix products, arithmetic and copies ran while one was open for 8% of the time, Pallas kernels for 0%

profile of v7, /device:TPU:0, one launch (start us, length us, event | category | flops | bytes accessed | tf_op | source)
XLA Modules:
  0.0 186.7 jit_solution(5718888797226656219)
XLA Ops:
  6.5 2.1 %multiply_reduce_fusion = (f32[64]{0:T(128)S(1)}, f32[64,7168]{1,0:T(8,128)S(1)}) fusion(bf16[64,7168]{1,0:T(8,128)(2,1)} %param.7, s32[64]{0:T(128)} %param.8), kind=kOutput, calls=%fused_computation.25 | convolution fusion | flops 60559296 | bytes 2753024 | tf_op jit(solution)/shard_map/dot_general | solution.py:52
  8.6 0.7 fusion.39
  9.3 0.1 fusion.28
  9.4 0.1 copy.9
  9.5 0.1 reduce_window_sum.11
  9.6 0.1 fusion.36
  9.6 0.1 copy.8
  9.7 0.5 convolution_convert_fusion.2
  10.2 0.9 slice_bitcast_fusion
  11.1 0.0 all-gather.6.cloned.1.call-update
  11.2 0.0 all-gather.4.cloned.1.call-start
  11.2 4.1 %collective-permute-start = (bf16[40,7168]{1,0:T(8,128)(2,1)S(1)}, bf16[40,7168]{1,0:T(8,128)(2,1)S(1)}, u32[]{:S(2)}, u32[]{:S(2)}) collective-permute-start(bf16[40,7168]{1,0:T(8,128)(2,1)S(1)} %get-tuple-element.19), channel_id=1, source_target_pairs={{0,8},{8,0},{1,9},{9,1},{2,10},{10,2},{3,11},{11,3},{4,12},{12,4},... | collective-permute-start | bytes 1720328 | tf_op jit(solution)/shard_map/ppermute | solution.py:74
  15.3 0.1 fusion.27
  15.4 0.1 copy.10
  15.5 0.1 select_reduce_fusion
  15.6 0.1 collective-permute-start.1
  15.7 25.0 %collective-permute-done.1 = f32[40]{0:T(128)S(1)} collective-permute-done((f32[40]{0:T(128)S(1)}, f32[40]{0:T(128)S(1)}, u32[]{:S(2)}, u32[]{:S(2)}) %collective-permute-start.1) | collective-permute-done | bytes 192 | tf_op jit(solution)/shard_map/ppermute | solution.py:75
  40.7 15.0 %all-gather.6.cloned.1.call-done = bf16[1,320,7168]{2,1,0:T(8,128)(2,1)} async-done(((bf16[1,40,7168]{2,1,0:T(8,128)(2,1)}), bf16[1,320,7168]{2,1,0:T(8,128)(2,1)}) %all-gather.6.cloned.1.call-update) | async-done | bytes 4587536 | tf_op jit(solution)/shard_map/all_gather | solution.py:18
  55.7 0.0 all-gather.4.cloned.1.call-update
  55.8 4.9 %fusion.7 = f32[320,256]{1,0:T(8,128)S(1)} fusion(bf16[320,7168]{1,0:T(8,128)(2,1)} %bitcast.68, bf16[1,7168,256]{2,1,0:T(8,128)(2,1)} %param.12), kind=kOutput, calls=%fused_computation.16 | convolution fusion | flops 1174405120 | bytes 8585216 | tf_op jit(solution)/shard_map/dot_general | solution.py:12
  60.7 0.9 copy-done.6
  61.6 1.4 fusion.11
  63.0 0.6 copy-done.1
  63.6 1.4 convolution_convert_fusion.1
  65.0 2.1 %copy-done = bf16[320,7168]{1,0:T(8,128)(2,1)} copy-done((bf16[320,7168]{1,0:T(8,128)(2,1)}, bf16[320,7168]{1,0:T(8,128)(2,1)S(1)}, u32[]{:S(2)}) %copy-start) | copy-done | bytes 4587544
  67.2 0.1 dynamic-slice_bitcast_fusion.1
  67.3 0.3 collective-permute-start.2
  67.6 4.3 %collective-permute-done.2 = bf16[160,7168]{1,0:T(8,128)(2,1)} collective-permute-done((bf16[160,7168]{1,0:T(8,128)(2,1)S(1)}, bf16[160,7168]{1,0:T(8,128)(2,1)}, u32[]{:S(2)}, u32[]{:S(2)}) %collective-permute-start.2) | collective-permute-done | bytes 2293792 | tf_op jit(solution)/shard_map/ppermute | solution.py:30
  72.0 4.5 %fusion.2 = bf16[160,7168]{1,0:T(8,128)(2,1)} fusion(bf16[160,7168]{1,0:T(8,128)(2,1)} %collective-permute-done.2, bf16[2,160,7168]{2,1,0:T(8,128)(2,1)} %bitcast.62, s32[]{:T(128)S(6)} %select_n.43), kind=kLoop, calls=%fused_computation.9 | loop fusion | flops 4587520 | bytes 6881284 | tf_op jit(solution)/shard_map/convert_element_type | solution.py:31
  76.5 12.7 %all-gather.4.cloned.1.call-done = bf16[320,7168]{1,0:T(8,128)(2,1)} async-done(((bf16[40,7168]{1,0:T(8,128)(2,1)}), bf16[320,7168]{1,0:T(8,128)(2,1)}) %all-gather.4.cloned.1.call-update) | async-done | bytes 4587536 | tf_op jit(solution)/shard_map/all_gather | solution.py:18
  89.2 4.9 %fusion.9 = f32[320,256]{1,0:T(8,128)S(1)} fusion(bf16[320,7168]{1,0:T(8,128)(2,1)} %all-gather.4.cloned.1.call-done, bf16[1,7168,256]{2,1,0:T(8,128)(2,1)} %param.11), kind=kOutput, calls=%fused_computation.18 | convolution fusion | flops 1174405120 | bytes 8585216 | tf_op jit(solution)/shard_map/dot_general | solution.py:11
  94.1 0.9 copy-done.7
  95.1 1.3 fusion.16
  96.4 0.7 copy-done.2
  97.1 1.4 convolution_convert_fusion
  98.5 0.2 dynamic-slice_bitcast_fusion
  98.6 0.3 collective-permute-start.3
  98.9 4.2 %collective-permute-done.3 = bf16[160,7168]{1,0:T(8,128)(2,1)S(1)} collective-permute-done((bf16[160,7168]{1,0:T(8,128)(2,1)S(1)}, bf16[160,7168]{1,0:T(8,128)(2,1)S(1)}, u32[]{:S(2)}, u32[]{:S(2)}) %collective-permute-start.3) | collective-permute-done | bytes 2293792 | tf_op jit(solution)/shard_map/ppermute | solution.py:30
  103.1 0.7 fusion.1
  103.9 31.6 %all_to_all.10 = bf16[4,40,7168]{2,1,0:T(8,128)(2,1)} all-to-all(bf16[4,40,7168]{2,1,0:T(8,128)(2,1)S(1)} %bitcast.65), channel_id=1, replica_groups=mesh['grp'=2,'eg'=2,'sc'=4,'core'=2] {'sc'}, dimensions={0} | all-to-all | bytes 4587520 | tf_op jit(solution)/shard_map/all_to_all | solution.py:36
  135.4 3.6 %all-to-all-start.1 = ((bf16[4,40,7168]{2,1,0:T(8,128)(2,1)}), bf16[4,40,7168]{2,1,0:T(8,128)(2,1)S(1)}, u32[]{:S(2)}, u32[]{:S(2)}) async-start(bf16[4,40,7168]{2,1,0:T(8,128)(2,1)} %bitcast.12), calls=%async_computation.1 | async-start | bytes 4587520 | tf_op jit(solution)/shard_map/all_to_all | solution.py:36
  139.1 2.1 %convert_reduce_fusion = f32[40,7168]{1,0:T(8,128)S(1)} fusion(bf16[4,40,7168]{2,1,0:T(8,128)(2,1)} %all_to_all.10), kind=kLoop, calls=%fused_computation.10 | loop fusion | flops 2007040 | bytes 3440640 | tf_op jit(solution)/shard_map/reduce_sum | solution.py:40
  141.2 0.1 multiply_convert_fusion.1
  141.4 2.5 %collective-permute-start.4 = (bf16[40,7168]{1,0:T(8,128)(2,1)S(1)}, bf16[40,7168]{1,0:T(8,128)(2,1)S(1)}, u32[]{:S(2)}, u32[]{:S(2)}) collective-permute-start(bf16[40,7168]{1,0:T(8,128)(2,1)S(1)} %multiply_convert_fusion.1), channel_id=1, source_target_pairs={{0,8},{8,0},{1,9},{9,1},{2,10},{10,2},{3,11},{11,3},{4,12},{12,4},... | collective-permute-start | bytes 1720328 | tf_op jit(solution)/shard_map/ppermute | solution.py:87
  143.8 34.2 %all-to-all-done.1 = bf16[4,40,7168]{2,1,0:T(8,128)(2,1)S(1)} async-done(((bf16[4,40,7168]{2,1,0:T(8,128)(2,1)}), bf16[4,40,7168]{2,1,0:T(8,128)(2,1)S(1)}, u32[]{:S(2)}, u32[]{:S(2)}) %all-to-all-start.1) | async-done | bytes 2293792 | tf_op jit(solution)/shard_map/all_to_all | solution.py:36
  178.0 0.3 convert_reduce_fusion.1
  178.3 0.1 fusion.22
  178.5 1.4 fusion
  (21 shorter events, 0.1 us)
Async XLA Ops:
  6.5 49.2 %all-gather.6.cloned.1.call-start = ((), (), s32[]{:S(2)}) async-start(), calls=%async_computation.3 | async-start | bytes 5160960 | tf_op jit(solution)/shard_map/all_gather | solution.py:18
  8.6 6.7 %copy-start.4 = (f32[64,1]{0,1:T(1,128)S(1)}, f32[64,1]{0,1:T(1,128)}, u32[]{:S(2)}) copy-start(f32[64,1]{0,1:T(1,128)} %param.10) | copy-start | bytes 772
  11.2 78.1 %all-gather.4.cloned.1.call-start = ((), (), s32[]{:S(2)}) async-start(), calls=%async_computation.2 | async-start | bytes 5160960 | tf_op jit(solution)/shard_map/all_gather | solution.py:18
  11.2 29.5 %collective-permute-start = (bf16[40,7168]{1,0:T(8,128)(2,1)S(1)}, bf16[40,7168]{1,0:T(8,128)(2,1)S(1)}, u32[]{:S(2)}, u32[]{:S(2)}) collective-permute-start(bf16[40,7168]{1,0:T(8,128)(2,1)S(1)} %get-tuple-element.19), channel_id=1, source_target_pairs={{0,8},{8,0},{1,9},{9,1},{2,10},{10,2},{3,11},{11,3},{4,12},{12,4},... | collective-permute-start | bytes 1720328 | tf_op jit(solution)/shard_map/ppermute | solution.py:74
  15.6 25.1 %collective-permute-start.1 = (f32[40]{0:T(128)S(1)}, f32[40]{0:T(128)S(1)}, u32[]{:S(2)}, u32[]{:S(2)}) collective-permute-start(f32[40]{0:T(128)S(1)} %get-tuple-element.22), channel_id=1, source_target_pairs={{0,8},{8,0},{1,9},{9,1},{2,10},{10,2},{3,11},{11,3},{4,12},{12,4},... | collective-permute-start | bytes 488 | tf_op jit(solution)/shard_map/ppermute | solution.py:75
  40.7 15.0 %copy-start.3 = (bf16[40,7168]{1,0:T(8,128)(2,1)}, bf16[40,7168]{1,0:T(8,128)(2,1)S(1)}, u32[]{:S(2)}) copy-start(bf16[40,7168]{1,0:T(8,128)(2,1)S(1)} %collective-permute-done) | copy-start | bytes 1720324
  55.7 5.0 %slice-start = ((s8[4587520]{0:T(1024)(128)(4,1)}), s8[393216]{0:T(1024)(128)(4,1)S(1)}, s32[]{:S(2)}) async-start(s8[4587520]{0:T(1024)(128)(4,1)} %bitcast.69), calls=%async_computation.4 | async-start | bytes 786432
  55.8 5.0 %slice-start.1 = ((s8[4587520]{0:T(1024)(128)(4,1)}), s8[4194304]{0:T(1024)(128)(4,1)S(1)}, s32[]{:S(2)}) async-start(s8[4587520]{0:T(1024)(128)(4,1)} %bitcast.69), calls=%async_computation.5 | async-start | bytes 8388608
  55.8 5.8 %copy-start.6 = (bf16[1,7168,256]{2,1,0:T(8,128)(2,1)S(1)}, bf16[1,7168,256]{2,1,0:T(8,128)(2,1)}, u32[]{:S(2)}) copy-start(bf16[1,7168,256]{2,1,0:T(8,128)(2,1)} %param.11) | copy-start | bytes 11010052
  61.6 2.0 %copy-start.1 = (bf16[1,256,7168]{2,1,0:T(8,128)(2,1)S(1)}, bf16[1,256,7168]{2,1,0:T(8,128)(2,1)}, u32[]{:S(2)}) copy-start(bf16[1,256,7168]{2,1,0:T(8,128)(2,1)} %param.13) | copy-start | bytes 11010052
  65.0 2.1 %copy-start = (bf16[320,7168]{1,0:T(8,128)(2,1)}, bf16[320,7168]{1,0:T(8,128)(2,1)S(1)}, u32[]{:S(2)}) copy-start(bf16[320,7168]{1,0:T(8,128)(2,1)S(1)} %convolution_convert_fusion.1) | copy-start | bytes 13762564
  67.3 4.6 %collective-permute-start.2 = (bf16[160,7168]{1,0:T(8,128)(2,1)S(1)}, bf16[160,7168]{1,0:T(8,128)(2,1)}, u32[]{:S(2)}, u32[]{:S(2)}) collective-permute-start(bf16[160,7168]{1,0:T(8,128)(2,1)S(1)} %dynamic-slice_bitcast_fusion.1), channel_id=1, source_target_pairs={{0,1},{1,0},{2,3},{3,2},{4,5},{5,4},{6,7},{7,6},{8,9},{9,8},{10,11... | collective-permute-start | bytes 6881288 | tf_op jit(solution)/shard_map/ppermute | solution.py:30
  89.2 4.9 %copy-start.5 = (bf16[320,7168]{1,0:T(8,128)(2,1)S(1)}, bf16[320,7168]{1,0:T(8,128)(2,1)}, u32[]{:S(2)}) copy-start(bf16[320,7168]{1,0:T(8,128)(2,1)} %all-gather.4.cloned.1.call-done) | copy-start | bytes 13762564
  89.2 5.9 %copy-start.7 = (bf16[1,7168,256]{2,1,0:T(8,128)(2,1)S(1)}, bf16[1,7168,256]{2,1,0:T(8,128)(2,1)}, u32[]{:S(2)}) copy-start(bf16[1,7168,256]{2,1,0:T(8,128)(2,1)} %param.12) | copy-start | bytes 11010052
  95.1 2.0 %copy-start.2 = (bf16[1,256,7168]{2,1,0:T(8,128)(2,1)S(1)}, bf16[1,256,7168]{2,1,0:T(8,128)(2,1)}, u32[]{:S(2)}) copy-start(bf16[1,256,7168]{2,1,0:T(8,128)(2,1)} %param.13) | copy-start | bytes 11010052
  98.6 4.5 %collective-permute-start.3 = (bf16[160,7168]{1,0:T(8,128)(2,1)S(1)}, bf16[160,7168]{1,0:T(8,128)(2,1)S(1)}, u32[]{:S(2)}, u32[]{:S(2)}) collective-permute-start(bf16[160,7168]{1,0:T(8,128)(2,1)S(1)} %dynamic-slice_bitcast_fusion), channel_id=1, source_target_pairs={{0,1},{1,0},{2,3},{3,2},{4,5},{5,4},{6,7},{7,6},{8,9},{9,8},{10,11... | collective-permute-start | bytes 6881288 | tf_op jit(solution)/shard_map/ppermute | solution.py:30
  135.4 42.6 %all-to-all-start.1 = ((bf16[4,40,7168]{2,1,0:T(8,128)(2,1)}), bf16[4,40,7168]{2,1,0:T(8,128)(2,1)S(1)}, u32[]{:S(2)}, u32[]{:S(2)}) async-start(bf16[4,40,7168]{2,1,0:T(8,128)(2,1)} %bitcast.12), calls=%async_computation.1 | async-start | bytes 4587520 | tf_op jit(solution)/shard_map/all_to_all | solution.py:36
  141.4 37.1 %collective-permute-start.4 = (bf16[40,7168]{1,0:T(8,128)(2,1)S(1)}, bf16[40,7168]{1,0:T(8,128)(2,1)S(1)}, u32[]{:S(2)}, u32[]{:S(2)}) collective-permute-start(bf16[40,7168]{1,0:T(8,128)(2,1)S(1)} %multiply_convert_fusion.1), channel_id=1, source_target_pairs={{0,8},{8,0},{1,9},{9,1},{2,10},{10,2},{3,11},{11,3},{4,12},{12,4},... | collective-permute-start | bytes 1720328 | tf_op jit(solution)/shard_map/ppermute | solution.py:87
Sparse Core Ops, SparseCore 0:
  11.3 44.4 all-gather.5
  57.3 31.8 all-gather.3

commit v8 on v7

--- a/solution.py
+++ b/solution.py
@@ -78,11 +78,15 @@
     own_parts = expert_parts(own_rows, *weights)
     away_rows = gather(jnp.concatenate(away, axis=0))
     own_parts, away_rows = lax.optimization_barrier((own_parts, away_rows))
+    half = slots // 2
+    own_early = chip_sums(own_parts[:, :half])
     away_parts = expert_parts(away_rows, *weights)
+    own_early, away_parts = lax.optimization_barrier((own_early, away_parts))
     away_back = chip_sums(away_parts)
-    own_parts, away_back = lax.optimization_barrier((own_parts, away_back))
+    own_late, away_back = lax.optimization_barrier((own_parts[:, half:], away_back))
     done = finish(away_back, jnp.concatenate(away_w, axis=0))
-    own = finish(chip_sums(own_parts), packed_w[0])
+    own_back = jnp.concatenate([own_early, chip_sums(own_late)], axis=1)
+    own = finish(own_back, packed_w[0])
     home = [own] + [
         lax.ppermute(done[(k - 1) * slots:k * slots], "eg", shift(experts - k))
         for k in range(1, experts)

time: 187 us -> 200 us (1.070)
  starting transfers between devices: 11 us -> 16 us
  local copies, waits for them, and re-layouts: 6.68 us -> 10.2 us
  waiting for transfers between devices: 95.5 us -> 98.8 us
    all_to_all x1 -> x2, waiting for transfers between devices: 34.2 us -> 40.2 us  [chip_sums(): return lax.all_to_all(paired, 'sc', split_axis=0, concat_axis=0, tiled=True)]
    all_to_all x1 -> x2, starting transfers between devices: 3.63 us -> 8.73 us  [chip_sums(): return lax.all_to_all(paired, 'sc', split_axis=0, concat_axis=0, tiled=True)]
    ppermute x2, waiting for transfers between devices: 8.52 us -> 4.33 us  [expert_parts(): sibling = lax.ppermute(halves[(core + 1) % cores], 'core', swap)]
    dot_general x2, matrix products: 6.31 us -> 9.83 us  [slice_ffn(): gate = jnp.dot(rows, gate_w, preferred_element_type=jnp.float32)]
    dot_general x2, matrix products: 6.26 us -> 2.75 us  [slice_ffn(): upper = jnp.dot(rows, up_w, preferred_element_type=jnp.float32)]
    unnamed x20 -> x24, local copies, waits for them, and re-layouts: 5.25 us -> 5.26 us
  transfers between devices with their start and end apart: 8 -> 9, of which waited for: 6 -> 6; matrix products, arithmetic and copies ran while one was open for 8% -> 10% of each run, Pallas kernels for 0% -> 0%
where the time goes in v8:
time: 200 us; the launch traced here: 199 us
  waiting for transfers between devices  98.8 us (49%)
  blocking collectives  30.8 us (15%)
  matrix products  19.3 us (10%)
  starting transfers between devices  16 us (8%)
  between operations  13.6 us (7%)
  other arithmetic  10.4 us (5%)
  local copies, waits for them, and re-layouts  10.2 us (5%)
    all_to_all x2, waiting for transfers between devices, chip_sums(): return lax.all_to_all(paired, 'sc', split_axis=0, concat_axis=0, tiled=True)  40.2 us
    all_to_all x1, blocking collectives, chip_sums(): return lax.all_to_all(paired, 'sc', split_axis=0, concat_axis=0, tiled=True)  30.8 us
    all_gather x2, waiting for transfers between devices, gather(): return lax.all_gather(held, ('core', 'sc'), axis=0, tiled=True)  29.1 us
    ppermute x1, waiting for transfers between devices, shards(): lax.ppermute(packed_w[k], 'eg', shift(k))  25 us
    dot_general x2, matrix products, slice_ffn(): gate = jnp.dot(rows, gate_w, preferred_element_type=jnp.float32)  9.83 us
    all_to_all x2, starting transfers between devices, chip_sums(): return lax.all_to_all(paired, 'sc', split_axis=0, concat_axis=0, tiled=True)  8.73 us
    convert_element_type x2, other arithmetic, expert_parts(): (halves[core].astype(jnp.float32) + sibling.astype(jnp.float32)).astype(j...  6.18 us
    unnamed x24, local copies, waits for them, and re-layouts  5.26 us
  transfers between devices with their start and end apart: 9, of which 6 were waited for; matrix products, arithmetic and copies ran while one was open for 10% of the time, Pallas kernels for 0%

profile of v8, /device:TPU:0, one launch (start us, length us, event | category | flops | bytes accessed | tf_op | source)
XLA Modules:
  0.0 199.1 jit_solution(3066624389795463290)
XLA Ops:
  6.5 0.7 fusion.39
  7.2 0.1 fusion.28
  7.3 0.1 copy.9
  7.4 0.1 reduce_window_sum.11
  7.5 0.1 fusion.36
  7.5 0.1 copy.8
  7.6 2.1 %multiply_reduce_fusion = (f32[64]{0:T(128)S(1)}, f32[64,7168]{1,0:T(8,128)S(1)}) fusion(bf16[64,7168]{1,0:T(8,128)(2,1)} %param.7, s32[64]{0:T(128)} %param.8), kind=kOutput, calls=%fused_computation.25 | convolution fusion | flops 60559296 | bytes 2753024 | tf_op jit(solution)/shard_map/dot_general | solution.py:52
  9.7 0.5 convolution_convert_fusion.2
  10.2 0.9 slice_bitcast_fusion
  11.1 0.0 all-gather.4.cloned.1.call-start
  11.2 4.1 %collective-permute-start = (bf16[40,7168]{1,0:T(8,128)(2,1)S(1)}, bf16[40,7168]{1,0:T(8,128)(2,1)S(1)}, u32[]{:S(2)}, u32[]{:S(2)}) collective-permute-start(bf16[40,7168]{1,0:T(8,128)(2,1)S(1)} %get-tuple-element.25), channel_id=1, source_target_pairs={{0,8},{8,0},{1,9},{9,1},{2,10},{10,2},{3,11},{11,3},{4,12},{12,4},... | collective-permute-start | bytes 1720328 | tf_op jit(solution)/shard_map/ppermute | solution.py:74
  15.3 0.1 fusion.27
  15.4 0.1 copy.10
  15.5 0.1 select_reduce_fusion
  15.6 0.1 collective-permute-start.1
  15.6 25.0 %collective-permute-done.1 = f32[40]{0:T(128)S(1)} collective-permute-done((f32[40]{0:T(128)S(1)}, f32[40]{0:T(128)S(1)}, u32[]{:S(2)}, u32[]{:S(2)}) %collective-permute-start.1) | collective-permute-done | bytes 192 | tf_op jit(solution)/shard_map/ppermute | solution.py:75
  40.7 15.0 %all-gather.6.cloned.1.call-done = bf16[1,320,7168]{2,1,0:T(8,128)(2,1)} async-done(((bf16[1,40,7168]{2,1,0:T(8,128)(2,1)}), bf16[1,320,7168]{2,1,0:T(8,128)(2,1)}) %all-gather.6.cloned.1.call-update) | async-done | bytes 4587536 | tf_op jit(solution)/shard_map/all_gather | solution.py:18
  55.8 4.9 %fusion.11 = f32[320,256]{1,0:T(8,128)S(1)} fusion(bf16[320,7168]{1,0:T(8,128)(2,1)} %bitcast.69, bf16[1,7168,256]{2,1,0:T(8,128)(2,1)} %param.11), kind=kOutput, calls=%fused_computation.20 | convolution fusion | flops 1174405120 | bytes 8585216 | tf_op jit(solution)/shard_map/dot_general | solution.py:11
  60.7 0.9 copy-done.8
  61.6 1.4 fusion.7
  63.0 0.6 copy-done.2
  63.6 1.4 convolution_convert_fusion.1
  65.0 2.1 %copy-done.1 = bf16[320,7168]{1,0:T(8,128)(2,1)} copy-done((bf16[320,7168]{1,0:T(8,128)(2,1)}, bf16[320,7168]{1,0:T(8,128)(2,1)S(1)}, u32[]{:S(2)}) %copy-start.1) | copy-done | bytes 4587544
  67.2 0.1 dynamic-slice_bitcast_fusion.1
  67.3 0.3 collective-permute-start.2
  67.6 4.3 %collective-permute-done.2 = bf16[160,7168]{1,0:T(8,128)(2,1)} collective-permute-done((bf16[160,7168]{1,0:T(8,128)(2,1)S(1)}, bf16[160,7168]{1,0:T(8,128)(2,1)}, u32[]{:S(2)}, u32[]{:S(2)}) %collective-permute-start.2) | collective-permute-done | bytes 2293792 | tf_op jit(solution)/shard_map/ppermute | solution.py:30
  72.0 3.1 %fusion.2 = bf16[160,7168]{1,0:T(8,128)(2,1)S(1)} fusion(bf16[160,7168]{1,0:T(8,128)(2,1)} %collective-permute-done.2, bf16[2,160,7168]{2,1,0:T(8,128)(2,1)} %bitcast.64, s32[]{:T(128)S(6)} %select_n.43), kind=kLoop, calls=%fused_computation.9 | loop fusion | flops 4587520 | bytes 6881284 | tf_op jit(solution)/shard_map/convert_element_type | solution.py:31
  75.1 14.1 %all-gather.4.cloned.1.call-done = bf16[320,7168]{1,0:T(8,128)(2,1)} async-done(((bf16[40,7168]{1,0:T(8,128)(2,1)}), bf16[320,7168]{1,0:T(8,128)(2,1)}) %all-gather.4.cloned.1.call-update) | async-done | bytes 4587536 | tf_op jit(solution)/shard_map/all_gather | solution.py:18
  89.2 4.9 %fusion.9 = f32[320,256]{1,0:T(8,128)S(1)} fusion(bf16[320,7168]{1,0:T(8,128)(2,1)} %all-gather.4.cloned.1.call-done, bf16[1,7168,256]{2,1,0:T(8,128)(2,1)} %param.11), kind=kOutput, calls=%fused_computation.18 | convolution fusion | flops 1174405120 | bytes 8585216 | tf_op jit(solution)/shard_map/dot_general | solution.py:11
  94.1 0.9 copy-done.9
  95.1 1.3 fusion.16
  96.4 0.7 copy-done.3
  97.1 1.4 convolution_convert_fusion
  98.5 1.7 dynamic-slice_bitcast_fusion
  100.2 0.2 collective-permute-start.3
  100.4 1.9 fusion.43
  102.4 4.3 %all-to-all-start = ((bf16[4,20,7168]{2,1,0:T(8,128)(2,1)}), bf16[4,20,7168]{2,1,0:T(8,128)(2,1)}, u32[]{:S(2)}, u32[]{:S(2)}) async-start(bf16[4,20,7168]{2,1,0:T(8,128)(2,1)} %get-tuple-element.23), calls=%async_computation | async-start | bytes 2752512 | tf_op jit(solution)/shard_map/all_to_all | solution.py:36
  106.7 3.0 %fusion.1 = bf16[160,7168]{1,0:T(8,128)(2,1)S(1)} fusion(bf16[160,7168]{1,0:T(8,128)(2,1)} %collective-permute-done.3, bf16[2,160,7168]{2,1,0:T(8,128)(2,1)} %bitcast.62, s32[]{:T(128)S(6)} %select_n.43), kind=kLoop, calls=%fused_computation.7 | loop fusion | flops 4587520 | bytes 6881284 | tf_op jit(solution)/shard_map/convert_element_type | solution.py:31
  109.7 14.9 %all-to-all-done = bf16[4,20,7168]{2,1,0:T(8,128)(2,1)} async-done(((bf16[4,20,7168]{2,1,0:T(8,128)(2,1)}), bf16[4,20,7168]{2,1,0:T(8,128)(2,1)}, u32[]{:S(2)}, u32[]{:S(2)}) %all-to-all-start) | async-done | bytes 1146912 | tf_op jit(solution)/shard_map/all_to_all | solution.py:36
  124.6 30.8 %all_to_all.15 = bf16[4,40,7168]{2,1,0:T(8,128)(2,1)} all-to-all(bf16[4,40,7168]{2,1,0:T(8,128)(2,1)S(1)} %bitcast.66), channel_id=1, replica_groups=mesh['grp'=2,'eg'=2,'sc'=4,'core'=2] {'sc'}, dimensions={0} | all-to-all | bytes 4587520 | tf_op jit(solution)/shard_map/all_to_all | solution.py:36
  155.4 4.4 %all-to-all-start.2 = ((bf16[4,20,7168]{2,1,0:T(8,128)(2,1)}), bf16[4,20,7168]{2,1,0:T(8,128)(2,1)}, u32[]{:S(2)}, u32[]{:S(2)}) async-start(bf16[4,20,7168]{2,1,0:T(8,128)(2,1)} %get-tuple-element.20), calls=%async_computation.2 | async-start | bytes 2752512 | tf_op jit(solution)/shard_map/all_to_all | solution.py:36
  159.9 0.3 convert_reduce_fusion
  160.2 0.1 multiply_convert_fusion.1
  160.4 2.5 %collective-permute-start.4 = (bf16[40,7168]{1,0:T(8,128)(2,1)S(1)}, bf16[40,7168]{1,0:T(8,128)(2,1)S(1)}, u32[]{:S(2)}, u32[]{:S(2)}) collective-permute-start(bf16[40,7168]{1,0:T(8,128)(2,1)S(1)} %multiply_convert_fusion.1), channel_id=1, source_target_pairs={{0,8},{8,0},{1,9},{9,1},{2,10},{10,2},{3,11},{11,3},{4,12},{12,4},... | collective-permute-start | bytes 1720328 | tf_op jit(solution)/shard_map/ppermute | solution.py:91
  162.8 25.4 %all-to-all-done.2 = bf16[4,20,7168]{2,1,0:T(8,128)(2,1)} async-done(((bf16[4,20,7168]{2,1,0:T(8,128)(2,1)}), bf16[4,20,7168]{2,1,0:T(8,128)(2,1)}, u32[]{:S(2)}, u32[]{:S(2)}) %all-to-all-start.2) | async-done | bytes 1146912 | tf_op jit(solution)/shard_map/all_to_all | solution.py:36
  188.2 2.5 %convert_reduce_fusion.1 = f32[40,7168]{1,0:T(8,128)S(1)} fusion(bf16[4,20,7168]{2,1,0:T(8,128)(2,1)} %all-to-all-done.2, bf16[4,20,7168]{2,1,0:T(8,128)(2,1)} %all-to-all-done), kind=kLoop, calls=%fused_computation.11 | loop fusion | flops 5447680 | bytes 3440640 | tf_op jit(solution)/shard_map/reduce_sum | solution.py:40
  190.8 0.1 fusion.22
  190.9 1.4 fusion
  (28 shorter events, 0.1 us)
Async XLA Ops:
  6.5 49.2 %all-gather.6.cloned.1.call-start = ((), (), s32[]{:S(2)}) async-start(), calls=%async_computation.4 | async-start | bytes 5160960 | tf_op jit(solution)/shard_map/all_gather | solution.py:18
  7.6 7.7 %copy-start.6 = (f32[64,1]{0,1:T(1,128)S(1)}, f32[64,1]{0,1:T(1,128)}, u32[]{:S(2)}) copy-start(f32[64,1]{0,1:T(1,128)} %param.10) | copy-start | bytes 772
  11.1 78.0 %all-gather.4.cloned.1.call-start = ((), (), s32[]{:S(2)}) async-start(), calls=%async_computation.3 | async-start | bytes 5160960 | tf_op jit(solution)/shard_map/all_gather | solution.py:18
  11.2 29.5 %collective-permute-start = (bf16[40,7168]{1,0:T(8,128)(2,1)S(1)}, bf16[40,7168]{1,0:T(8,128)(2,1)S(1)}, u32[]{:S(2)}, u32[]{:S(2)}) collective-permute-start(bf16[40,7168]{1,0:T(8,128)(2,1)S(1)} %get-tuple-element.25), channel_id=1, source_target_pairs={{0,8},{8,0},{1,9},{9,1},{2,10},{10,2},{3,11},{11,3},{4,12},{12,4},... | collective-permute-start | bytes 1720328 | tf_op jit(solution)/shard_map/ppermute | solution.py:74
  15.6 25.1 %collective-permute-start.1 = (f32[40]{0:T(128)S(1)}, f32[40]{0:T(128)S(1)}, u32[]{:S(2)}, u32[]{:S(2)}) collective-permute-start(f32[40]{0:T(128)S(1)} %get-tuple-element.28), channel_id=1, source_target_pairs={{0,8},{8,0},{1,9},{9,1},{2,10},{10,2},{3,11},{11,3},{4,12},{12,4},... | collective-permute-start | bytes 488 | tf_op jit(solution)/shard_map/ppermute | solution.py:75
  40.7 15.0 %copy-start.5 = (bf16[40,7168]{1,0:T(8,128)(2,1)}, bf16[40,7168]{1,0:T(8,128)(2,1)S(1)}, u32[]{:S(2)}) copy-start(bf16[40,7168]{1,0:T(8,128)(2,1)S(1)} %collective-permute-done) | copy-start | bytes 1720324
  55.7 5.0 %slice-start = ((s8[4587520]{0:T(1024)(128)(4,1)}), s8[393216]{0:T(1024)(128)(4,1)S(1)}, s32[]{:S(2)}) async-start(s8[4587520]{0:T(1024)(128)(4,1)} %bitcast.70), calls=%async_computation.5 | async-start | bytes 786432
  55.8 5.0 %slice-start.1 = ((s8[4587520]{0:T(1024)(128)(4,1)}), s8[4194304]{0:T(1024)(128)(4,1)S(1)}, s32[]{:S(2)}) async-start(s8[4587520]{0:T(1024)(128)(4,1)} %bitcast.70), calls=%async_computation.6 | async-start | bytes 8388608
  55.8 5.8 %copy-start.8 = (bf16[1,7168,256]{2,1,0:T(8,128)(2,1)S(1)}, bf16[1,7168,256]{2,1,0:T(8,128)(2,1)}, u32[]{:S(2)}) copy-start(bf16[1,7168,256]{2,1,0:T(8,128)(2,1)} %param.12) | copy-start | bytes 11010052
  61.6 2.0 %copy-start.2 = (bf16[1,256,7168]{2,1,0:T(8,128)(2,1)S(1)}, bf16[1,256,7168]{2,1,0:T(8,128)(2,1)}, u32[]{:S(2)}) copy-start(bf16[1,256,7168]{2,1,0:T(8,128)(2,1)} %param.13) | copy-start | bytes 11010052
  65.0 2.1 %copy-start.1 = (bf16[320,7168]{1,0:T(8,128)(2,1)}, bf16[320,7168]{1,0:T(8,128)(2,1)S(1)}, u32[]{:S(2)}) copy-start(bf16[320,7168]{1,0:T(8,128)(2,1)S(1)} %convolution_convert_fusion.1) | copy-start | bytes 13762564
  67.3 4.6 %collective-permute-start.2 = (bf16[160,7168]{1,0:T(8,128)(2,1)S(1)}, bf16[160,7168]{1,0:T(8,128)(2,1)}, u32[]{:S(2)}, u32[]{:S(2)}) collective-permute-start(bf16[160,7168]{1,0:T(8,128)(2,1)S(1)} %dynamic-slice_bitcast_fusion.1), channel_id=1, source_target_pairs={{0,1},{1,0},{2,3},{3,2},{4,5},{5,4},{6,7},{7,6},{8,9},{9,8},{10,11... | collective-permute-start | bytes 6881288 | tf_op jit(solution)/shard_map/ppermute | solution.py:30
  89.2 4.9 %copy-start.7 = (bf16[320,7168]{1,0:T(8,128)(2,1)S(1)}, bf16[320,7168]{1,0:T(8,128)(2,1)}, u32[]{:S(2)}) copy-start(bf16[320,7168]{1,0:T(8,128)(2,1)} %all-gather.4.cloned.1.call-done) | copy-start | bytes 13762564
  89.2 5.9 %copy-start.9 = (bf16[1,7168,256]{2,1,0:T(8,128)(2,1)S(1)}, bf16[1,7168,256]{2,1,0:T(8,128)(2,1)}, u32[]{:S(2)}) copy-start(bf16[1,7168,256]{2,1,0:T(8,128)(2,1)} %param.12) | copy-start | bytes 11010052
  95.1 2.0 %copy-start.3 = (bf16[1,256,7168]{2,1,0:T(8,128)(2,1)S(1)}, bf16[1,256,7168]{2,1,0:T(8,128)(2,1)}, u32[]{:S(2)}) copy-start(bf16[1,256,7168]{2,1,0:T(8,128)(2,1)} %param.13) | copy-start | bytes 11010052
  98.5 3.9 %copy-start = (bf16[320,7168]{1,0:T(8,128)(2,1)}, bf16[320,7168]{1,0:T(8,128)(2,1)S(1)}, u32[]{:S(2)}) copy-start(bf16[320,7168]{1,0:T(8,128)(2,1)S(1)} %convolution_convert_fusion) | copy-start | bytes 13762564
  100.2 6.5 %collective-permute-start.3 = (bf16[160,7168]{1,0:T(8,128)(2,1)}, bf16[160,7168]{1,0:T(8,128)(2,1)}, u32[]{:S(2)}, u32[]{:S(2)}) collective-permute-start(bf16[160,7168]{1,0:T(8,128)(2,1)} %dynamic-slice_bitcast_fusion), channel_id=1, source_target_pairs={{0,1},{1,0},{2,3},{3,2},{4,5},{5,4},{6,7},{7,6},{8,9},{9,8},{10,11... | collective-permute-start | bytes 6881288 | tf_op jit(solution)/shard_map/ppermute | solution.py:30
  102.4 22.2 %all-to-all-start = ((bf16[4,20,7168]{2,1,0:T(8,128)(2,1)}), bf16[4,20,7168]{2,1,0:T(8,128)(2,1)}, u32[]{:S(2)}, u32[]{:S(2)}) async-start(bf16[4,20,7168]{2,1,0:T(8,128)(2,1)} %get-tuple-element.23), calls=%async_computation | async-start | bytes 2752512 | tf_op jit(solution)/shard_map/all_to_all | solution.py:36
  155.4 4.4 %copy-start.4 = (bf16[4,40,7168]{2,1,0:T(8,128)(2,1)S(1)}, bf16[4,40,7168]{2,1,0:T(8,128)(2,1)}, u32[]{:S(2)}) copy-start(bf16[4,40,7168]{2,1,0:T(8,128)(2,1)} %all_to_all.15) | copy-start | bytes 6881284
  155.4 32.8 %all-to-all-start.2 = ((bf16[4,20,7168]{2,1,0:T(8,128)(2,1)}), bf16[4,20,7168]{2,1,0:T(8,128)(2,1)}, u32[]{:S(2)}, u32[]{:S(2)}) async-start(bf16[4,20,7168]{2,1,0:T(8,128)(2,1)} %get-tuple-element.20), calls=%async_computation.2 | async-start | bytes 2752512 | tf_op jit(solution)/shard_map/all_to_all | solution.py:36
  160.4 30.5 %collective-permute-start.4 = (bf16[40,7168]{1,0:T(8,128)(2,1)S(1)}, bf16[40,7168]{1,0:T(8,128)(2,1)S(1)}, u32[]{:S(2)}, u32[]{:S(2)}) collective-permute-start(bf16[40,7168]{1,0:T(8,128)(2,1)S(1)} %multiply_convert_fusion.1), channel_id=1, source_target_pairs={{0,8},{8,0},{1,9},{9,1},{2,10},{10,2},{3,11},{11,3},{4,12},{12,4},... | collective-permute-start | bytes 1720328 | tf_op jit(solution)/shard_map/ppermute | solution.py:91
Sparse Core Ops, SparseCore 0:
  11.3 44.4 all-gather.5
  57.3 31.8 all-gather.3

commit v9 on v7

--- a/solution.py
+++ b/solution.py
@@ -15,21 +15,18 @@
 
 
 def gather(held):
-    return lax.all_gather(held, ("core", "sc"), axis=0, tiled=True)
+    return lax.all_gather(held, "sc", axis=0, tiled=True)
 
 
-def expert_parts(gathered, gate_w, up_w, down_w):
+def expert_parts(gathered, slices):
     chips = lax.axis_size("sc")
-    cores = lax.axis_size("core")
-    count = gathered.shape[0] // (chips * cores)
+    count = gathered.shape[0] // chips
     width = gathered.shape[1]
-    parts = slice_ffn(gathered, gate_w, up_w, down_w)
-    halves = parts.reshape(cores, chips * count, width)
-    core = lax.axis_index("core")
-    swap = [(c, (c + 1) % cores) for c in range(cores)]
-    sibling = lax.ppermute(halves[(core + 1) % cores], "core", swap)
-    paired = (halves[core].astype(jnp.float32) + sibling.astype(jnp.float32)).astype(jnp.bfloat16)
-    return paired.reshape(chips, count, width)
+    total = None
+    for gate_w, up_w, down_w in slices:
+        part = slice_ffn(gathered, gate_w, up_w, down_w).astype(jnp.float32)
+        total = part if total is None else total + part
+    return total.astype(jnp.bfloat16).reshape(chips, count, width)
 
 
 def chip_sums(paired):
@@ -66,7 +63,10 @@
         "tkc,td->kcd", place.astype(jnp.bfloat16), normed, preferred_element_type=jnp.float32
     ).astype(jnp.bfloat16)
     packed_w = jnp.sum(jnp.where(place, weight_te[:, :, None], 0.0), axis=0)
-    weights = (w_gate[0], w_up[0], w_down[0])
+    cores = lax.axis_size("core")
+    swap = [(c, (c + 1) % cores) for c in range(cores)]
+    mine = (w_gate[0], w_up[0], w_down[0])
+    weights = (mine, tuple(lax.ppermute(w, "core", swap) for w in mine))
 
     def shift(k):
         return [(g, (g + k) % experts) for g in range(experts)]
@@ -75,10 +75,10 @@
     away_w = [lax.ppermute(packed_w[k], "eg", shift(k)) for k in range(1, experts)]
     own_rows = gather(packed[0])
     own_rows, away, away_w = lax.optimization_barrier((own_rows, away, away_w))
-    own_parts = expert_parts(own_rows, *weights)
+    own_parts = expert_parts(own_rows, weights)
     away_rows = gather(jnp.concatenate(away, axis=0))
     own_parts, away_rows = lax.optimization_barrier((own_parts, away_rows))
-    away_parts = expert_parts(away_rows, *weights)
+    away_parts = expert_parts(away_rows, weights)
     away_back = chip_sums(away_parts)
     own_parts, away_back = lax.optimization_barrier((own_parts, away_back))
     done = finish(away_back, jnp.concatenate(away_w, axis=0))

time: 187 us -> 217 us (1.16)
  matrix products: 19.3 us -> 49.5 us
  waiting for transfers between devices: 95.5 us -> 105 us
  local copies, waits for them, and re-layouts: 6.68 us -> 1.14 us
  other arithmetic: 9.07 us -> 3.87 us
    dot_general x2 -> x4, matrix products: 2.75 us -> 32.6 us  [slice_ffn(): jnp.dot(hidden, down_w, preferred_element_type=jnp.float32)]
    all_gather x2, waiting for transfers between devices: 27.8 us -> 45.7 us  [gather(): return lax.all_gather(held, 'sc', axis=0, tiled=True)]
    ppermute x2 -> x3, waiting for transfers between devices: 8.52 us -> 0.01 us  [shards(): weights = (mine, tuple((lax.ppermute(w, 'core', swap) for w in mine)))]
    dot_general x2 -> x4, matrix products: 6.31 us -> 12.9 us  [slice_ffn(): gate = jnp.dot(rows, gate_w, preferred_element_type=jnp.float32)]
    dot_general x2 -> x0, matrix products: 6.26 us -> none  [slice_ffn(): upper = jnp.dot(rows, up_w, preferred_element_type=jnp.float32)]
    unnamed x20 -> x8, local copies, waits for them, and re-layouts: 5.25 us -> 0.02 us
    convert_element_type x2 -> x0, other arithmetic: 5.2 us -> none  [expert_parts(): (halves[core].astype(jnp.float32) + sibling.astype(jnp.float32)).astype(j...]
  transfers between devices with their start and end apart: 8 -> 9, of which waited for: 6 -> 4; matrix products, arithmetic and copies ran while one was open for 8% -> 12% of each run, Pallas kernels for 0% -> 0%
where the time goes in v9:
time: 217 us; the launch traced here: 216 us
  waiting for transfers between devices  105 us (48%)
  matrix products  49.5 us (23%)
  blocking collectives  32.4 us (15%)
  between operations  13.6 us (6%)
  starting transfers between devices  10.9 us (5%)
  other arithmetic  3.87 us (2%)
    all_gather x2, waiting for transfers between devices, gather(): return lax.all_gather(held, 'sc', axis=0, tiled=True)  45.7 us
    all_to_all x1, waiting for transfers between devices, chip_sums(): return lax.all_to_all(paired, 'sc', split_axis=0, concat_axis=0, tiled=True)  33.5 us
    dot_general x4, matrix products, slice_ffn(): jnp.dot(hidden, down_w, preferred_element_type=jnp.float32)  32.6 us
    all_to_all x1, blocking collectives, chip_sums(): return lax.all_to_all(paired, 'sc', split_axis=0, concat_axis=0, tiled=True)  32.4 us
    ppermute x1, waiting for transfers between devices, shards(): lax.ppermute(packed_w[k], 'eg', shift(k))  25.6 us
    dot_general x4, matrix products, slice_ffn(): gate = jnp.dot(rows, gate_w, preferred_element_type=jnp.float32)  12.9 us
  transfers between devices with their start and end apart: 9, of which 4 were waited for; matrix products, arithmetic and copies ran while one was open for 12% of the time, Pallas kernels for 0%

profile of v9, /device:TPU:0, one launch (start us, length us, event | category | flops | bytes accessed | tf_op | source)
XLA Modules:
  0.0 216.3 jit_solution(11251102587008485679)
XLA Ops:
  6.5 0.0 all-gather.6.cloned.1.call-start
  6.5 0.7 fusion.36
  7.2 0.1 fusion.27
  7.3 0.1 copy.9
  7.4 0.1 reduce_window_sum.11
  7.5 0.1 fusion.35
  7.5 0.1 copy.8
  7.6 2.1 multiply_reduce_fusion
  9.8 0.0 copy-start.3
  9.8 0.5 convolution_convert_fusion.4
  10.3 0.9 slice_bitcast_fusion
  11.2 0.0 all-gather.6.cloned.1.call-update
  11.2 0.0 all-gather.4.cloned.1.call-start
  11.3 0.5 collective-permute-start.2
  11.8 0.1 collective-permute-start.3
  11.9 0.4 collective-permute-start.4
  12.3 3.7 %collective-permute-start = (bf16[40,7168]{1,0:T(8,128)(2,1)S(1)}, bf16[40,7168]{1,0:T(8,128)(2,1)S(1)}, u32[]{:S(2)}, u32[]{:S(2)}) collective-permute-start(bf16[40,7168]{1,0:T(8,128)(2,1)S(1)} %get-tuple-element.19), channel_id=1, source_target_pairs={{0,8},{8,0},{1,9},{9,1},{2,10},{10,2},{3,11},{11,3},{4,12},{12,4},... | collective-permute-start | bytes 1720328 | tf_op jit(solution)/shard_map/ppermute | solution.py:74
  16.0 0.1 fusion.26
  16.0 0.1 copy.10
  16.1 0.1 select_reduce_fusion
  16.2 0.1 collective-permute-start.1
  16.3 25.6 %collective-permute-done.1 = f32[40]{0:T(128)S(1)} collective-permute-done((f32[40]{0:T(128)S(1)}, f32[40]{0:T(128)S(1)}, u32[]{:S(2)}, u32[]{:S(2)}) %collective-permute-start.1) | collective-permute-done | bytes 192 | tf_op jit(solution)/shard_map/ppermute | solution.py:75
  41.9 0.0 collective-permute-done
  41.9 19.6 %all-gather.6.cloned.1.call-done = bf16[1,160,7168]{2,1,0:T(8,128)(2,1)} async-done(((bf16[1,40,7168]{2,1,0:T(8,128)(2,1)}), bf16[1,160,7168]{2,1,0:T(8,128)(2,1)}) %all-gather.6.cloned.1.call-update) | async-done | bytes 2293776 | tf_op jit(solution)/shard_map/all_gather | solution.py:18
  61.5 0.0 all-gather.4.cloned.1.call-update
  61.6 3.6 %fusion.51 = f32[160,256]{1,0:T(8,128)S(1)} fusion(bf16[160,7168]{1,0:T(8,128)(2,1)} %bitcast.59, bf16[1,7168,256]{2,1,0:T(8,128)(2,1)} %param.11), kind=kOutput, calls=%fused_computation.74 | convolution fusion | flops 587202560 | bytes 6127616 | tf_op jit(solution)/shard_map/dot_general | solution.py:11
  65.2 0.0 copy-done
  65.2 7.8 %fusion.7 = f32[160,7168]{1,0:T(8,128)} fusion(f32[160,256]{1,0:T(8,128)S(1)} %fusion.51, bf16[1,256,7168]{2,1,0:T(8,128)(2,1)} %param.13, bf16[160,7168]{1,0:T(8,128)(2,1)S(1)} %bitcast.60, bf16[1,7168,256]{2,1,0:T(8,128)(2,1)} %param.12), kind=kOutput, calls=%fused_computation.11 | convolution fusion | flops 1176944640 | bytes 14385152 | tf_op jit(solution)/shard_map/dot_general | solution.py:14
  73.0 0.0 collective-permute-done.2
  73.1 2.8 %fusion.63 = f32[160,256]{1,0:T(8,128)S(1)} fusion(bf16[160,7168]{1,0:T(8,128)(2,1)S(1)} %bitcast.61, bf16[7168,256]{1,0:T(8,128)(2,1)} %collective-permute-done.2), kind=kOutput, calls=%fused_computation.84 | convolution fusion | flops 587202560 | bytes 6127616 | tf_op jit(solution)/shard_map/dot_general | solution.py:11
  75.9 0.0 collective-permute-done.3
  75.9 0.0 collective-permute-done.4
  75.9 8.5 %fusion.6 = bf16[160,7168]{1,0:T(8,128)(2,1)} fusion(f32[160,7168]{1,0:T(8,128)} %fusion.7, bf16[256,7168]{1,0:T(8,128)(2,1)} %collective-permute-done.4, f32[160,256]{1,0:T(8,128)S(1)} %fusion.63, bf16[160,7168]{1,0:T(8,128)(2,1)S(1)} %bitcast.62, bf16[7168,256]{1,0:T(8,128)(2,1)} %collective-permute-done.3), kind=kOutput, calls=%fused_computation.9 | convolution fusion | flops 1179238400 | bytes 16678912 | tf_op jit(solution)/shard_map/dot_general | solution.py:14
  84.3 26.1 %all-gather.4.cloned.1.call-done = bf16[160,7168]{1,0:T(8,128)(2,1)} async-done(((bf16[40,7168]{1,0:T(8,128)(2,1)}), bf16[160,7168]{1,0:T(8,128)(2,1)}) %all-gather.4.cloned.1.call-update) | async-done | bytes 2293776 | tf_op jit(solution)/shard_map/all_gather | solution.py:18
  110.5 3.6 %fusion.49 = f32[160,256]{1,0:T(8,128)S(1)} fusion(bf16[160,7168]{1,0:T(8,128)(2,1)} %all-gather.4.cloned.1.call-done, bf16[1,7168,256]{2,1,0:T(8,128)(2,1)} %param.11), kind=kOutput, calls=%fused_computation.72 | convolution fusion | flops 587202560 | bytes 6127616 | tf_op jit(solution)/shard_map/dot_general | solution.py:11
  114.1 7.8 %fusion.3 = f32[160,7168]{1,0:T(8,128)} fusion(bf16[160,7168]{1,0:T(8,128)(2,1)S(1)} %copy-done.1, f32[160,256]{1,0:T(8,128)S(1)} %fusion.49, bf16[1,256,7168]{2,1,0:T(8,128)(2,1)} %param.13, bf16[1,7168,256]{2,1,0:T(8,128)(2,1)} %param.12), kind=kOutput, calls=%fused_computation.5 | convolution fusion | flops 1176944640 | bytes 14385152 | tf_op jit(solution)/shard_map/dot_general | solution.py:14
  121.9 2.8 %fusion.64 = f32[160,256]{1,0:T(8,128)S(1)} fusion(bf16[160,7168]{1,0:T(8,128)(2,1)S(1)} %copy-done.1, bf16[7168,256]{1,0:T(8,128)(2,1)} %collective-permute-done.2), kind=kOutput, calls=%fused_computation.85 | convolution fusion | flops 587202560 | bytes 6127616 | tf_op jit(solution)/shard_map/dot_general | solution.py:11
  124.8 8.5 %fusion.2 = bf16[160,7168]{1,0:T(8,128)(2,1)} fusion(f32[160,7168]{1,0:T(8,128)} %fusion.3, bf16[256,7168]{1,0:T(8,128)(2,1)} %collective-permute-done.4, f32[160,256]{1,0:T(8,128)S(1)} %fusion.64, bf16[160,7168]{1,0:T(8,128)(2,1)S(1)} %copy-done.1, bf16[7168,256]{1,0:T(8,128)(2,1)} %collective-permute-done.3), kind=kOutput, calls=%fused_computation.3 | convolution fusion | flops 1179238400 | bytes 16678912 | tf_op jit(solution)/shard_map/dot_general | solution.py:14
  133.3 32.4 %all_to_all.10 = bf16[4,40,7168]{2,1,0:T(8,128)(2,1)} all-to-all(bf16[4,40,7168]{2,1,0:T(8,128)(2,1)} %bitcast.67), channel_id=1, replica_groups=mesh['grp'=2,'eg'=2,'sc'=4,'core'=2] {'sc'}, dimensions={0} | all-to-all | bytes 4587520 | tf_op jit(solution)/shard_map/all_to_all | solution.py:33
  165.7 3.6 %all-to-all-start.1 = ((bf16[4,40,7168]{2,1,0:T(8,128)(2,1)}), bf16[4,40,7168]{2,1,0:T(8,128)(2,1)S(1)}, u32[]{:S(2)}, u32[]{:S(2)}) async-start(bf16[4,40,7168]{2,1,0:T(8,128)(2,1)} %bitcast.66), calls=%async_computation.1 | async-start | bytes 4587520 | tf_op jit(solution)/shard_map/all_to_all | solution.py:33
  169.3 2.1 convert_reduce_fusion
  171.5 0.1 multiply_convert_fusion.1
  171.6 2.5 %collective-permute-start.5 = (bf16[40,7168]{1,0:T(8,128)(2,1)S(1)}, bf16[40,7168]{1,0:T(8,128)(2,1)S(1)}, u32[]{:S(2)}, u32[]{:S(2)}) collective-permute-start(bf16[40,7168]{1,0:T(8,128)(2,1)S(1)} %multiply_convert_fusion.1), channel_id=1, source_target_pairs={{0,8},{8,0},{1,9},{9,1},{2,10},{10,2},{3,11},{11,3},{4,12},{12,4},... | collective-permute-start | bytes 1720328 | tf_op jit(solution)/shard_map/ppermute | solution.py:87
  174.1 33.5 %all-to-all-done.1 = bf16[4,40,7168]{2,1,0:T(8,128)(2,1)S(1)} async-done(((bf16[4,40,7168]{2,1,0:T(8,128)(2,1)}), bf16[4,40,7168]{2,1,0:T(8,128)(2,1)S(1)}, u32[]{:S(2)}, u32[]{:S(2)}) %all-to-all-start.1) | async-done | bytes 2293792 | tf_op jit(solution)/shard_map/all_to_all | solution.py:33
  207.6 0.3 convert_reduce_fusion.1
  208.0 0.1 fusion.12
  208.1 0.0 collective-permute-done.5
  208.1 1.4 fusion.8
  (8 shorter events, 0.0 us)
Async XLA Ops:
  6.5 55.0 %all-gather.6.cloned.1.call-start = ((), (), s32[]{:S(2)}) async-start(), calls=%async_computation.3 | async-start | bytes 2867200 | tf_op jit(solution)/shard_map/all_gather | solution.py:18
  9.8 6.2 %copy-start.3 = (f32[64,1]{0,1:T(1,128)S(1)}, f32[64,1]{0,1:T(1,128)}, u32[]{:S(2)}) copy-start(f32[64,1]{0,1:T(1,128)} %param.10) | copy-start | bytes 772
  11.2 99.2 %all-gather.4.cloned.1.call-start = ((), (), s32[]{:S(2)}) async-start(), calls=%async_computation.2 | async-start | bytes 2867200 | tf_op jit(solution)/shard_map/all_gather | solution.py:18
  11.3 61.8 %collective-permute-start.2 = (bf16[7168,256]{1,0:T(8,128)(2,1)}, bf16[7168,256]{1,0:T(8,128)(2,1)}, u32[]{:S(2)}, u32[]{:S(2)}) collective-permute-start(bf16[7168,256]{1,0:T(8,128)(2,1)} %bitcast.65), channel_id=1, source_target_pairs={{0,1},{1,0},{2,3},{3,2},{4,5},{5,4},{6,7},{7,6},{8,9},{9,8},{10,11... | collective-permute-start | bytes 11010056 | tf_op jit(solution)/shard_map/ppermute | solution.py:69
  11.8 64.1 %collective-permute-start.3 = (bf16[7168,256]{1,0:T(8,128)(2,1)}, bf16[7168,256]{1,0:T(8,128)(2,1)}, u32[]{:S(2)}, u32[]{:S(2)}) collective-permute-start(bf16[7168,256]{1,0:T(8,128)(2,1)} %bitcast.64), channel_id=1, source_target_pairs={{0,1},{1,0},{2,3},{3,2},{4,5},{5,4},{6,7},{7,6},{8,9},{9,8},{10,11... | collective-permute-start | bytes 11010056 | tf_op jit(solution)/shard_map/ppermute | solution.py:69
  11.9 64.0 %collective-permute-start.4 = (bf16[256,7168]{1,0:T(8,128)(2,1)}, bf16[256,7168]{1,0:T(8,128)(2,1)}, u32[]{:S(2)}, u32[]{:S(2)}) collective-permute-start(bf16[256,7168]{1,0:T(8,128)(2,1)} %bitcast.63), channel_id=1, source_target_pairs={{0,1},{1,0},{2,3},{3,2},{4,5},{5,4},{6,7},{7,6},{8,9},{9,8},{10,11... | collective-permute-start | bytes 11010056 | tf_op jit(solution)/shard_map/ppermute | solution.py:69
  12.3 29.6 %collective-permute-start = (bf16[40,7168]{1,0:T(8,128)(2,1)S(1)}, bf16[40,7168]{1,0:T(8,128)(2,1)S(1)}, u32[]{:S(2)}, u32[]{:S(2)}) collective-permute-start(bf16[40,7168]{1,0:T(8,128)(2,1)S(1)} %get-tuple-element.19), channel_id=1, source_target_pairs={{0,8},{8,0},{1,9},{9,1},{2,10},{10,2},{3,11},{11,3},{4,12},{12,4},... | collective-permute-start | bytes 1720328 | tf_op jit(solution)/shard_map/ppermute | solution.py:74
  16.2 25.7 %collective-permute-start.1 = (f32[40]{0:T(128)S(1)}, f32[40]{0:T(128)S(1)}, u32[]{:S(2)}, u32[]{:S(2)}) collective-permute-start(f32[40]{0:T(128)S(1)} %get-tuple-element.22), channel_id=1, source_target_pairs={{0,8},{8,0},{1,9},{9,1},{2,10},{10,2},{3,11},{11,3},{4,12},{12,4},... | collective-permute-start | bytes 488 | tf_op jit(solution)/shard_map/ppermute | solution.py:75
  41.9 19.6 %copy-start.2 = (bf16[40,7168]{1,0:T(8,128)(2,1)}, bf16[40,7168]{1,0:T(8,128)(2,1)S(1)}, u32[]{:S(2)}) copy-start(bf16[40,7168]{1,0:T(8,128)(2,1)S(1)} %collective-permute-done) | copy-start | bytes 1720324
  61.5 3.7 %copy-start = (bf16[1,160,7168]{2,1,0:T(8,128)(2,1)S(1)}, bf16[1,160,7168]{2,1,0:T(8,128)(2,1)}, u32[]{:S(2)}) copy-start(bf16[1,160,7168]{2,1,0:T(8,128)(2,1)} %all-gather.6.cloned.1.call-done) | copy-start | bytes 6881284
  110.5 3.6 %copy-start.1 = (bf16[160,7168]{1,0:T(8,128)(2,1)S(1)}, bf16[160,7168]{1,0:T(8,128)(2,1)}, u32[]{:S(2)}) copy-start(bf16[160,7168]{1,0:T(8,128)(2,1)} %all-gather.4.cloned.1.call-done) | copy-start | bytes 6881284
  165.7 41.9 %all-to-all-start.1 = ((bf16[4,40,7168]{2,1,0:T(8,128)(2,1)}), bf16[4,40,7168]{2,1,0:T(8,128)(2,1)S(1)}, u32[]{:S(2)}, u32[]{:S(2)}) async-start(bf16[4,40,7168]{2,1,0:T(8,128)(2,1)} %bitcast.66), calls=%async_computation.1 | async-start | bytes 4587520 | tf_op jit(solution)/shard_map/all_to_all | solution.py:33
  171.6 36.5 %collective-permute-start.5 = (bf16[40,7168]{1,0:T(8,128)(2,1)S(1)}, bf16[40,7168]{1,0:T(8,128)(2,1)S(1)}, u32[]{:S(2)}, u32[]{:S(2)}) collective-permute-start(bf16[40,7168]{1,0:T(8,128)(2,1)S(1)} %multiply_convert_fusion.1), channel_id=1, source_target_pairs={{0,8},{8,0},{1,9},{9,1},{2,10},{10,2},{3,11},{11,3},{4,12},{12,4},... | collective-permute-start | bytes 1720328 | tf_op jit(solution)/shard_map/ppermute | solution.py:87
Sparse Core Ops, SparseCore 0:
  11.3 50.1 all-gather.5
  63.1 47.3 all-gather.3

commit v10 on v7

--- a/solution.py
+++ b/solution.py
@@ -23,12 +23,13 @@
     cores = lax.axis_size("core")
     count = gathered.shape[0] // (chips * cores)
     width = gathered.shape[1]
-    parts = slice_ffn(gathered, gate_w, up_w, down_w)
-    halves = parts.reshape(cores, chips * count, width)
+    halves = gathered.reshape(cores, chips * count, width)
     core = lax.axis_index("core")
     swap = [(c, (c + 1) % cores) for c in range(cores)]
-    sibling = lax.ppermute(halves[(core + 1) % cores], "core", swap)
-    paired = (halves[core].astype(jnp.float32) + sibling.astype(jnp.float32)).astype(jnp.bfloat16)
+    sent = slice_ffn(halves[(core + 1) % cores], gate_w, up_w, down_w)
+    sibling = lax.ppermute(sent, "core", swap)
+    kept = slice_ffn(halves[core], gate_w, up_w, down_w)
+    paired = (kept.astype(jnp.float32) + sibling.astype(jnp.float32)).astype(jnp.bfloat16)
     return paired.reshape(chips, count, width)
 
 

time: 187 us -> 194 us (1.037)
  matrix products: 19.3 us -> 47 us
  waiting for transfers between devices: 95.5 us -> 85.7 us
  local copies, waits for them, and re-layouts: 6.68 us -> 1.13 us
  other arithmetic: 9.07 us -> 3.87 us
    dot_general x2 -> x4, matrix products: 2.75 us -> 28.6 us  [slice_ffn(): jnp.dot(hidden, down_w, preferred_element_type=jnp.float32)]
    dot_general x2 -> x4, matrix products: 6.31 us -> 14.3 us  [slice_ffn(): gate = jnp.dot(rows, gate_w, preferred_element_type=jnp.float32)]
    ppermute x2, waiting for transfers between devices: 8.52 us -> 2.1 us  [expert_parts(): sibling = lax.ppermute(sent, 'core', swap)]
    dot_general x2 -> x0, matrix products: 6.26 us -> none  [slice_ffn(): upper = jnp.dot(rows, up_w, preferred_element_type=jnp.float32)]
    unnamed x20 -> x4, local copies, waits for them, and re-layouts: 5.25 us -> 0.01 us
    convert_element_type x2 -> x0, other arithmetic: 5.2 us -> none  [expert_parts(): (halves[core].astype(jnp.float32) + sibling.astype(jnp.float32)).astype(j...]
    all_gather x2, waiting for transfers between devices: 27.8 us -> 24.3 us  [gather(): return lax.all_gather(held, ('core', 'sc'), axis=0, tiled=True)]
  transfers between devices with their start and end apart: 8 -> 8, of which waited for: 6 -> 6; matrix products, arithmetic and copies ran while one was open for 8% -> 15% of each run, Pallas kernels for 0% -> 0%
where the time goes in v10:
time: 194 us
  waiting for transfers between devices  85.7 us (44%)
  matrix products  47 us (24%)
  blocking collectives  31.6 us (16%)
  between operations  13.5 us (7%)
  starting transfers between devices  11 us (6%)
  other arithmetic  3.87 us (2%)
    all_to_all x1, waiting for transfers between devices, chip_sums(): return lax.all_to_all(paired, 'sc', split_axis=0, concat_axis=0, tiled=True)  34.2 us
    all_to_all x1, blocking collectives, chip_sums(): return lax.all_to_all(paired, 'sc', split_axis=0, concat_axis=0, tiled=True)  31.6 us
    dot_general x4, matrix products, slice_ffn(): jnp.dot(hidden, down_w, preferred_element_type=jnp.float32)  28.6 us
    ppermute x1, waiting for transfers between devices, shards(): lax.ppermute(packed_w[k], 'eg', shift(k))  25 us
    all_gather x2, waiting for transfers between devices, gather(): return lax.all_gather(held, ('core', 'sc'), axis=0, tiled=True)  24.3 us
    dot_general x4, matrix products, slice_ffn(): gate = jnp.dot(rows, gate_w, preferred_element_type=jnp.float32)  14.3 us
    ppermute x1, starting transfers between devices, shards(): away = [lax.ppermute(packed[k], 'eg', shift(k)) for k in range(1, experts)]  4.11 us
  transfers between devices with their start and end apart: 8, of which 6 were waited for; matrix products, arithmetic and copies ran while one was open for 15% of the time, Pallas kernels for 0%

profile of v10, /device:TPU:0, one launch (start us, length us, event | category | flops | bytes accessed | tf_op | source)
XLA Modules:
  0.0 193.7 jit_solution(167196308632544513)
XLA Ops:
  6.5 0.0 all-gather.6.cloned.1.call-start
  6.5 2.1 %multiply_reduce_fusion = (f32[64]{0:T(128)S(1)}, f32[64,7168]{1,0:T(8,128)S(1)}) fusion(bf16[64,7168]{1,0:T(8,128)(2,1)} %param.7, s32[64]{0:T(128)} %param.8), kind=kOutput, calls=%fused_computation.51 | convolution fusion | flops 60559296 | bytes 2753024 | tf_op jit(solution)/shard_map/dot_general | solution.py:53
  8.6 0.0 copy-start.1
  8.6 0.7 fusion.154
  9.3 0.1 fusion.131
  9.4 0.1 copy.9
  9.5 0.1 reduce_window_sum.11
  9.6 0.1 fusion.139
  9.6 0.1 copy.8
  9.7 0.5 convolution_convert_fusion.4
  10.2 0.9 slice_bitcast_fusion
  11.1 0.0 all-gather.6.cloned.1.call-update
  11.2 0.0 all-gather.4.cloned.1.call-start
  11.2 4.1 %collective-permute-start = (bf16[40,7168]{1,0:T(8,128)(2,1)S(1)}, bf16[40,7168]{1,0:T(8,128)(2,1)S(1)}, u32[]{:S(2)}, u32[]{:S(2)}) collective-permute-start(bf16[40,7168]{1,0:T(8,128)(2,1)S(1)} %get-tuple-element.19), channel_id=1, source_target_pairs={{0,8},{8,0},{1,9},{9,1},{2,10},{10,2},{3,11},{11,3},{4,12},{12,4},... | collective-permute-start | bytes 1720328 | tf_op jit(solution)/shard_map/ppermute | solution.py:75
  15.3 0.0 copy-done.1
  15.3 0.1 fusion.130
  15.4 0.1 copy.10
  15.5 0.1 select_reduce_fusion
  15.6 0.1 collective-permute-start.1
  15.7 25.0 %collective-permute-done.1 = f32[40]{0:T(128)S(1)} collective-permute-done((f32[40]{0:T(128)S(1)}, f32[40]{0:T(128)S(1)}, u32[]{:S(2)}, u32[]{:S(2)}) %collective-permute-start.1) | collective-permute-done | bytes 192 | tf_op jit(solution)/shard_map/ppermute | solution.py:76
  40.7 0.0 collective-permute-done
  40.7 0.0 copy-start
  40.7 15.0 %all-gather.6.cloned.1.call-done = bf16[1,320,7168]{2,1,0:T(8,128)(2,1)} async-done(((bf16[1,40,7168]{2,1,0:T(8,128)(2,1)}), bf16[1,320,7168]{2,1,0:T(8,128)(2,1)}) %all-gather.6.cloned.1.call-update) | async-done | bytes 4587536 | tf_op jit(solution)/shard_map/all_gather | solution.py:18
  55.7 0.0 copy-done
  55.7 0.0 all-gather.4.cloned.1.call-update
  55.8 3.5 %fusion.23 = f32[160,256]{1,0:T(8,128)S(1)} fusion(bf16[1,7168,256]{2,1,0:T(8,128)(2,1)} %param.11, bf16[2,160,7168]{2,1,0:T(8,128)(2,1)} %bitcast.126, s32[]{:T(128)S(6)} %select_n.45), kind=kOutput, calls=%fused_computation.30 | convolution fusion | flops 587202560 | bytes 6127620 | tf_op jit(solution)/shard_map/dot_general | solution.py:11
  59.3 6.4 %convolution_convert_fusion.2 = bf16[160,7168]{1,0:T(8,128)(2,1)S(1)} fusion(bf16[1,256,7168]{2,1,0:T(8,128)(2,1)} %param.13, bf16[1,7168,256]{2,1,0:T(8,128)(2,1)} %param.12, bf16[2,160,7168]{2,1,0:T(8,128)(2,1)} %bitcast.127, s32[]{:T(128)S(6)} %select_n.45, f32[160,256]{1,0:T(8,128)S(1)} %fusion.23), kind=kOutput, calls=%fused_computation.3 | convolution fusion | flops 1175797760 | bytes 12091396 | tf_op jit(solution)/shard_map/dot_general | solution.py:14
  65.7 0.3 collective-permute-start.2
  66.0 3.9 %fusion.25 = f32[160,256]{1,0:T(8,128)S(1)} fusion(bf16[1,7168,256]{2,1,0:T(8,128)(2,1)} %param.11, bf16[2,160,7168]{2,1,0:T(8,128)(2,1)} %bitcast.128, s32[]{:T(128)S(6)} %select_n.43), kind=kOutput, calls=%fused_computation.32 | convolution fusion | flops 587202560 | bytes 6127620 | tf_op jit(solution)/shard_map/dot_general | solution.py:11
  69.9 1.3 collective-permute-done.2
  71.2 8.7 %add_convert_fusion.1 = bf16[160,7168]{1,0:T(8,128)(2,1)} fusion(bf16[160,7168]{1,0:T(8,128)(2,1)} %collective-permute-done.2, bf16[1,256,7168]{2,1,0:T(8,128)(2,1)} %param.13, bf16[1,7168,256]{2,1,0:T(8,128)(2,1)} %param.12, bf16[2,160,7168]{2,1,0:T(8,128)(2,1)} %bitcast.129, s32[]{:T(128)S(6)} %select_n.43, f32[160,256]{1,0:T(8,128)S(1)} %fusion.25), kind=kOutput, calls=%fused_computation.13 | convolution fusion | flops 1180385280 | bytes 14385156 | tf_op jit(solution)/shard_map/dot_general | solution.py:14
  79.9 9.3 %all-gather.4.cloned.1.call-done = bf16[320,7168]{1,0:T(8,128)(2,1)} async-done(((bf16[40,7168]{1,0:T(8,128)(2,1)}), bf16[320,7168]{1,0:T(8,128)(2,1)}) %all-gather.4.cloned.1.call-update) | async-done | bytes 4587536 | tf_op jit(solution)/shard_map/all_gather | solution.py:18
  89.2 3.5 %fusion.19 = f32[160,256]{1,0:T(8,128)S(1)} fusion(bf16[1,7168,256]{2,1,0:T(8,128)(2,1)} %param.11, bf16[2,160,7168]{2,1,0:T(8,128)(2,1)} %bitcast.130, s32[]{:T(128)S(6)} %select_n.45), kind=kOutput, calls=%fused_computation.26 | convolution fusion | flops 587202560 | bytes 6127620 | tf_op jit(solution)/shard_map/dot_general | solution.py:11
  92.7 6.4 %convolution_convert_fusion = bf16[160,7168]{1,0:T(8,128)(2,1)S(1)} fusion(bf16[1,256,7168]{2,1,0:T(8,128)(2,1)} %param.13, bf16[1,7168,256]{2,1,0:T(8,128)(2,1)} %param.12, bf16[2,160,7168]{2,1,0:T(8,128)(2,1)} %bitcast.131, s32[]{:T(128)S(6)} %select_n.45, f32[160,256]{1,0:T(8,128)S(1)} %fusion.19), kind=kOutput, calls=%fused_computation | convolution fusion | flops 1175797760 | bytes 12091396 | tf_op jit(solution)/shard_map/dot_general | solution.py:14
  99.1 0.3 collective-permute-start.3
  99.4 3.5 %fusion.21 = f32[160,256]{1,0:T(8,128)S(1)} fusion(bf16[1,7168,256]{2,1,0:T(8,128)(2,1)} %param.11, bf16[2,160,7168]{2,1,0:T(8,128)(2,1)} %bitcast.132, s32[]{:T(128)S(6)} %select_n.43), kind=kOutput, calls=%fused_computation.28 | convolution fusion | flops 587202560 | bytes 6127620 | tf_op jit(solution)/shard_map/dot_general | solution.py:11
  102.9 0.8 collective-permute-done.3
  103.8 7.1 %add_convert_fusion = bf16[160,7168]{1,0:T(8,128)(2,1)S(1)} fusion(bf16[160,7168]{1,0:T(8,128)(2,1)} %collective-permute-done.3, bf16[1,256,7168]{2,1,0:T(8,128)(2,1)} %param.13, bf16[1,7168,256]{2,1,0:T(8,128)(2,1)} %param.12, bf16[2,160,7168]{2,1,0:T(8,128)(2,1)} %bitcast.133, s32[]{:T(128)S(6)} %select_n.43, f32[160,256]{1,0:T(8,128)S(1)} %fusion.21), kind=kOutput, calls=%fused_computation.12 | convolution fusion | flops 1180385280 | bytes 14385156 | tf_op jit(solution)/shard_map/dot_general | solution.py:14
  110.9 31.6 %all_to_all.10 = bf16[4,40,7168]{2,1,0:T(8,128)(2,1)} all-to-all(bf16[4,40,7168]{2,1,0:T(8,128)(2,1)S(1)} %bitcast.135), channel_id=1, replica_groups=mesh['grp'=2,'eg'=2,'sc'=4,'core'=2] {'sc'}, dimensions={0} | all-to-all | bytes 4587520 | tf_op jit(solution)/shard_map/all_to_all | solution.py:37
  142.5 3.6 %all-to-all-start.1 = ((bf16[4,40,7168]{2,1,0:T(8,128)(2,1)}), bf16[4,40,7168]{2,1,0:T(8,128)(2,1)S(1)}, u32[]{:S(2)}, u32[]{:S(2)}) async-start(bf16[4,40,7168]{2,1,0:T(8,128)(2,1)} %bitcast.134), calls=%async_computation.1 | async-start | bytes 4587520 | tf_op jit(solution)/shard_map/all_to_all | solution.py:37
  146.1 2.1 %convert_reduce_fusion = f32[40,7168]{1,0:T(8,128)S(1)} fusion(bf16[4,40,7168]{2,1,0:T(8,128)(2,1)} %all_to_all.10), kind=kLoop, calls=%fused_computation.10 | loop fusion | flops 2007040 | bytes 3440640 | tf_op jit(solution)/shard_map/reduce_sum | solution.py:41
  148.2 0.1 multiply_convert_fusion.1
  148.4 2.5 %collective-permute-start.4 = (bf16[40,7168]{1,0:T(8,128)(2,1)S(1)}, bf16[40,7168]{1,0:T(8,128)(2,1)S(1)}, u32[]{:S(2)}, u32[]{:S(2)}) collective-permute-start(bf16[40,7168]{1,0:T(8,128)(2,1)S(1)} %multiply_convert_fusion.1), channel_id=1, source_target_pairs={{0,8},{8,0},{1,9},{9,1},{2,10},{10,2},{3,11},{11,3},{4,12},{12,4},... | collective-permute-start | bytes 1720328 | tf_op jit(solution)/shard_map/ppermute | solution.py:88
  150.8 34.2 %all-to-all-done.1 = bf16[4,40,7168]{2,1,0:T(8,128)(2,1)S(1)} async-done(((bf16[4,40,7168]{2,1,0:T(8,128)(2,1)}), bf16[4,40,7168]{2,1,0:T(8,128)(2,1)S(1)}, u32[]{:S(2)}, u32[]{:S(2)}) %all-to-all-start.1) | async-done | bytes 2293792 | tf_op jit(solution)/shard_map/all_to_all | solution.py:37
  185.0 0.3 convert_reduce_fusion.1
  185.4 0.1 fusion.46
  185.5 0.0 collective-permute-done.4
  185.5 1.4 fusion.2
  (2 shorter events, 0.0 us)
Async XLA Ops:
  6.5 49.2 %all-gather.6.cloned.1.call-start = ((), (), s32[]{:S(2)}) async-start(), calls=%async_computation.3 | async-start | bytes 5160960 | tf_op jit(solution)/shard_map/all_gather | solution.py:18
  8.6 6.7 %copy-start.1 = (f32[64,1]{0,1:T(1,128)S(1)}, f32[64,1]{0,1:T(1,128)}, u32[]{:S(2)}) copy-start(f32[64,1]{0,1:T(1,128)} %param.10) | copy-start | bytes 772
  11.2 78.1 %all-gather.4.cloned.1.call-start = ((), (), s32[]{:S(2)}) async-start(), calls=%async_computation.2 | async-start | bytes 5160960 | tf_op jit(solution)/shard_map/all_gather | solution.py:18
  11.2 29.5 %collective-permute-start = (bf16[40,7168]{1,0:T(8,128)(2,1)S(1)}, bf16[40,7168]{1,0:T(8,128)(2,1)S(1)}, u32[]{:S(2)}, u32[]{:S(2)}) collective-permute-start(bf16[40,7168]{1,0:T(8,128)(2,1)S(1)} %get-tuple-element.19), channel_id=1, source_target_pairs={{0,8},{8,0},{1,9},{9,1},{2,10},{10,2},{3,11},{11,3},{4,12},{12,4},... | collective-permute-start | bytes 1720328 | tf_op jit(solution)/shard_map/ppermute | solution.py:75
  15.6 25.1 %collective-permute-start.1 = (f32[40]{0:T(128)S(1)}, f32[40]{0:T(128)S(1)}, u32[]{:S(2)}, u32[]{:S(2)}) collective-permute-start(f32[40]{0:T(128)S(1)} %get-tuple-element.22), channel_id=1, source_target_pairs={{0,8},{8,0},{1,9},{9,1},{2,10},{10,2},{3,11},{11,3},{4,12},{12,4},... | collective-permute-start | bytes 488 | tf_op jit(solution)/shard_map/ppermute | solution.py:76
  40.7 15.0 %copy-start = (bf16[40,7168]{1,0:T(8,128)(2,1)}, bf16[40,7168]{1,0:T(8,128)(2,1)S(1)}, u32[]{:S(2)}) copy-start(bf16[40,7168]{1,0:T(8,128)(2,1)S(1)} %collective-permute-done) | copy-start | bytes 1720324
  65.7 5.5 %collective-permute-start.2 = (bf16[160,7168]{1,0:T(8,128)(2,1)S(1)}, bf16[160,7168]{1,0:T(8,128)(2,1)}, u32[]{:S(2)}, u32[]{:S(2)}) collective-permute-start(bf16[160,7168]{1,0:T(8,128)(2,1)S(1)} %convolution_convert_fusion.2), channel_id=1, source_target_pairs={{0,1},{1,0},{2,3},{3,2},{4,5},{5,4},{6,7},{7,6},{8,9},{9,8},{10,11... | collective-permute-start | bytes 6881288 | tf_op jit(solution)/shard_map/ppermute | solution.py:30
  99.1 4.6 %collective-permute-start.3 = (bf16[160,7168]{1,0:T(8,128)(2,1)S(1)}, bf16[160,7168]{1,0:T(8,128)(2,1)}, u32[]{:S(2)}, u32[]{:S(2)}) collective-permute-start(bf16[160,7168]{1,0:T(8,128)(2,1)S(1)} %convolution_convert_fusion), channel_id=1, source_target_pairs={{0,1},{1,0},{2,3},{3,2},{4,5},{5,4},{6,7},{7,6},{8,9},{9,8},{10,11... | collective-permute-start | bytes 6881288 | tf_op jit(solution)/shard_map/ppermute | solution.py:30
  142.5 42.6 %all-to-all-start.1 = ((bf16[4,40,7168]{2,1,0:T(8,128)(2,1)}), bf16[4,40,7168]{2,1,0:T(8,128)(2,1)S(1)}, u32[]{:S(2)}, u32[]{:S(2)}) async-start(bf16[4,40,7168]{2,1,0:T(8,128)(2,1)} %bitcast.134), calls=%async_computation.1 | async-start | bytes 4587520 | tf_op jit(solution)/shard_map/all_to_all | solution.py:37
  148.4 37.1 %collective-permute-start.4 = (bf16[40,7168]{1,0:T(8,128)(2,1)S(1)}, bf16[40,7168]{1,0:T(8,128)(2,1)S(1)}, u32[]{:S(2)}, u32[]{:S(2)}) collective-permute-start(bf16[40,7168]{1,0:T(8,128)(2,1)S(1)} %multiply_convert_fusion.1), channel_id=1, source_target_pairs={{0,8},{8,0},{1,9},{9,1},{2,10},{10,2},{3,11},{11,3},{4,12},{12,4},... | collective-permute-start | bytes 1720328 | tf_op jit(solution)/shard_map/ppermute | solution.py:88
Sparse Core Ops, SparseCore 0:
  11.3 44.4 all-gather.5
  57.3 31.8 all-gather.3

commit v11 on v7

--- a/solution.py
+++ b/solution.py
@@ -7,9 +7,9 @@
 SLICES = 8
 
 
-def slice_ffn(rows, gate_w, up_w, down_w):
-    gate = jnp.dot(rows, gate_w, preferred_element_type=jnp.float32)
-    upper = jnp.dot(rows, up_w, preferred_element_type=jnp.float32)
+def slice_ffn(rows, gate_up_w, down_w):
+    both = jnp.dot(rows, gate_up_w, preferred_element_type=jnp.float32)
+    gate, upper = jnp.split(both, 2, axis=1)
     hidden = (jax.nn.silu(gate) * upper).astype(jnp.bfloat16)
     return jnp.dot(hidden, down_w, preferred_element_type=jnp.float32).astype(jnp.bfloat16)
 
@@ -18,12 +18,12 @@
     return lax.all_gather(held, ("core", "sc"), axis=0, tiled=True)
 
 
-def expert_parts(gathered, gate_w, up_w, down_w):
+def expert_parts(gathered, gate_up_w, down_w):
     chips = lax.axis_size("sc")
     cores = lax.axis_size("core")
     count = gathered.shape[0] // (chips * cores)
     width = gathered.shape[1]
-    parts = slice_ffn(gathered, gate_w, up_w, down_w)
+    parts = slice_ffn(gathered, gate_up_w, down_w)
     halves = parts.reshape(cores, chips * count, width)
     core = lax.axis_index("core")
     swap = [(c, (c + 1) % cores) for c in range(cores)]
@@ -66,7 +66,7 @@
         "tkc,td->kcd", place.astype(jnp.bfloat16), normed, preferred_element_type=jnp.float32
     ).astype(jnp.bfloat16)
     packed_w = jnp.sum(jnp.where(place, weight_te[:, :, None], 0.0), axis=0)
-    weights = (w_gate[0], w_up[0], w_down[0])
+    weights = (jnp.concatenate([w_gate[0], w_up[0]], axis=1), w_down[0])
 
     def shift(k):
         return [(g, (g + k) % experts) for g in range(experts)]

time: 187 us -> 186 us (level)
  local copies, waits for them, and re-layouts: 6.68 us -> 3.57 us
    unnamed x20 -> x10, local copies, waits for them, and re-layouts: 5.25 us -> 2.14 us
    dot_general x4 -> x2, matrix products: 12.6 us -> 14.3 us  [slice_ffn(): both = jnp.dot(rows, gate_up_w, preferred_element_type=jnp.float32)]
  transfers between devices with their start and end apart: 8 -> 8, of which waited for: 6 -> 6; matrix products, arithmetic and copies ran while one was open for 8% -> 9% of each run, Pallas kernels for 0% -> 0%
where the time goes in v11:
time: 186 us
  waiting for transfers between devices  96.2 us (52%)
  blocking collectives  31.6 us (17%)
  matrix products  21 us (11%)
  between operations  13.6 us (7%)
  starting transfers between devices  11 us (6%)
  other arithmetic  9.09 us (5%)
  local copies, waits for them, and re-layouts  3.57 us (2%)
    all_to_all x1, waiting for transfers between devices, chip_sums(): return lax.all_to_all(paired, 'sc', split_axis=0, concat_axis=0, tiled=True)  34.2 us
    all_to_all x1, blocking collectives, chip_sums(): return lax.all_to_all(paired, 'sc', split_axis=0, concat_axis=0, tiled=True)  31.6 us
    all_gather x2, waiting for transfers between devices, gather(): return lax.all_gather(held, ('core', 'sc'), axis=0, tiled=True)  28.3 us
    ppermute x1, waiting for transfers between devices, shards(): lax.ppermute(packed_w[k], 'eg', shift(k))  25 us
    dot_general x2, matrix products, slice_ffn(): both = jnp.dot(rows, gate_up_w, preferred_element_type=jnp.float32)  14.3 us
    ppermute x2, waiting for transfers between devices, expert_parts(): sibling = lax.ppermute(halves[(core + 1) % cores], 'core', swap)  8.65 us
    convert_element_type x2, other arithmetic, expert_parts(): (halves[core].astype(jnp.float32) + sibling.astype(jnp.float32)).astype(j...  5.22 us
    ppermute x1, starting transfers between devices, shards(): away = [lax.ppermute(packed[k], 'eg', shift(k)) for k in range(1, experts)]  4.11 us
  transfers between devices with their start and end apart: 8, of which 6 were waited for; matrix products, arithmetic and copies ran while one was open for 9% of the time, Pallas kernels for 0%

profile of v11, /device:TPU:0, one launch (start us, length us, event | category | flops | bytes accessed | tf_op | source)
XLA Modules:
  0.0 186.0 jit_solution(652805338016009684)
XLA Ops:
  6.5 0.0 all-gather.6.cloned.1.call-start
  6.5 2.1 %multiply_reduce_fusion = (f32[64]{0:T(128)S(1)}, f32[64,7168]{1,0:T(8,128)S(1)}) fusion(bf16[64,7168]{1,0:T(8,128)(2,1)} %param.7, s32[64]{0:T(128)} %param.8), kind=kOutput, calls=%fused_computation.20 | convolution fusion | flops 60559296 | bytes 2753024 | tf_op jit(solution)/shard_map/dot_general | solution.py:52
  8.6 0.0 copy-start.4
  8.6 0.7 fusion.32
  9.3 0.1 fusion.21
  9.4 0.1 copy.9
  9.5 0.1 reduce_window_sum.11
  9.6 0.1 fusion.29
  9.6 0.1 copy.8
  9.7 0.5 convolution_convert_fusion.2
  10.2 0.9 slice_bitcast_fusion
  11.1 0.0 all-gather.6.cloned.1.call-update
  11.2 0.0 all-gather.4.cloned.1.call-start
  11.2 4.1 %collective-permute-start = (bf16[40,7168]{1,0:T(8,128)(2,1)S(1)}, bf16[40,7168]{1,0:T(8,128)(2,1)S(1)}, u32[]{:S(2)}, u32[]{:S(2)}) collective-permute-start(bf16[40,7168]{1,0:T(8,128)(2,1)S(1)} %get-tuple-element.19), channel_id=1, source_target_pairs={{0,8},{8,0},{1,9},{9,1},{2,10},{10,2},{3,11},{11,3},{4,12},{12,4},... | collective-permute-start | bytes 1720328 | tf_op jit(solution)/shard_map/ppermute | solution.py:74
  15.3 0.1 fusion.20
  15.4 0.1 copy.10
  15.5 0.1 select_reduce_fusion
  15.6 0.1 collective-permute-start.1
  15.7 25.0 %collective-permute-done.1 = f32[40]{0:T(128)S(1)} collective-permute-done((f32[40]{0:T(128)S(1)}, f32[40]{0:T(128)S(1)}, u32[]{:S(2)}, u32[]{:S(2)}) %collective-permute-start.1) | collective-permute-done | bytes 192 | tf_op jit(solution)/shard_map/ppermute | solution.py:75
  40.7 0.0 collective-permute-done
  40.7 15.0 %all-gather.6.cloned.1.call-done = bf16[1,320,7168]{2,1,0:T(8,128)(2,1)} async-done(((bf16[1,40,7168]{2,1,0:T(8,128)(2,1)}), bf16[1,320,7168]{2,1,0:T(8,128)(2,1)}) %all-gather.6.cloned.1.call-update) | async-done | bytes 4587536 | tf_op jit(solution)/shard_map/all_gather | solution.py:18
  55.7 0.0 copy-done.3
  55.7 0.0 all-gather.4.cloned.1.call-update
  55.8 0.0 copy-start.1
  55.8 7.1 %fusion.2 = f32[320,512]{1,0:T(8,128)S(1)} fusion(bf16[320,7168]{1,0:T(8,128)(2,1)} %bitcast.53, bf16[7168,256]{1,0:T(8,128)(2,1)} %bitcast.54, bf16[7168,256]{1,0:T(8,128)(2,1)} %bitcast.56), kind=kOutput, calls=%fused_computation.8 | convolution fusion | flops 2363490304 | bytes 12582912 | tf_op jit(solution)/shard_map/dot_general | solution.py:11
  62.9 1.4 convolution_convert_fusion.1
  64.3 2.1 %copy-done = bf16[320,7168]{1,0:T(8,128)(2,1)} copy-done((bf16[320,7168]{1,0:T(8,128)(2,1)}, bf16[320,7168]{1,0:T(8,128)(2,1)S(1)}, u32[]{:S(2)}) %copy-start) | copy-done | bytes 4587544
  66.4 0.1 dynamic-slice_bitcast_fusion.1
  66.6 0.3 collective-permute-start.2
  66.9 4.5 %collective-permute-done.2 = bf16[160,7168]{1,0:T(8,128)(2,1)} collective-permute-done((bf16[160,7168]{1,0:T(8,128)(2,1)S(1)}, bf16[160,7168]{1,0:T(8,128)(2,1)}, u32[]{:S(2)}, u32[]{:S(2)}) %collective-permute-start.2) | collective-permute-done | bytes 2293792 | tf_op jit(solution)/shard_map/ppermute | solution.py:30
  71.4 4.5 %fusion.4 = bf16[160,7168]{1,0:T(8,128)(2,1)} fusion(bf16[160,7168]{1,0:T(8,128)(2,1)} %collective-permute-done.2, bf16[2,160,7168]{2,1,0:T(8,128)(2,1)} %bitcast.47, s32[]{:T(128)S(6)} %select_n.43), kind=kLoop, calls=%fused_computation.12 | loop fusion | flops 4587520 | bytes 6881284 | tf_op jit(solution)/shard_map/convert_element_type | solution.py:31
  75.9 13.3 %all-gather.4.cloned.1.call-done = bf16[320,7168]{1,0:T(8,128)(2,1)} async-done(((bf16[40,7168]{1,0:T(8,128)(2,1)}), bf16[320,7168]{1,0:T(8,128)(2,1)}) %all-gather.4.cloned.1.call-update) | async-done | bytes 4587536 | tf_op jit(solution)/shard_map/all_gather | solution.py:18
  89.2 7.1 %fusion.1 = f32[320,512]{1,0:T(8,128)S(1)} fusion(bf16[320,7168]{1,0:T(8,128)(2,1)} %all-gather.4.cloned.1.call-done, bf16[7168,256]{1,0:T(8,128)(2,1)} %bitcast.55, bf16[7168,256]{1,0:T(8,128)(2,1)} %bitcast.57), kind=kOutput, calls=%fused_computation.7 | convolution fusion | flops 2363490304 | bytes 12582912 | tf_op jit(solution)/shard_map/dot_general | solution.py:11
  96.4 1.4 convolution_convert_fusion
  97.7 0.2 dynamic-slice_bitcast_fusion
  97.9 0.3 collective-permute-start.3
  98.2 4.2 %collective-permute-done.3 = bf16[160,7168]{1,0:T(8,128)(2,1)S(1)} collective-permute-done((bf16[160,7168]{1,0:T(8,128)(2,1)S(1)}, bf16[160,7168]{1,0:T(8,128)(2,1)S(1)}, u32[]{:S(2)}, u32[]{:S(2)}) %collective-permute-start.3) | collective-permute-done | bytes 2293792 | tf_op jit(solution)/shard_map/ppermute | solution.py:30
  102.4 0.7 fusion.3
  103.1 31.6 %all_to_all.10 = bf16[4,40,7168]{2,1,0:T(8,128)(2,1)} all-to-all(bf16[4,40,7168]{2,1,0:T(8,128)(2,1)S(1)} %bitcast.50), channel_id=1, replica_groups=mesh['grp'=2,'eg'=2,'sc'=4,'core'=2] {'sc'}, dimensions={0} | all-to-all | bytes 4587520 | tf_op jit(solution)/shard_map/all_to_all | solution.py:36
  134.7 3.6 %all-to-all-start.1 = ((bf16[4,40,7168]{2,1,0:T(8,128)(2,1)}), bf16[4,40,7168]{2,1,0:T(8,128)(2,1)S(1)}, u32[]{:S(2)}, u32[]{:S(2)}) async-start(bf16[4,40,7168]{2,1,0:T(8,128)(2,1)} %bitcast.12), calls=%async_computation.1 | async-start | bytes 4587520 | tf_op jit(solution)/shard_map/all_to_all | solution.py:36
  138.4 2.1 %convert_reduce_fusion = f32[40,7168]{1,0:T(8,128)S(1)} fusion(bf16[4,40,7168]{2,1,0:T(8,128)(2,1)} %all_to_all.10), kind=kLoop, calls=%fused_computation.13 | loop fusion | flops 2007040 | bytes 3440640 | tf_op jit(solution)/shard_map/reduce_sum | solution.py:40
  140.5 0.1 multiply_convert_fusion.1
  140.7 2.5 %collective-permute-start.4 = (bf16[40,7168]{1,0:T(8,128)(2,1)S(1)}, bf16[40,7168]{1,0:T(8,128)(2,1)S(1)}, u32[]{:S(2)}, u32[]{:S(2)}) collective-permute-start(bf16[40,7168]{1,0:T(8,128)(2,1)S(1)} %multiply_convert_fusion.1), channel_id=1, source_target_pairs={{0,8},{8,0},{1,9},{9,1},{2,10},{10,2},{3,11},{11,3},{4,12},{12,4},... | collective-permute-start | bytes 1720328 | tf_op jit(solution)/shard_map/ppermute | solution.py:87
  143.1 34.2 %all-to-all-done.1 = bf16[4,40,7168]{2,1,0:T(8,128)(2,1)S(1)} async-done(((bf16[4,40,7168]{2,1,0:T(8,128)(2,1)}), bf16[4,40,7168]{2,1,0:T(8,128)(2,1)S(1)}, u32[]{:S(2)}, u32[]{:S(2)}) %all-to-all-start.1) | async-done | bytes 2293792 | tf_op jit(solution)/shard_map/all_to_all | solution.py:36
  177.3 0.3 convert_reduce_fusion.1
  177.7 0.1 fusion.10
  177.8 0.0 collective-permute-done.4
  177.8 1.4 fusion
  (8 shorter events, 0.0 us)
Async XLA Ops:
  6.5 49.2 %all-gather.6.cloned.1.call-start = ((), (), s32[]{:S(2)}) async-start(), calls=%async_computation.3 | async-start | bytes 5160960 | tf_op jit(solution)/shard_map/all_gather | solution.py:18
  8.6 6.7 %copy-start.4 = (f32[64,1]{0,1:T(1,128)S(1)}, f32[64,1]{0,1:T(1,128)}, u32[]{:S(2)}) copy-start(f32[64,1]{0,1:T(1,128)} %param.10) | copy-start | bytes 772
  11.2 78.1 %all-gather.4.cloned.1.call-start = ((), (), s32[]{:S(2)}) async-start(), calls=%async_computation.2 | async-start | bytes 5160960 | tf_op jit(solution)/shard_map/all_gather | solution.py:18
  11.2 29.5 %collective-permute-start = (bf16[40,7168]{1,0:T(8,128)(2,1)S(1)}, bf16[40,7168]{1,0:T(8,128)(2,1)S(1)}, u32[]{:S(2)}, u32[]{:S(2)}) collective-permute-start(bf16[40,7168]{1,0:T(8,128)(2,1)S(1)} %get-tuple-element.19), channel_id=1, source_target_pairs={{0,8},{8,0},{1,9},{9,1},{2,10},{10,2},{3,11},{11,3},{4,12},{12,4},... | collective-permute-start | bytes 1720328 | tf_op jit(solution)/shard_map/ppermute | solution.py:74
  15.6 25.1 %collective-permute-start.1 = (f32[40]{0:T(128)S(1)}, f32[40]{0:T(128)S(1)}, u32[]{:S(2)}, u32[]{:S(2)}) collective-permute-start(f32[40]{0:T(128)S(1)} %get-tuple-element.22), channel_id=1, source_target_pairs={{0,8},{8,0},{1,9},{9,1},{2,10},{10,2},{3,11},{11,3},{4,12},{12,4},... | collective-permute-start | bytes 488 | tf_op jit(solution)/shard_map/ppermute | solution.py:75
  40.7 15.0 %copy-start.3 = (bf16[40,7168]{1,0:T(8,128)(2,1)}, bf16[40,7168]{1,0:T(8,128)(2,1)S(1)}, u32[]{:S(2)}) copy-start(bf16[40,7168]{1,0:T(8,128)(2,1)S(1)} %collective-permute-done) | copy-start | bytes 1720324
  55.8 7.2 %copy-start.1 = (bf16[1,256,7168]{2,1,0:T(8,128)(2,1)S(1)}, bf16[1,256,7168]{2,1,0:T(8,128)(2,1)}, u32[]{:S(2)}) copy-start(bf16[1,256,7168]{2,1,0:T(8,128)(2,1)} %param.13) | copy-start | bytes 11010052
  64.3 2.1 %copy-start = (bf16[320,7168]{1,0:T(8,128)(2,1)}, bf16[320,7168]{1,0:T(8,128)(2,1)S(1)}, u32[]{:S(2)}) copy-start(bf16[320,7168]{1,0:T(8,128)(2,1)S(1)} %convolution_convert_fusion.1) | copy-start | bytes 13762564
  66.6 4.8 %collective-permute-start.2 = (bf16[160,7168]{1,0:T(8,128)(2,1)S(1)}, bf16[160,7168]{1,0:T(8,128)(2,1)}, u32[]{:S(2)}, u32[]{:S(2)}) collective-permute-start(bf16[160,7168]{1,0:T(8,128)(2,1)S(1)} %dynamic-slice_bitcast_fusion.1), channel_id=1, source_target_pairs={{0,1},{1,0},{2,3},{3,2},{4,5},{5,4},{6,7},{7,6},{8,9},{9,8},{10,11... | collective-permute-start | bytes 6881288 | tf_op jit(solution)/shard_map/ppermute | solution.py:30
  89.2 7.1 %copy-start.2 = (bf16[1,256,7168]{2,1,0:T(8,128)(2,1)S(1)}, bf16[1,256,7168]{2,1,0:T(8,128)(2,1)}, u32[]{:S(2)}) copy-start(bf16[1,256,7168]{2,1,0:T(8,128)(2,1)} %param.13) | copy-start | bytes 11010052
  97.9 4.5 %collective-permute-start.3 = (bf16[160,7168]{1,0:T(8,128)(2,1)S(1)}, bf16[160,7168]{1,0:T(8,128)(2,1)S(1)}, u32[]{:S(2)}, u32[]{:S(2)}) collective-permute-start(bf16[160,7168]{1,0:T(8,128)(2,1)S(1)} %dynamic-slice_bitcast_fusion), channel_id=1, source_target_pairs={{0,1},{1,0},{2,3},{3,2},{4,5},{5,4},{6,7},{7,6},{8,9},{9,8},{10,11... | collective-permute-start | bytes 6881288 | tf_op jit(solution)/shard_map/ppermute | solution.py:30
  134.7 42.6 %all-to-all-start.1 = ((bf16[4,40,7168]{2,1,0:T(8,128)(2,1)}), bf16[4,40,7168]{2,1,0:T(8,128)(2,1)S(1)}, u32[]{:S(2)}, u32[]{:S(2)}) async-start(bf16[4,40,7168]{2,1,0:T(8,128)(2,1)} %bitcast.12), calls=%async_computation.1 | async-start | bytes 4587520 | tf_op jit(solution)/shard_map/all_to_all | solution.py:36
  140.7 37.1 %collective-permute-start.4 = (bf16[40,7168]{1,0:T(8,128)(2,1)S(1)}, bf16[40,7168]{1,0:T(8,128)(2,1)S(1)}, u32[]{:S(2)}, u32[]{:S(2)}) collective-permute-start(bf16[40,7168]{1,0:T(8,128)(2,1)S(1)} %multiply_convert_fusion.1), channel_id=1, source_target_pairs={{0,8},{8,0},{1,9},{9,1},{2,10},{10,2},{3,11},{11,3},{4,12},{12,4},... | collective-permute-start | bytes 1720328 | tf_op jit(solution)/shard_map/ppermute | solution.py:87
Sparse Core Ops, SparseCore 0:
  11.3 44.4 all-gather.5
  57.3 31.8 all-gather.3

commit v12 on v11

--- a/solution.py
+++ b/solution.py
@@ -29,6 +29,29 @@
     swap = [(c, (c + 1) % cores) for c in range(cores)]
     sibling = lax.ppermute(halves[(core + 1) % cores], "core", swap)
     paired = (halves[core].astype(jnp.float32) + sibling.astype(jnp.float32)).astype(jnp.bfloat16)
+    return paired.reshape(chips, count, width)
+
+
+def gather_by_core(held):
+    chips = lax.axis_size("sc")
+    cores = lax.axis_size("core")
+    swap = [(c, (c + 1) % cores) for c in range(cores)]
+    spread = jnp.broadcast_to(held[None], (chips,) + held.shape)
+    mine = lax.all_to_all(spread, "sc", split_axis=0, concat_axis=0, tiled=True)
+    return mine, lax.ppermute(mine, "core", swap)
+
+
+def expert_parts_by_core(rows, gate_up_w, down_w):
+    mine, theirs = rows
+    cores = lax.axis_size("core")
+    swap = [(c, (c + 1) % cores) for c in range(cores)]
+    chips, count, width = mine.shape
+    parts = slice_ffn(
+        jnp.concatenate([theirs, mine], axis=0).reshape(2 * chips * count, width), gate_up_w, down_w
+    )
+    sibling = lax.ppermute(parts[:chips * count], "core", swap)
+    kept = parts[chips * count:]
+    paired = (kept.astype(jnp.float32) + sibling.astype(jnp.float32)).astype(jnp.bfloat16)
     return paired.reshape(chips, count, width)
 
 
@@ -74,11 +97,11 @@
     away = [lax.ppermute(packed[k], "eg", shift(k)) for k in range(1, experts)]
     away_w = [lax.ppermute(packed_w[k], "eg", shift(k)) for k in range(1, experts)]
     own_rows = gather(packed[0])
-    own_rows, away, away_w = lax.optimization_barrier((own_rows, away, away_w))
+    away, away_w = lax.optimization_barrier((away, away_w))
     own_parts = expert_parts(own_rows, *weights)
-    away_rows = gather(jnp.concatenate(away, axis=0))
+    away_rows = gather_by_core(jnp.concatenate(away, axis=0))
     own_parts, away_rows = lax.optimization_barrier((own_parts, away_rows))
-    away_parts = expert_parts(away_rows, *weights)
+    away_parts = expert_parts_by_core(away_rows, *weights)
     away_back = chip_sums(away_parts)
     own_parts, away_back = lax.optimization_barrier((own_parts, away_back))
     done = finish(away_back, jnp.concatenate(away_w, axis=0))

time: 186 us -> 190 us (1.022)
  local copies, waits for them, and re-layouts: 3.57 us -> 8.35 us
  matrix products: 21 us -> 16.4 us
  starting transfers between devices: 11 us -> 13.5 us
  other arithmetic: 9.09 us -> 11.3 us
    dot_general x2, matrix products: 14.3 us -> 9.65 us  [slice_ffn(): both = jnp.dot(rows, gate_up_w, preferred_element_type=jnp.float32)]
    ppermute x0 -> x2, waiting for transfers between devices: none -> 4.33 us  [the longest x1 4.32 us: expert_parts_by_core(): sibling = lax.ppermute(parts[:chips * count], 'core', swap)]
    all_to_all x0 -> x1, starting transfers between devices: none -> 3.64 us  [gather_by_core(): mine = lax.all_to_all(spread, 'sc', split_axis=0, concat_axis=0, tiled=True)]
    ppermute x2 -> x1, waiting for transfers between devices: 8.65 us -> 5.15 us  [expert_parts(): sibling = lax.ppermute(halves[(core + 1) % cores], 'core', swap)]
    all_gather x2 -> x1, waiting for transfers between devices: 28.3 us -> 25.2 us  [gather(): return lax.all_gather(held, ('core', 'sc'), axis=0, tiled=True)]
    concatenate x0 -> x1, other arithmetic: none -> 2.19 us  [expert_parts_by_core(): jnp.concatenate([theirs, mine], axis=0).reshape(2 * chips * count, width)]
    convert_element_type x2 -> x1, other arithmetic: 5.22 us -> 4.49 us  [expert_parts(): (halves[core].astype(jnp.float32) + sibling.astype(jnp.float32)).astype(j...]
  transfers between devices with their start and end apart: 8 -> 9, of which waited for: 6 -> 5; matrix products, arithmetic and copies ran while one was open for 9% -> 10% of each run, Pallas kernels for 0% -> 0%
where the time goes in v12:
time: 190 us; the launch traced here: 189 us
  waiting for transfers between devices  94.9 us (50%)
  blocking collectives  31.5 us (17%)
  matrix products  16.4 us (9%)
  between operations  13.6 us (7%)
  starting transfers between devices  13.5 us (7%)
  other arithmetic  11.3 us (6%)
  local copies, waits for them, and re-layouts  8.35 us (4%)
    all_to_all x1, waiting for transfers between devices, chip_sums(): return lax.all_to_all(paired, 'sc', split_axis=0, concat_axis=0, tiled=True)  35.2 us
    all_to_all x1, blocking collectives, chip_sums(): return lax.all_to_all(paired, 'sc', split_axis=0, concat_axis=0, tiled=True)  31.5 us
    all_gather x1, waiting for transfers between devices, gather(): return lax.all_gather(held, ('core', 'sc'), axis=0, tiled=True)  25.2 us
    ppermute x1, waiting for transfers between devices, shards(): lax.ppermute(packed_w[k], 'eg', shift(k))  25 us
    dot_general x2, matrix products, slice_ffn(): both = jnp.dot(rows, gate_up_w, preferred_element_type=jnp.float32)  9.65 us
    ppermute x1, waiting for transfers between devices, expert_parts(): sibling = lax.ppermute(halves[(core + 1) % cores], 'core', swap)  5.15 us
    convert_element_type x1, other arithmetic, expert_parts(): (halves[core].astype(jnp.float32) + sibling.astype(jnp.float32)).astype(j...  4.49 us
    ppermute x1, waiting for transfers between devices, expert_parts_by_core(): sibling = lax.ppermute(parts[:chips * count], 'core', swap)  4.32 us
  transfers between devices with their start and end apart: 9, of which 5 were waited for; matrix products, arithmetic and copies ran while one was open for 10% of the time, Pallas kernels for 0%

profile of v12, /device:TPU:0, one launch (start us, length us, event | category | flops | bytes accessed | tf_op | source)
XLA Modules:
  0.0 189.5 jit_solution(5295207901227356406)
XLA Ops:
  6.5 2.0 %multiply_reduce_fusion = (f32[64]{0:T(128)S(1)}, f32[64,7168]{1,0:T(8,128)S(1)}) fusion(bf16[64,7168]{1,0:T(8,128)(2,1)} %param.7, s32[64]{0:T(128)} %param.8), kind=kOutput, calls=%fused_computation.20 | convolution fusion | flops 60559296 | bytes 2753024 | tf_op jit(solution)/shard_map/dot_general | solution.py:75
  8.6 0.0 copy-start.3
  8.6 0.7 fusion.30
  9.3 0.1 fusion.21
  9.4 0.1 copy.9
  9.4 0.1 reduce_window_sum.11
  9.5 0.1 fusion.29
  9.6 0.1 copy.8
  9.7 0.5 convolution_convert_fusion.2
  10.2 0.9 slice_bitcast_fusion
  11.1 0.0 all-gather.3.cloned.1.call-update
  11.1 4.1 %collective-permute-start.1 = (bf16[40,7168]{1,0:T(8,128)(2,1)S(1)}, bf16[40,7168]{1,0:T(8,128)(2,1)S(1)}, u32[]{:S(2)}, u32[]{:S(2)}) collective-permute-start(bf16[40,7168]{1,0:T(8,128)(2,1)S(1)} %get-tuple-element.19), channel_id=1, source_target_pairs={{0,8},{8,0},{1,9},{9,1},{2,10},{10,2},{3,11},{11,3},{4,12},{12,4},... | collective-permute-start | bytes 1720328 | tf_op jit(solution)/shard_map/ppermute | solution.py:97
  15.2 0.1 fusion.20
  15.3 0.1 copy.10
  15.4 0.1 select_reduce_fusion
  15.5 0.1 collective-permute-start.2
  15.6 25.0 %collective-permute-done.2 = f32[40]{0:T(128)S(1)} collective-permute-done((f32[40]{0:T(128)S(1)}, f32[40]{0:T(128)S(1)}, u32[]{:S(2)}, u32[]{:S(2)}) %collective-permute-start.2) | collective-permute-done | bytes 192 | tf_op jit(solution)/shard_map/ppermute | solution.py:98
  40.6 0.0 collective-permute-done.1
  40.6 1.7 broadcast_in_dim.30
  42.3 3.6 %all-to-all-start = ((bf16[4,40,7168]{2,1,0:T(8,128)(2,1)}), bf16[4,40,7168]{2,1,0:T(8,128)(2,1)S(1)}, u32[]{:S(2)}, u32[]{:S(2)}) async-start(bf16[4,40,7168]{2,1,0:T(8,128)(2,1)} %broadcast_in_dim.30), calls=%async_computation | async-start | bytes 4587520 | tf_op jit(solution)/shard_map/all_to_all | solution.py:40
  46.0 25.2 %all-gather.3.cloned.1.call-done = bf16[1,320,7168]{2,1,0:T(8,128)(2,1)} async-done(((bf16[1,40,7168]{2,1,0:T(8,128)(2,1)}), bf16[1,320,7168]{2,1,0:T(8,128)(2,1)}) %all-gather.3.cloned.1.call-update) | async-done | bytes 4587536 | tf_op jit(solution)/shard_map/all_gather | solution.py:18
  71.2 7.1 %fusion.2 = f32[320,512]{1,0:T(8,128)S(1)} fusion(bf16[7168,256]{1,0:T(8,128)(2,1)} %bitcast.48, bf16[7168,256]{1,0:T(8,128)(2,1)} %bitcast.50, bf16[1,320,7168]{2,1,0:T(8,128)(2,1)} %all-gather.3.cloned.1.call-done), kind=kOutput, calls=%fused_computation.8 | convolution fusion | flops 2363490304 | bytes 12582912 | tf_op jit(solution)/shard_map/dot_general | solution.py:11
  78.3 1.4 convolution_convert_fusion.1
  79.7 2.1 %copy-done = bf16[320,7168]{1,0:T(8,128)(2,1)} copy-done((bf16[320,7168]{1,0:T(8,128)(2,1)}, bf16[320,7168]{1,0:T(8,128)(2,1)S(1)}, u32[]{:S(2)}) %copy-start) | copy-done | bytes 4587544
  81.8 1.7 dynamic-slice_bitcast_fusion
  83.5 0.2 collective-permute-start
  83.7 0.0 all-to-all-done
  83.7 0.3 collective-permute-start.3
  84.0 5.2 %collective-permute-done = bf16[160,7168]{1,0:T(8,128)(2,1)} collective-permute-done((bf16[160,7168]{1,0:T(8,128)(2,1)}, bf16[160,7168]{1,0:T(8,128)(2,1)}, u32[]{:S(2)}, u32[]{:S(2)}) %collective-permute-start) | collective-permute-done | bytes 2293792 | tf_op jit(solution)/shard_map/ppermute | solution.py:30
  89.1 4.5 %fusion.3 = bf16[160,7168]{1,0:T(8,128)(2,1)} fusion(bf16[160,7168]{1,0:T(8,128)(2,1)} %collective-permute-done, bf16[2,160,7168]{2,1,0:T(8,128)(2,1)} %bitcast.43, s32[]{:T(128)S(6)} %select_n.37), kind=kLoop, calls=%fused_computation.11 | loop fusion | flops 4587520 | bytes 6881284 | tf_op jit(solution)/shard_map/convert_element_type | solution.py:31
  93.6 2.2 %pad_maximum_fusion.3 = bf16[8,40,7168]{2,1,0:T(8,128)(2,1)S(1)} fusion(bf16[4,40,7168]{2,1,0:T(8,128)(2,1)S(1)} %all-to-all-done, bf16[4,40,7168]{2,1,0:T(8,128)(2,1)} %collective-permute-done.3), kind=kLoop, calls=%fused_computation.9 | loop fusion | flops 2293760 | bytes 9175040 | tf_op jit(solution)/shard_map/concatenate | solution.py:50
  95.8 0.5 copy-done.4
  96.4 1.1 copy-done.5
  97.5 2.5 %fusion.1 = f32[320,512]{1,0:T(8,128)S(1)} fusion(bf16[320,7168]{1,0:T(8,128)(2,1)S(1)} %bitcast.45, bf16[7168,256]{1,0:T(8,128)(2,1)S(1)} %bitcast.49, bf16[7168,256]{1,0:T(8,128)(2,1)S(1)} %bitcast.51), kind=kOutput, calls=%fused_computation.7 | convolution fusion | flops 2363490304 | bytes 12582912 | tf_op jit(solution)/shard_map/dot_general | solution.py:11
  100.0 1.4 convolution_convert_fusion
  101.4 0.2 slice.30
  101.6 0.2 collective-permute-start.4
  101.8 4.3 %collective-permute-done.4 = bf16[160,7168]{1,0:T(8,128)(2,1)S(1)} collective-permute-done((bf16[160,7168]{1,0:T(8,128)(2,1)S(1)}, bf16[160,7168]{1,0:T(8,128)(2,1)S(1)}, u32[]{:S(2)}, u32[]{:S(2)}) %collective-permute-start.4) | collective-permute-done | bytes 2293792 | tf_op jit(solution)/shard_map/ppermute | solution.py:52
  106.1 0.7 add_convert_fusion
  106.8 31.5 %all_to_all.15 = bf16[4,40,7168]{2,1,0:T(8,128)(2,1)} all-to-all(bf16[4,40,7168]{2,1,0:T(8,128)(2,1)S(1)} %bitcast.44), channel_id=1, replica_groups=mesh['grp'=2,'eg'=2,'sc'=4,'core'=2] {'sc'}, dimensions={0} | all-to-all | bytes 4587520 | tf_op jit(solution)/shard_map/all_to_all | solution.py:59
  138.3 3.6 %all-to-all-start.2 = ((bf16[4,40,7168]{2,1,0:T(8,128)(2,1)}), bf16[4,40,7168]{2,1,0:T(8,128)(2,1)S(1)}, u32[]{:S(2)}, u32[]{:S(2)}) async-start(bf16[4,40,7168]{2,1,0:T(8,128)(2,1)} %bitcast.9), calls=%async_computation.2 | async-start | bytes 4587520 | tf_op jit(solution)/shard_map/all_to_all | solution.py:59
  141.9 2.2 %convert_reduce_fusion = f32[40,7168]{1,0:T(8,128)S(1)} fusion(bf16[4,40,7168]{2,1,0:T(8,128)(2,1)} %all_to_all.15), kind=kLoop, calls=%fused_computation.13 | loop fusion | flops 2007040 | bytes 3440640 | tf_op jit(solution)/shard_map/reduce_sum | solution.py:63
  144.1 0.1 multiply_convert_fusion.1
  144.2 1.3 collective-permute-start.5
  145.6 35.2 %all-to-all-done.2 = bf16[4,40,7168]{2,1,0:T(8,128)(2,1)S(1)} async-done(((bf16[4,40,7168]{2,1,0:T(8,128)(2,1)}), bf16[4,40,7168]{2,1,0:T(8,128)(2,1)S(1)}, u32[]{:S(2)}, u32[]{:S(2)}) %all-to-all-start.2) | async-done | bytes 2293792 | tf_op jit(solution)/shard_map/all_to_all | solution.py:59
  180.7 0.4 convert_reduce_fusion.1
  181.1 0.1 fusion.10
  181.3 1.4 fusion
  (13 shorter events, 0.0 us)
Async XLA Ops:
  6.5 64.6 %all-gather.3.cloned.1.call-start = ((), (), s32[]{:S(2)}) async-start(), calls=%async_computation.3 | async-start | bytes 5160960 | tf_op jit(solution)/shard_map/all_gather | solution.py:18
  8.6 6.7 %copy-start.3 = (f32[64,1]{0,1:T(1,128)S(1)}, f32[64,1]{0,1:T(1,128)}, u32[]{:S(2)}) copy-start(f32[64,1]{0,1:T(1,128)} %param.10) | copy-start | bytes 772
  11.1 29.5 %collective-permute-start.1 = (bf16[40,7168]{1,0:T(8,128)(2,1)S(1)}, bf16[40,7168]{1,0:T(8,128)(2,1)S(1)}, u32[]{:S(2)}, u32[]{:S(2)}) collective-permute-start(bf16[40,7168]{1,0:T(8,128)(2,1)S(1)} %get-tuple-element.19), channel_id=1, source_target_pairs={{0,8},{8,0},{1,9},{9,1},{2,10},{10,2},{3,11},{11,3},{4,12},{12,4},... | collective-permute-start | bytes 1720328 | tf_op jit(solution)/shard_map/ppermute | solution.py:97
  15.5 25.1 %collective-permute-start.2 = (f32[40]{0:T(128)S(1)}, f32[40]{0:T(128)S(1)}, u32[]{:S(2)}, u32[]{:S(2)}) collective-permute-start(f32[40]{0:T(128)S(1)} %get-tuple-element.22), channel_id=1, source_target_pairs={{0,8},{8,0},{1,9},{9,1},{2,10},{10,2},{3,11},{11,3},{4,12},{12,4},... | collective-permute-start | bytes 488 | tf_op jit(solution)/shard_map/ppermute | solution.py:98
  42.3 41.4 %all-to-all-start = ((bf16[4,40,7168]{2,1,0:T(8,128)(2,1)}), bf16[4,40,7168]{2,1,0:T(8,128)(2,1)S(1)}, u32[]{:S(2)}, u32[]{:S(2)}) async-start(bf16[4,40,7168]{2,1,0:T(8,128)(2,1)} %broadcast_in_dim.30), calls=%async_computation | async-start | bytes 4587520 | tf_op jit(solution)/shard_map/all_to_all | solution.py:40
  71.2 7.1 %copy-start.1 = (bf16[1,256,7168]{2,1,0:T(8,128)(2,1)S(1)}, bf16[1,256,7168]{2,1,0:T(8,128)(2,1)}, u32[]{:S(2)}) copy-start(bf16[1,256,7168]{2,1,0:T(8,128)(2,1)} %param.13) | copy-start | bytes 11010052
  79.7 2.1 %copy-start = (bf16[320,7168]{1,0:T(8,128)(2,1)}, bf16[320,7168]{1,0:T(8,128)(2,1)S(1)}, u32[]{:S(2)}) copy-start(bf16[320,7168]{1,0:T(8,128)(2,1)S(1)} %convolution_convert_fusion.1) | copy-start | bytes 13762564
  83.5 5.7 %collective-permute-start = (bf16[160,7168]{1,0:T(8,128)(2,1)}, bf16[160,7168]{1,0:T(8,128)(2,1)}, u32[]{:S(2)}, u32[]{:S(2)}) collective-permute-start(bf16[160,7168]{1,0:T(8,128)(2,1)} %dynamic-slice_bitcast_fusion), channel_id=1, source_target_pairs={{0,1},{1,0},{2,3},{3,2},{4,5},{5,4},{6,7},{7,6},{8,9},{9,8},{10,11... | collective-permute-start | bytes 6881288 | tf_op jit(solution)/shard_map/ppermute | solution.py:30
  83.7 9.9 %collective-permute-start.3 = (bf16[4,40,7168]{2,1,0:T(8,128)(2,1)S(1)}, bf16[4,40,7168]{2,1,0:T(8,128)(2,1)}, u32[]{:S(2)}, u32[]{:S(2)}) collective-permute-start(bf16[4,40,7168]{2,1,0:T(8,128)(2,1)S(1)} %all-to-all-done), channel_id=1, source_target_pairs={{0,1},{1,0},{2,3},{3,2},{4,5},{5,4},{6,7},{7,6},{8,9},{9,8},{10,11... | collective-permute-start | bytes 6881288 | tf_op jit(solution)/shard_map/ppermute | solution.py:41
  93.6 2.7 %copy-start.4 = (bf16[1,7168,256]{2,1,0:T(8,128)(2,1)S(1)}, bf16[1,7168,256]{2,1,0:T(8,128)(2,1)}, u32[]{:S(2)}) copy-start(bf16[1,7168,256]{2,1,0:T(8,128)(2,1)} %param.12) | copy-start | bytes 11010052
  93.6 3.8 %copy-start.5 = (bf16[1,7168,256]{2,1,0:T(8,128)(2,1)S(1)}, bf16[1,7168,256]{2,1,0:T(8,128)(2,1)}, u32[]{:S(2)}) copy-start(bf16[1,7168,256]{2,1,0:T(8,128)(2,1)} %param.11) | copy-start | bytes 11010052
  97.5 2.5 %copy-start.2 = (bf16[1,256,7168]{2,1,0:T(8,128)(2,1)S(1)}, bf16[1,256,7168]{2,1,0:T(8,128)(2,1)}, u32[]{:S(2)}) copy-start(bf16[1,256,7168]{2,1,0:T(8,128)(2,1)} %param.13) | copy-start | bytes 11010052
  101.6 4.5 %collective-permute-start.4 = (bf16[160,7168]{1,0:T(8,128)(2,1)S(1)}, bf16[160,7168]{1,0:T(8,128)(2,1)S(1)}, u32[]{:S(2)}, u32[]{:S(2)}) collective-permute-start(bf16[160,7168]{1,0:T(8,128)(2,1)S(1)} %slice.30), channel_id=1, source_target_pairs={{0,1},{1,0},{2,3},{3,2},{4,5},{5,4},{6,7},{7,6},{8,9},{9,8},{10,11... | collective-permute-start | bytes 6881288 | tf_op jit(solution)/shard_map/ppermute | solution.py:52
  138.3 42.4 %all-to-all-start.2 = ((bf16[4,40,7168]{2,1,0:T(8,128)(2,1)}), bf16[4,40,7168]{2,1,0:T(8,128)(2,1)S(1)}, u32[]{:S(2)}, u32[]{:S(2)}) async-start(bf16[4,40,7168]{2,1,0:T(8,128)(2,1)} %bitcast.9), calls=%async_computation.2 | async-start | bytes 4587520 | tf_op jit(solution)/shard_map/all_to_all | solution.py:59
  144.2 37.0 %collective-permute-start.5 = (bf16[40,7168]{1,0:T(8,128)(2,1)S(1)}, bf16[40,7168]{1,0:T(8,128)(2,1)S(1)}, u32[]{:S(2)}, u32[]{:S(2)}) collective-permute-start(bf16[40,7168]{1,0:T(8,128)(2,1)S(1)} %multiply_convert_fusion.1), channel_id=1, source_target_pairs={{0,8},{8,0},{1,9},{9,1},{2,10},{10,2},{3,11},{11,3},{4,12},{12,4},... | collective-permute-start | bytes 1720328 | tf_op jit(solution)/shard_map/ppermute | solution.py:110
Sparse Core Ops, SparseCore 0:
  11.2 59.8 all-gather.2

commit v13 on v11

--- a/solution.py
+++ b/solution.py
@@ -80,8 +80,8 @@
     own_parts, away_rows = lax.optimization_barrier((own_parts, away_rows))
     away_parts = expert_parts(away_rows, *weights)
     away_back = chip_sums(away_parts)
-    own_parts, away_back = lax.optimization_barrier((own_parts, away_back))
     done = finish(away_back, jnp.concatenate(away_w, axis=0))
+    own_parts, done = lax.optimization_barrier((own_parts, done))
     own = finish(chip_sums(own_parts), packed_w[0])
     home = [own] + [
         lax.ppermute(done[(k - 1) * slots:k * slots], "eg", shift(experts - k))

time: 186 us -> 186 us (level)
  waiting for transfers between devices: 96.2 us -> 98.3 us
    all_to_all x1, waiting for transfers between devices: 34.2 us -> 36.3 us  [chip_sums(): return lax.all_to_all(paired, 'sc', split_axis=0, concat_axis=0, tiled=True)]
  transfers between devices with their start and end apart: 8 -> 8, of which waited for: 6 -> 6; matrix products, arithmetic and copies ran while one was open for 9% -> 8% of each run, Pallas kernels for 0% -> 0%
where the time goes in v13:
time: 186 us
  waiting for transfers between devices  98.3 us (53%)
  blocking collectives  30.8 us (17%)
  matrix products  21 us (11%)
  between operations  13.6 us (7%)
  starting transfers between devices  11 us (6%)
  other arithmetic  7.3 us (4%)
  local copies, waits for them, and re-layouts  3.57 us (2%)
    all_to_all x1, waiting for transfers between devices, chip_sums(): return lax.all_to_all(paired, 'sc', split_axis=0, concat_axis=0, tiled=True)  36.3 us
    all_to_all x1, blocking collectives, chip_sums(): return lax.all_to_all(paired, 'sc', split_axis=0, concat_axis=0, tiled=True)  30.8 us
    all_gather x2, waiting for transfers between devices, gather(): return lax.all_gather(held, ('core', 'sc'), axis=0, tiled=True)  28.3 us
    ppermute x1, waiting for transfers between devices, shards(): lax.ppermute(packed_w[k], 'eg', shift(k))  25 us
    dot_general x2, matrix products, slice_ffn(): both = jnp.dot(rows, gate_up_w, preferred_element_type=jnp.float32)  14.3 us
    ppermute x2, waiting for transfers between devices, expert_parts(): sibling = lax.ppermute(halves[(core + 1) % cores], 'core', swap)  8.65 us
    convert_element_type x2, other arithmetic, expert_parts(): (halves[core].astype(jnp.float32) + sibling.astype(jnp.float32)).astype(j...  5.22 us
    ppermute x1, starting transfers between devices, shards(): away = [lax.ppermute(packed[k], 'eg', shift(k)) for k in range(1, experts)]  4.11 us
  transfers between devices with their start and end apart: 8, of which 6 were waited for; matrix products, arithmetic and copies ran while one was open for 8% of the time, Pallas kernels for 0%

profile of v13, /device:TPU:0, one launch (start us, length us, event | category | flops | bytes accessed | tf_op | source)
XLA Modules:
  0.0 185.6 jit_solution(1469651335823000031)
XLA Ops:
  6.5 2.1 %multiply_reduce_fusion = (f32[64]{0:T(128)S(1)}, f32[64,7168]{1,0:T(8,128)S(1)}) fusion(bf16[64,7168]{1,0:T(8,128)(2,1)} %param.7, s32[64]{0:T(128)} %param.8), kind=kOutput, calls=%fused_computation.20 | convolution fusion | flops 60559296 | bytes 2753024 | tf_op jit(solution)/shard_map/dot_general | solution.py:52
  8.6 0.0 copy-start.4
  8.6 0.7 fusion.32
  9.3 0.1 fusion.21
  9.4 0.1 copy.9
  9.5 0.1 reduce_window_sum.11
  9.6 0.1 fusion.29
  9.6 0.1 copy.8
  9.7 0.5 convolution_convert_fusion.2
  10.2 0.9 slice_bitcast_fusion
  11.1 0.0 all-gather.6.cloned.1.call-update
  11.1 0.0 all-gather.4.cloned.1.call-start
  11.2 4.1 %collective-permute-start = (bf16[40,7168]{1,0:T(8,128)(2,1)S(1)}, bf16[40,7168]{1,0:T(8,128)(2,1)S(1)}, u32[]{:S(2)}, u32[]{:S(2)}) collective-permute-start(bf16[40,7168]{1,0:T(8,128)(2,1)S(1)} %get-tuple-element.19), channel_id=1, source_target_pairs={{0,8},{8,0},{1,9},{9,1},{2,10},{10,2},{3,11},{11,3},{4,12},{12,4},... | collective-permute-start | bytes 1720328 | tf_op jit(solution)/shard_map/ppermute | solution.py:74
  15.3 0.1 fusion.20
  15.4 0.1 copy.10
  15.5 0.1 select_reduce_fusion
  15.6 0.1 collective-permute-start.1
  15.7 25.0 %collective-permute-done.1 = f32[40]{0:T(128)S(1)} collective-permute-done((f32[40]{0:T(128)S(1)}, f32[40]{0:T(128)S(1)}, u32[]{:S(2)}, u32[]{:S(2)}) %collective-permute-start.1) | collective-permute-done | bytes 192 | tf_op jit(solution)/shard_map/ppermute | solution.py:75
  40.7 0.0 collective-permute-done
  40.7 15.0 %all-gather.6.cloned.1.call-done = bf16[1,320,7168]{2,1,0:T(8,128)(2,1)} async-done(((bf16[1,40,7168]{2,1,0:T(8,128)(2,1)}), bf16[1,320,7168]{2,1,0:T(8,128)(2,1)}) %all-gather.6.cloned.1.call-update) | async-done | bytes 4587536 | tf_op jit(solution)/shard_map/all_gather | solution.py:18
  55.7 0.0 copy-done.3
  55.7 0.0 all-gather.4.cloned.1.call-update
  55.8 0.0 copy-start.1
  55.8 7.1 %fusion.2 = f32[320,512]{1,0:T(8,128)S(1)} fusion(bf16[320,7168]{1,0:T(8,128)(2,1)} %bitcast.53, bf16[7168,256]{1,0:T(8,128)(2,1)} %bitcast.54, bf16[7168,256]{1,0:T(8,128)(2,1)} %bitcast.56), kind=kOutput, calls=%fused_computation.8 | convolution fusion | flops 2363490304 | bytes 12582912 | tf_op jit(solution)/shard_map/dot_general | solution.py:11
  62.9 1.4 convolution_convert_fusion.1
  64.3 0.0 copy-start
  64.3 2.1 %copy-done = bf16[320,7168]{1,0:T(8,128)(2,1)} copy-done((bf16[320,7168]{1,0:T(8,128)(2,1)}, bf16[320,7168]{1,0:T(8,128)(2,1)S(1)}, u32[]{:S(2)}) %copy-start) | copy-done | bytes 4587544
  66.4 0.1 dynamic-slice_bitcast_fusion.1
  66.6 0.3 collective-permute-start.2
  66.9 4.5 %collective-permute-done.2 = bf16[160,7168]{1,0:T(8,128)(2,1)} collective-permute-done((bf16[160,7168]{1,0:T(8,128)(2,1)S(1)}, bf16[160,7168]{1,0:T(8,128)(2,1)}, u32[]{:S(2)}, u32[]{:S(2)}) %collective-permute-start.2) | collective-permute-done | bytes 2293792 | tf_op jit(solution)/shard_map/ppermute | solution.py:30
  71.4 4.5 %fusion.4 = bf16[160,7168]{1,0:T(8,128)(2,1)} fusion(bf16[160,7168]{1,0:T(8,128)(2,1)} %collective-permute-done.2, bf16[2,160,7168]{2,1,0:T(8,128)(2,1)} %bitcast.47, s32[]{:T(128)S(6)} %select_n.43), kind=kLoop, calls=%fused_computation.12 | loop fusion | flops 4587520 | bytes 6881284 | tf_op jit(solution)/shard_map/convert_element_type | solution.py:31
  75.9 13.3 %all-gather.4.cloned.1.call-done = bf16[320,7168]{1,0:T(8,128)(2,1)} async-done(((bf16[40,7168]{1,0:T(8,128)(2,1)}), bf16[320,7168]{1,0:T(8,128)(2,1)}) %all-gather.4.cloned.1.call-update) | async-done | bytes 4587536 | tf_op jit(solution)/shard_map/all_gather | solution.py:18
  89.2 7.1 %fusion.1 = f32[320,512]{1,0:T(8,128)S(1)} fusion(bf16[320,7168]{1,0:T(8,128)(2,1)} %all-gather.4.cloned.1.call-done, bf16[7168,256]{1,0:T(8,128)(2,1)} %bitcast.55, bf16[7168,256]{1,0:T(8,128)(2,1)} %bitcast.57), kind=kOutput, calls=%fused_computation.7 | convolution fusion | flops 2363490304 | bytes 12582912 | tf_op jit(solution)/shard_map/dot_general | solution.py:11
  96.3 1.4 convolution_convert_fusion
  97.7 0.2 dynamic-slice_bitcast_fusion
  97.9 0.3 collective-permute-start.3
  98.2 4.2 %collective-permute-done.3 = bf16[160,7168]{1,0:T(8,128)(2,1)S(1)} collective-permute-done((bf16[160,7168]{1,0:T(8,128)(2,1)S(1)}, bf16[160,7168]{1,0:T(8,128)(2,1)S(1)}, u32[]{:S(2)}, u32[]{:S(2)}) %collective-permute-start.3) | collective-permute-done | bytes 2293792 | tf_op jit(solution)/shard_map/ppermute | solution.py:30
  102.4 0.7 fusion.3
  103.1 30.8 %all_to_all.10 = bf16[4,40,7168]{2,1,0:T(8,128)(2,1)S(1)} all-to-all(bf16[4,40,7168]{2,1,0:T(8,128)(2,1)S(1)} %bitcast.50), channel_id=1, replica_groups=mesh['grp'=2,'eg'=2,'sc'=4,'core'=2] {'sc'}, dimensions={0} | all-to-all | bytes 4587520 | tf_op jit(solution)/shard_map/all_to_all | solution.py:36
  133.9 0.4 convert_reduce_fusion.1
  134.3 0.1 multiply_convert_fusion.1
  134.4 3.6 %all-to-all-start.1 = ((bf16[4,40,7168]{2,1,0:T(8,128)(2,1)}), bf16[4,40,7168]{2,1,0:T(8,128)(2,1)S(1)}, u32[]{:S(2)}, u32[]{:S(2)}) async-start(bf16[4,40,7168]{2,1,0:T(8,128)(2,1)} %bitcast.12), calls=%async_computation.1 | async-start | bytes 4587520 | tf_op jit(solution)/shard_map/all_to_all | solution.py:36
  138.1 2.5 %collective-permute-start.4 = (bf16[40,7168]{1,0:T(8,128)(2,1)S(1)}, bf16[40,7168]{1,0:T(8,128)(2,1)S(1)}, u32[]{:S(2)}, u32[]{:S(2)}) collective-permute-start(bf16[40,7168]{1,0:T(8,128)(2,1)S(1)} %multiply_convert_fusion.1), channel_id=1, source_target_pairs={{0,8},{8,0},{1,9},{9,1},{2,10},{10,2},{3,11},{11,3},{4,12},{12,4},... | collective-permute-start | bytes 1720328 | tf_op jit(solution)/shard_map/ppermute | solution.py:87
  140.5 36.3 %all-to-all-done.1 = bf16[4,40,7168]{2,1,0:T(8,128)(2,1)S(1)} async-done(((bf16[4,40,7168]{2,1,0:T(8,128)(2,1)}), bf16[4,40,7168]{2,1,0:T(8,128)(2,1)S(1)}, u32[]{:S(2)}, u32[]{:S(2)}) %all-to-all-start.1) | async-done | bytes 2293792 | tf_op jit(solution)/shard_map/all_to_all | solution.py:36
  176.9 0.3 convert_reduce_fusion
  177.2 0.1 fusion.10
  177.3 0.0 collective-permute-done.4
  177.4 1.4 fusion
  (8 shorter events, 0.0 us)
Async XLA Ops:
  6.5 49.2 %all-gather.6.cloned.1.call-start = ((), (), s32[]{:S(2)}) async-start(), calls=%async_computation.3 | async-start | bytes 5160960 | tf_op jit(solution)/shard_map/all_gather | solution.py:18
  8.6 6.7 %copy-start.4 = (f32[64,1]{0,1:T(1,128)S(1)}, f32[64,1]{0,1:T(1,128)}, u32[]{:S(2)}) copy-start(f32[64,1]{0,1:T(1,128)} %param.10) | copy-start | bytes 772
  11.1 78.1 %all-gather.4.cloned.1.call-start = ((), (), s32[]{:S(2)}) async-start(), calls=%async_computation.2 | async-start | bytes 5160960 | tf_op jit(solution)/shard_map/all_gather | solution.py:18
  11.2 29.5 %collective-permute-start = (bf16[40,7168]{1,0:T(8,128)(2,1)S(1)}, bf16[40,7168]{1,0:T(8,128)(2,1)S(1)}, u32[]{:S(2)}, u32[]{:S(2)}) collective-permute-start(bf16[40,7168]{1,0:T(8,128)(2,1)S(1)} %get-tuple-element.19), channel_id=1, source_target_pairs={{0,8},{8,0},{1,9},{9,1},{2,10},{10,2},{3,11},{11,3},{4,12},{12,4},... | collective-permute-start | bytes 1720328 | tf_op jit(solution)/shard_map/ppermute | solution.py:74
  15.6 25.1 %collective-permute-start.1 = (f32[40]{0:T(128)S(1)}, f32[40]{0:T(128)S(1)}, u32[]{:S(2)}, u32[]{:S(2)}) collective-permute-start(f32[40]{0:T(128)S(1)} %get-tuple-element.22), channel_id=1, source_target_pairs={{0,8},{8,0},{1,9},{9,1},{2,10},{10,2},{3,11},{11,3},{4,12},{12,4},... | collective-permute-start | bytes 488 | tf_op jit(solution)/shard_map/ppermute | solution.py:75
  40.7 15.0 %copy-start.3 = (bf16[40,7168]{1,0:T(8,128)(2,1)}, bf16[40,7168]{1,0:T(8,128)(2,1)S(1)}, u32[]{:S(2)}) copy-start(bf16[40,7168]{1,0:T(8,128)(2,1)S(1)} %collective-permute-done) | copy-start | bytes 1720324
  55.8 7.2 %copy-start.1 = (bf16[1,256,7168]{2,1,0:T(8,128)(2,1)S(1)}, bf16[1,256,7168]{2,1,0:T(8,128)(2,1)}, u32[]{:S(2)}) copy-start(bf16[1,256,7168]{2,1,0:T(8,128)(2,1)} %param.13) | copy-start | bytes 11010052
  64.3 2.1 %copy-start = (bf16[320,7168]{1,0:T(8,128)(2,1)}, bf16[320,7168]{1,0:T(8,128)(2,1)S(1)}, u32[]{:S(2)}) copy-start(bf16[320,7168]{1,0:T(8,128)(2,1)S(1)} %convolution_convert_fusion.1) | copy-start | bytes 13762564
  66.6 4.8 %collective-permute-start.2 = (bf16[160,7168]{1,0:T(8,128)(2,1)S(1)}, bf16[160,7168]{1,0:T(8,128)(2,1)}, u32[]{:S(2)}, u32[]{:S(2)}) collective-permute-start(bf16[160,7168]{1,0:T(8,128)(2,1)S(1)} %dynamic-slice_bitcast_fusion.1), channel_id=1, source_target_pairs={{0,1},{1,0},{2,3},{3,2},{4,5},{5,4},{6,7},{7,6},{8,9},{9,8},{10,11... | collective-permute-start | bytes 6881288 | tf_op jit(solution)/shard_map/ppermute | solution.py:30
  89.2 7.1 %copy-start.2 = (bf16[1,256,7168]{2,1,0:T(8,128)(2,1)S(1)}, bf16[1,256,7168]{2,1,0:T(8,128)(2,1)}, u32[]{:S(2)}) copy-start(bf16[1,256,7168]{2,1,0:T(8,128)(2,1)} %param.13) | copy-start | bytes 11010052
  97.9 4.5 %collective-permute-start.3 = (bf16[160,7168]{1,0:T(8,128)(2,1)S(1)}, bf16[160,7168]{1,0:T(8,128)(2,1)S(1)}, u32[]{:S(2)}, u32[]{:S(2)}) collective-permute-start(bf16[160,7168]{1,0:T(8,128)(2,1)S(1)} %dynamic-slice_bitcast_fusion), channel_id=1, source_target_pairs={{0,1},{1,0},{2,3},{3,2},{4,5},{5,4},{6,7},{7,6},{8,9},{9,8},{10,11... | collective-permute-start | bytes 6881288 | tf_op jit(solution)/shard_map/ppermute | solution.py:30
  134.4 42.4 %all-to-all-start.1 = ((bf16[4,40,7168]{2,1,0:T(8,128)(2,1)}), bf16[4,40,7168]{2,1,0:T(8,128)(2,1)S(1)}, u32[]{:S(2)}, u32[]{:S(2)}) async-start(bf16[4,40,7168]{2,1,0:T(8,128)(2,1)} %bitcast.12), calls=%async_computation.1 | async-start | bytes 4587520 | tf_op jit(solution)/shard_map/all_to_all | solution.py:36
  138.1 39.3 %collective-permute-start.4 = (bf16[40,7168]{1,0:T(8,128)(2,1)S(1)}, bf16[40,7168]{1,0:T(8,128)(2,1)S(1)}, u32[]{:S(2)}, u32[]{:S(2)}) collective-permute-start(bf16[40,7168]{1,0:T(8,128)(2,1)S(1)} %multiply_convert_fusion.1), channel_id=1, source_target_pairs={{0,8},{8,0},{1,9},{9,1},{2,10},{10,2},{3,11},{11,3},{4,12},{12,4},... | collective-permute-start | bytes 1720328 | tf_op jit(solution)/shard_map/ppermute | solution.py:87
Sparse Core Ops, SparseCore 0:
  11.3 44.4 all-gather.5
  57.3 31.8 all-gather.3

commit v14 on v13

--- a/solution.py
+++ b/solution.py
@@ -73,16 +73,22 @@
 
     away = [lax.ppermute(packed[k], "eg", shift(k)) for k in range(1, experts)]
     away_w = [lax.ppermute(packed_w[k], "eg", shift(k)) for k in range(1, experts)]
-    own_rows = gather(packed[0])
+    early = slots * 3 // 5
+    own_rows = gather(packed[0][:early])
     own_rows, away, away_w = lax.optimization_barrier((own_rows, away, away_w))
     own_parts = expert_parts(own_rows, *weights)
-    away_rows = gather(jnp.concatenate(away, axis=0))
+    late_rows = jnp.concatenate(away + [packed[0][early:]], axis=0)
+    late_w = jnp.concatenate(away_w + [packed_w[0][early:]], axis=0)
+    away_rows = gather(late_rows)
     own_parts, away_rows = lax.optimization_barrier((own_parts, away_rows))
     away_parts = expert_parts(away_rows, *weights)
     away_back = chip_sums(away_parts)
-    done = finish(away_back, jnp.concatenate(away_w, axis=0))
+    late = finish(away_back, late_w)
+    done = late[:(experts - 1) * slots]
     own_parts, done = lax.optimization_barrier((own_parts, done))
-    own = finish(chip_sums(own_parts), packed_w[0])
+    own = jnp.concatenate(
+        [finish(chip_sums(own_parts), packed_w[0][:early]), late[(experts - 1) * slots:]], axis=0
+    )
     home = [own] + [
         lax.ppermute(done[(k - 1) * slots:k * slots], "eg", shift(experts - k))
         for k in range(1, experts)

time: 186 us -> 192 us (1.032)
  waiting for transfers between devices: 98.3 us -> 132 us
  blocking collectives: 30.8 us -> 0 us
  starting transfers between devices: 11 us -> 14.5 us
    all_to_all x1 -> x0, blocking collectives: 30.8 us -> none  [chip_sums(): return lax.all_to_all(paired, 'sc', split_axis=0, concat_axis=0, tiled=True)]
    all_to_all x1 -> x2, waiting for transfers between devices: 36.3 us -> 64.3 us  [chip_sums(): return lax.all_to_all(paired, 'sc', split_axis=0, concat_axis=0, tiled=True)]
    ppermute x1, waiting for transfers between devices: 0.01 us -> 26.3 us  [shards(): away = [lax.ppermute(packed[k], 'eg', shift(k)) for k in range(1, experts)]]
    ppermute x1, waiting for transfers between devices: 25 us -> 1.38 us  [shards(): lax.ppermute(packed_w[k], 'eg', shift(k))]
    ppermute x1, starting transfers between devices: 4.11 us -> 0.08 us  [shards(): away = [lax.ppermute(packed[k], 'eg', shift(k)) for k in range(1, experts)]]
    ppermute x1, starting transfers between devices: 0.09 us -> 4.09 us  [shards(): lax.ppermute(packed_w[k], 'eg', shift(k))]
    all_to_all x1 -> x2, starting transfers between devices: 3.64 us -> 7.26 us  [chip_sums(): return lax.all_to_all(paired, 'sc', split_axis=0, concat_axis=0, tiled=True)]
    all_gather x2, waiting for transfers between devices: 28.3 us -> 30.9 us  [gather(): return lax.all_gather(held, ('core', 'sc'), axis=0, tiled=True)]
  transfers between devices with their start and end apart: 8 -> 9, of which waited for: 6 -> 8; matrix products, arithmetic and copies ran while one was open for 8% -> 6% of each run, Pallas kernels for 0% -> 0%
where the time goes in v14:
time: 192 us
  waiting for transfers between devices  132 us (69%)
  matrix products  20.9 us (11%)
  starting transfers between devices  14.5 us (8%)
  between operations  13.6 us (7%)
  other arithmetic  8.81 us (5%)
  local copies, waits for them, and re-layouts  2.57 us (1%)
    all_to_all x2, waiting for transfers between devices, chip_sums(): return lax.all_to_all(paired, 'sc', split_axis=0, concat_axis=0, tiled=True)  64.3 us
    all_gather x2, waiting for transfers between devices, gather(): return lax.all_gather(held, ('core', 'sc'), axis=0, tiled=True)  30.9 us
    ppermute x1, waiting for transfers between devices, shards(): away = [lax.ppermute(packed[k], 'eg', shift(k)) for k in range(1, experts)]  26.3 us
    dot_general x2, matrix products, slice_ffn(): both = jnp.dot(rows, gate_up_w, preferred_element_type=jnp.float32)  14.2 us
    ppermute x2, waiting for transfers between devices, expert_parts(): sibling = lax.ppermute(halves[(core + 1) % cores], 'core', swap)  8.73 us
    all_to_all x2, starting transfers between devices, chip_sums(): return lax.all_to_all(paired, 'sc', split_axis=0, concat_axis=0, tiled=True)  7.26 us
    convert_element_type x2, other arithmetic, expert_parts(): (halves[core].astype(jnp.float32) + sibling.astype(jnp.float32)).astype(j...  5.67 us
    ppermute x1, starting transfers between devices, shards(): lax.ppermute(packed_w[k], 'eg', shift(k))  4.09 us
  transfers between devices with their start and end apart: 9, of which 8 were waited for; matrix products, arithmetic and copies ran while one was open for 6% of the time, Pallas kernels for 0%

profile of v14, /device:TPU:0, one launch (start us, length us, event | category | flops | bytes accessed | tf_op | source)
XLA Modules:
  0.0 192.1 jit_solution(6728647770382433950)
XLA Ops:
  6.5 0.7 fusion.31
  7.2 0.1 fusion.20
  7.3 0.1 copy.9
  7.4 0.1 reduce_window_sum.11
  7.5 0.1 fusion.28
  7.5 0.1 copy.8
  7.6 2.1 %multiply_reduce_fusion = (f32[64]{0:T(128)S(1)}, f32[64,7168]{1,0:T(8,128)S(1)}) fusion(bf16[64,7168]{1,0:T(8,128)(2,1)} %param.7, s32[64]{0:T(128)} %param.8), kind=kOutput, calls=%fused_computation.19 | convolution fusion | flops 60559296 | bytes 2753024 | tf_op jit(solution)/shard_map/dot_general | solution.py:52
  9.7 0.5 convolution_convert_fusion.2
  10.2 0.8 slice.53
  11.0 0.0 all-gather.6.cloned.1.call-update
  11.0 0.0 all-gather.4.cloned.1.call-start
  11.1 0.1 fusion.19
  11.2 0.1 copy.10
  11.2 0.1 select_reduce_fusion
  11.3 4.1 %collective-permute-start.1 = (f32[40]{0:T(128)S(1)}, f32[40]{0:T(128)S(1)}, u32[]{:S(2)}, u32[]{:S(2)}) collective-permute-start(f32[40]{0:T(128)S(1)} %slice_bitcast_fusion.4), channel_id=1, source_target_pairs={{0,8},{8,0},{1,9},{9,1},{2,10},{10,2},{3,11},{11,3},{4,12},{12,4},... | collective-permute-start | bytes 488 | tf_op jit(solution)/shard_map/ppermute | solution.py:75
  15.5 0.1 collective-permute-start
  15.6 1.4 collective-permute-done.1
  16.9 26.3 %collective-permute-done = bf16[40,7168]{1,0:T(8,128)(2,1)S(1)} collective-permute-done((bf16[40,7168]{1,0:T(8,128)(2,1)S(1)}, bf16[40,7168]{1,0:T(8,128)(2,1)S(1)}, u32[]{:S(2)}, u32[]{:S(2)}) %collective-permute-start) | collective-permute-done | bytes 573472 | tf_op jit(solution)/shard_map/ppermute | solution.py:74
  43.2 4.8 %all-gather.6.cloned.1.call-done = bf16[1,192,7168]{2,1,0:T(8,128)(2,1)} async-done(((bf16[1,24,7168]{2,1,0:T(8,128)(2,1)}), bf16[1,192,7168]{2,1,0:T(8,128)(2,1)}) %all-gather.6.cloned.1.call-update) | async-done | bytes 2752528 | tf_op jit(solution)/shard_map/all_gather | solution.py:18
  48.0 0.9 pad_maximum_fusion.3
  48.9 0.0 all-gather.4.cloned.1.call-update
  49.0 0.0 copy-start
  49.0 5.7 %fusion.3 = f32[192,512]{1,0:T(8,128)S(1)} fusion(bf16[192,7168]{1,0:T(8,128)(2,1)} %bitcast.60, bf16[7168,256]{1,0:T(8,128)(2,1)} %bitcast.56, bf16[7168,256]{1,0:T(8,128)(2,1)} %bitcast.58), kind=kOutput, calls=%fused_computation.11 | convolution fusion | flops 1423966208 | bytes 10485760 | tf_op jit(solution)/shard_map/dot_general | solution.py:11
  54.6 0.9 convolution_convert_fusion.1
  55.5 1.2 dynamic-slice_bitcast_fusion.1
  56.7 0.3 collective-permute-start.2
  57.0 3.2 %collective-permute-done.2 = bf16[96,7168]{1,0:T(8,128)(2,1)} collective-permute-done((bf16[96,7168]{1,0:T(8,128)(2,1)}, bf16[96,7168]{1,0:T(8,128)(2,1)}, u32[]{:S(2)}, u32[]{:S(2)}) %collective-permute-start.2) | collective-permute-done | bytes 1376288 | tf_op jit(solution)/shard_map/ppermute | solution.py:30
  60.2 2.8 %fusion.6 = bf16[96,7168]{1,0:T(8,128)(2,1)} fusion(bf16[96,7168]{1,0:T(8,128)(2,1)} %collective-permute-done.2, bf16[2,96,7168]{2,1,0:T(8,128)(2,1)S(1)} %bitcast.51, s32[]{:T(128)S(6)} %select_n.43), kind=kLoop, calls=%fused_computation.16 | loop fusion | flops 2752512 | bytes 4128772 | tf_op jit(solution)/shard_map/convert_element_type | solution.py:31
  63.0 26.2 %all-gather.4.cloned.1.call-done = bf16[448,7168]{1,0:T(8,128)(2,1)} async-done(((bf16[56,7168]{1,0:T(8,128)(2,1)}), bf16[448,7168]{1,0:T(8,128)(2,1)}) %all-gather.4.cloned.1.call-update) | async-done | bytes 6422544 | tf_op jit(solution)/shard_map/all_gather | solution.py:18
  89.2 8.5 %fusion.2 = f32[448,512]{1,0:T(8,128)S(1)} fusion(bf16[448,7168]{1,0:T(8,128)(2,1)} %all-gather.4.cloned.1.call-done, bf16[7168,256]{1,0:T(8,128)(2,1)} %bitcast.57, bf16[7168,256]{1,0:T(8,128)(2,1)} %bitcast.59), kind=kOutput, calls=%fused_computation.10 | convolution fusion | flops 3303014400 | bytes 14680064 | tf_op jit(solution)/shard_map/dot_general | solution.py:11
  97.8 1.9 convolution_convert_fusion
  99.6 0.2 dynamic-slice_bitcast_fusion
  99.9 0.3 collective-permute-start.3
  100.2 5.5 %collective-permute-done.3 = bf16[224,7168]{1,0:T(8,128)(2,1)S(1)} collective-permute-done((bf16[224,7168]{1,0:T(8,128)(2,1)S(1)}, bf16[224,7168]{1,0:T(8,128)(2,1)S(1)}, u32[]{:S(2)}, u32[]{:S(2)}) %collective-permute-start.3) | collective-permute-done | bytes 3211296 | tf_op jit(solution)/shard_map/ppermute | solution.py:30
  105.7 2.8 %fusion.1 = bf16[224,7168]{1,0:T(8,128)(2,1)} fusion(bf16[224,7168]{1,0:T(8,128)(2,1)S(1)} %collective-permute-done.3, bf16[2,224,7168]{2,1,0:T(8,128)(2,1)S(1)} %bitcast.49, s32[]{:T(128)S(6)} %select_n.43), kind=kLoop, calls=%fused_computation.8 | loop fusion | flops 6422528 | bytes 9633796 | tf_op jit(solution)/shard_map/convert_element_type | solution.py:31
  108.5 3.7 %all-to-all-start = ((bf16[4,56,7168]{2,1,0:T(8,128)(2,1)}), bf16[4,56,7168]{2,1,0:T(8,128)(2,1)S(1)}, u32[]{:S(2)}, u32[]{:S(2)}) async-start(bf16[4,56,7168]{2,1,0:T(8,128)(2,1)} %bitcast.52), calls=%async_computation | async-start | bytes 6422528 | tf_op jit(solution)/shard_map/all_to_all | solution.py:36
  112.2 0.1 slice_bitcast_fusion.3
  112.3 0.1 pad_maximum_fusion.4
  112.4 37.3 %all-to-all-done = bf16[4,56,7168]{2,1,0:T(8,128)(2,1)S(1)} async-done(((bf16[4,56,7168]{2,1,0:T(8,128)(2,1)}), bf16[4,56,7168]{2,1,0:T(8,128)(2,1)S(1)}, u32[]{:S(2)}, u32[]{:S(2)}) %all-to-all-start) | async-done | bytes 3211296 | tf_op jit(solution)/shard_map/all_to_all | solution.py:36
  149.7 0.5 convert_reduce_fusion
  150.2 0.2 multiply_convert_fusion.1
  150.4 3.6 %all-to-all-start.1 = ((bf16[4,24,7168]{2,1,0:T(8,128)(2,1)}), bf16[4,24,7168]{2,1,0:T(8,128)(2,1)S(1)}, u32[]{:S(2)}, u32[]{:S(2)}) async-start(bf16[4,24,7168]{2,1,0:T(8,128)(2,1)} %bitcast.53), calls=%async_computation.1 | async-start | bytes 2752512 | tf_op jit(solution)/shard_map/all_to_all | solution.py:36
  154.0 2.5 %collective-permute-start.4 = (bf16[40,7168]{1,0:T(8,128)(2,1)S(1)}, bf16[40,7168]{1,0:T(8,128)(2,1)S(1)}, u32[]{:S(2)}, u32[]{:S(2)}) collective-permute-start(bf16[40,7168]{1,0:T(8,128)(2,1)S(1)} %slice.56), channel_id=1, source_target_pairs={{0,8},{8,0},{1,9},{9,1},{2,10},{10,2},{3,11},{11,3},{4,12},{12,4},... | collective-permute-start | bytes 1720328 | tf_op jit(solution)/shard_map/ppermute | solution.py:93
  156.5 27.0 %all-to-all-done.1 = bf16[4,24,7168]{2,1,0:T(8,128)(2,1)S(1)} async-done(((bf16[4,24,7168]{2,1,0:T(8,128)(2,1)}), bf16[4,24,7168]{2,1,0:T(8,128)(2,1)S(1)}, u32[]{:S(2)}, u32[]{:S(2)}) %all-to-all-start.1) | async-done | bytes 1376288 | tf_op jit(solution)/shard_map/all_to_all | solution.py:36
  183.5 0.2 convert_reduce_fusion.1
  183.7 0.1 multiply_convert_fusion.2
  183.9 0.0 collective-permute-done.4
  183.9 1.4 fusion
  (14 shorter events, 0.2 us)
Async XLA Ops:
  6.5 41.4 %all-gather.6.cloned.1.call-start = ((), (), s32[]{:S(2)}) async-start(), calls=%async_computation.3 | async-start | bytes 3096576 | tf_op jit(solution)/shard_map/all_gather | solution.py:18
  7.6 3.5 %copy-start.2 = (f32[64,1]{0,1:T(1,128)S(1)}, f32[64,1]{0,1:T(1,128)}, u32[]{:S(2)}) copy-start(f32[64,1]{0,1:T(1,128)} %param.10) | copy-start | bytes 772
  11.0 78.2 %all-gather.4.cloned.1.call-start = ((), (), s32[]{:S(2)}) async-start(), calls=%async_computation.2 | async-start | bytes 7225344 | tf_op jit(solution)/shard_map/all_gather | solution.py:18
  11.3 5.6 %collective-permute-start.1 = (f32[40]{0:T(128)S(1)}, f32[40]{0:T(128)S(1)}, u32[]{:S(2)}, u32[]{:S(2)}) collective-permute-start(f32[40]{0:T(128)S(1)} %slice_bitcast_fusion.4), channel_id=1, source_target_pairs={{0,8},{8,0},{1,9},{9,1},{2,10},{10,2},{3,11},{11,3},{4,12},{12,4},... | collective-permute-start | bytes 488 | tf_op jit(solution)/shard_map/ppermute | solution.py:75
  15.5 27.7 %collective-permute-start = (bf16[40,7168]{1,0:T(8,128)(2,1)S(1)}, bf16[40,7168]{1,0:T(8,128)(2,1)S(1)}, u32[]{:S(2)}, u32[]{:S(2)}) collective-permute-start(bf16[40,7168]{1,0:T(8,128)(2,1)S(1)} %slice_bitcast_fusion), channel_id=1, source_target_pairs={{0,8},{8,0},{1,9},{9,1},{2,10},{10,2},{3,11},{11,3},{4,12},{12,4},... | collective-permute-start | bytes 1720328 | tf_op jit(solution)/shard_map/ppermute | solution.py:74
  49.0 5.7 %copy-start = (bf16[1,256,7168]{2,1,0:T(8,128)(2,1)S(1)}, bf16[1,256,7168]{2,1,0:T(8,128)(2,1)}, u32[]{:S(2)}) copy-start(bf16[1,256,7168]{2,1,0:T(8,128)(2,1)} %param.13) | copy-start | bytes 11010052
  56.7 3.5 %collective-permute-start.2 = (bf16[96,7168]{1,0:T(8,128)(2,1)}, bf16[96,7168]{1,0:T(8,128)(2,1)}, u32[]{:S(2)}, u32[]{:S(2)}) collective-permute-start(bf16[96,7168]{1,0:T(8,128)(2,1)} %dynamic-slice_bitcast_fusion.1), channel_id=1, source_target_pairs={{0,1},{1,0},{2,3},{3,2},{4,5},{5,4},{6,7},{7,6},{8,9},{9,8},{10,11... | collective-permute-start | bytes 4128776 | tf_op jit(solution)/shard_map/ppermute | solution.py:30
  89.2 8.6 %copy-start.1 = (bf16[1,256,7168]{2,1,0:T(8,128)(2,1)S(1)}, bf16[1,256,7168]{2,1,0:T(8,128)(2,1)}, u32[]{:S(2)}) copy-start(bf16[1,256,7168]{2,1,0:T(8,128)(2,1)} %param.13) | copy-start | bytes 11010052
  99.9 5.8 %collective-permute-start.3 = (bf16[224,7168]{1,0:T(8,128)(2,1)S(1)}, bf16[224,7168]{1,0:T(8,128)(2,1)S(1)}, u32[]{:S(2)}, u32[]{:S(2)}) collective-permute-start(bf16[224,7168]{1,0:T(8,128)(2,1)S(1)} %dynamic-slice_bitcast_fusion), channel_id=1, source_target_pairs={{0,1},{1,0},{2,3},{3,2},{4,5},{5,4},{6,7},{7,6},{8,9},{9,8},{10,11... | collective-permute-start | bytes 9633800 | tf_op jit(solution)/shard_map/ppermute | solution.py:30
  108.5 41.2 %all-to-all-start = ((bf16[4,56,7168]{2,1,0:T(8,128)(2,1)}), bf16[4,56,7168]{2,1,0:T(8,128)(2,1)S(1)}, u32[]{:S(2)}, u32[]{:S(2)}) async-start(bf16[4,56,7168]{2,1,0:T(8,128)(2,1)} %bitcast.52), calls=%async_computation | async-start | bytes 6422528 | tf_op jit(solution)/shard_map/all_to_all | solution.py:36
  150.4 33.1 %all-to-all-start.1 = ((bf16[4,24,7168]{2,1,0:T(8,128)(2,1)}), bf16[4,24,7168]{2,1,0:T(8,128)(2,1)S(1)}, u32[]{:S(2)}, u32[]{:S(2)}) async-start(bf16[4,24,7168]{2,1,0:T(8,128)(2,1)} %bitcast.53), calls=%async_computation.1 | async-start | bytes 2752512 | tf_op jit(solution)/shard_map/all_to_all | solution.py:36
  154.0 29.9 %collective-permute-start.4 = (bf16[40,7168]{1,0:T(8,128)(2,1)S(1)}, bf16[40,7168]{1,0:T(8,128)(2,1)S(1)}, u32[]{:S(2)}, u32[]{:S(2)}) collective-permute-start(bf16[40,7168]{1,0:T(8,128)(2,1)S(1)} %slice.56), channel_id=1, source_target_pairs={{0,8},{8,0},{1,9},{9,1},{2,10},{10,2},{3,11},{11,3},{4,12},{12,4},... | collective-permute-start | bytes 1720328 | tf_op jit(solution)/shard_map/ppermute | solution.py:93
Sparse Core Ops, SparseCore 0:
  11.1 36.7 all-gather.5
  49.6 39.5 all-gather.3

commit v15 on v13

--- a/solution.py
+++ b/solution.py
@@ -71,7 +71,14 @@
     def shift(k):
         return [(g, (g + k) % experts) for g in range(experts)]
 
-    away = [lax.ppermute(packed[k], "eg", shift(k)) for k in range(1, experts)]
+    half = slots // 2
+
+    def cross(rows, k):
+        return jnp.concatenate(
+            [lax.ppermute(rows[:half], "eg", shift(k)), lax.ppermute(rows[half:], "eg", shift(k))]
+        )
+
+    away = [cross(packed[k], k) for k in range(1, experts)]
     away_w = [lax.ppermute(packed_w[k], "eg", shift(k)) for k in range(1, experts)]
     own_rows = gather(packed[0])
     own_rows, away, away_w = lax.optimization_barrier((own_rows, away, away_w))
@@ -84,7 +91,7 @@
     own_parts, done = lax.optimization_barrier((own_parts, done))
     own = finish(chip_sums(own_parts), packed_w[0])
     home = [own] + [
-        lax.ppermute(done[(k - 1) * slots:k * slots], "eg", shift(experts - k))
+        cross(done[(k - 1) * slots:k * slots], experts - k)
         for k in range(1, experts)
     ]
     result = jnp.einsum(

time: 186 us -> 191 us (1.027)
  starting transfers between devices: 11 us -> 14.4 us
    ppermute x2 -> x4, waiting for transfers between devices: 0.01 us -> 63 us  [the longest x2 50.7 us: cross(): lax.ppermute(rows[half:], 'eg', shift(k))]
    all_to_all x1, waiting for transfers between devices: 36.3 us -> 2.02 us  [chip_sums(): return lax.all_to_all(paired, 'sc', split_axis=0, concat_axis=0, tiled=True)]
    ppermute x1, waiting for transfers between devices: 25 us -> 0.01 us  [shards(): lax.ppermute(packed_w[k], 'eg', shift(k))]
    all_gather x2, waiting for transfers between devices: 28.3 us -> 24.9 us  [gather(): return lax.all_gather(held, ('core', 'sc'), axis=0, tiled=True)]
    ppermute x1, starting transfers between devices: 0.09 us -> 2.9 us  [shards(): lax.ppermute(packed_w[k], 'eg', shift(k))]
    ppermute x2 -> x4, starting transfers between devices: 6.57 us -> 7.18 us  [the longest x2 6.58 us: cross(): lax.ppermute(rows[half:], 'eg', shift(k))]
  transfers between devices with their start and end apart: 8 -> 10, of which waited for: 6 -> 9; matrix products, arithmetic and copies ran while one was open for 8% -> 8% of each run, Pallas kernels for 0% -> 0%
where the time goes in v15:
time: 191 us; the launch traced here: 190 us
  waiting for transfers between devices  98.6 us (52%)
  blocking collectives  30.8 us (16%)
  matrix products  21 us (11%)
  starting transfers between devices  14.4 us (8%)
  between operations  13.6 us (7%)
  other arithmetic  8.35 us (4%)
  local copies, waits for them, and re-layouts  3.68 us (2%)
    ppermute x2, waiting for transfers between devices, cross(): lax.ppermute(rows[half:], 'eg', shift(k))  50.7 us
    all_to_all x1, blocking collectives, chip_sums(): return lax.all_to_all(paired, 'sc', split_axis=0, concat_axis=0, tiled=True)  30.8 us
    all_gather x2, waiting for transfers between devices, gather(): return lax.all_gather(held, ('core', 'sc'), axis=0, tiled=True)  24.9 us
    dot_general x2, matrix products, slice_ffn(): both = jnp.dot(rows, gate_up_w, preferred_element_type=jnp.float32)  14.3 us
    ppermute x2, waiting for transfers between devices, cross(): lax.ppermute(rows[:half], 'eg', shift(k))  12.3 us
    ppermute x2, waiting for transfers between devices, expert_parts(): sibling = lax.ppermute(halves[(core + 1) % cores], 'core', swap)  8.68 us
    ppermute x2, starting transfers between devices, cross(): lax.ppermute(rows[half:], 'eg', shift(k))  6.58 us
    convert_element_type x2, other arithmetic, expert_parts(): (halves[core].astype(jnp.float32) + sibling.astype(jnp.float32)).astype(j...  5.21 us
  transfers between devices with their start and end apart: 10, of which 9 were waited for; matrix products, arithmetic and copies ran while one was open for 8% of the time, Pallas kernels for 0%

profile of v15, /device:TPU:0, one launch (start us, length us, event | category | flops | bytes accessed | tf_op | source)
XLA Modules:
  0.0 190.4 jit_solution(16581536922657297526)
XLA Ops:
  6.5 2.0 %multiply_reduce_fusion = (f32[64]{0:T(128)S(1)}, f32[64,7168]{1,0:T(8,128)S(1)}) fusion(bf16[64,7168]{1,0:T(8,128)(2,1)} %param.7, s32[64]{0:T(128)} %param.8), kind=kOutput, calls=%fused_computation.20 | convolution fusion | flops 60559296 | bytes 2753024 | tf_op jit(solution)/shard_map/dot_general | solution.py:52
  8.6 0.7 fusion.32
  9.3 0.1 fusion.21
  9.4 0.1 copy.9
  9.4 0.1 reduce_window_sum.11
  9.5 0.1 fusion.29
  9.6 0.1 copy.8
  9.7 0.5 convolution_convert_fusion.2
  10.2 0.8 slice.42
  11.1 0.1 slice_bitcast_fusion.1
  11.2 4.1 %collective-permute-start.1 = (bf16[20,7168]{1,0:T(8,128)(2,1)S(1)}, bf16[20,7168]{1,0:T(8,128)(2,1)S(1)}, u32[]{:S(2)}, u32[]{:S(2)}) collective-permute-start(bf16[20,7168]{1,0:T(8,128)(2,1)S(1)} %get-tuple-element.20), channel_id=1, source_target_pairs={{0,8},{8,0},{1,9},{9,1},{2,10},{10,2},{3,11},{11,3},{4,12},{12,4},... | collective-permute-start | bytes 860168 | tf_op jit(solution)/shard_map/ppermute | solution.py:78
  15.3 0.1 collective-permute-start
  15.4 0.1 fusion.20
  15.5 0.1 copy.10
  15.6 0.1 select_reduce_fusion
  15.7 2.9 %collective-permute-start.2 = (f32[40]{0:T(128)S(1)}, f32[40]{0:T(128)S(1)}, u32[]{:S(2)}, u32[]{:S(2)}) collective-permute-start(f32[40]{0:T(128)S(1)} %get-tuple-element.24), channel_id=1, source_target_pairs={{0,8},{8,0},{1,9},{9,1},{2,10},{10,2},{3,11},{11,3},{4,12},{12,4},... | collective-permute-start | bytes 488 | tf_op jit(solution)/shard_map/ppermute | solution.py:82
  18.6 20.4 %collective-permute-done.1 = bf16[20,7168]{1,0:T(8,128)(2,1)S(1)} collective-permute-done((bf16[20,7168]{1,0:T(8,128)(2,1)S(1)}, bf16[20,7168]{1,0:T(8,128)(2,1)S(1)}, u32[]{:S(2)}, u32[]{:S(2)}) %collective-permute-start.1) | collective-permute-done | bytes 286752 | tf_op jit(solution)/shard_map/ppermute | solution.py:78
  39.0 6.5 %collective-permute-done = bf16[20,7168]{1,0:T(8,128)(2,1)S(1)} collective-permute-done((bf16[20,7168]{1,0:T(8,128)(2,1)S(1)}, bf16[20,7168]{1,0:T(8,128)(2,1)S(1)}, u32[]{:S(2)}, u32[]{:S(2)}) %collective-permute-start) | collective-permute-done | bytes 286752 | tf_op jit(solution)/shard_map/ppermute | solution.py:78
  45.6 0.9 pad_maximum_fusion.3
  46.5 11.6 %all-gather.6.cloned.1.call-done = bf16[1,320,7168]{2,1,0:T(8,128)(2,1)} async-done(((bf16[1,40,7168]{2,1,0:T(8,128)(2,1)}), bf16[1,320,7168]{2,1,0:T(8,128)(2,1)}) %all-gather.6.cloned.1.call-update) | async-done | bytes 4587536 | tf_op jit(solution)/shard_map/all_gather | solution.py:18
  58.2 7.1 %fusion.2 = f32[320,512]{1,0:T(8,128)S(1)} fusion(bf16[320,7168]{1,0:T(8,128)(2,1)} %bitcast.55, bf16[7168,256]{1,0:T(8,128)(2,1)} %bitcast.56, bf16[7168,256]{1,0:T(8,128)(2,1)} %bitcast.58), kind=kOutput, calls=%fused_computation.8 | convolution fusion | flops 2363490304 | bytes 12582912 | tf_op jit(solution)/shard_map/dot_general | solution.py:11
  65.3 1.4 convolution_convert_fusion.1
  66.7 2.1 %copy-done = bf16[320,7168]{1,0:T(8,128)(2,1)} copy-done((bf16[320,7168]{1,0:T(8,128)(2,1)}, bf16[320,7168]{1,0:T(8,128)(2,1)S(1)}, u32[]{:S(2)}) %copy-start) | copy-done | bytes 4587544
  68.8 0.1 dynamic-slice_bitcast_fusion.1
  69.0 0.3 collective-permute-start.3
  69.3 4.5 %collective-permute-done.3 = bf16[160,7168]{1,0:T(8,128)(2,1)} collective-permute-done((bf16[160,7168]{1,0:T(8,128)(2,1)S(1)}, bf16[160,7168]{1,0:T(8,128)(2,1)}, u32[]{:S(2)}, u32[]{:S(2)}) %collective-permute-start.3) | collective-permute-done | bytes 2293792 | tf_op jit(solution)/shard_map/ppermute | solution.py:30
  73.8 4.5 %fusion.4 = bf16[160,7168]{1,0:T(8,128)(2,1)} fusion(bf16[160,7168]{1,0:T(8,128)(2,1)} %collective-permute-done.3, bf16[2,160,7168]{2,1,0:T(8,128)(2,1)} %bitcast.50, s32[]{:T(128)S(6)} %select_n.43), kind=kLoop, calls=%fused_computation.12 | loop fusion | flops 4587520 | bytes 6881284 | tf_op jit(solution)/shard_map/convert_element_type | solution.py:31
  78.3 13.3 %all-gather.4.cloned.1.call-done = bf16[320,7168]{1,0:T(8,128)(2,1)} async-done(((bf16[40,7168]{1,0:T(8,128)(2,1)}), bf16[320,7168]{1,0:T(8,128)(2,1)}) %all-gather.4.cloned.1.call-update) | async-done | bytes 4587536 | tf_op jit(solution)/shard_map/all_gather | solution.py:18
  91.6 7.1 %fusion.1 = f32[320,512]{1,0:T(8,128)S(1)} fusion(bf16[320,7168]{1,0:T(8,128)(2,1)} %all-gather.4.cloned.1.call-done, bf16[7168,256]{1,0:T(8,128)(2,1)} %bitcast.57, bf16[7168,256]{1,0:T(8,128)(2,1)} %bitcast.59), kind=kOutput, calls=%fused_computation.7 | convolution fusion | flops 2363490304 | bytes 12582912 | tf_op jit(solution)/shard_map/dot_general | solution.py:11
  98.7 1.4 convolution_convert_fusion
  100.1 0.2 dynamic-slice_bitcast_fusion
  100.3 0.3 collective-permute-start.4
  100.6 4.2 %collective-permute-done.4 = bf16[160,7168]{1,0:T(8,128)(2,1)S(1)} collective-permute-done((bf16[160,7168]{1,0:T(8,128)(2,1)S(1)}, bf16[160,7168]{1,0:T(8,128)(2,1)S(1)}, u32[]{:S(2)}, u32[]{:S(2)}) %collective-permute-start.4) | collective-permute-done | bytes 2293792 | tf_op jit(solution)/shard_map/ppermute | solution.py:30
  104.8 0.7 fusion.3
  105.5 30.8 %all_to_all.10 = bf16[4,40,7168]{2,1,0:T(8,128)(2,1)S(1)} all-to-all(bf16[4,40,7168]{2,1,0:T(8,128)(2,1)S(1)} %bitcast.53), channel_id=1, replica_groups=mesh['grp'=2,'eg'=2,'sc'=4,'core'=2] {'sc'}, dimensions={0} | all-to-all | bytes 4587520 | tf_op jit(solution)/shard_map/all_to_all | solution.py:36
  136.3 0.4 convert_reduce_fusion.1
  136.7 0.1 multiply_convert_fusion.1
  136.8 3.6 %all-to-all-start.1 = ((bf16[4,40,7168]{2,1,0:T(8,128)(2,1)}), bf16[4,40,7168]{2,1,0:T(8,128)(2,1)S(1)}, u32[]{:S(2)}, u32[]{:S(2)}) async-start(bf16[4,40,7168]{2,1,0:T(8,128)(2,1)} %bitcast.13), calls=%async_computation.1 | async-start | bytes 4587520 | tf_op jit(solution)/shard_map/all_to_all | solution.py:36
  140.5 0.1 fusion.39
  140.5 2.5 %collective-permute-start.6 = (bf16[20,7168]{1,0:T(8,128)(2,1)S(1)}, bf16[20,7168]{1,0:T(8,128)(2,1)S(1)}, u32[]{:S(2)}, u32[]{:S(2)}) collective-permute-start(bf16[20,7168]{1,0:T(8,128)(2,1)S(1)} %get-tuple-element.22), channel_id=1, source_target_pairs={{0,8},{8,0},{1,9},{9,1},{2,10},{10,2},{3,11},{11,3},{4,12},{12,4},... | collective-permute-start | bytes 860168 | tf_op jit(solution)/shard_map/ppermute | solution.py:78
  143.0 0.5 collective-permute-start.5
  143.5 30.3 %collective-permute-done.6 = bf16[20,7168]{1,0:T(8,128)(2,1)S(1)} collective-permute-done((bf16[20,7168]{1,0:T(8,128)(2,1)S(1)}, bf16[20,7168]{1,0:T(8,128)(2,1)S(1)}, u32[]{:S(2)}, u32[]{:S(2)}) %collective-permute-start.6) | collective-permute-done | bytes 286752 | tf_op jit(solution)/shard_map/ppermute | solution.py:78
  173.8 5.7 %collective-permute-done.5 = bf16[20,7168]{1,0:T(8,128)(2,1)S(1)} collective-permute-done((bf16[20,7168]{1,0:T(8,128)(2,1)S(1)}, bf16[20,7168]{1,0:T(8,128)(2,1)S(1)}, u32[]{:S(2)}, u32[]{:S(2)}) %collective-permute-start.5) | collective-permute-done | bytes 286752 | tf_op jit(solution)/shard_map/ppermute | solution.py:78
  179.5 0.1 maximum_bitcast_fusion
  179.6 2.0 %all-to-all-done.1 = bf16[4,40,7168]{2,1,0:T(8,128)(2,1)S(1)} async-done(((bf16[4,40,7168]{2,1,0:T(8,128)(2,1)}), bf16[4,40,7168]{2,1,0:T(8,128)(2,1)S(1)}, u32[]{:S(2)}, u32[]{:S(2)}) %all-to-all-start.1) | async-done | bytes 2293792 | tf_op jit(solution)/shard_map/all_to_all | solution.py:36
  181.7 0.4 convert_reduce_fusion
  182.0 0.1 fusion.10
  182.2 1.4 fusion
  (14 shorter events, 0.1 us)
Async XLA Ops:
  6.5 51.6 %all-gather.6.cloned.1.call-start = ((), (), s32[]{:S(2)}) async-start(), calls=%async_computation.3 | async-start | bytes 5160960 | tf_op jit(solution)/shard_map/all_gather | solution.py:18
  8.6 6.8 %copy-start.3 = (f32[64,1]{0,1:T(1,128)S(1)}, f32[64,1]{0,1:T(1,128)}, u32[]{:S(2)}) copy-start(f32[64,1]{0,1:T(1,128)} %param.10) | copy-start | bytes 772
  11.1 80.5 %all-gather.4.cloned.1.call-start = ((), (), s32[]{:S(2)}) async-start(), calls=%async_computation.2 | async-start | bytes 5160960 | tf_op jit(solution)/shard_map/all_gather | solution.py:18
  11.2 27.8 %collective-permute-start.1 = (bf16[20,7168]{1,0:T(8,128)(2,1)S(1)}, bf16[20,7168]{1,0:T(8,128)(2,1)S(1)}, u32[]{:S(2)}, u32[]{:S(2)}) collective-permute-start(bf16[20,7168]{1,0:T(8,128)(2,1)S(1)} %get-tuple-element.20), channel_id=1, source_target_pairs={{0,8},{8,0},{1,9},{9,1},{2,10},{10,2},{3,11},{11,3},{4,12},{12,4},... | collective-permute-start | bytes 860168 | tf_op jit(solution)/shard_map/ppermute | solution.py:78
  15.3 30.2 %collective-permute-start = (bf16[20,7168]{1,0:T(8,128)(2,1)S(1)}, bf16[20,7168]{1,0:T(8,128)(2,1)S(1)}, u32[]{:S(2)}, u32[]{:S(2)}) collective-permute-start(bf16[20,7168]{1,0:T(8,128)(2,1)S(1)} %get-tuple-element.19), channel_id=1, source_target_pairs={{0,8},{8,0},{1,9},{9,1},{2,10},{10,2},{3,11},{11,3},{4,12},{12,4},... | collective-permute-start | bytes 860168 | tf_op jit(solution)/shard_map/ppermute | solution.py:78
  15.7 30.8 %collective-permute-start.2 = (f32[40]{0:T(128)S(1)}, f32[40]{0:T(128)S(1)}, u32[]{:S(2)}, u32[]{:S(2)}) collective-permute-start(f32[40]{0:T(128)S(1)} %get-tuple-element.24), channel_id=1, source_target_pairs={{0,8},{8,0},{1,9},{9,1},{2,10},{10,2},{3,11},{11,3},{4,12},{12,4},... | collective-permute-start | bytes 488 | tf_op jit(solution)/shard_map/ppermute | solution.py:82
  58.2 7.2 %copy-start.1 = (bf16[1,256,7168]{2,1,0:T(8,128)(2,1)S(1)}, bf16[1,256,7168]{2,1,0:T(8,128)(2,1)}, u32[]{:S(2)}) copy-start(bf16[1,256,7168]{2,1,0:T(8,128)(2,1)} %param.13) | copy-start | bytes 11010052
  66.7 2.1 %copy-start = (bf16[320,7168]{1,0:T(8,128)(2,1)}, bf16[320,7168]{1,0:T(8,128)(2,1)S(1)}, u32[]{:S(2)}) copy-start(bf16[320,7168]{1,0:T(8,128)(2,1)S(1)} %convolution_convert_fusion.1) | copy-start | bytes 13762564
  69.0 4.8 %collective-permute-start.3 = (bf16[160,7168]{1,0:T(8,128)(2,1)S(1)}, bf16[160,7168]{1,0:T(8,128)(2,1)}, u32[]{:S(2)}, u32[]{:S(2)}) collective-permute-start(bf16[160,7168]{1,0:T(8,128)(2,1)S(1)} %dynamic-slice_bitcast_fusion.1), channel_id=1, source_target_pairs={{0,1},{1,0},{2,3},{3,2},{4,5},{5,4},{6,7},{7,6},{8,9},{9,8},{10,11... | collective-permute-start | bytes 6881288 | tf_op jit(solution)/shard_map/ppermute | solution.py:30
  91.6 7.1 %copy-start.2 = (bf16[1,256,7168]{2,1,0:T(8,128)(2,1)S(1)}, bf16[1,256,7168]{2,1,0:T(8,128)(2,1)}, u32[]{:S(2)}) copy-start(bf16[1,256,7168]{2,1,0:T(8,128)(2,1)} %param.13) | copy-start | bytes 11010052
  100.3 4.5 %collective-permute-start.4 = (bf16[160,7168]{1,0:T(8,128)(2,1)S(1)}, bf16[160,7168]{1,0:T(8,128)(2,1)S(1)}, u32[]{:S(2)}, u32[]{:S(2)}) collective-permute-start(bf16[160,7168]{1,0:T(8,128)(2,1)S(1)} %dynamic-slice_bitcast_fusion), channel_id=1, source_target_pairs={{0,1},{1,0},{2,3},{3,2},{4,5},{5,4},{6,7},{7,6},{8,9},{9,8},{10,11... | collective-permute-start | bytes 6881288 | tf_op jit(solution)/shard_map/ppermute | solution.py:30
  136.8 44.9 %all-to-all-start.1 = ((bf16[4,40,7168]{2,1,0:T(8,128)(2,1)}), bf16[4,40,7168]{2,1,0:T(8,128)(2,1)S(1)}, u32[]{:S(2)}, u32[]{:S(2)}) async-start(bf16[4,40,7168]{2,1,0:T(8,128)(2,1)} %bitcast.13), calls=%async_computation.1 | async-start | bytes 4587520 | tf_op jit(solution)/shard_map/all_to_all | solution.py:36
  140.5 33.2 %collective-permute-start.6 = (bf16[20,7168]{1,0:T(8,128)(2,1)S(1)}, bf16[20,7168]{1,0:T(8,128)(2,1)S(1)}, u32[]{:S(2)}, u32[]{:S(2)}) collective-permute-start(bf16[20,7168]{1,0:T(8,128)(2,1)S(1)} %get-tuple-element.22), channel_id=1, source_target_pairs={{0,8},{8,0},{1,9},{9,1},{2,10},{10,2},{3,11},{11,3},{4,12},{12,4},... | collective-permute-start | bytes 860168 | tf_op jit(solution)/shard_map/ppermute | solution.py:78
  143.0 36.5 %collective-permute-start.5 = (bf16[20,7168]{1,0:T(8,128)(2,1)S(1)}, bf16[20,7168]{1,0:T(8,128)(2,1)S(1)}, u32[]{:S(2)}, u32[]{:S(2)}) collective-permute-start(bf16[20,7168]{1,0:T(8,128)(2,1)S(1)} %get-tuple-element.21), channel_id=1, source_target_pairs={{0,8},{8,0},{1,9},{9,1},{2,10},{10,2},{3,11},{11,3},{4,12},{12,4},... | collective-permute-start | bytes 860168 | tf_op jit(solution)/shard_map/ppermute | solution.py:78
Sparse Core Ops, SparseCore 0:
  11.2 46.8 all-gather.5
  59.7 31.8 all-gather.3

commit v16 on v13

--- a/solution.py
+++ b/solution.py
@@ -30,6 +30,10 @@
     sibling = lax.ppermute(halves[(core + 1) % cores], "core", swap)
     paired = (halves[core].astype(jnp.float32) + sibling.astype(jnp.float32)).astype(jnp.bfloat16)
     return paired.reshape(chips, count, width)
+
+
+def group_sums(parts):
+    return lax.psum_scatter(parts, ("core", "sc"), scatter_dimension=0, tiled=True)
 
 
 def chip_sums(paired):
@@ -75,14 +79,14 @@
     away_w = [lax.ppermute(packed_w[k], "eg", shift(k)) for k in range(1, experts)]
     own_rows = gather(packed[0])
     own_rows, away, away_w = lax.optimization_barrier((own_rows, away, away_w))
-    own_parts = expert_parts(own_rows, *weights)
+    own_parts = slice_ffn(own_rows, *weights)
     away_rows = gather(jnp.concatenate(away, axis=0))
     own_parts, away_rows = lax.optimization_barrier((own_parts, away_rows))
     away_parts = expert_parts(away_rows, *weights)
     away_back = chip_sums(away_parts)
+    own_sums = group_sums(own_parts)
     done = finish(away_back, jnp.concatenate(away_w, axis=0))
-    own_parts, done = lax.optimization_barrier((own_parts, done))
-    own = finish(chip_sums(own_parts), packed_w[0])
+    own = finish(own_sums[None], packed_w[0])
     home = [own] + [
         lax.ppermute(done[(k - 1) * slots:k * slots], "eg", shift(experts - k))
         for k in range(1, experts)

time: 186 us -> 230 us (1.24)
  blocking collectives: 30.8 us -> 55.1 us
  waiting for transfers between devices: 98.3 us -> 121 us
  starting transfers between devices: 11 us -> 7.04 us
    reduce_scatter x0 -> x1, waiting for transfers between devices: none -> 54 us  [group_sums(): lax.psum_scatter(parts, ('core', 'sc'), scatter_dimension=0, tiled=True)]
    all_to_all x1 -> x0, waiting for transfers between devices: 36.3 us -> none  [chip_sums(): return lax.all_to_all(paired, 'sc', split_axis=0, concat_axis=0, tiled=True)]
    all_to_all x1, blocking collectives: 30.8 us -> 55.1 us  [chip_sums(): return lax.all_to_all(paired, 'sc', split_axis=0, concat_axis=0, tiled=True)]
    all_gather x2, waiting for transfers between devices: 28.3 us -> 37.8 us  [gather(): return lax.all_gather(held, ('core', 'sc'), axis=0, tiled=True)]
    ppermute x2 -> x1, waiting for transfers between devices: 8.65 us -> 4.31 us  [expert_parts(): sibling = lax.ppermute(halves[(core + 1) % cores], 'core', swap)]
    all_to_all x1 -> x0, starting transfers between devices: 3.64 us -> none  [chip_sums(): return lax.all_to_all(paired, 'sc', split_axis=0, concat_axis=0, tiled=True)]
    convert_element_type x2 -> x1, other arithmetic: 5.22 us -> 3.42 us  [expert_parts(): (halves[core].astype(jnp.float32) + sibling.astype(jnp.float32)).astype(j...]
  transfers between devices with their start and end apart: 8 -> 7, of which waited for: 6 -> 5; matrix products, arithmetic and copies ran while one was open for 8% -> 7% of each run, Pallas kernels for 0% -> 0%
where the time goes in v16:
time: 230 us; the launch traced here: 229 us
  waiting for transfers between devices  121 us (53%)
  blocking collectives  55.1 us (24%)
  matrix products  23.1 us (10%)
  between operations  13.2 us (6%)
  starting transfers between devices  7.04 us (3%)
  other arithmetic  6.24 us (3%)
  local copies, waits for them, and re-layouts  3.41 us (1%)
    all_to_all x1, blocking collectives, chip_sums(): return lax.all_to_all(paired, 'sc', split_axis=0, concat_axis=0, tiled=True)  55.1 us
    reduce_scatter x1, waiting for transfers between devices, group_sums(): lax.psum_scatter(parts, ('core', 'sc'), scatter_dimension=0, tiled=True)  54 us
    all_gather x2, waiting for transfers between devices, gather(): return lax.all_gather(held, ('core', 'sc'), axis=0, tiled=True)  37.8 us
    ppermute x1, waiting for transfers between devices, shards(): lax.ppermute(packed_w[k], 'eg', shift(k))  25 us
    dot_general x2, matrix products, slice_ffn(): both = jnp.dot(rows, gate_up_w, preferred_element_type=jnp.float32)  14.3 us
    dot_general x2, matrix products, slice_ffn(): jnp.dot(hidden, down_w, preferred_element_type=jnp.float32)  4.82 us
  transfers between devices with their start and end apart: 7, of which 5 were waited for; matrix products, arithmetic and copies ran while one was open for 7% of the time, Pallas kernels for 0%

profile of v16, /device:TPU:0, one launch (start us, length us, event | category | flops | bytes accessed | tf_op | source)
XLA Modules:
  0.0 229.3 jit_solution(8095023957201175886)
XLA Ops:
  6.5 0.0 all-gather.6.cloned.1.call-start
  6.5 0.7 fusion.29
  7.2 0.1 fusion.20
  7.3 0.1 copy.9
  7.4 0.1 reduce_window_sum.11
  7.5 0.1 fusion.28
  7.5 0.1 copy.8
  7.6 0.0 copy-start.4
  7.6 2.1 multiply_reduce_fusion
  9.7 0.5 convolution_convert_fusion.2
  10.2 0.9 slice_bitcast_fusion
  11.1 0.0 all-gather.6.cloned.1.call-update
  11.1 0.0 all-gather.4.cloned.1.call-start
  11.2 4.1 %collective-permute-start = (bf16[40,7168]{1,0:T(8,128)(2,1)S(1)}, bf16[40,7168]{1,0:T(8,128)(2,1)S(1)}, u32[]{:S(2)}, u32[]{:S(2)}) collective-permute-start(bf16[40,7168]{1,0:T(8,128)(2,1)S(1)} %get-tuple-element.15), channel_id=1, source_target_pairs={{0,8},{8,0},{1,9},{9,1},{2,10},{10,2},{3,11},{11,3},{4,12},{12,4},... | collective-permute-start | bytes 1720328 | tf_op jit(solution)/shard_map/ppermute | solution.py:78
  15.3 0.0 copy-done.4
  15.3 0.1 fusion.19
  15.4 0.1 copy.10
  15.5 0.1 select_reduce_fusion
  15.6 0.1 collective-permute-start.1
  15.6 25.0 %collective-permute-done.1 = f32[40]{0:T(128)S(1)} collective-permute-done((f32[40]{0:T(128)S(1)}, f32[40]{0:T(128)S(1)}, u32[]{:S(2)}, u32[]{:S(2)}) %collective-permute-start.1) | collective-permute-done | bytes 192 | tf_op jit(solution)/shard_map/ppermute | solution.py:79
  40.7 0.0 collective-permute-done
  40.7 15.0 %all-gather.6.cloned.1.call-done = bf16[1,320,7168]{2,1,0:T(8,128)(2,1)} async-done(((bf16[1,40,7168]{2,1,0:T(8,128)(2,1)}), bf16[1,320,7168]{2,1,0:T(8,128)(2,1)}) %all-gather.6.cloned.1.call-update) | async-done | bytes 4587536 | tf_op jit(solution)/shard_map/all_gather | solution.py:18
  55.7 0.0 copy-done.3
  55.7 0.0 all-gather.4.cloned.1.call-update
  55.7 0.0 reduce-scatter.2.cloned.1.call-start
  55.8 0.0 copy-start.1
  55.8 7.1 %fusion.2 = f32[320,512]{1,0:T(8,128)S(1)} fusion(bf16[320,7168]{1,0:T(8,128)(2,1)} %bitcast.42, bf16[7168,256]{1,0:T(8,128)(2,1)} %bitcast.43, bf16[7168,256]{1,0:T(8,128)(2,1)} %bitcast.45), kind=kOutput, calls=%fused_computation.8 | convolution fusion | flops 2363490304 | bytes 12582912 | tf_op jit(solution)/shard_map/dot_general | solution.py:11
  63.0 0.0 copy-done.1
  63.0 3.5 %convolution_convert_fusion.1 = bf16[320,7168]{1,0:T(8,128)(2,1)} fusion(bf16[1,256,7168]{2,1,0:T(8,128)(2,1)S(1)} %copy-done.1, f32[320,512]{1,0:T(8,128)S(1)} %fusion.2), kind=kOutput, calls=%fused_computation.1 | convolution fusion | flops 1177190400 | bytes 8912896 | tf_op jit(solution)/shard_map/dot_general | solution.py:14
  66.4 22.8 %all-gather.4.cloned.1.call-done = bf16[320,7168]{1,0:T(8,128)(2,1)} async-done(((bf16[40,7168]{1,0:T(8,128)(2,1)}), bf16[320,7168]{1,0:T(8,128)(2,1)}) %all-gather.4.cloned.1.call-update) | async-done | bytes 4587536 | tf_op jit(solution)/shard_map/all_gather | solution.py:18
  89.2 7.1 %fusion.1 = f32[320,512]{1,0:T(8,128)S(1)} fusion(bf16[320,7168]{1,0:T(8,128)(2,1)} %all-gather.4.cloned.1.call-done, bf16[7168,256]{1,0:T(8,128)(2,1)} %bitcast.44, bf16[7168,256]{1,0:T(8,128)(2,1)} %bitcast.46), kind=kOutput, calls=%fused_computation.7 | convolution fusion | flops 2363490304 | bytes 12582912 | tf_op jit(solution)/shard_map/dot_general | solution.py:11
  96.3 0.0 copy-done.2
  96.3 1.4 convolution_convert_fusion
  97.7 0.0 copy-start
  97.7 2.1 copy-done
  99.9 0.1 dynamic-slice_bitcast_fusion
  100.0 0.3 collective-permute-start.2
  100.3 0.0 reduce-scatter.2.cloned.1.call-update
  100.3 4.3 %collective-permute-done.2 = bf16[160,7168]{1,0:T(8,128)(2,1)} collective-permute-done((bf16[160,7168]{1,0:T(8,128)(2,1)S(1)}, bf16[160,7168]{1,0:T(8,128)(2,1)}, u32[]{:S(2)}, u32[]{:S(2)}) %collective-permute-start.2) | collective-permute-done | bytes 2293792 | tf_op jit(solution)/shard_map/ppermute | solution.py:30
  104.7 3.4 %fusion.3 = bf16[160,7168]{1,0:T(8,128)(2,1)S(1)} fusion(bf16[160,7168]{1,0:T(8,128)(2,1)} %collective-permute-done.2, bf16[2,160,7168]{2,1,0:T(8,128)(2,1)} %bitcast.38, s32[]{:T(128)S(6)} %select_n.39), kind=kLoop, calls=%fused_computation.10 | loop fusion | flops 4587520 | bytes 6881284 | tf_op jit(solution)/shard_map/convert_element_type | solution.py:31
  108.1 55.1 %all_to_all.5 = bf16[4,40,7168]{2,1,0:T(8,128)(2,1)S(1)} all-to-all(bf16[4,40,7168]{2,1,0:T(8,128)(2,1)S(1)} %bitcast.39), channel_id=1, replica_groups=mesh['grp'=2,'eg'=2,'sc'=4,'core'=2] {'sc'}, dimensions={0} | all-to-all | bytes 4587520 | tf_op jit(solution)/shard_map/all_to_all | solution.py:40
  163.2 0.4 convert_reduce_fusion
  163.6 0.1 multiply_convert_fusion.1
  163.7 2.5 %collective-permute-start.3 = (bf16[40,7168]{1,0:T(8,128)(2,1)S(1)}, bf16[40,7168]{1,0:T(8,128)(2,1)S(1)}, u32[]{:S(2)}, u32[]{:S(2)}) collective-permute-start(bf16[40,7168]{1,0:T(8,128)(2,1)S(1)} %multiply_convert_fusion.1), channel_id=1, source_target_pairs={{0,8},{8,0},{1,9},{9,1},{2,10},{10,2},{3,11},{11,3},{4,12},{12,4},... | collective-permute-start | bytes 1720328 | tf_op jit(solution)/shard_map/ppermute | solution.py:91
  166.2 54.0 %reduce-scatter.2.cloned.1.call-done = bf16[40,7168]{1,0:T(8,128)(2,1)} async-done(((bf16[320,7168]{1,0:T(8,128)(2,1)}), bf16[40,7168]{1,0:T(8,128)(2,1)}) %reduce-scatter.2.cloned.1.call-update) | async-done | bytes 573456 | tf_op jit(solution)/shard_map/reduce_scatter | solution.py:36
  220.2 1.2 fusion.12
  221.4 0.0 collective-permute-done.3
  221.4 1.4 fusion
  (4 shorter events, 0.0 us)
Async XLA Ops:
  6.5 49.2 %all-gather.6.cloned.1.call-start = ((), (), s32[]{:S(2)}) async-start(), calls=%async_computation.4 | async-start | bytes 5160960 | tf_op jit(solution)/shard_map/all_gather | solution.py:18
  7.6 7.7 %copy-start.4 = (f32[64,1]{0,1:T(1,128)S(1)}, f32[64,1]{0,1:T(1,128)}, u32[]{:S(2)}) copy-start(f32[64,1]{0,1:T(1,128)} %param.10) | copy-start | bytes 772
  11.1 78.0 %all-gather.4.cloned.1.call-start = ((), (), s32[]{:S(2)}) async-start(), calls=%async_computation.2 | async-start | bytes 5160960 | tf_op jit(solution)/shard_map/all_gather | solution.py:18
  11.2 29.5 %collective-permute-start = (bf16[40,7168]{1,0:T(8,128)(2,1)S(1)}, bf16[40,7168]{1,0:T(8,128)(2,1)S(1)}, u32[]{:S(2)}, u32[]{:S(2)}) collective-permute-start(bf16[40,7168]{1,0:T(8,128)(2,1)S(1)} %get-tuple-element.15), channel_id=1, source_target_pairs={{0,8},{8,0},{1,9},{9,1},{2,10},{10,2},{3,11},{11,3},{4,12},{12,4},... | collective-permute-start | bytes 1720328 | tf_op jit(solution)/shard_map/ppermute | solution.py:78
  15.6 25.1 %collective-permute-start.1 = (f32[40]{0:T(128)S(1)}, f32[40]{0:T(128)S(1)}, u32[]{:S(2)}, u32[]{:S(2)}) collective-permute-start(f32[40]{0:T(128)S(1)} %get-tuple-element.18), channel_id=1, source_target_pairs={{0,8},{8,0},{1,9},{9,1},{2,10},{10,2},{3,11},{11,3},{4,12},{12,4},... | collective-permute-start | bytes 488 | tf_op jit(solution)/shard_map/ppermute | solution.py:79
  40.7 15.0 %copy-start.3 = (bf16[40,7168]{1,0:T(8,128)(2,1)}, bf16[40,7168]{1,0:T(8,128)(2,1)S(1)}, u32[]{:S(2)}) copy-start(bf16[40,7168]{1,0:T(8,128)(2,1)S(1)} %collective-permute-done) | copy-start | bytes 1720324
  55.7 164.4 %reduce-scatter.2.cloned.1.call-start = ((), (), s32[]{:S(2)}) async-start(), calls=%async_computation.3 | async-start | bytes 5160960 | tf_op jit(solution)/shard_map/reduce_scatter | solution.py:36
  55.8 7.2 %copy-start.1 = (bf16[1,256,7168]{2,1,0:T(8,128)(2,1)S(1)}, bf16[1,256,7168]{2,1,0:T(8,128)(2,1)}, u32[]{:S(2)}) copy-start(bf16[1,256,7168]{2,1,0:T(8,128)(2,1)} %param.13) | copy-start | bytes 11010052
  89.2 7.1 %copy-start.2 = (bf16[1,256,7168]{2,1,0:T(8,128)(2,1)S(1)}, bf16[1,256,7168]{2,1,0:T(8,128)(2,1)}, u32[]{:S(2)}) copy-start(bf16[1,256,7168]{2,1,0:T(8,128)(2,1)} %param.13) | copy-start | bytes 11010052
  97.7 2.1 copy-start
  100.0 4.6 %collective-permute-start.2 = (bf16[160,7168]{1,0:T(8,128)(2,1)S(1)}, bf16[160,7168]{1,0:T(8,128)(2,1)}, u32[]{:S(2)}, u32[]{:S(2)}) collective-permute-start(bf16[160,7168]{1,0:T(8,128)(2,1)S(1)} %dynamic-slice_bitcast_fusion), channel_id=1, source_target_pairs={{0,1},{1,0},{2,3},{3,2},{4,5},{5,4},{6,7},{7,6},{8,9},{9,8},{10,11... | collective-permute-start | bytes 6881288 | tf_op jit(solution)/shard_map/ppermute | solution.py:30
  163.7 57.7 %collective-permute-start.3 = (bf16[40,7168]{1,0:T(8,128)(2,1)S(1)}, bf16[40,7168]{1,0:T(8,128)(2,1)S(1)}, u32[]{:S(2)}, u32[]{:S(2)}) collective-permute-start(bf16[40,7168]{1,0:T(8,128)(2,1)S(1)} %multiply_convert_fusion.1), channel_id=1, source_target_pairs={{0,8},{8,0},{1,9},{9,1},{2,10},{10,2},{3,11},{11,3},{4,12},{12,4},... | collective-permute-start | bytes 1720328 | tf_op jit(solution)/shard_map/ppermute | solution.py:91
Sparse Core Ops, SparseCore 0:
  11.3 44.4 all-gather.5
  57.3 31.8 all-gather.3
  100.5 119.6 reduce-scatter.1

commit v17 on v7

--- a/solution.py
+++ b/solution.py
@@ -80,8 +80,8 @@
     own_parts, away_rows = lax.optimization_barrier((own_parts, away_rows))
     away_parts = expert_parts(away_rows, *weights)
     away_back = chip_sums(away_parts)
-    own_parts, away_back = lax.optimization_barrier((own_parts, away_back))
     done = finish(away_back, jnp.concatenate(away_w, axis=0))
+    own_parts, done = lax.optimization_barrier((own_parts, done))
     own = finish(chip_sums(own_parts), packed_w[0])
     home = [own] + [
         lax.ppermute(done[(k - 1) * slots:k * slots], "eg", shift(experts - k))

time: 187 us -> 187 us (level)
  waiting for transfers between devices: 95.5 us -> 97.6 us
    all_to_all x1, waiting for transfers between devices: 34.2 us -> 36.3 us  [chip_sums(): return lax.all_to_all(paired, 'sc', split_axis=0, concat_axis=0, tiled=True)]
    unnamed x20 -> x18, local copies, waits for them, and re-layouts: 5.25 us -> 5.34 us
  transfers between devices with their start and end apart: 8 -> 8, of which waited for: 6 -> 6; matrix products, arithmetic and copies ran while one was open for 8% -> 7% of each run, Pallas kernels for 0% -> 0%
where the time goes in v17:
time: 187 us; the launch traced here: 186 us
  waiting for transfers between devices  97.6 us (52%)
  blocking collectives  30.8 us (16%)
  matrix products  19.2 us (10%)
  between operations  13.6 us (7%)
  starting transfers between devices  11 us (6%)
  other arithmetic  7.3 us (4%)
  local copies, waits for them, and re-layouts  6.76 us (4%)
    all_to_all x1, waiting for transfers between devices, chip_sums(): return lax.all_to_all(paired, 'sc', split_axis=0, concat_axis=0, tiled=True)  36.3 us
    all_to_all x1, blocking collectives, chip_sums(): return lax.all_to_all(paired, 'sc', split_axis=0, concat_axis=0, tiled=True)  30.8 us
    all_gather x2, waiting for transfers between devices, gather(): return lax.all_gather(held, ('core', 'sc'), axis=0, tiled=True)  27.7 us
    ppermute x1, waiting for transfers between devices, shards(): lax.ppermute(packed_w[k], 'eg', shift(k))  25 us
    ppermute x2, waiting for transfers between devices, expert_parts(): sibling = lax.ppermute(halves[(core + 1) % cores], 'core', swap)  8.53 us
    dot_general x2, matrix products, slice_ffn(): upper = jnp.dot(rows, up_w, preferred_element_type=jnp.float32)  6.26 us
    dot_general x2, matrix products, slice_ffn(): gate = jnp.dot(rows, gate_w, preferred_element_type=jnp.float32)  6.26 us
    unnamed x18, local copies, waits for them, and re-layouts  5.34 us
  transfers between devices with their start and end apart: 8, of which 6 were waited for; matrix products, arithmetic and copies ran while one was open for 7% of the time, Pallas kernels for 0%

profile of v17, /device:TPU:0, one launch (start us, length us, event | category | flops | bytes accessed | tf_op | source)
XLA Modules:
  0.0 186.3 jit_solution(3180921477322147813)
XLA Ops:
  6.5 2.1 %multiply_reduce_fusion = (f32[64]{0:T(128)S(1)}, f32[64,7168]{1,0:T(8,128)S(1)}) fusion(bf16[64,7168]{1,0:T(8,128)(2,1)} %param.7, s32[64]{0:T(128)} %param.8), kind=kOutput, calls=%fused_computation.25 | convolution fusion | flops 60559296 | bytes 2753024 | tf_op jit(solution)/shard_map/dot_general | solution.py:52
  8.6 0.7 fusion.39
  9.3 0.1 fusion.28
  9.4 0.1 copy.9
  9.5 0.1 reduce_window_sum.11
  9.6 0.1 fusion.36
  9.6 0.1 copy.8
  9.7 0.5 convolution_convert_fusion.2
  10.2 0.9 slice_bitcast_fusion
  11.1 0.0 all-gather.6.cloned.1.call-update
  11.1 0.0 all-gather.4.cloned.1.call-start
  11.2 4.1 %collective-permute-start = (bf16[40,7168]{1,0:T(8,128)(2,1)S(1)}, bf16[40,7168]{1,0:T(8,128)(2,1)S(1)}, u32[]{:S(2)}, u32[]{:S(2)}) collective-permute-start(bf16[40,7168]{1,0:T(8,128)(2,1)S(1)} %get-tuple-element.19), channel_id=1, source_target_pairs={{0,8},{8,0},{1,9},{9,1},{2,10},{10,2},{3,11},{11,3},{4,12},{12,4},... | collective-permute-start | bytes 1720328 | tf_op jit(solution)/shard_map/ppermute | solution.py:74
  15.3 0.1 fusion.27
  15.4 0.1 copy.10
  15.5 0.1 select_reduce_fusion
  15.6 0.1 collective-permute-start.1
  15.7 25.0 %collective-permute-done.1 = f32[40]{0:T(128)S(1)} collective-permute-done((f32[40]{0:T(128)S(1)}, f32[40]{0:T(128)S(1)}, u32[]{:S(2)}, u32[]{:S(2)}) %collective-permute-start.1) | collective-permute-done | bytes 192 | tf_op jit(solution)/shard_map/ppermute | solution.py:75
  40.7 15.0 %all-gather.6.cloned.1.call-done = bf16[1,320,7168]{2,1,0:T(8,128)(2,1)} async-done(((bf16[1,40,7168]{2,1,0:T(8,128)(2,1)}), bf16[1,320,7168]{2,1,0:T(8,128)(2,1)}) %all-gather.6.cloned.1.call-update) | async-done | bytes 4587536 | tf_op jit(solution)/shard_map/all_gather | solution.py:18
  55.7 0.0 all-gather.4.cloned.1.call-update
  55.8 4.9 %fusion.7 = f32[320,256]{1,0:T(8,128)S(1)} fusion(bf16[320,7168]{1,0:T(8,128)(2,1)} %bitcast.68, bf16[1,7168,256]{2,1,0:T(8,128)(2,1)} %param.12), kind=kOutput, calls=%fused_computation.16 | convolution fusion | flops 1174405120 | bytes 8585216 | tf_op jit(solution)/shard_map/dot_general | solution.py:12
  60.7 0.9 copy-done.7
  61.6 1.3 fusion.11
  63.0 0.7 copy-done.1
  63.7 1.4 convolution_convert_fusion.1
  65.1 2.1 %copy-done = bf16[320,7168]{1,0:T(8,128)(2,1)} copy-done((bf16[320,7168]{1,0:T(8,128)(2,1)}, bf16[320,7168]{1,0:T(8,128)(2,1)S(1)}, u32[]{:S(2)}) %copy-start) | copy-done | bytes 4587544
  67.2 0.1 dynamic-slice_bitcast_fusion.1
  67.3 0.3 collective-permute-start.2
  67.6 4.3 %collective-permute-done.2 = bf16[160,7168]{1,0:T(8,128)(2,1)} collective-permute-done((bf16[160,7168]{1,0:T(8,128)(2,1)S(1)}, bf16[160,7168]{1,0:T(8,128)(2,1)}, u32[]{:S(2)}, u32[]{:S(2)}) %collective-permute-start.2) | collective-permute-done | bytes 2293792 | tf_op jit(solution)/shard_map/ppermute | solution.py:30
  72.0 4.5 %fusion.2 = bf16[160,7168]{1,0:T(8,128)(2,1)} fusion(bf16[160,7168]{1,0:T(8,128)(2,1)} %collective-permute-done.2, bf16[2,160,7168]{2,1,0:T(8,128)(2,1)} %bitcast.62, s32[]{:T(128)S(6)} %select_n.43), kind=kLoop, calls=%fused_computation.9 | loop fusion | flops 4587520 | bytes 6881284 | tf_op jit(solution)/shard_map/convert_element_type | solution.py:31
  76.5 12.7 %all-gather.4.cloned.1.call-done = bf16[320,7168]{1,0:T(8,128)(2,1)} async-done(((bf16[40,7168]{1,0:T(8,128)(2,1)}), bf16[320,7168]{1,0:T(8,128)(2,1)}) %all-gather.4.cloned.1.call-update) | async-done | bytes 4587536 | tf_op jit(solution)/shard_map/all_gather | solution.py:18
  89.2 4.9 %fusion.9 = f32[320,256]{1,0:T(8,128)S(1)} fusion(bf16[320,7168]{1,0:T(8,128)(2,1)} %all-gather.4.cloned.1.call-done, bf16[1,7168,256]{2,1,0:T(8,128)(2,1)} %param.11), kind=kOutput, calls=%fused_computation.18 | convolution fusion | flops 1174405120 | bytes 8585216 | tf_op jit(solution)/shard_map/dot_general | solution.py:11
  94.1 0.9 copy-done.8
  95.1 1.3 fusion.16
  96.4 0.7 copy-done.2
  97.1 1.4 convolution_convert_fusion
  98.5 0.2 dynamic-slice_bitcast_fusion
  98.6 0.3 collective-permute-start.3
  98.9 4.2 %collective-permute-done.3 = bf16[160,7168]{1,0:T(8,128)(2,1)S(1)} collective-permute-done((bf16[160,7168]{1,0:T(8,128)(2,1)S(1)}, bf16[160,7168]{1,0:T(8,128)(2,1)S(1)}, u32[]{:S(2)}, u32[]{:S(2)}) %collective-permute-start.3) | collective-permute-done | bytes 2293792 | tf_op jit(solution)/shard_map/ppermute | solution.py:30
  103.1 0.7 fusion.1
  103.8 30.8 %all_to_all.10 = bf16[4,40,7168]{2,1,0:T(8,128)(2,1)S(1)} all-to-all(bf16[4,40,7168]{2,1,0:T(8,128)(2,1)S(1)} %bitcast.65), channel_id=1, replica_groups=mesh['grp'=2,'eg'=2,'sc'=4,'core'=2] {'sc'}, dimensions={0} | all-to-all | bytes 4587520 | tf_op jit(solution)/shard_map/all_to_all | solution.py:36
  134.6 0.4 convert_reduce_fusion.1
  135.0 0.1 multiply_convert_fusion.1
  135.1 3.6 %all-to-all-start.1 = ((bf16[4,40,7168]{2,1,0:T(8,128)(2,1)}), bf16[4,40,7168]{2,1,0:T(8,128)(2,1)S(1)}, u32[]{:S(2)}, u32[]{:S(2)}) async-start(bf16[4,40,7168]{2,1,0:T(8,128)(2,1)} %bitcast.12), calls=%async_computation.1 | async-start | bytes 4587520 | tf_op jit(solution)/shard_map/all_to_all | solution.py:36
  138.8 2.5 %collective-permute-start.4 = (bf16[40,7168]{1,0:T(8,128)(2,1)S(1)}, bf16[40,7168]{1,0:T(8,128)(2,1)S(1)}, u32[]{:S(2)}, u32[]{:S(2)}) collective-permute-start(bf16[40,7168]{1,0:T(8,128)(2,1)S(1)} %multiply_convert_fusion.1), channel_id=1, source_target_pairs={{0,8},{8,0},{1,9},{9,1},{2,10},{10,2},{3,11},{11,3},{4,12},{12,4},... | collective-permute-start | bytes 1720328 | tf_op jit(solution)/shard_map/ppermute | solution.py:87
  141.3 36.3 %all-to-all-done.1 = bf16[4,40,7168]{2,1,0:T(8,128)(2,1)S(1)} async-done(((bf16[4,40,7168]{2,1,0:T(8,128)(2,1)}), bf16[4,40,7168]{2,1,0:T(8,128)(2,1)S(1)}, u32[]{:S(2)}, u32[]{:S(2)}) %all-to-all-start.1) | async-done | bytes 2293792 | tf_op jit(solution)/shard_map/all_to_all | solution.py:36
  177.6 0.3 convert_reduce_fusion
  177.9 0.1 fusion.22
  178.1 1.4 fusion
  (18 shorter events, 0.0 us)
Async XLA Ops:
  6.5 49.2 %all-gather.6.cloned.1.call-start = ((), (), s32[]{:S(2)}) async-start(), calls=%async_computation.3 | async-start | bytes 5160960 | tf_op jit(solution)/shard_map/all_gather | solution.py:18
  8.6 6.7 %copy-start.4 = (f32[64,1]{0,1:T(1,128)S(1)}, f32[64,1]{0,1:T(1,128)}, u32[]{:S(2)}) copy-start(f32[64,1]{0,1:T(1,128)} %param.10) | copy-start | bytes 772
  11.1 78.1 %all-gather.4.cloned.1.call-start = ((), (), s32[]{:S(2)}) async-start(), calls=%async_computation.2 | async-start | bytes 5160960 | tf_op jit(solution)/shard_map/all_gather | solution.py:18
  11.2 29.5 %collective-permute-start = (bf16[40,7168]{1,0:T(8,128)(2,1)S(1)}, bf16[40,7168]{1,0:T(8,128)(2,1)S(1)}, u32[]{:S(2)}, u32[]{:S(2)}) collective-permute-start(bf16[40,7168]{1,0:T(8,128)(2,1)S(1)} %get-tuple-element.19), channel_id=1, source_target_pairs={{0,8},{8,0},{1,9},{9,1},{2,10},{10,2},{3,11},{11,3},{4,12},{12,4},... | collective-permute-start | bytes 1720328 | tf_op jit(solution)/shard_map/ppermute | solution.py:74
  15.6 25.1 %collective-permute-start.1 = (f32[40]{0:T(128)S(1)}, f32[40]{0:T(128)S(1)}, u32[]{:S(2)}, u32[]{:S(2)}) collective-permute-start(f32[40]{0:T(128)S(1)} %get-tuple-element.22), channel_id=1, source_target_pairs={{0,8},{8,0},{1,9},{9,1},{2,10},{10,2},{3,11},{11,3},{4,12},{12,4},... | collective-permute-start | bytes 488 | tf_op jit(solution)/shard_map/ppermute | solution.py:75
  40.7 15.0 %copy-start.3 = (bf16[40,7168]{1,0:T(8,128)(2,1)}, bf16[40,7168]{1,0:T(8,128)(2,1)S(1)}, u32[]{:S(2)}) copy-start(bf16[40,7168]{1,0:T(8,128)(2,1)S(1)} %collective-permute-done) | copy-start | bytes 1720324
  55.8 4.9 %copy-start.5 = (bf16[1,320,7168]{2,1,0:T(8,128)(2,1)S(1)}, bf16[1,320,7168]{2,1,0:T(8,128)(2,1)}, u32[]{:S(2)}) copy-start(bf16[1,320,7168]{2,1,0:T(8,128)(2,1)} %all-gather.6.cloned.1.call-done) | copy-start | bytes 13762564
  55.8 5.9 %copy-start.7 = (bf16[1,7168,256]{2,1,0:T(8,128)(2,1)S(1)}, bf16[1,7168,256]{2,1,0:T(8,128)(2,1)}, u32[]{:S(2)}) copy-start(bf16[1,7168,256]{2,1,0:T(8,128)(2,1)} %param.11) | copy-start | bytes 11010052
  61.6 2.0 %copy-start.1 = (bf16[1,256,7168]{2,1,0:T(8,128)(2,1)S(1)}, bf16[1,256,7168]{2,1,0:T(8,128)(2,1)}, u32[]{:S(2)}) copy-start(bf16[1,256,7168]{2,1,0:T(8,128)(2,1)} %param.13) | copy-start | bytes 11010052
  65.1 2.1 %copy-start = (bf16[320,7168]{1,0:T(8,128)(2,1)}, bf16[320,7168]{1,0:T(8,128)(2,1)S(1)}, u32[]{:S(2)}) copy-start(bf16[320,7168]{1,0:T(8,128)(2,1)S(1)} %convolution_convert_fusion.1) | copy-start | bytes 13762564
  67.3 4.6 %collective-permute-start.2 = (bf16[160,7168]{1,0:T(8,128)(2,1)S(1)}, bf16[160,7168]{1,0:T(8,128)(2,1)}, u32[]{:S(2)}, u32[]{:S(2)}) collective-permute-start(bf16[160,7168]{1,0:T(8,128)(2,1)S(1)} %dynamic-slice_bitcast_fusion.1), channel_id=1, source_target_pairs={{0,1},{1,0},{2,3},{3,2},{4,5},{5,4},{6,7},{7,6},{8,9},{9,8},{10,11... | collective-permute-start | bytes 6881288 | tf_op jit(solution)/shard_map/ppermute | solution.py:30
  89.2 4.9 %copy-start.6 = (bf16[320,7168]{1,0:T(8,128)(2,1)S(1)}, bf16[320,7168]{1,0:T(8,128)(2,1)}, u32[]{:S(2)}) copy-start(bf16[320,7168]{1,0:T(8,128)(2,1)} %all-gather.4.cloned.1.call-done) | copy-start | bytes 13762564
  89.2 5.9 %copy-start.8 = (bf16[1,7168,256]{2,1,0:T(8,128)(2,1)S(1)}, bf16[1,7168,256]{2,1,0:T(8,128)(2,1)}, u32[]{:S(2)}) copy-start(bf16[1,7168,256]{2,1,0:T(8,128)(2,1)} %param.12) | copy-start | bytes 11010052
  95.1 2.0 %copy-start.2 = (bf16[1,256,7168]{2,1,0:T(8,128)(2,1)S(1)}, bf16[1,256,7168]{2,1,0:T(8,128)(2,1)}, u32[]{:S(2)}) copy-start(bf16[1,256,7168]{2,1,0:T(8,128)(2,1)} %param.13) | copy-start | bytes 11010052
  98.6 4.5 %collective-permute-start.3 = (bf16[160,7168]{1,0:T(8,128)(2,1)S(1)}, bf16[160,7168]{1,0:T(8,128)(2,1)S(1)}, u32[]{:S(2)}, u32[]{:S(2)}) collective-permute-start(bf16[160,7168]{1,0:T(8,128)(2,1)S(1)} %dynamic-slice_bitcast_fusion), channel_id=1, source_target_pairs={{0,1},{1,0},{2,3},{3,2},{4,5},{5,4},{6,7},{7,6},{8,9},{9,8},{10,11... | collective-permute-start | bytes 6881288 | tf_op jit(solution)/shard_map/ppermute | solution.py:30
  135.1 42.4 %all-to-all-start.1 = ((bf16[4,40,7168]{2,1,0:T(8,128)(2,1)}), bf16[4,40,7168]{2,1,0:T(8,128)(2,1)S(1)}, u32[]{:S(2)}, u32[]{:S(2)}) async-start(bf16[4,40,7168]{2,1,0:T(8,128)(2,1)} %bitcast.12), calls=%async_computation.1 | async-start | bytes 4587520 | tf_op jit(solution)/shard_map/all_to_all | solution.py:36
  138.8 39.3 %collective-permute-start.4 = (bf16[40,7168]{1,0:T(8,128)(2,1)S(1)}, bf16[40,7168]{1,0:T(8,128)(2,1)S(1)}, u32[]{:S(2)}, u32[]{:S(2)}) collective-permute-start(bf16[40,7168]{1,0:T(8,128)(2,1)S(1)} %multiply_convert_fusion.1), channel_id=1, source_target_pairs={{0,8},{8,0},{1,9},{9,1},{2,10},{10,2},{3,11},{11,3},{4,12},{12,4},... | collective-permute-start | bytes 1720328 | tf_op jit(solution)/shard_map/ppermute | solution.py:87
Sparse Core Ops, SparseCore 0:
  11.3 44.4 all-gather.5
  57.3 31.8 all-gather.3

commit v18 on v13

--- a/solution.py
+++ b/solution.py
@@ -7,10 +7,13 @@
 SLICES = 8
 
 
-def slice_ffn(rows, gate_up_w, down_w):
+def slice_hidden(rows, gate_up_w):
     both = jnp.dot(rows, gate_up_w, preferred_element_type=jnp.float32)
     gate, upper = jnp.split(both, 2, axis=1)
-    hidden = (jax.nn.silu(gate) * upper).astype(jnp.bfloat16)
+    return (jax.nn.silu(gate) * upper).astype(jnp.bfloat16)
+
+
+def slice_down(hidden, down_w):
     return jnp.dot(hidden, down_w, preferred_element_type=jnp.float32).astype(jnp.bfloat16)
 
 
@@ -23,12 +26,14 @@
     cores = lax.axis_size("core")
     count = gathered.shape[0] // (chips * cores)
     width = gathered.shape[1]
-    parts = slice_ffn(gathered, gate_up_w, down_w)
-    halves = parts.reshape(cores, chips * count, width)
+    hidden = slice_hidden(gathered, gate_up_w)
+    halves = hidden.reshape(cores, chips * count, hidden.shape[1])
     core = lax.axis_index("core")
     swap = [(c, (c + 1) % cores) for c in range(cores)]
-    sibling = lax.ppermute(halves[(core + 1) % cores], "core", swap)
-    paired = (halves[core].astype(jnp.float32) + sibling.astype(jnp.float32)).astype(jnp.bfloat16)
+    sibling = lax.ppermute(slice_down(halves[(core + 1) % cores], down_w), "core", swap)
+    kept = slice_down(halves[core], down_w)
+    kept, sibling = lax.optimization_barrier((kept, sibling))
+    paired = (kept.astype(jnp.float32) + sibling.astype(jnp.float32)).astype(jnp.bfloat16)
     return paired.reshape(chips, count, width)
 
 

time: 186 us -> 185 us (level)
  matrix products: 21 us -> 23.6 us
  local copies, waits for them, and re-layouts: 3.57 us -> 1.13 us
    ppermute x2, waiting for transfers between devices: 8.65 us -> 4.67 us  [expert_parts(): lax.ppermute(slice_down(halves[(core + 1) % cores], down_w), 'core', swap)]
    all_gather x2, waiting for transfers between devices: 28.3 us -> 31.9 us  [gather(): return lax.all_gather(held, ('core', 'sc'), axis=0, tiled=True)]
    dot_general x4 -> x6, matrix products: 17 us -> 19.6 us  [the longest x2 14.3 us: slice_hidden(): both = jnp.dot(rows, gate_up_w, preferred_element_type=jnp.float32)]
    unnamed x10 -> x8, local copies, waits for them, and re-layouts: 2.14 us -> 0.02 us
    convert_element_type x2 -> x4, other arithmetic: 5.22 us -> 4.74 us  [the longest x2 4.53 us: expert_parts(): (kept.astype(jnp.float32) + sibling.astype(jnp.float32)).astype(jnp.bfloa...]
  transfers between devices with their start and end apart: 8 -> 8, of which waited for: 6 -> 6; matrix products, arithmetic and copies ran while one was open for 8% -> 9% of each run, Pallas kernels for 0% -> 0%
where the time goes in v18:
time: 185 us
  waiting for transfers between devices  98 us (53%)
  blocking collectives  30.8 us (17%)
  matrix products  23.6 us (13%)
  between operations  13.6 us (7%)
  starting transfers between devices  11 us (6%)
  other arithmetic  6.82 us (4%)
    all_to_all x1, waiting for transfers between devices, chip_sums(): return lax.all_to_all(paired, 'sc', split_axis=0, concat_axis=0, tiled=True)  36.3 us
    all_gather x2, waiting for transfers between devices, gather(): return lax.all_gather(held, ('core', 'sc'), axis=0, tiled=True)  31.9 us
    all_to_all x1, blocking collectives, chip_sums(): return lax.all_to_all(paired, 'sc', split_axis=0, concat_axis=0, tiled=True)  30.8 us
    ppermute x1, waiting for transfers between devices, shards(): lax.ppermute(packed_w[k], 'eg', shift(k))  25 us
    dot_general x2, matrix products, slice_hidden(): both = jnp.dot(rows, gate_up_w, preferred_element_type=jnp.float32)  14.3 us
    dot_general x4, matrix products, slice_down(): jnp.dot(hidden, down_w, preferred_element_type=jnp.float32)  5.38 us
    ppermute x2, waiting for transfers between devices, expert_parts(): lax.ppermute(slice_down(halves[(core + 1) % cores], down_w), 'core', swap)  4.67 us
    convert_element_type x2, other arithmetic, expert_parts(): (kept.astype(jnp.float32) + sibling.astype(jnp.float32)).astype(jnp.bfloa...  4.53 us
  transfers between devices with their start and end apart: 8, of which 6 were waited for; matrix products, arithmetic and copies ran while one was open for 9% of the time, Pallas kernels for 0%

profile of v18, /device:TPU:0, one launch (start us, length us, event | category | flops | bytes accessed | tf_op | source)
XLA Modules:
  0.0 184.9 jit_solution(7391254162515274805)
XLA Ops:
  6.5 0.7 fusion.40
  7.2 0.1 fusion.25
  7.3 0.1 copy.9
  7.4 0.1 reduce_window_sum.11
  7.5 0.1 fusion.33
  7.5 0.1 copy.8
  7.6 2.1 %multiply_reduce_fusion = (f32[64]{0:T(128)S(1)}, f32[64,7168]{1,0:T(8,128)S(1)}) fusion(bf16[64,7168]{1,0:T(8,128)(2,1)} %param.7, s32[64]{0:T(128)} %param.8), kind=kOutput, calls=%fused_computation.20 | convolution fusion | flops 60559296 | bytes 2753024 | tf_op jit(solution)/shard_map/dot_general | solution.py:57
  9.7 0.5 convolution_convert_fusion.4
  10.2 0.9 slice_bitcast_fusion
  11.1 0.0 all-gather.6.cloned.1.call-update
  11.1 0.0 all-gather.4.cloned.1.call-start
  11.2 4.1 %collective-permute-start = (bf16[40,7168]{1,0:T(8,128)(2,1)S(1)}, bf16[40,7168]{1,0:T(8,128)(2,1)S(1)}, u32[]{:S(2)}, u32[]{:S(2)}) collective-permute-start(bf16[40,7168]{1,0:T(8,128)(2,1)S(1)} %get-tuple-element.27), channel_id=1, source_target_pairs={{0,8},{8,0},{1,9},{9,1},{2,10},{10,2},{3,11},{11,3},{4,12},{12,4},... | collective-permute-start | bytes 1720328 | tf_op jit(solution)/shard_map/ppermute | solution.py:79
  15.3 0.0 copy-done.3
  15.3 0.1 fusion.24
  15.4 0.1 copy.10
  15.4 0.1 select_reduce_fusion
  15.6 0.1 collective-permute-start.1
  15.6 25.0 %collective-permute-done.1 = f32[40]{0:T(128)S(1)} collective-permute-done((f32[40]{0:T(128)S(1)}, f32[40]{0:T(128)S(1)}, u32[]{:S(2)}, u32[]{:S(2)}) %collective-permute-start.1) | collective-permute-done | bytes 192 | tf_op jit(solution)/shard_map/ppermute | solution.py:80
  40.7 0.0 collective-permute-done
  40.7 15.0 %all-gather.6.cloned.1.call-done = bf16[1,320,7168]{2,1,0:T(8,128)(2,1)} async-done(((bf16[1,40,7168]{2,1,0:T(8,128)(2,1)}), bf16[1,320,7168]{2,1,0:T(8,128)(2,1)}) %all-gather.6.cloned.1.call-update) | async-done | bytes 4587536 | tf_op jit(solution)/shard_map/all_gather | solution.py:21
  55.7 0.0 all-gather.4.cloned.1.call-update
  55.8 0.0 copy-start
  55.8 7.1 %fusion.2 = f32[320,512]{1,0:T(8,128)S(1)} fusion(bf16[320,7168]{1,0:T(8,128)(2,1)} %bitcast.59, bf16[7168,256]{1,0:T(8,128)(2,1)} %bitcast.60, bf16[7168,256]{1,0:T(8,128)(2,1)} %bitcast.62), kind=kOutput, calls=%fused_computation.10 | convolution fusion | flops 2363490304 | bytes 12582912 | tf_op jit(solution)/shard_map/dot_general | solution.py:11
  62.9 0.1 fusion.15
  63.0 0.8 convolution_convert_fusion.2
  63.8 0.3 collective-permute-start.2
  64.1 3.1 %convolution_convert_fusion.3 = bf16[160,7168]{1,0:T(8,128)(2,1)S(1)} fusion(bf16[1,256,7168]{2,1,0:T(8,128)(2,1)} %param.13, bf16[2,160,256]{2,1,0:T(8,128)(2,1)S(1)} %bitcast.54, s32[]{:T(128)S(6)} %select_n.43), kind=kOutput, calls=%fused_computation.3 | convolution fusion | flops 588349440 | bytes 6045700 | tf_op jit(solution)/shard_map/dot_general | solution.py:17
  67.2 1.2 collective-permute-done.2
  68.4 3.8 %add_convert_fusion.1 = bf16[160,7168]{1,0:T(8,128)(2,1)} fusion(bf16[160,7168]{1,0:T(8,128)(2,1)} %collective-permute-done.2, bf16[160,7168]{1,0:T(8,128)(2,1)S(1)} %convolution_convert_fusion.3), kind=kLoop, calls=%fused_computation.14 | loop fusion | flops 4587520 | bytes 6881280 | tf_op jit(solution)/shard_map/convert_element_type | solution.py:36
  72.3 16.9 %all-gather.4.cloned.1.call-done = bf16[320,7168]{1,0:T(8,128)(2,1)} async-done(((bf16[40,7168]{1,0:T(8,128)(2,1)}), bf16[320,7168]{1,0:T(8,128)(2,1)}) %all-gather.4.cloned.1.call-update) | async-done | bytes 4587536 | tf_op jit(solution)/shard_map/all_gather | solution.py:21
  89.2 7.1 %fusion.1 = f32[320,512]{1,0:T(8,128)S(1)} fusion(bf16[320,7168]{1,0:T(8,128)(2,1)} %all-gather.4.cloned.1.call-done, bf16[7168,256]{1,0:T(8,128)(2,1)} %bitcast.61, bf16[7168,256]{1,0:T(8,128)(2,1)} %bitcast.63), kind=kOutput, calls=%fused_computation.9 | convolution fusion | flops 2363490304 | bytes 12582912 | tf_op jit(solution)/shard_map/dot_general | solution.py:11
  96.3 0.1 fusion.14
  96.4 0.0 copy-done.1
  96.4 0.8 convolution_convert_fusion
  97.2 0.3 collective-permute-start.3
  97.5 0.8 convolution_convert_fusion.1
  98.3 3.4 %collective-permute-done.3 = bf16[160,7168]{1,0:T(8,128)(2,1)S(1)} collective-permute-done((bf16[160,7168]{1,0:T(8,128)(2,1)S(1)}, bf16[160,7168]{1,0:T(8,128)(2,1)S(1)}, u32[]{:S(2)}, u32[]{:S(2)}) %collective-permute-start.3) | collective-permute-done | bytes 2293792 | tf_op jit(solution)/shard_map/ppermute | solution.py:33
  101.7 0.7 add_convert_fusion
  102.4 30.8 %all_to_all.10 = bf16[4,40,7168]{2,1,0:T(8,128)(2,1)S(1)} all-to-all(bf16[4,40,7168]{2,1,0:T(8,128)(2,1)S(1)} %bitcast.52), channel_id=1, replica_groups=mesh['grp'=2,'eg'=2,'sc'=4,'core'=2] {'sc'}, dimensions={0} | all-to-all | bytes 4587520 | tf_op jit(solution)/shard_map/all_to_all | solution.py:41
  133.2 0.4 convert_reduce_fusion.1
  133.6 0.1 multiply_convert_fusion.1
  133.7 3.6 %all-to-all-start.1 = ((bf16[4,40,7168]{2,1,0:T(8,128)(2,1)}), bf16[4,40,7168]{2,1,0:T(8,128)(2,1)S(1)}, u32[]{:S(2)}, u32[]{:S(2)}) async-start(bf16[4,40,7168]{2,1,0:T(8,128)(2,1)} %bitcast.12), calls=%async_computation.1 | async-start | bytes 4587520 | tf_op jit(solution)/shard_map/all_to_all | solution.py:41
  137.4 2.5 %collective-permute-start.4 = (bf16[40,7168]{1,0:T(8,128)(2,1)S(1)}, bf16[40,7168]{1,0:T(8,128)(2,1)S(1)}, u32[]{:S(2)}, u32[]{:S(2)}) collective-permute-start(bf16[40,7168]{1,0:T(8,128)(2,1)S(1)} %multiply_convert_fusion.1), channel_id=1, source_target_pairs={{0,8},{8,0},{1,9},{9,1},{2,10},{10,2},{3,11},{11,3},{4,12},{12,4},... | collective-permute-start | bytes 1720328 | tf_op jit(solution)/shard_map/ppermute | solution.py:92
  139.9 36.3 %all-to-all-done.1 = bf16[4,40,7168]{2,1,0:T(8,128)(2,1)S(1)} async-done(((bf16[4,40,7168]{2,1,0:T(8,128)(2,1)}), bf16[4,40,7168]{2,1,0:T(8,128)(2,1)S(1)}, u32[]{:S(2)}, u32[]{:S(2)}) %all-to-all-start.1) | async-done | bytes 2293792 | tf_op jit(solution)/shard_map/all_to_all | solution.py:41
  176.2 0.3 convert_reduce_fusion
  176.5 0.1 fusion.10
  176.7 0.0 collective-permute-done.4
  176.7 1.4 fusion
  (8 shorter events, 0.0 us)
Async XLA Ops:
  6.5 49.2 %all-gather.6.cloned.1.call-start = ((), (), s32[]{:S(2)}) async-start(), calls=%async_computation.3 | async-start | bytes 5160960 | tf_op jit(solution)/shard_map/all_gather | solution.py:21
  7.6 7.7 %copy-start.3 = (f32[64,1]{0,1:T(1,128)S(1)}, f32[64,1]{0,1:T(1,128)}, u32[]{:S(2)}) copy-start(f32[64,1]{0,1:T(1,128)} %param.10) | copy-start | bytes 772
  11.1 78.0 %all-gather.4.cloned.1.call-start = ((), (), s32[]{:S(2)}) async-start(), calls=%async_computation.2 | async-start | bytes 5160960 | tf_op jit(solution)/shard_map/all_gather | solution.py:21
  11.2 29.5 %collective-permute-start = (bf16[40,7168]{1,0:T(8,128)(2,1)S(1)}, bf16[40,7168]{1,0:T(8,128)(2,1)S(1)}, u32[]{:S(2)}, u32[]{:S(2)}) collective-permute-start(bf16[40,7168]{1,0:T(8,128)(2,1)S(1)} %get-tuple-element.27), channel_id=1, source_target_pairs={{0,8},{8,0},{1,9},{9,1},{2,10},{10,2},{3,11},{11,3},{4,12},{12,4},... | collective-permute-start | bytes 1720328 | tf_op jit(solution)/shard_map/ppermute | solution.py:79
  15.6 25.1 %collective-permute-start.1 = (f32[40]{0:T(128)S(1)}, f32[40]{0:T(128)S(1)}, u32[]{:S(2)}, u32[]{:S(2)}) collective-permute-start(f32[40]{0:T(128)S(1)} %get-tuple-element.30), channel_id=1, source_target_pairs={{0,8},{8,0},{1,9},{9,1},{2,10},{10,2},{3,11},{11,3},{4,12},{12,4},... | collective-permute-start | bytes 488 | tf_op jit(solution)/shard_map/ppermute | solution.py:80
  40.7 15.0 %copy-start.2 = (bf16[40,7168]{1,0:T(8,128)(2,1)}, bf16[40,7168]{1,0:T(8,128)(2,1)S(1)}, u32[]{:S(2)}) copy-start(bf16[40,7168]{1,0:T(8,128)(2,1)S(1)} %collective-permute-done) | copy-start | bytes 1720324
  55.8 7.3 %copy-start = (bf16[1,256,7168]{2,1,0:T(8,128)(2,1)S(1)}, bf16[1,256,7168]{2,1,0:T(8,128)(2,1)}, u32[]{:S(2)}) copy-start(bf16[1,256,7168]{2,1,0:T(8,128)(2,1)} %param.13) | copy-start | bytes 11010052
  63.8 4.6 %collective-permute-start.2 = (bf16[160,7168]{1,0:T(8,128)(2,1)S(1)}, bf16[160,7168]{1,0:T(8,128)(2,1)}, u32[]{:S(2)}, u32[]{:S(2)}) collective-permute-start(bf16[160,7168]{1,0:T(8,128)(2,1)S(1)} %convolution_convert_fusion.2), channel_id=1, source_target_pairs={{0,1},{1,0},{2,3},{3,2},{4,5},{5,4},{6,7},{7,6},{8,9},{9,8},{10,11... | collective-permute-start | bytes 6881288 | tf_op jit(solution)/shard_map/ppermute | solution.py:33
  89.2 7.3 %copy-start.1 = (bf16[1,256,7168]{2,1,0:T(8,128)(2,1)S(1)}, bf16[1,256,7168]{2,1,0:T(8,128)(2,1)}, u32[]{:S(2)}) copy-start(bf16[1,256,7168]{2,1,0:T(8,128)(2,1)} %param.13) | copy-start | bytes 11010052
  97.2 4.5 %collective-permute-start.3 = (bf16[160,7168]{1,0:T(8,128)(2,1)S(1)}, bf16[160,7168]{1,0:T(8,128)(2,1)S(1)}, u32[]{:S(2)}, u32[]{:S(2)}) collective-permute-start(bf16[160,7168]{1,0:T(8,128)(2,1)S(1)} %convolution_convert_fusion), channel_id=1, source_target_pairs={{0,1},{1,0},{2,3},{3,2},{4,5},{5,4},{6,7},{7,6},{8,9},{9,8},{10,11... | collective-permute-start | bytes 6881288 | tf_op jit(solution)/shard_map/ppermute | solution.py:33
  133.7 42.4 %all-to-all-start.1 = ((bf16[4,40,7168]{2,1,0:T(8,128)(2,1)}), bf16[4,40,7168]{2,1,0:T(8,128)(2,1)S(1)}, u32[]{:S(2)}, u32[]{:S(2)}) async-start(bf16[4,40,7168]{2,1,0:T(8,128)(2,1)} %bitcast.12), calls=%async_computation.1 | async-start | bytes 4587520 | tf_op jit(solution)/shard_map/all_to_all | solution.py:41
  137.4 39.3 %collective-permute-start.4 = (bf16[40,7168]{1,0:T(8,128)(2,1)S(1)}, bf16[40,7168]{1,0:T(8,128)(2,1)S(1)}, u32[]{:S(2)}, u32[]{:S(2)}) collective-permute-start(bf16[40,7168]{1,0:T(8,128)(2,1)S(1)} %multiply_convert_fusion.1), channel_id=1, source_target_pairs={{0,8},{8,0},{1,9},{9,1},{2,10},{10,2},{3,11},{11,3},{4,12},{12,4},... | collective-permute-start | bytes 1720328 | tf_op jit(solution)/shard_map/ppermute | solution.py:92
Sparse Core Ops, SparseCore 0:
  11.3 44.4 all-gather.5
  57.3 31.8 all-gather.3

commit v19 on v18

--- a/solution.py
+++ b/solution.py
@@ -26,12 +26,12 @@
     cores = lax.axis_size("core")
     count = gathered.shape[0] // (chips * cores)
     width = gathered.shape[1]
-    hidden = slice_hidden(gathered, gate_up_w)
-    halves = hidden.reshape(cores, chips * count, hidden.shape[1])
+    halves = gathered.reshape(cores, chips * count, width)
     core = lax.axis_index("core")
     swap = [(c, (c + 1) % cores) for c in range(cores)]
-    sibling = lax.ppermute(slice_down(halves[(core + 1) % cores], down_w), "core", swap)
-    kept = slice_down(halves[core], down_w)
+    theirs = halves[(core + 1) % cores]
+    sibling = lax.ppermute(slice_down(slice_hidden(theirs, gate_up_w), down_w), "core", swap)
+    kept = slice_down(slice_hidden(halves[core], gate_up_w), down_w)
     kept, sibling = lax.optimization_barrier((kept, sibling))
     paired = (kept.astype(jnp.float32) + sibling.astype(jnp.float32)).astype(jnp.bfloat16)
     return paired.reshape(chips, count, width)

time: 185 us -> 183 us (0.989)
  waiting for transfers between devices: 98 us -> 93.2 us
  local copies, waits for them, and re-layouts: 1.13 us -> 3.27 us
    ppermute x2, waiting for transfers between devices: 4.67 us -> 0.01 us  [expert_parts(): lax.ppermute(slice_down(slice_hidden(theirs, gate_up_w), down_w), 'core',...]
    dot_general x2 -> x4, matrix products: 14.3 us -> 17.5 us  [slice_hidden(): both = jnp.dot(rows, gate_up_w, preferred_element_type=jnp.float32)]
    dot_general x4, matrix products: 5.38 us -> 3.08 us  [slice_down(): jnp.dot(hidden, down_w, preferred_element_type=jnp.float32)]
    unnamed x8 -> x16, local copies, waits for them, and re-layouts: 0.02 us -> 2.16 us
  transfers between devices with their start and end apart: 8 -> 8, of which waited for: 6 -> 4; matrix products, arithmetic and copies ran while one was open for 9% -> 10% of each run, Pallas kernels for 0% -> 0%
where the time goes in v19:
time: 183 us
  waiting for transfers between devices  93.2 us (51%)
  blocking collectives  30.8 us (17%)
  matrix products  24.6 us (13%)
  between operations  13.6 us (7%)
  starting transfers between devices  11 us (6%)
  other arithmetic  6.62 us (4%)
  local copies, waits for them, and re-layouts  3.27 us (2%)
    all_to_all x1, waiting for transfers between devices, chip_sums(): return lax.all_to_all(paired, 'sc', split_axis=0, concat_axis=0, tiled=True)  36.3 us
    all_gather x2, waiting for transfers between devices, gather(): return lax.all_gather(held, ('core', 'sc'), axis=0, tiled=True)  31.8 us
    all_to_all x1, blocking collectives, chip_sums(): return lax.all_to_all(paired, 'sc', split_axis=0, concat_axis=0, tiled=True)  30.8 us
    ppermute x1, waiting for transfers between devices, shards(): lax.ppermute(packed_w[k], 'eg', shift(k))  25 us
    dot_general x4, matrix products, slice_hidden(): both = jnp.dot(rows, gate_up_w, preferred_element_type=jnp.float32)  17.5 us
    convert_element_type x2, other arithmetic, expert_parts(): (kept.astype(jnp.float32) + sibling.astype(jnp.float32)).astype(jnp.bfloa...  4.53 us
    ppermute x1, starting transfers between devices, shards(): away = [lax.ppermute(packed[k], 'eg', shift(k)) for k in range(1, experts)]  4.11 us
  transfers between devices with their start and end apart: 8, of which 4 were waited for; matrix products, arithmetic and copies ran while one was open for 10% of the time, Pallas kernels for 0%

profile of v19, /device:TPU:0, one launch (start us, length us, event | category | flops | bytes accessed | tf_op | source)
XLA Modules:
  0.0 183.0 jit_solution(17742106865376857485)
XLA Ops:
  6.5 2.0 %multiply_reduce_fusion = (f32[64]{0:T(128)S(1)}, f32[64,7168]{1,0:T(8,128)S(1)}) fusion(bf16[64,7168]{1,0:T(8,128)(2,1)} %param.7, s32[64]{0:T(128)} %param.8), kind=kOutput, calls=%fused_computation.30 | convolution fusion | flops 60559296 | bytes 2753024 | tf_op jit(solution)/shard_map/dot_general | solution.py:57
  8.6 0.0 copy-start.4
  8.6 0.7 fusion.52
  9.3 0.1 fusion.37
  9.4 0.1 copy.9
  9.4 0.1 reduce_window_sum.11
  9.5 0.1 fusion.45
  9.6 0.1 copy.8
  9.7 0.5 convolution_convert_fusion.4
  10.2 0.9 slice_bitcast_fusion
  11.1 0.0 all-gather.6.cloned.1.call-update
  11.1 0.0 all-gather.4.cloned.1.call-start
  11.2 4.1 %collective-permute-start = (bf16[40,7168]{1,0:T(8,128)(2,1)S(1)}, bf16[40,7168]{1,0:T(8,128)(2,1)S(1)}, u32[]{:S(2)}, u32[]{:S(2)}) collective-permute-start(bf16[40,7168]{1,0:T(8,128)(2,1)S(1)} %get-tuple-element.27), channel_id=1, source_target_pairs={{0,8},{8,0},{1,9},{9,1},{2,10},{10,2},{3,11},{11,3},{4,12},{12,4},... | collective-permute-start | bytes 1720328 | tf_op jit(solution)/shard_map/ppermute | solution.py:79
  15.3 0.1 fusion.36
  15.4 0.1 copy.10
  15.4 0.1 select_reduce_fusion
  15.6 0.1 collective-permute-start.1
  15.6 25.0 %collective-permute-done.1 = f32[40]{0:T(128)S(1)} collective-permute-done((f32[40]{0:T(128)S(1)}, f32[40]{0:T(128)S(1)}, u32[]{:S(2)}, u32[]{:S(2)}) %collective-permute-start.1) | collective-permute-done | bytes 192 | tf_op jit(solution)/shard_map/ppermute | solution.py:80
  40.7 0.0 collective-permute-done
  40.7 15.0 %all-gather.6.cloned.1.call-done = bf16[1,320,7168]{2,1,0:T(8,128)(2,1)} async-done(((bf16[1,40,7168]{2,1,0:T(8,128)(2,1)}), bf16[1,320,7168]{2,1,0:T(8,128)(2,1)}) %all-gather.6.cloned.1.call-update) | async-done | bytes 4587536 | tf_op jit(solution)/shard_map/all_gather | solution.py:21
  55.7 0.0 all-gather.4.cloned.1.call-update
  55.7 0.0 copy-start
  55.8 5.3 %fusion.9 = f32[160,512]{1,0:T(8,128)S(1)} fusion(bf16[2,160,7168]{2,1,0:T(8,128)(2,1)} %bitcast.53, s32[]{:T(128)S(6)} %select_n.45, bf16[7168,256]{1,0:T(8,128)(2,1)} %bitcast.57, bf16[7168,256]{1,0:T(8,128)(2,1)} %bitcast.61), kind=kOutput, calls=%fused_computation.21 | convolution fusion | flops 1189085184 | bytes 9961476 | tf_op jit(solution)/shard_map/dot_general | solution.py:11
  61.1 0.8 convolution_convert_fusion.2
  61.8 0.3 collective-permute-start.2
  62.2 5.6 %fusion.11 = f32[160,512]{1,0:T(8,128)S(1)} fusion(bf16[2,160,7168]{2,1,0:T(8,128)(2,1)} %bitcast.54, s32[]{:T(128)S(6)} %select_n.43, bf16[7168,256]{1,0:T(8,128)(2,1)} %bitcast.58, bf16[7168,256]{1,0:T(8,128)(2,1)} %bitcast.62), kind=kOutput, calls=%fused_computation.23 | convolution fusion | flops 1189085184 | bytes 9961476 | tf_op jit(solution)/shard_map/dot_general | solution.py:11
  67.8 0.8 convolution_convert_fusion.3
  68.6 0.0 collective-permute-done.2
  68.6 3.8 %add_convert_fusion.1 = bf16[160,7168]{1,0:T(8,128)(2,1)} fusion(bf16[160,7168]{1,0:T(8,128)(2,1)} %collective-permute-done.2, bf16[160,7168]{1,0:T(8,128)(2,1)S(1)} %convolution_convert_fusion.3), kind=kLoop, calls=%fused_computation.12 | loop fusion | flops 4587520 | bytes 6881280 | tf_op jit(solution)/shard_map/convert_element_type | solution.py:36
  72.4 16.8 %all-gather.4.cloned.1.call-done = bf16[320,7168]{1,0:T(8,128)(2,1)} async-done(((bf16[40,7168]{1,0:T(8,128)(2,1)}), bf16[320,7168]{1,0:T(8,128)(2,1)}) %all-gather.4.cloned.1.call-update) | async-done | bytes 4587536 | tf_op jit(solution)/shard_map/all_gather | solution.py:21
  89.2 5.3 %fusion.5 = f32[160,512]{1,0:T(8,128)S(1)} fusion(bf16[2,160,7168]{2,1,0:T(8,128)(2,1)} %bitcast.55, s32[]{:T(128)S(6)} %select_n.45, bf16[7168,256]{1,0:T(8,128)(2,1)} %bitcast.59, bf16[7168,256]{1,0:T(8,128)(2,1)} %bitcast.63), kind=kOutput, calls=%fused_computation.17 | convolution fusion | flops 1189085184 | bytes 9961476 | tf_op jit(solution)/shard_map/dot_general | solution.py:11
  94.5 0.8 convolution_convert_fusion
  95.3 0.3 collective-permute-start.3
  95.6 0.6 copy-done.7
  96.2 1.5 copy-done.5
  97.7 1.3 fusion.7
  99.1 0.8 convolution_convert_fusion.1
  99.9 0.7 add_convert_fusion
  100.6 30.8 %all_to_all.10 = bf16[4,40,7168]{2,1,0:T(8,128)(2,1)S(1)} all-to-all(bf16[4,40,7168]{2,1,0:T(8,128)(2,1)S(1)} %bitcast.50), channel_id=1, replica_groups=mesh['grp'=2,'eg'=2,'sc'=4,'core'=2] {'sc'}, dimensions={0} | all-to-all | bytes 4587520 | tf_op jit(solution)/shard_map/all_to_all | solution.py:41
  131.4 0.4 convert_reduce_fusion.1
  131.7 0.1 multiply_convert_fusion.1
  131.9 3.6 %all-to-all-start.1 = ((bf16[4,40,7168]{2,1,0:T(8,128)(2,1)}), bf16[4,40,7168]{2,1,0:T(8,128)(2,1)S(1)}, u32[]{:S(2)}, u32[]{:S(2)}) async-start(bf16[4,40,7168]{2,1,0:T(8,128)(2,1)} %bitcast.12), calls=%async_computation.1 | async-start | bytes 4587520 | tf_op jit(solution)/shard_map/all_to_all | solution.py:41
  135.5 2.5 %collective-permute-start.4 = (bf16[40,7168]{1,0:T(8,128)(2,1)S(1)}, bf16[40,7168]{1,0:T(8,128)(2,1)S(1)}, u32[]{:S(2)}, u32[]{:S(2)}) collective-permute-start(bf16[40,7168]{1,0:T(8,128)(2,1)S(1)} %multiply_convert_fusion.1), channel_id=1, source_target_pairs={{0,8},{8,0},{1,9},{9,1},{2,10},{10,2},{3,11},{11,3},{4,12},{12,4},... | collective-permute-start | bytes 1720328 | tf_op jit(solution)/shard_map/ppermute | solution.py:92
  138.0 36.3 %all-to-all-done.1 = bf16[4,40,7168]{2,1,0:T(8,128)(2,1)S(1)} async-done(((bf16[4,40,7168]{2,1,0:T(8,128)(2,1)}), bf16[4,40,7168]{2,1,0:T(8,128)(2,1)S(1)}, u32[]{:S(2)}, u32[]{:S(2)}) %all-to-all-start.1) | async-done | bytes 2293792 | tf_op jit(solution)/shard_map/all_to_all | solution.py:41
  174.3 0.3 convert_reduce_fusion
  174.6 0.1 fusion.20
  174.8 0.0 collective-permute-done.4
  174.8 1.4 fusion
  (16 shorter events, 0.0 us)
Async XLA Ops:
  6.5 49.2 %all-gather.6.cloned.1.call-start = ((), (), s32[]{:S(2)}) async-start(), calls=%async_computation.3 | async-start | bytes 5160960 | tf_op jit(solution)/shard_map/all_gather | solution.py:21
  8.6 6.7 %copy-start.4 = (f32[64,1]{0,1:T(1,128)S(1)}, f32[64,1]{0,1:T(1,128)}, u32[]{:S(2)}) copy-start(f32[64,1]{0,1:T(1,128)} %param.10) | copy-start | bytes 772
  11.1 78.1 %all-gather.4.cloned.1.call-start = ((), (), s32[]{:S(2)}) async-start(), calls=%async_computation.2 | async-start | bytes 5160960 | tf_op jit(solution)/shard_map/all_gather | solution.py:21
  11.2 29.5 %collective-permute-start = (bf16[40,7168]{1,0:T(8,128)(2,1)S(1)}, bf16[40,7168]{1,0:T(8,128)(2,1)S(1)}, u32[]{:S(2)}, u32[]{:S(2)}) collective-permute-start(bf16[40,7168]{1,0:T(8,128)(2,1)S(1)} %get-tuple-element.27), channel_id=1, source_target_pairs={{0,8},{8,0},{1,9},{9,1},{2,10},{10,2},{3,11},{11,3},{4,12},{12,4},... | collective-permute-start | bytes 1720328 | tf_op jit(solution)/shard_map/ppermute | solution.py:79
  15.6 25.1 %collective-permute-start.1 = (f32[40]{0:T(128)S(1)}, f32[40]{0:T(128)S(1)}, u32[]{:S(2)}, u32[]{:S(2)}) collective-permute-start(f32[40]{0:T(128)S(1)} %get-tuple-element.30), channel_id=1, source_target_pairs={{0,8},{8,0},{1,9},{9,1},{2,10},{10,2},{3,11},{11,3},{4,12},{12,4},... | collective-permute-start | bytes 488 | tf_op jit(solution)/shard_map/ppermute | solution.py:80
  40.7 15.0 %copy-start.3 = (bf16[40,7168]{1,0:T(8,128)(2,1)}, bf16[40,7168]{1,0:T(8,128)(2,1)S(1)}, u32[]{:S(2)}) copy-start(bf16[40,7168]{1,0:T(8,128)(2,1)S(1)} %collective-permute-done) | copy-start | bytes 1720324
  55.7 5.3 %copy-start = (bf16[1,256,7168]{2,1,0:T(8,128)(2,1)S(1)}, bf16[1,256,7168]{2,1,0:T(8,128)(2,1)}, u32[]{:S(2)}) copy-start(bf16[1,256,7168]{2,1,0:T(8,128)(2,1)} %param.13) | copy-start | bytes 11010052
  61.8 6.7 %collective-permute-start.2 = (bf16[160,7168]{1,0:T(8,128)(2,1)S(1)}, bf16[160,7168]{1,0:T(8,128)(2,1)}, u32[]{:S(2)}, u32[]{:S(2)}) collective-permute-start(bf16[160,7168]{1,0:T(8,128)(2,1)S(1)} %convolution_convert_fusion.2), channel_id=1, source_target_pairs={{0,1},{1,0},{2,3},{3,2},{4,5},{5,4},{6,7},{7,6},{8,9},{9,8},{10,11... | collective-permute-start | bytes 6881288 | tf_op jit(solution)/shard_map/ppermute | solution.py:33
  62.2 5.6 %copy-start.1 = (bf16[1,256,7168]{2,1,0:T(8,128)(2,1)S(1)}, bf16[1,256,7168]{2,1,0:T(8,128)(2,1)}, u32[]{:S(2)}) copy-start(bf16[1,256,7168]{2,1,0:T(8,128)(2,1)} %param.13) | copy-start | bytes 11010052
  89.2 5.3 %copy-start.2 = (bf16[1,256,7168]{2,1,0:T(8,128)(2,1)S(1)}, bf16[1,256,7168]{2,1,0:T(8,128)(2,1)}, u32[]{:S(2)}) copy-start(bf16[1,256,7168]{2,1,0:T(8,128)(2,1)} %param.13) | copy-start | bytes 11010052
  89.2 6.4 %copy-start.6 = (bf16[1,7168,256]{2,1,0:T(8,128)(2,1)S(1)}, bf16[1,7168,256]{2,1,0:T(8,128)(2,1)}, u32[]{:S(2)}) copy-start(bf16[1,7168,256]{2,1,0:T(8,128)(2,1)} %param.12) | copy-start | bytes 11010052
  89.2 7.0 %copy-start.7 = (bf16[1,7168,256]{2,1,0:T(8,128)(2,1)S(1)}, bf16[1,7168,256]{2,1,0:T(8,128)(2,1)}, u32[]{:S(2)}) copy-start(bf16[1,7168,256]{2,1,0:T(8,128)(2,1)} %param.11) | copy-start | bytes 11010052
  94.5 3.2 %copy-start.5 = (bf16[320,7168]{1,0:T(8,128)(2,1)S(1)}, bf16[320,7168]{1,0:T(8,128)(2,1)}, u32[]{:S(2)}) copy-start(bf16[320,7168]{1,0:T(8,128)(2,1)} %all-gather.4.cloned.1.call-done) | copy-start | bytes 13762564
  95.3 4.6 %collective-permute-start.3 = (bf16[160,7168]{1,0:T(8,128)(2,1)S(1)}, bf16[160,7168]{1,0:T(8,128)(2,1)S(1)}, u32[]{:S(2)}, u32[]{:S(2)}) collective-permute-start(bf16[160,7168]{1,0:T(8,128)(2,1)S(1)} %convolution_convert_fusion), channel_id=1, source_target_pairs={{0,1},{1,0},{2,3},{3,2},{4,5},{5,4},{6,7},{7,6},{8,9},{9,8},{10,11... | collective-permute-start | bytes 6881288 | tf_op jit(solution)/shard_map/ppermute | solution.py:33
  131.9 42.4 %all-to-all-start.1 = ((bf16[4,40,7168]{2,1,0:T(8,128)(2,1)}), bf16[4,40,7168]{2,1,0:T(8,128)(2,1)S(1)}, u32[]{:S(2)}, u32[]{:S(2)}) async-start(bf16[4,40,7168]{2,1,0:T(8,128)(2,1)} %bitcast.12), calls=%async_computation.1 | async-start | bytes 4587520 | tf_op jit(solution)/shard_map/all_to_all | solution.py:41
  135.5 39.3 %collective-permute-start.4 = (bf16[40,7168]{1,0:T(8,128)(2,1)S(1)}, bf16[40,7168]{1,0:T(8,128)(2,1)S(1)}, u32[]{:S(2)}, u32[]{:S(2)}) collective-permute-start(bf16[40,7168]{1,0:T(8,128)(2,1)S(1)} %multiply_convert_fusion.1), channel_id=1, source_target_pairs={{0,8},{8,0},{1,9},{9,1},{2,10},{10,2},{3,11},{11,3},{4,12},{12,4},... | collective-permute-start | bytes 1720328 | tf_op jit(solution)/shard_map/ppermute | solution.py:92
Sparse Core Ops, SparseCore 0:
  11.2 44.4 all-gather.5
  57.3 31.8 all-gather.3

commit v20 on v19

--- a/solution.py
+++ b/solution.py
@@ -92,6 +92,9 @@
         lax.ppermute(done[(k - 1) * slots:k * slots], "eg", shift(experts - k))
         for k in range(1, experts)
     ]
+    if picks_row == 1:
+        spot = relative[:, 0] * slots + jnp.take_along_axis(before, relative, axis=1)[:, 0]
+        return jnp.take(jnp.concatenate(home, axis=0), spot, axis=0, mode="clip")
     result = jnp.einsum(
         "tkc,kcd->td",
         place.astype(jnp.bfloat16),

time: 183 us -> 184 us (level)
  local copies, waits for them, and re-layouts: 3.27 us -> 6.13 us
    gather x0 -> x2, local copies, waits for them, and re-layouts: none -> 2.86 us  [the longest x1 2.05 us: shards(): return jnp.take(jnp.concatenate(home, axis=0), spot, axis=0, mode='clip')]
  transfers between devices with their start and end apart: 8 -> 8, of which waited for: 4 -> 4; matrix products, arithmetic and copies ran while one was open for 10% -> 11% of each run, Pallas kernels for 0% -> 0%
where the time goes in v20:
time: 184 us
  waiting for transfers between devices  92.3 us (50%)
  blocking collectives  30.8 us (17%)
  matrix products  23.2 us (13%)
  between operations  13.6 us (7%)
  starting transfers between devices  11 us (6%)
  other arithmetic  6.72 us (4%)
  local copies, waits for them, and re-layouts  6.13 us (3%)
    all_to_all x1, waiting for transfers between devices, chip_sums(): return lax.all_to_all(paired, 'sc', split_axis=0, concat_axis=0, tiled=True)  35.5 us
    all_gather x2, waiting for transfers between devices, gather(): return lax.all_gather(held, ('core', 'sc'), axis=0, tiled=True)  31.8 us
    all_to_all x1, blocking collectives, chip_sums(): return lax.all_to_all(paired, 'sc', split_axis=0, concat_axis=0, tiled=True)  30.8 us
    ppermute x1, waiting for transfers between devices, shards(): lax.ppermute(packed_w[k], 'eg', shift(k))  25 us
    dot_general x4, matrix products, slice_hidden(): both = jnp.dot(rows, gate_up_w, preferred_element_type=jnp.float32)  17.5 us
    convert_element_type x2, other arithmetic, expert_parts(): (kept.astype(jnp.float32) + sibling.astype(jnp.float32)).astype(jnp.bfloa...  4.53 us
    ppermute x1, starting transfers between devices, shards(): away = [lax.ppermute(packed[k], 'eg', shift(k)) for k in range(1, experts)]  4.11 us
  transfers between devices with their start and end apart: 8, of which 4 were waited for; matrix products, arithmetic and copies ran while one was open for 11% of the time, Pallas kernels for 0%

profile of v20, /device:TPU:0, one launch (start us, length us, event | category | flops | bytes accessed | tf_op | source)
XLA Modules:
  0.0 183.8 jit_solution(9741134030490948885)
XLA Ops:
  6.5 2.0 %multiply_reduce_fusion = (f32[64]{0:T(128)S(1)}, f32[64,7168]{1,0:T(8,128)S(1)}) fusion(bf16[64,7168]{1,0:T(8,128)(2,1)} %param.7, s32[64]{0:T(128)} %param.8), kind=kOutput, calls=%fused_computation.30 | convolution fusion | flops 60559296 | bytes 2753024 | tf_op jit(solution)/shard_map/dot_general | solution.py:57
  8.6 0.0 copy-start.4
  8.6 0.7 fusion.46
  9.3 0.1 fusion.32
  9.4 0.1 copy.12
  9.4 0.1 reduce_window_sum.11
  9.5 0.1 fusion.37
  9.6 0.1 copy.11
  9.7 0.5 convolution_convert_fusion.4
  10.2 0.9 slice_bitcast_fusion
  11.1 0.0 all-gather.6.cloned.1.call-update
  11.1 0.0 all-gather.4.cloned.1.call-start
  11.2 4.1 %collective-permute-start = (bf16[40,7168]{1,0:T(8,128)(2,1)S(1)}, bf16[40,7168]{1,0:T(8,128)(2,1)S(1)}, u32[]{:S(2)}, u32[]{:S(2)}) collective-permute-start(bf16[40,7168]{1,0:T(8,128)(2,1)S(1)} %get-tuple-element.29), channel_id=1, source_target_pairs={{0,8},{8,0},{1,9},{9,1},{2,10},{10,2},{3,11},{11,3},{4,12},{12,4},... | collective-permute-start | bytes 1720328 | tf_op jit(solution)/shard_map/ppermute | solution.py:79
  15.3 0.1 fusion.31
  15.4 0.1 copy.13
  15.4 0.1 select_reduce_fusion
  15.6 0.1 collective-permute-start.1
  15.6 25.0 %collective-permute-done.1 = f32[40]{0:T(128)S(1)} collective-permute-done((f32[40]{0:T(128)S(1)}, f32[40]{0:T(128)S(1)}, u32[]{:S(2)}, u32[]{:S(2)}) %collective-permute-start.1) | collective-permute-done | bytes 192 | tf_op jit(solution)/shard_map/ppermute | solution.py:80
  40.7 0.0 collective-permute-done
  40.7 15.0 %all-gather.6.cloned.1.call-done = bf16[1,320,7168]{2,1,0:T(8,128)(2,1)} async-done(((bf16[1,40,7168]{2,1,0:T(8,128)(2,1)}), bf16[1,320,7168]{2,1,0:T(8,128)(2,1)}) %all-gather.6.cloned.1.call-update) | async-done | bytes 4587536 | tf_op jit(solution)/shard_map/all_gather | solution.py:21
  55.7 0.0 all-gather.4.cloned.1.call-update
  55.7 0.0 copy-start
  55.8 5.3 %fusion.8 = f32[160,512]{1,0:T(8,128)S(1)} fusion(bf16[2,160,7168]{2,1,0:T(8,128)(2,1)} %bitcast.57, s32[]{:T(128)S(6)} %select_n.52, bf16[7168,256]{1,0:T(8,128)(2,1)} %bitcast.61, bf16[7168,256]{1,0:T(8,128)(2,1)} %bitcast.65), kind=kOutput, calls=%fused_computation.21 | convolution fusion | flops 1189085184 | bytes 9961476 | tf_op jit(solution)/shard_map/dot_general | solution.py:11
  61.1 0.8 convolution_convert_fusion.2
  61.8 0.3 collective-permute-start.2
  62.2 5.6 %fusion.10 = f32[160,512]{1,0:T(8,128)S(1)} fusion(bf16[2,160,7168]{2,1,0:T(8,128)(2,1)} %bitcast.58, s32[]{:T(128)S(6)} %select_n.50, bf16[7168,256]{1,0:T(8,128)(2,1)} %bitcast.62, bf16[7168,256]{1,0:T(8,128)(2,1)} %bitcast.66), kind=kOutput, calls=%fused_computation.23 | convolution fusion | flops 1189085184 | bytes 9961476 | tf_op jit(solution)/shard_map/dot_general | solution.py:11
  67.8 0.8 convolution_convert_fusion.3
  68.6 3.8 %add_convert_fusion.1 = bf16[160,7168]{1,0:T(8,128)(2,1)} fusion(bf16[160,7168]{1,0:T(8,128)(2,1)} %collective-permute-done.2, bf16[160,7168]{1,0:T(8,128)(2,1)S(1)} %convolution_convert_fusion.3), kind=kLoop, calls=%fused_computation.12 | loop fusion | flops 4587520 | bytes 6881280 | tf_op jit(solution)/shard_map/convert_element_type | solution.py:36
  72.4 16.8 %all-gather.4.cloned.1.call-done = bf16[320,7168]{1,0:T(8,128)(2,1)} async-done(((bf16[40,7168]{1,0:T(8,128)(2,1)}), bf16[320,7168]{1,0:T(8,128)(2,1)}) %all-gather.4.cloned.1.call-update) | async-done | bytes 4587536 | tf_op jit(solution)/shard_map/all_gather | solution.py:21
  89.2 5.3 %fusion.4 = f32[160,512]{1,0:T(8,128)S(1)} fusion(bf16[2,160,7168]{2,1,0:T(8,128)(2,1)} %bitcast.59, s32[]{:T(128)S(6)} %select_n.52, bf16[7168,256]{1,0:T(8,128)(2,1)} %bitcast.63, bf16[7168,256]{1,0:T(8,128)(2,1)} %bitcast.67), kind=kOutput, calls=%fused_computation.17 | convolution fusion | flops 1189085184 | bytes 9961476 | tf_op jit(solution)/shard_map/dot_general | solution.py:11
  94.5 0.8 convolution_convert_fusion
  95.3 0.3 collective-permute-start.3
  95.6 0.6 copy-done.7
  96.2 1.5 copy-done.5
  97.7 1.3 fusion.6
  99.1 0.8 convolution_convert_fusion.1
  99.9 0.7 add_convert_fusion
  100.6 30.8 %all_to_all.10 = bf16[4,40,7168]{2,1,0:T(8,128)(2,1)S(1)} all-to-all(bf16[4,40,7168]{2,1,0:T(8,128)(2,1)S(1)} %bitcast.52), channel_id=1, replica_groups=mesh['grp'=2,'eg'=2,'sc'=4,'core'=2] {'sc'}, dimensions={0} | all-to-all | bytes 4587520 | tf_op jit(solution)/shard_map/all_to_all | solution.py:41
  131.4 0.4 convert_reduce_fusion.1
  131.7 0.1 multiply_convert_fusion.2
  131.9 3.6 %all-to-all-start.1 = ((bf16[4,40,7168]{2,1,0:T(8,128)(2,1)}), bf16[4,40,7168]{2,1,0:T(8,128)(2,1)S(1)}, u32[]{:S(2)}, u32[]{:S(2)}) async-start(bf16[4,40,7168]{2,1,0:T(8,128)(2,1)} %bitcast.12), calls=%async_computation.1 | async-start | bytes 4587520 | tf_op jit(solution)/shard_map/all_to_all | solution.py:41
  135.6 0.8 gather_fusion.1
  136.4 2.5 %collective-permute-start.4 = (bf16[40,7168]{1,0:T(8,128)(2,1)S(1)}, bf16[40,7168]{1,0:T(8,128)(2,1)S(1)}, u32[]{:S(2)}, u32[]{:S(2)}) collective-permute-start(bf16[40,7168]{1,0:T(8,128)(2,1)S(1)} %multiply_convert_fusion.2), channel_id=1, source_target_pairs={{0,8},{8,0},{1,9},{9,1},{2,10},{10,2},{3,11},{11,3},{4,12},{12,4},... | collective-permute-start | bytes 1720328 | tf_op jit(solution)/shard_map/ppermute | solution.py:92
  138.8 35.5 %all-to-all-done.1 = bf16[4,40,7168]{2,1,0:T(8,128)(2,1)S(1)} async-done(((bf16[4,40,7168]{2,1,0:T(8,128)(2,1)}), bf16[4,40,7168]{2,1,0:T(8,128)(2,1)S(1)}, u32[]{:S(2)}, u32[]{:S(2)}) %all-to-all-start.1) | async-done | bytes 2293792 | tf_op jit(solution)/shard_map/all_to_all | solution.py:41
  174.3 0.3 convert_reduce_fusion
  174.7 0.1 multiply_convert_fusion.1
  174.8 0.1 pad_maximum_fusion.1
  174.9 2.0 %gather_fusion = bf16[64,7168]{1,0:T(8,128)(2,1)} fusion(bf16[80,7168]{1,0:T(8,128)(2,1)S(1)} %pad_maximum_fusion.1, s32[1024]{0:T(1024)S(1)} %pad_clamp_fusion), kind=kCustom, calls=%fused_computation | custom fusion | bytes 1835264 | tf_op jit(solution)/shard_map/jit(_take)/gather | solution.py:97
  (23 shorter events, 0.1 us)
Async XLA Ops:
  6.5 49.2 %all-gather.6.cloned.1.call-start = ((), (), s32[]{:S(2)}) async-start(), calls=%async_computation.3 | async-start | bytes 5160960 | tf_op jit(solution)/shard_map/all_gather | solution.py:21
  8.6 6.7 %copy-start.4 = (f32[64,1]{0,1:T(1,128)S(1)}, f32[64,1]{0,1:T(1,128)}, u32[]{:S(2)}) copy-start(f32[64,1]{0,1:T(1,128)} %param.10) | copy-start | bytes 772
  11.1 78.1 %all-gather.4.cloned.1.call-start = ((), (), s32[]{:S(2)}) async-start(), calls=%async_computation.2 | async-start | bytes 5160960 | tf_op jit(solution)/shard_map/all_gather | solution.py:21
  11.2 29.5 %collective-permute-start = (bf16[40,7168]{1,0:T(8,128)(2,1)S(1)}, bf16[40,7168]{1,0:T(8,128)(2,1)S(1)}, u32[]{:S(2)}, u32[]{:S(2)}) collective-permute-start(bf16[40,7168]{1,0:T(8,128)(2,1)S(1)} %get-tuple-element.29), channel_id=1, source_target_pairs={{0,8},{8,0},{1,9},{9,1},{2,10},{10,2},{3,11},{11,3},{4,12},{12,4},... | collective-permute-start | bytes 1720328 | tf_op jit(solution)/shard_map/ppermute | solution.py:79
  15.6 25.1 %collective-permute-start.1 = (f32[40]{0:T(128)S(1)}, f32[40]{0:T(128)S(1)}, u32[]{:S(2)}, u32[]{:S(2)}) collective-permute-start(f32[40]{0:T(128)S(1)} %get-tuple-element.32), channel_id=1, source_target_pairs={{0,8},{8,0},{1,9},{9,1},{2,10},{10,2},{3,11},{11,3},{4,12},{12,4},... | collective-permute-start | bytes 488 | tf_op jit(solution)/shard_map/ppermute | solution.py:80
  40.7 15.0 %copy-start.3 = (bf16[40,7168]{1,0:T(8,128)(2,1)}, bf16[40,7168]{1,0:T(8,128)(2,1)S(1)}, u32[]{:S(2)}) copy-start(bf16[40,7168]{1,0:T(8,128)(2,1)S(1)} %collective-permute-done) | copy-start | bytes 1720324
  55.7 5.3 %copy-start = (bf16[1,256,7168]{2,1,0:T(8,128)(2,1)S(1)}, bf16[1,256,7168]{2,1,0:T(8,128)(2,1)}, u32[]{:S(2)}) copy-start(bf16[1,256,7168]{2,1,0:T(8,128)(2,1)} %param.13) | copy-start | bytes 11010052
  61.8 6.7 %collective-permute-start.2 = (bf16[160,7168]{1,0:T(8,128)(2,1)S(1)}, bf16[160,7168]{1,0:T(8,128)(2,1)}, u32[]{:S(2)}, u32[]{:S(2)}) collective-permute-start(bf16[160,7168]{1,0:T(8,128)(2,1)S(1)} %convolution_convert_fusion.2), channel_id=1, source_target_pairs={{0,1},{1,0},{2,3},{3,2},{4,5},{5,4},{6,7},{7,6},{8,9},{9,8},{10,11... | collective-permute-start | bytes 6881288 | tf_op jit(solution)/shard_map/ppermute | solution.py:33
  62.2 5.6 %copy-start.1 = (bf16[1,256,7168]{2,1,0:T(8,128)(2,1)S(1)}, bf16[1,256,7168]{2,1,0:T(8,128)(2,1)}, u32[]{:S(2)}) copy-start(bf16[1,256,7168]{2,1,0:T(8,128)(2,1)} %param.13) | copy-start | bytes 11010052
  89.2 5.3 %copy-start.2 = (bf16[1,256,7168]{2,1,0:T(8,128)(2,1)S(1)}, bf16[1,256,7168]{2,1,0:T(8,128)(2,1)}, u32[]{:S(2)}) copy-start(bf16[1,256,7168]{2,1,0:T(8,128)(2,1)} %param.13) | copy-start | bytes 11010052
  89.2 6.4 %copy-start.6 = (bf16[1,7168,256]{2,1,0:T(8,128)(2,1)S(1)}, bf16[1,7168,256]{2,1,0:T(8,128)(2,1)}, u32[]{:S(2)}) copy-start(bf16[1,7168,256]{2,1,0:T(8,128)(2,1)} %param.12) | copy-start | bytes 11010052
  89.2 7.0 %copy-start.7 = (bf16[1,7168,256]{2,1,0:T(8,128)(2,1)S(1)}, bf16[1,7168,256]{2,1,0:T(8,128)(2,1)}, u32[]{:S(2)}) copy-start(bf16[1,7168,256]{2,1,0:T(8,128)(2,1)} %param.11) | copy-start | bytes 11010052
  94.5 3.2 %copy-start.5 = (bf16[320,7168]{1,0:T(8,128)(2,1)S(1)}, bf16[320,7168]{1,0:T(8,128)(2,1)}, u32[]{:S(2)}) copy-start(bf16[320,7168]{1,0:T(8,128)(2,1)} %all-gather.4.cloned.1.call-done) | copy-start | bytes 13762564
  95.3 4.6 %collective-permute-start.3 = (bf16[160,7168]{1,0:T(8,128)(2,1)S(1)}, bf16[160,7168]{1,0:T(8,128)(2,1)S(1)}, u32[]{:S(2)}, u32[]{:S(2)}) collective-permute-start(bf16[160,7168]{1,0:T(8,128)(2,1)S(1)} %convolution_convert_fusion), channel_id=1, source_target_pairs={{0,1},{1,0},{2,3},{3,2},{4,5},{5,4},{6,7},{7,6},{8,9},{9,8},{10,11... | collective-permute-start | bytes 6881288 | tf_op jit(solution)/shard_map/ppermute | solution.py:33
  131.9 42.5 %all-to-all-start.1 = ((bf16[4,40,7168]{2,1,0:T(8,128)(2,1)}), bf16[4,40,7168]{2,1,0:T(8,128)(2,1)S(1)}, u32[]{:S(2)}, u32[]{:S(2)}) async-start(bf16[4,40,7168]{2,1,0:T(8,128)(2,1)} %bitcast.12), calls=%async_computation.1 | async-start | bytes 4587520 | tf_op jit(solution)/shard_map/all_to_all | solution.py:41
  136.4 38.4 %collective-permute-start.4 = (bf16[40,7168]{1,0:T(8,128)(2,1)S(1)}, bf16[40,7168]{1,0:T(8,128)(2,1)S(1)}, u32[]{:S(2)}, u32[]{:S(2)}) collective-permute-start(bf16[40,7168]{1,0:T(8,128)(2,1)S(1)} %multiply_convert_fusion.2), channel_id=1, source_target_pairs={{0,8},{8,0},{1,9},{9,1},{2,10},{10,2},{3,11},{11,3},{4,12},{12,4},... | collective-permute-start | bytes 1720328 | tf_op jit(solution)/shard_map/ppermute | solution.py:92
Sparse Core Ops, SparseCore 0:
  11.2 44.4 all-gather.5
  57.3 31.8 all-gather.3

commit v21 on v19

--- a/solution.py
+++ b/solution.py
@@ -8,8 +8,9 @@
 
 
 def slice_hidden(rows, gate_up_w):
-    both = jnp.dot(rows, gate_up_w, preferred_element_type=jnp.float32)
-    gate, upper = jnp.split(both, 2, axis=1)
+    gate_w, up_w = gate_up_w
+    gate = jnp.dot(rows, gate_w, preferred_element_type=jnp.float32)
+    upper = jnp.dot(rows, up_w, preferred_element_type=jnp.float32)
     return (jax.nn.silu(gate) * upper).astype(jnp.bfloat16)
 
 
@@ -71,7 +72,7 @@
         "tkc,td->kcd", place.astype(jnp.bfloat16), normed, preferred_element_type=jnp.float32
     ).astype(jnp.bfloat16)
     packed_w = jnp.sum(jnp.where(place, weight_te[:, :, None], 0.0), axis=0)
-    weights = (jnp.concatenate([w_gate[0], w_up[0]], axis=1), w_down[0])
+    weights = ((w_gate[0], w_up[0]), w_down[0])
 
     def shift(k):
         return [(g, (g + k) % experts) for g in range(experts)]

time: 183 us -> 196 us (1.071)
  matrix products: 24.6 us -> 47 us
  waiting for transfers between devices: 93.2 us -> 84.2 us
  local copies, waits for them, and re-layouts: 3.27 us -> 1.13 us
    dot_general x4, matrix products: 3.08 us -> 29 us  [slice_down(): jnp.dot(hidden, down_w, preferred_element_type=jnp.float32)]
    all_gather x2, waiting for transfers between devices: 31.8 us -> 22.8 us  [gather(): return lax.all_gather(held, ('core', 'sc'), axis=0, tiled=True)]
    dot_general x4, matrix products: 17.5 us -> 14 us  [slice_hidden(): gate = jnp.dot(rows, gate_w, preferred_element_type=jnp.float32)]
    unnamed x16 -> x4, local copies, waits for them, and re-layouts: 2.16 us -> 0.01 us
  transfers between devices with their start and end apart: 8 -> 8, of which waited for: 4 -> 4; matrix products, arithmetic and copies ran while one was open for 10% -> 18% of each run, Pallas kernels for 0% -> 0%
where the time goes in v21:
time: 196 us
  waiting for transfers between devices  84.2 us (43%)
  matrix products  47 us (24%)
  blocking collectives  30.8 us (16%)
  between operations  13.6 us (7%)
  starting transfers between devices  10.8 us (6%)
  other arithmetic  8.27 us (4%)
    all_to_all x1, waiting for transfers between devices, chip_sums(): return lax.all_to_all(paired, 'sc', split_axis=0, concat_axis=0, tiled=True)  36.3 us
    all_to_all x1, blocking collectives, chip_sums(): return lax.all_to_all(paired, 'sc', split_axis=0, concat_axis=0, tiled=True)  30.8 us
    dot_general x4, matrix products, slice_down(): jnp.dot(hidden, down_w, preferred_element_type=jnp.float32)  29 us
    ppermute x1, waiting for transfers between devices, shards(): lax.ppermute(packed_w[k], 'eg', shift(k))  25.1 us
    all_gather x2, waiting for transfers between devices, gather(): return lax.all_gather(held, ('core', 'sc'), axis=0, tiled=True)  22.8 us
    dot_general x4, matrix products, slice_hidden(): gate = jnp.dot(rows, gate_w, preferred_element_type=jnp.float32)  14 us
    convert_element_type x2, other arithmetic, expert_parts(): (kept.astype(jnp.float32) + sibling.astype(jnp.float32)).astype(jnp.bfloa...  6.2 us
    ppermute x1, starting transfers between devices, shards(): away = [lax.ppermute(packed[k], 'eg', shift(k)) for k in range(1, experts)]  4.09 us
  transfers between devices with their start and end apart: 8, of which 4 were waited for; matrix products, arithmetic and copies ran while one was open for 18% of the time, Pallas kernels for 0%

profile of v21, /device:TPU:0, one launch (start us, length us, event | category | flops | bytes accessed | tf_op | source)
XLA Modules:
  0.0 195.8 jit_solution(9224504442899464147)
XLA Ops:
  6.5 0.0 all-gather.6.cloned.1.call-start
  6.5 2.1 %multiply_reduce_fusion = (f32[64]{0:T(128)S(1)}, f32[64,7168]{1,0:T(8,128)S(1)}) fusion(bf16[64,7168]{1,0:T(8,128)(2,1)} %param.7, s32[64]{0:T(128)} %param.8), kind=kOutput, calls=%fused_computation.49 | convolution fusion | flops 60559296 | bytes 2753024 | tf_op jit(solution)/shard_map/dot_general | solution.py:58
  8.6 0.0 copy-start.1
  8.6 0.7 fusion.148
  9.3 0.1 fusion.125
  9.4 0.1 copy.9
  9.5 0.1 reduce_window_sum.11
  9.6 0.1 fusion.133
  9.6 0.1 copy.8
  9.7 0.5 convolution_convert_fusion.4
  10.2 0.9 slice_bitcast_fusion
  11.1 0.0 all-gather.6.cloned.1.call-update
  11.2 0.0 all-gather.4.cloned.1.call-start
  11.2 4.1 %collective-permute-start = (bf16[40,7168]{1,0:T(8,128)(2,1)S(1)}, bf16[40,7168]{1,0:T(8,128)(2,1)S(1)}, u32[]{:S(2)}, u32[]{:S(2)}) collective-permute-start(bf16[40,7168]{1,0:T(8,128)(2,1)S(1)} %get-tuple-element.27), channel_id=1, source_target_pairs={{0,8},{8,0},{1,9},{9,1},{2,10},{10,2},{3,11},{11,3},{4,12},{12,4},... | collective-permute-start | bytes 1720328 | tf_op jit(solution)/shard_map/ppermute | solution.py:80
  15.3 0.0 copy-done.1
  15.3 0.1 fusion.124
  15.4 0.1 copy.10
  15.5 0.1 select_reduce_fusion
  15.6 0.1 collective-permute-start.1
  15.7 25.1 %collective-permute-done.1 = f32[40]{0:T(128)S(1)} collective-permute-done((f32[40]{0:T(128)S(1)}, f32[40]{0:T(128)S(1)}, u32[]{:S(2)}, u32[]{:S(2)}) %collective-permute-start.1) | collective-permute-done | bytes 192 | tf_op jit(solution)/shard_map/ppermute | solution.py:81
  40.7 0.0 collective-permute-done
  40.7 15.0 %all-gather.6.cloned.1.call-done = bf16[1,320,7168]{2,1,0:T(8,128)(2,1)} async-done(((bf16[1,40,7168]{2,1,0:T(8,128)(2,1)}), bf16[1,320,7168]{2,1,0:T(8,128)(2,1)}) %all-gather.6.cloned.1.call-update) | async-done | bytes 4587536 | tf_op jit(solution)/shard_map/all_gather | solution.py:22
  55.7 0.0 all-gather.4.cloned.1.call-update
  55.8 3.5 %fusion.17 = f32[160,256]{1,0:T(8,128)S(1)} fusion(bf16[1,7168,256]{2,1,0:T(8,128)(2,1)} %param.11, bf16[2,160,7168]{2,1,0:T(8,128)(2,1)} %bitcast.122, s32[]{:T(128)S(6)} %select_n.45), kind=kOutput, calls=%fused_computation.28 | convolution fusion | flops 587202560 | bytes 6127620 | tf_op jit(solution)/shard_map/dot_general | solution.py:12
  59.3 7.9 %convolution_convert_fusion.2 = bf16[160,7168]{1,0:T(8,128)(2,1)} fusion(bf16[1,256,7168]{2,1,0:T(8,128)(2,1)} %param.13, bf16[1,7168,256]{2,1,0:T(8,128)(2,1)} %param.12, bf16[2,160,7168]{2,1,0:T(8,128)(2,1)} %bitcast.123, s32[]{:T(128)S(6)} %select_n.45, f32[160,256]{1,0:T(8,128)S(1)} %fusion.17), kind=kOutput, calls=%fused_computation.2 | convolution fusion | flops 1175797760 | bytes 12091396 | tf_op jit(solution)/shard_map/dot_general | solution.py:18
  67.2 0.3 collective-permute-start.2
  67.5 3.5 %fusion.19 = f32[160,256]{1,0:T(8,128)S(1)} fusion(bf16[1,7168,256]{2,1,0:T(8,128)(2,1)} %param.11, bf16[2,160,7168]{2,1,0:T(8,128)(2,1)} %bitcast.124, s32[]{:T(128)S(6)} %select_n.43), kind=kOutput, calls=%fused_computation.30 | convolution fusion | flops 587202560 | bytes 6127620 | tf_op jit(solution)/shard_map/dot_general | solution.py:12
  71.0 6.6 %convolution_convert_fusion.3 = bf16[160,7168]{1,0:T(8,128)(2,1)S(1)} fusion(bf16[1,256,7168]{2,1,0:T(8,128)(2,1)} %param.13, bf16[1,7168,256]{2,1,0:T(8,128)(2,1)} %param.12, bf16[2,160,7168]{2,1,0:T(8,128)(2,1)} %bitcast.125, s32[]{:T(128)S(6)} %select_n.43, f32[160,256]{1,0:T(8,128)S(1)} %fusion.19), kind=kOutput, calls=%fused_computation.3 | convolution fusion | flops 1175797760 | bytes 12091396 | tf_op jit(solution)/shard_map/dot_general | solution.py:18
  77.6 0.0 collective-permute-done.2
  77.6 3.8 %add_convert_fusion.1 = bf16[160,7168]{1,0:T(8,128)(2,1)} fusion(bf16[160,7168]{1,0:T(8,128)(2,1)} %collective-permute-done.2, bf16[160,7168]{1,0:T(8,128)(2,1)S(1)} %convolution_convert_fusion.3), kind=kLoop, calls=%fused_computation.11 | loop fusion | flops 4587520 | bytes 6881280 | tf_op jit(solution)/shard_map/convert_element_type | solution.py:37
  81.4 7.8 %all-gather.4.cloned.1.call-done = bf16[320,7168]{1,0:T(8,128)(2,1)} async-done(((bf16[40,7168]{1,0:T(8,128)(2,1)}), bf16[320,7168]{1,0:T(8,128)(2,1)}) %all-gather.4.cloned.1.call-update) | async-done | bytes 4587536 | tf_op jit(solution)/shard_map/all_gather | solution.py:22
  89.2 3.5 %fusion.13 = f32[160,256]{1,0:T(8,128)S(1)} fusion(bf16[1,7168,256]{2,1,0:T(8,128)(2,1)} %param.11, bf16[2,160,7168]{2,1,0:T(8,128)(2,1)} %bitcast.126, s32[]{:T(128)S(6)} %select_n.45), kind=kOutput, calls=%fused_computation.24 | convolution fusion | flops 587202560 | bytes 6127620 | tf_op jit(solution)/shard_map/dot_general | solution.py:12
  92.7 7.9 %convolution_convert_fusion = bf16[160,7168]{1,0:T(8,128)(2,1)} fusion(bf16[1,256,7168]{2,1,0:T(8,128)(2,1)} %param.13, bf16[1,7168,256]{2,1,0:T(8,128)(2,1)} %param.12, bf16[2,160,7168]{2,1,0:T(8,128)(2,1)} %bitcast.127, s32[]{:T(128)S(6)} %select_n.45, f32[160,256]{1,0:T(8,128)S(1)} %fusion.13), kind=kOutput, calls=%fused_computation | convolution fusion | flops 1175797760 | bytes 12091396 | tf_op jit(solution)/shard_map/dot_general | solution.py:18
  100.6 0.2 collective-permute-start.3
  100.8 3.5 %fusion.15 = f32[160,256]{1,0:T(8,128)S(1)} fusion(bf16[1,7168,256]{2,1,0:T(8,128)(2,1)} %param.11, bf16[2,160,7168]{2,1,0:T(8,128)(2,1)} %bitcast.128, s32[]{:T(128)S(6)} %select_n.43), kind=kOutput, calls=%fused_computation.26 | convolution fusion | flops 587202560 | bytes 6127620 | tf_op jit(solution)/shard_map/dot_general | solution.py:12
  104.3 6.6 %convolution_convert_fusion.1 = bf16[160,7168]{1,0:T(8,128)(2,1)S(1)} fusion(bf16[1,256,7168]{2,1,0:T(8,128)(2,1)} %param.13, bf16[1,7168,256]{2,1,0:T(8,128)(2,1)} %param.12, bf16[2,160,7168]{2,1,0:T(8,128)(2,1)} %bitcast.129, s32[]{:T(128)S(6)} %select_n.43, f32[160,256]{1,0:T(8,128)S(1)} %fusion.15), kind=kOutput, calls=%fused_computation.1 | convolution fusion | flops 1175797760 | bytes 12091396 | tf_op jit(solution)/shard_map/dot_general | solution.py:18
  110.9 0.0 collective-permute-done.3
  110.9 2.3 %add_convert_fusion = bf16[160,7168]{1,0:T(8,128)(2,1)S(1)} fusion(bf16[160,7168]{1,0:T(8,128)(2,1)} %collective-permute-done.3, bf16[160,7168]{1,0:T(8,128)(2,1)S(1)} %convolution_convert_fusion.1), kind=kLoop, calls=%fused_computation.10 | loop fusion | flops 4587520 | bytes 6881280 | tf_op jit(solution)/shard_map/convert_element_type | solution.py:37
  113.3 30.8 %all_to_all.10 = bf16[4,40,7168]{2,1,0:T(8,128)(2,1)S(1)} all-to-all(bf16[4,40,7168]{2,1,0:T(8,128)(2,1)S(1)} %bitcast.130), channel_id=1, replica_groups=mesh['grp'=2,'eg'=2,'sc'=4,'core'=2] {'sc'}, dimensions={0} | all-to-all | bytes 4587520 | tf_op jit(solution)/shard_map/all_to_all | solution.py:42
  144.1 0.4 convert_reduce_fusion.1
  144.5 0.1 multiply_convert_fusion.1
  144.6 3.6 %all-to-all-start.1 = ((bf16[4,40,7168]{2,1,0:T(8,128)(2,1)}), bf16[4,40,7168]{2,1,0:T(8,128)(2,1)S(1)}, u32[]{:S(2)}, u32[]{:S(2)}) async-start(bf16[4,40,7168]{2,1,0:T(8,128)(2,1)} %bitcast.12), calls=%async_computation.1 | async-start | bytes 4587520 | tf_op jit(solution)/shard_map/all_to_all | solution.py:42
  148.3 2.5 %collective-permute-start.4 = (bf16[40,7168]{1,0:T(8,128)(2,1)S(1)}, bf16[40,7168]{1,0:T(8,128)(2,1)S(1)}, u32[]{:S(2)}, u32[]{:S(2)}) collective-permute-start(bf16[40,7168]{1,0:T(8,128)(2,1)S(1)} %multiply_convert_fusion.1), channel_id=1, source_target_pairs={{0,8},{8,0},{1,9},{9,1},{2,10},{10,2},{3,11},{11,3},{4,12},{12,4},... | collective-permute-start | bytes 1720328 | tf_op jit(solution)/shard_map/ppermute | solution.py:93
  150.8 36.3 %all-to-all-done.1 = bf16[4,40,7168]{2,1,0:T(8,128)(2,1)S(1)} async-done(((bf16[4,40,7168]{2,1,0:T(8,128)(2,1)}), bf16[4,40,7168]{2,1,0:T(8,128)(2,1)S(1)}, u32[]{:S(2)}, u32[]{:S(2)}) %all-to-all-start.1) | async-done | bytes 2293792 | tf_op jit(solution)/shard_map/all_to_all | solution.py:42
  187.1 0.3 convert_reduce_fusion
  187.4 0.1 fusion.40
  187.6 0.0 collective-permute-done.4
  187.6 1.4 fusion
  (4 shorter events, 0.0 us)
Async XLA Ops:
  6.5 49.2 %all-gather.6.cloned.1.call-start = ((), (), s32[]{:S(2)}) async-start(), calls=%async_computation.3 | async-start | bytes 5160960 | tf_op jit(solution)/shard_map/all_gather | solution.py:22
  8.6 6.7 %copy-start.1 = (f32[64,1]{0,1:T(1,128)S(1)}, f32[64,1]{0,1:T(1,128)}, u32[]{:S(2)}) copy-start(f32[64,1]{0,1:T(1,128)} %param.10) | copy-start | bytes 772
  11.2 78.0 %all-gather.4.cloned.1.call-start = ((), (), s32[]{:S(2)}) async-start(), calls=%async_computation.2 | async-start | bytes 5160960 | tf_op jit(solution)/shard_map/all_gather | solution.py:22
  11.2 29.5 %collective-permute-start = (bf16[40,7168]{1,0:T(8,128)(2,1)S(1)}, bf16[40,7168]{1,0:T(8,128)(2,1)S(1)}, u32[]{:S(2)}, u32[]{:S(2)}) collective-permute-start(bf16[40,7168]{1,0:T(8,128)(2,1)S(1)} %get-tuple-element.27), channel_id=1, source_target_pairs={{0,8},{8,0},{1,9},{9,1},{2,10},{10,2},{3,11},{11,3},{4,12},{12,4},... | collective-permute-start | bytes 1720328 | tf_op jit(solution)/shard_map/ppermute | solution.py:80
  15.6 25.1 %collective-permute-start.1 = (f32[40]{0:T(128)S(1)}, f32[40]{0:T(128)S(1)}, u32[]{:S(2)}, u32[]{:S(2)}) collective-permute-start(f32[40]{0:T(128)S(1)} %get-tuple-element.30), channel_id=1, source_target_pairs={{0,8},{8,0},{1,9},{9,1},{2,10},{10,2},{3,11},{11,3},{4,12},{12,4},... | collective-permute-start | bytes 488 | tf_op jit(solution)/shard_map/ppermute | solution.py:81
  40.7 15.0 %copy-start = (bf16[40,7168]{1,0:T(8,128)(2,1)}, bf16[40,7168]{1,0:T(8,128)(2,1)S(1)}, u32[]{:S(2)}) copy-start(bf16[40,7168]{1,0:T(8,128)(2,1)S(1)} %collective-permute-done) | copy-start | bytes 1720324
  67.2 10.4 %collective-permute-start.2 = (bf16[160,7168]{1,0:T(8,128)(2,1)}, bf16[160,7168]{1,0:T(8,128)(2,1)}, u32[]{:S(2)}, u32[]{:S(2)}) collective-permute-start(bf16[160,7168]{1,0:T(8,128)(2,1)} %convolution_convert_fusion.2), channel_id=1, source_target_pairs={{0,1},{1,0},{2,3},{3,2},{4,5},{5,4},{6,7},{7,6},{8,9},{9,8},{10,11... | collective-permute-start | bytes 6881288 | tf_op jit(solution)/shard_map/ppermute | solution.py:34
  100.6 10.4 %collective-permute-start.3 = (bf16[160,7168]{1,0:T(8,128)(2,1)}, bf16[160,7168]{1,0:T(8,128)(2,1)}, u32[]{:S(2)}, u32[]{:S(2)}) collective-permute-start(bf16[160,7168]{1,0:T(8,128)(2,1)} %convolution_convert_fusion), channel_id=1, source_target_pairs={{0,1},{1,0},{2,3},{3,2},{4,5},{5,4},{6,7},{7,6},{8,9},{9,8},{10,11... | collective-permute-start | bytes 6881288 | tf_op jit(solution)/shard_map/ppermute | solution.py:34
  144.6 42.5 %all-to-all-start.1 = ((bf16[4,40,7168]{2,1,0:T(8,128)(2,1)}), bf16[4,40,7168]{2,1,0:T(8,128)(2,1)S(1)}, u32[]{:S(2)}, u32[]{:S(2)}) async-start(bf16[4,40,7168]{2,1,0:T(8,128)(2,1)} %bitcast.12), calls=%async_computation.1 | async-start | bytes 4587520 | tf_op jit(solution)/shard_map/all_to_all | solution.py:42
  148.3 39.3 %collective-permute-start.4 = (bf16[40,7168]{1,0:T(8,128)(2,1)S(1)}, bf16[40,7168]{1,0:T(8,128)(2,1)S(1)}, u32[]{:S(2)}, u32[]{:S(2)}) collective-permute-start(bf16[40,7168]{1,0:T(8,128)(2,1)S(1)} %multiply_convert_fusion.1), channel_id=1, source_target_pairs={{0,8},{8,0},{1,9},{9,1},{2,10},{10,2},{3,11},{11,3},{4,12},{12,4},... | collective-permute-start | bytes 1720328 | tf_op jit(solution)/shard_map/ppermute | solution.py:93
Sparse Core Ops, SparseCore 0:
  11.3 44.4 all-gather.5
  57.3 31.8 all-gather.3
